TPU v7x, 32 devices: a whole 2x2x4 slice. The times are simulated.
32 devices in a mesh: dp: 2 (over y), mp: 16 (over z, x, core).
Axes of the slice: x: 2, y: 2, z: 4, core: 2. Of those that a mesh axis runs over, the one named last changes fastest.
Arguments:
- queries: bfloat16 [2048, 1024], P(('dp', 'mp')), may hold values from -16 to 16
- hidden: bfloat16 [2048, 2048], P(('dp', 'mp')), may hold values from -6 to 6
- kv_pages: bfloat16 [192, 16, 2, 1024], P(('dp', 'mp')), may hold values from -8 to 8
- page_table: int32 [2, 96], replicated, may hold values from 0 to 191, as said below
- cache_len: int32 [2], replicated, may hold values from 1 to 512, as said below
- deal_table: int32 [2, 16], P('dp'), may hold values from 0 to 15, as said below
- out_weight: bfloat16 [1024, 2048], P('dp', 'mp'), may hold values from -0.1875 to 0.1875
- norm_gain: float32 [2048], replicated, may hold values from 0.1 to 1.9
- expert_ids: int32 [2048, 6], P(('dp', 'mp')), may hold values from 0 to 15, all different within a row; in each aligned block of 64 rows (0 to 63, 64 to 127, ...) at most 32 rows name the same one
- expert_gates: float32 [2048, 6], P(('dp', 'mp')), may hold values from 0.05 to 0.5
- experts_in: bfloat16 [16, 2048, 1408], P('mp', 'dp'), may hold values from -0.125 to 0.125
- experts_out: bfloat16 [16, 704, 2048], P('mp', None, 'dp'), may hold values from -0.21875 to 0.21875
Outputs:
- mixed: bfloat16 [2048, 2048], P(('dp', 'mp'))
Inputs may be any that keep to these rules, and one draw needn't show every extreme that they name: `deal_table`: each row is an ordering of 0 to 15: every piece of the 1 request of row d is held by one device of that row. For request r = d + j, the entries page_table[r, l] over all l are exactly the pages (d * 16 + m) * 6 + j * 6 + k for m < 16, k < 6, each once, in an order given by the draw. `cache_len`: some request has 512 cached tokens and some has 1. `expert_ids`: the 6 ids of a token differ; among the 64 tokens of one device no expert is named more than 32 times, and in some device one expert is named exactly 32 times.
All inputs are finite; a program needn't handle non-finite values.
Results may differ from a plain program's by a relative error of at most 0.0095.
Values may be sent and summed in bfloat16 or wider, within the bound.
No kernel may reach another device: no remote copies, remote signals or barrier semaphores. Data moves between devices by JAX's collectives and lax.ppermute only.
A program may use at most 128 MiB of HBM per device.

v0:
```python
import math

import jax
import jax.numpy as jnp
from jax import lax
from jax.sharding import PartitionSpec as P

HEADS = 8
HD = 128
TOPK = 6
PAGE = 16


epsilon = 1e-06


def attend(q_rows, key_rows, value_rows, key_pos, first_pos):
    q_count = q_rows.shape[0]
    heads_q = q_rows.reshape(q_count, HEADS, HD)
    scores = jnp.einsum("qhd,khd->hqk", heads_q, key_rows, preferred_element_type=jnp.float32) * (
        1.0 / math.sqrt(HD)
    )
    query_pos = first_pos + jnp.arange(q_count, dtype=jnp.int32)
    allowed = key_pos[None, :] <= query_pos[:, None]
    scores = jnp.where(allowed[None, :, :], scores, -1e30)
    row_max = jnp.max(scores, axis=2, keepdims=True)
    weights = jnp.exp(scores - row_max)
    weights_bf = (weights / jnp.sum(weights, axis=2, keepdims=True)).astype(jnp.bfloat16)
    blended = jnp.einsum("hqk,khd->qhd", weights_bf, value_rows, preferred_element_type=jnp.float32)
    return blended.reshape(q_count, HEADS * HD).astype(jnp.bfloat16)


def on_device(
    queries,
    hidden,
    kv_pages,
    page_table,
    cache_len,
    deal_table,
    out_weight,
    norm_gain,
    expert_ids,
    expert_gates,
    experts_in,
    experts_out,
):
    n_mp = lax.axis_size("mp")
    row_index = lax.axis_index("dp")
    column = lax.axis_index("mp")
    q_count = queries.shape[0]
    width = queries.shape[1]
    d_model = hidden.shape[1]
    req_row = n_mp // n_mp
    page_share = page_table.shape[1] // n_mp
    pages_dev = kv_pages.shape[0]
    deal_row = deal_table[0]
    piece_id = deal_row[column]
    local_req = piece_id // n_mp
    request = row_index * req_row + local_req
    first_pos = cache_len[request] + piece_id % n_mp * q_count
    page_count = page_table.shape[1]
    by_request = kv_pages.reshape(req_row, page_share, PAGE, 2, width)
    outgoing = jnp.take(by_request, deal_row // n_mp, axis=0)
    arrived = lax.all_to_all(outgoing, "mp", split_axis=0, concat_axis=0, tiled=True)
    slot_ids = jnp.arange(n_mp * page_share, dtype=jnp.int32)
    physical = (
        (row_index * n_mp + slot_ids // page_share) * pages_dev
        + local_req * page_share
        + slot_ids % page_share
    )
    table_row = page_table[request]
    matches = table_row[None, :] == physical[:, None]
    logical = jnp.sum(
        jnp.where(matches, jnp.arange(page_count, dtype=jnp.int32)[None, :], 0), axis=1
    )
    key_pos = (logical[:, None] * PAGE + jnp.arange(PAGE, dtype=jnp.int32)[None, :]).reshape(-1)
    key_rows = arrived[:, :, :, 0, :].reshape(-1, HEADS, HD)
    value_rows = arrived[:, :, :, 1, :].reshape(-1, HEADS, HD)
    attended = attend(queries, key_rows, value_rows, key_pos, first_pos)
    wo_rows, gate_up, down = (
        lax.all_gather(out_weight, "dp", axis=0, tiled=True),
        lax.all_gather(experts_in, "dp", axis=1, tiled=True),
        lax.all_gather(experts_out, "dp", axis=2, tiled=True),
    )
    projected = jnp.dot(
        attended,
        lax.all_gather(wo_rows, "mp", axis=1, tiled=True),
        preferred_element_type=jnp.float32,
    )
    resid_f = (hidden.astype(jnp.float32) + projected).astype(jnp.bfloat16).astype(jnp.float32)
    mean_square = jnp.mean(resid_f * resid_f, axis=1, keepdims=True)
    normed = (resid_f * lax.rsqrt(mean_square + epsilon) * norm_gain[None, :]).astype(jnp.bfloat16)
    capacity = min(q_count, q_count * TOPK * 4 // (3 * n_mp))
    flat_ids = expert_ids.reshape(-1)
    one_hot = (flat_ids[:, None] == jnp.arange(n_mp, dtype=jnp.int32)[None, :]).astype(jnp.int32)
    slot_of = jnp.sum(jnp.cumsum(one_hot, axis=0) * one_hot, axis=1) - 1
    target = flat_ids * capacity + slot_of
    token_of_pair = jnp.arange(q_count * TOPK, dtype=jnp.int32) // TOPK
    sending = (
        jnp.zeros((n_mp * capacity, d_model), jnp.bfloat16)
        .at[target]
        .set(jnp.take(normed, token_of_pair, axis=0))
    )
    sending = sending.reshape(n_mp, capacity, d_model)
    ff_width = down.shape[1]
    received = lax.all_to_all(sending, "mp", split_axis=0, concat_axis=0, tiled=True)
    flat_rows = received.reshape(-1, d_model)
    gate_vals = jnp.dot(flat_rows, gate_up[0], preferred_element_type=jnp.float32)
    act = (jax.nn.silu(gate_vals[:, :ff_width]) * gate_vals[:, ff_width:]).astype(jnp.bfloat16)
    outcome = jnp.dot(act, down[0], preferred_element_type=jnp.float32).astype(jnp.bfloat16)
    results = lax.all_to_all(
        outcome.reshape(received.shape), "mp", split_axis=0, concat_axis=0, tiled=True
    )
    picked = jnp.take(results.reshape(-1, d_model), target, axis=0)
    weighted = picked.astype(jnp.float32) * expert_gates.reshape(-1)[:, None]
    expert_sum = jnp.sum(weighted.reshape(q_count, TOPK, d_model), axis=1)
    return (resid_f + expert_sum).astype(jnp.bfloat16)


def solution(mesh):
    in_specs = (
        P(("dp", "mp"), None),
        P(("dp", "mp"), None),
        P(("dp", "mp"), None, None, None),
        P(),
        P(),
        P("dp", None),
        P("dp", "mp"),
        P(),
        P(("dp", "mp"), None),
        P(("dp", "mp"), None),
        P("mp", "dp", None),
        P("mp", None, "dp"),
    )
    out_specs = P(("dp", "mp"), None)
    return jax.shard_map(
        on_device, mesh=mesh, in_specs=in_specs, out_specs=out_specs, check_vma=False
    )
```

profile of v0, /device:TPU:11, one launch (start us, length us, event | category | flops | bytes accessed | tf_op | source)
XLA Modules:
  0.0 351.9 jit_solution(14371258071019248741)
XLA Ops:
  6.5 1.1 copy.46
  7.7 0.7 compare_and_fusion.2
  8.3 3.3 broadcast_select_fusion
  11.6 6.7 %all-to-all-start = ((bf16[16,6,16,2,1024]{4,2,1,3,0:T(8,128)(2,1)}), bf16[16,6,16,2,1024]{4,2,1,3,0:T(8,128)(2,1)}, u32[]{:S(2)}, u32[]{:S(2)}) async-start(bf16[16,6,16,2,1024]{4,2,1,3,0:T(8,128)(2,1)} %broadcast_select_fusion), calls=%async_computation | async-start | bytes 12582912 | tf_op jit(solution)/shard_map/all_to_all | solution.py:64
  18.4 5.5 %all_gather.12 = bf16[1024,128]{1,0:T(8,128)(2,1)} all-gather(bf16[512,128]{1,0:T(8,128)(2,1)S(1)} %copy-done.3), channel_id=1, replica_groups=mesh['dp'=2,'mp'=16] {'dp'}, dimensions={0}, use_global_device_ids=true | all-gather | bytes 393216 | tf_op jit(solution)/shard_map/all_gather | solution.py:81
  24.0 0.7 all-gather.6.cloned.1.call-update
  24.7 0.6 constant_dynamic-slice_fusion
  27.9 0.1 copy.51
  28.0 0.1 eq.49
  28.1 0.1 reshape.313
  28.3 0.2 select_reduce_fusion
  28.5 0.1 iota_add_fusion
  28.6 0.1 add.233
  28.7 0.6 dynamic_slice.11
  29.3 0.9 reduce-window.6
  30.1 0.2 slice_reduce_fusion
  30.4 0.1 copy.56
  30.5 0.1 mul.106
  31.3 0.6 compare_and_fusion.1
  31.9 0.1 fusion.33
  32.0 0.1 broadcast_compare_fusion
  32.1 149.1 %all-to-all-done = bf16[16,6,16,2,1024]{4,2,1,3,0:T(8,128)(2,1)} async-done(((bf16[16,6,16,2,1024]{4,2,1,3,0:T(8,128)(2,1)}), bf16[16,6,16,2,1024]{4,2,1,3,0:T(8,128)(2,1)}, u32[]{:S(2)}, u32[]{:S(2)}) %all-to-all-start) | async-done | bytes 6291488 | tf_op jit(solution)/shard_map/all_to_all | solution.py:64
  181.3 3.6 %fusion.47 = (bf16[16,6,16,1,1024]{4,2,1,3,0:T(8,128)(2,1)S(1)}, bf16[16,6,16,1,1024]{4,2,1,3,0:T(8,128)(2,1)S(1)}) fusion(bf16[16,6,16,2,1024]{4,2,1,3,0:T(8,128)(2,1)} %all-to-all-done), kind=kLoop, calls=%fused_computation.98 | loop fusion | bytes 12582912 | tf_op jit(solution)/shard_map/slice | solution.py:77
  184.9 0.8 copy.61
  185.7 0.8 copy.62
  186.5 1.4 fusion.5
  188.0 1.7 copy-done.1
  189.6 1.2 fusion.48
  190.9 5.0 %fusion.21 = bf16[8,8,8,128]{3,2,1,0:T(8,128)(2,1)} fusion(bf16[1536,8,128]{2,1,0:T(8,128)(2,1)S(1)} %bitcast.77, f32[8,64]{1,0:T(8,128)} %fusion.48, f32[8,64,1536]{2,1,0:T(8,128)} %copy-done.1), kind=kOutput, calls=%fused_computation.29 | convolution fusion | flops 203753472 | bytes 6424576 | tf_op jit(solution)/shard_map/hqk,khd->qhd/dot_general | solution.py:29
  195.9 3.2 multiply_reduce_fusion.1
  199.1 0.1 multiply_convert_fusion
  199.3 9.6 %scatter_custom_fusion = bf16[512,2048]{1,0:T(8,128)(2,1)} fusion(s32[384]{0:T(512)S(1)} %fusion.38, pred[384]{0:T(512)(128)(4,1)S(1)} %copy-done.7, bf16[]{:T(256)} %constant.135.clone.1, bf16[]{:T(256)} %constant.120.clone.1, bf16[64,2048]{1,0:T(8,128)(2,1)S(1)} %multiply_convert_fusion, s32[1024]{0:T(1024)S(1)} %pad_clamp_fusion.1), kind=kCustom, calls=%fused_computation.24 | custom fusion | flops 786432 | bytes 2363908 | tf_op jit(solution)/shard_map/scatter | solution.py:102
  208.9 4.6 %all-to-all-start.1 = ((bf16[16,32,2048]{2,1,0:T(8,128)(2,1)}), bf16[16,32,2048]{2,1,0:T(8,128)(2,1)S(1)}, u32[]{:S(2)}, u32[]{:S(2)}) async-start(bf16[16,32,2048]{2,1,0:T(8,128)(2,1)} %bitcast.7), calls=%async_computation.1 | async-start | bytes 4194304 | tf_op jit(solution)/shard_map/all_to_all | solution.py:106
  213.5 0.7 all-gather.8.cloned.1.call-update
  214.2 18.9 %all-gather.6.cloned.1.call-done = bf16[1,2048,1408]{2,1,0:T(8,128)(2,1)} async-done(((bf16[1,1024,1408]{2,1,0:T(8,128)(2,1)}), bf16[1,2048,1408]{2,1,0:T(8,128)(2,1)}) %all-gather.6.cloned.1.call-update) | async-done | bytes 5767184 | tf_op jit(solution)/shard_map/all_gather | solution.py:82
  233.2 28.2 %all-to-all-done.1 = bf16[16,32,2048]{2,1,0:T(8,128)(2,1)S(1)} async-done(((bf16[16,32,2048]{2,1,0:T(8,128)(2,1)}), bf16[16,32,2048]{2,1,0:T(8,128)(2,1)S(1)}, u32[]{:S(2)}, u32[]{:S(2)}) %all-to-all-start.1) | async-done | bytes 2097184 | tf_op jit(solution)/shard_map/all_to_all | solution.py:106
  261.3 7.7 %fusion.1 = f32[512,1408]{1,0:T(8,128)} fusion(bf16[512,2048]{1,0:T(8,128)(2,1)S(1)} %bitcast.78, bf16[1,2048,1408]{2,1,0:T(8,128)(2,1)} %all-gather.6.cloned.1.call-done), kind=kOutput, calls=%fused_computation.5 | convolution fusion | flops 2952790016 | bytes 10747904 | tf_op jit(solution)/shard_map/dot_general | solution.py:108
  269.0 7.8 %all-gather.8.cloned.1.call-done = bf16[1,704,2048]{2,1,0:T(8,128)(2,1)} async-done(((bf16[1,704,1024]{2,1,0:T(8,128)(2,1)}), bf16[1,704,2048]{2,1,0:T(8,128)(2,1)}) %all-gather.8.cloned.1.call-update) | async-done | bytes 2883600 | tf_op jit(solution)/shard_map/all_gather | solution.py:83
  276.7 5.9 %convolution_convert_fusion = bf16[512,2048]{1,0:T(8,128)(2,1)} fusion(bf16[1,704,2048]{2,1,0:T(8,128)(2,1)} %all-gather.8.cloned.1.call-done, f32[512,1408]{1,0:T(8,128)} %fusion.1), kind=kOutput, calls=%fused_computation.17 | convolution fusion | flops 1479606272 | bytes 8126464 | tf_op jit(solution)/shard_map/dot_general | solution.py:110
  282.7 6.5 %all-to-all-start.2 = ((bf16[16,32,2048]{2,1,0:T(8,128)(2,1)}), bf16[16,32,2048]{2,1,0:T(8,128)(2,1)S(1)}, u32[]{:S(2)}, u32[]{:S(2)}) async-start(bf16[16,32,2048]{2,1,0:T(8,128)(2,1)} %bitcast.79), calls=%async_computation.2 | async-start | bytes 4194304 | tf_op jit(solution)/shard_map/all_to_all | solution.py:111
  289.2 0.1 sub.47
  289.4 0.1 copy.55
  289.5 0.1 copy.57
  289.6 47.0 %all-to-all-done.2 = bf16[16,32,2048]{2,1,0:T(8,128)(2,1)S(1)} async-done(((bf16[16,32,2048]{2,1,0:T(8,128)(2,1)}), bf16[16,32,2048]{2,1,0:T(8,128)(2,1)S(1)}, u32[]{:S(2)}, u32[]{:S(2)}) %all-to-all-start.2) | async-done | bytes 2097184 | tf_op jit(solution)/shard_map/all_to_all | solution.py:111
  336.6 3.1 gather_fusion
  339.7 2.5 gather.17
  342.2 2.4 multiply_reduce_fusion
  344.6 0.8 add_convert_fusion
  (41 shorter events, 0.4 us)
Async XLA Ops:
  6.5 180.0 %copy-start = (bf16[64,1024]{1,0:T(8,128)(2,1)S(1)}, bf16[64,1024]{1,0:T(8,128)(2,1)}, u32[]{:S(2)}) copy-start(bf16[64,1024]{1,0:T(8,128)(2,1)} %param.12) | copy-start | bytes 393220
  11.6 6.8 %copy-start.3 = (bf16[512,128]{1,0:T(8,128)(2,1)S(1)}, bf16[512,128]{1,0:T(8,128)(2,1)}, u32[]{:S(2)}) copy-start(bf16[512,128]{1,0:T(8,128)(2,1)} %param.18) | copy-start | bytes 393220
  11.6 169.7 %all-to-all-start = ((bf16[16,6,16,2,1024]{4,2,1,3,0:T(8,128)(2,1)}), bf16[16,6,16,2,1024]{4,2,1,3,0:T(8,128)(2,1)}, u32[]{:S(2)}, u32[]{:S(2)}) async-start(bf16[16,6,16,2,1024]{4,2,1,3,0:T(8,128)(2,1)} %broadcast_select_fusion), calls=%async_computation | async-start | bytes 12582912 | tf_op jit(solution)/shard_map/all_to_all | solution.py:64
  18.3 6.4 %copy-start.9 = (s32[1,16]{1,0:T(1,128)S(1)}, s32[1,16]{1,0:T(1,128)}, u32[]{:S(2)}) copy-start(s32[1,16]{1,0:T(1,128)} %param.17) | copy-start | bytes 196
  18.3 9.6 %copy-start.4 = (s32[64,6]{0,1:T(8,128)S(1)}, s32[64,6]{0,1:T(8,128)}, u32[]{:S(2)}) copy-start(s32[64,6]{0,1:T(8,128)} %param.20) | copy-start | bytes 4612
  18.3 10.0 %copy-start.8 = (s32[2,96]{1,0:T(2,128)S(1)}, s32[2,96]{1,0:T(2,128)}, u32[]{:S(2)}) copy-start(s32[2,96]{1,0:T(2,128)} %param.15) | copy-start | bytes 2308
  18.3 10.4 %copy-start.10 = (s32[2]{0:T(128)S(1)}, s32[2]{0:T(128)}, u32[]{:S(2)}) copy-start(s32[2]{0:T(128)} %param.16) | copy-start | bytes 28
  18.3 177.6 %all-gather.4.cloned.1.call-start = ((), (), s32[]{:S(2)}) async-start(), calls=%async_computation.3 | async-start | bytes 4456448 | tf_op jit(solution)/shard_map/all_gather | solution.py:87
  23.9 209.3 %all-gather.6.cloned.1.call-start = ((), (), s32[]{:S(2)}) async-start(), calls=%async_computation.4 | async-start | bytes 8650752 | tf_op jit(solution)/shard_map/all_gather | solution.py:82
  188.0 1.7 copy-start.1
  190.9 5.0 %copy-start.2 = (bf16[64,2048]{1,0:T(8,128)(2,1)S(1)}, bf16[64,2048]{1,0:T(8,128)(2,1)}, u32[]{:S(2)}) copy-start(bf16[64,2048]{1,0:T(8,128)(2,1)} %param.13) | copy-start | bytes 786436
  195.9 3.3 copy-start.5
  195.9 3.4 copy-start.7
  208.9 52.4 %all-to-all-start.1 = ((bf16[16,32,2048]{2,1,0:T(8,128)(2,1)}), bf16[16,32,2048]{2,1,0:T(8,128)(2,1)S(1)}, u32[]{:S(2)}, u32[]{:S(2)}) async-start(bf16[16,32,2048]{2,1,0:T(8,128)(2,1)} %bitcast.7), calls=%async_computation.1 | async-start | bytes 4194304 | tf_op jit(solution)/shard_map/all_to_all | solution.py:106
  213.5 63.2 %all-gather.8.cloned.1.call-start = ((), (), s32[]{:S(2)}) async-start(), calls=%async_computation.5 | async-start | bytes 4325376 | tf_op jit(solution)/shard_map/all_gather | solution.py:83
  282.7 6.9 %copy-start.6 = (f32[64,6]{0,1:T(8,128)S(1)}, f32[64,6]{0,1:T(8,128)}, u32[]{:S(2)}) copy-start(f32[64,6]{0,1:T(8,128)} %param.21) | copy-start | bytes 4612
  282.7 53.9 %all-to-all-start.2 = ((bf16[16,32,2048]{2,1,0:T(8,128)(2,1)}), bf16[16,32,2048]{2,1,0:T(8,128)(2,1)S(1)}, u32[]{:S(2)}, u32[]{:S(2)}) async-start(bf16[16,32,2048]{2,1,0:T(8,128)(2,1)} %bitcast.79), calls=%async_computation.2 | async-start | bytes 4194304 | tf_op jit(solution)/shard_map/all_to_all | solution.py:111
Sparse Core Ops, SparseCore 0:
  24.0 131.1 all-gather.3
  156.8 76.3 all-gather.5
  234.7 41.9 all-gather.7
where the time goes:
time: 352 us
  waiting for transfers between devices  252 us (72%)
  matrix products  23.3 us (7%)
  other arithmetic  20.1 us (6%)
  starting transfers between devices  17.9 us (5%)
  between operations  16.7 us (5%)
  local copies, waits for them, and re-layouts  16.1 us (5%)
  blocking collectives  5.51 us (2%)
    all_to_all x1, waiting for transfers between devices, on_device(): lax.all_to_all(outgoing, 'mp', split_axis=0, concat_axis=0, tiled=True)  149 us
    all_to_all x1, waiting for transfers between devices, on_device(): lax.all_to_all(outcome.reshape(received.shape), 'mp', split_axis=0, conca...  47 us
    all_to_all x1, waiting for transfers between devices, on_device(): lax.all_to_all(sending, 'mp', split_axis=0, concat_axis=0, tiled=True)  28.2 us
    all_gather x1, waiting for transfers between devices, on_device(): lax.all_gather(experts_in, 'dp', axis=1, tiled=True)  18.9 us
    scatter x1, other arithmetic, on_device(): sending = jnp.zeros((n_mp * capacity, d_model), jnp.bfloat16).at[target]....  9.64 us
    all_gather x1, waiting for transfers between devices, on_device(): lax.all_gather(experts_out, 'dp', axis=2, tiled=True)  7.75 us
    dot_general x1, matrix products, on_device(): jnp.dot(flat_rows, gate_up[0], preferred_element_type=jnp.float32)  7.66 us
  transfers between devices with their start and end apart: 6, of which 5 were waited for; matrix products, arithmetic and copies ran while one was open for 11% of the time, Pallas kernels for 0%

commit v1 on v0

v1 whole, which is shorter than its diff:
```python
import math

import jax
import jax.numpy as jnp
from jax import lax
from jax.sharding import PartitionSpec as P

HEADS = 8
HD = 128
TOPK = 6
PAGE = 16


epsilon = 1e-06


def attend_head(q_rows, key_rows, value_rows, key_pos, query_pos):
    scores = jnp.dot(q_rows, key_rows.T, preferred_element_type=jnp.float32) * (1.0 / math.sqrt(HD))
    allowed = key_pos[None, :] <= query_pos[:, None]
    scores = jnp.where(allowed, scores, -1e30)
    row_max = jnp.max(scores, axis=1, keepdims=True)
    weights = jnp.exp(scores - row_max)
    weights_bf = (weights / jnp.sum(weights, axis=1, keepdims=True)).astype(jnp.bfloat16)
    blended = jnp.dot(weights_bf, value_rows, preferred_element_type=jnp.float32)
    return blended.astype(jnp.bfloat16)


def swap_dp(x):
    return lax.ppermute(x, "dp", [(0, 1), (1, 0)])


def on_device(
    queries,
    hidden,
    kv_pages,
    page_table,
    cache_len,
    deal_table,
    out_weight,
    norm_gain,
    expert_ids,
    expert_gates,
    experts_in,
    experts_out,
):
    n_mp = lax.axis_size("mp")
    n_dp = lax.axis_size("dp")
    row_index = lax.axis_index("dp")
    column = lax.axis_index("mp")
    q_count = queries.shape[0]
    width = queries.shape[1]
    d_model = hidden.shape[1]
    heads = width // HD
    groups = n_mp // heads
    sub = q_count // groups
    my_head = column % heads
    my_group = column // heads
    page_share = page_table.shape[1] // n_mp
    pages_dev = kv_pages.shape[0]
    deal_row = deal_table[0]
    request = row_index
    page_count = page_table.shape[1]

    q_out = queries.reshape(sub, groups, heads, HD).transpose(1, 2, 0, 3).reshape(n_mp, sub, HD)
    q_in = lax.all_to_all(q_out, "mp", split_axis=0, concat_axis=0, tiled=True)
    first_pos = cache_len[request] + deal_row % n_mp * q_count
    query_pos = (
        first_pos[:, None] + jnp.arange(sub, dtype=jnp.int32)[None, :] * groups + my_group
    ).reshape(-1)

    kv_heads = kv_pages.reshape(pages_dev, PAGE, 2, heads, HD).transpose(3, 0, 1, 2, 4)
    kv_out = jnp.tile(kv_heads, (groups, 1, 1, 1, 1))
    arrived = lax.all_to_all(kv_out, "mp", split_axis=0, concat_axis=0, tiled=True)
    slot_ids = jnp.arange(n_mp * page_share, dtype=jnp.int32)
    physical = (row_index * n_mp + slot_ids // page_share) * pages_dev + slot_ids % page_share
    table_row = page_table[request]
    matches = table_row[None, :] == physical[:, None]
    logical = jnp.sum(
        jnp.where(matches, jnp.arange(page_count, dtype=jnp.int32)[None, :], 0), axis=1
    )
    key_pos = (logical[:, None] * PAGE + jnp.arange(PAGE, dtype=jnp.int32)[None, :]).reshape(-1)
    key_rows = arrived[:, :, :, 0, :].reshape(-1, HD)
    value_rows = arrived[:, :, :, 1, :].reshape(-1, HD)
    blended = attend_head(q_in.reshape(-1, HD), key_rows, value_rows, key_pos, query_pos)
    back = lax.all_to_all(blended.reshape(n_mp, sub, HD), "mp", split_axis=0, concat_axis=0, tiled=True)
    attended = back.reshape(groups, heads, sub, HD).transpose(2, 0, 1, 3).reshape(q_count, width)

    wo_rows = lax.all_gather(out_weight, "dp", axis=0, tiled=True)
    projected = jnp.dot(
        attended,
        lax.all_gather(wo_rows, "mp", axis=1, tiled=True),
        preferred_element_type=jnp.float32,
    )
    resid_f = (hidden.astype(jnp.float32) + projected).astype(jnp.bfloat16).astype(jnp.float32)
    mean_square = jnp.mean(resid_f * resid_f, axis=1, keepdims=True)
    normed = (resid_f * lax.rsqrt(mean_square + epsilon) * norm_gain[None, :]).astype(jnp.bfloat16)
    capacity = min(q_count, q_count * TOPK * 4 // (3 * n_mp))
    flat_ids = expert_ids.reshape(-1)
    one_hot = (flat_ids[:, None] == jnp.arange(n_mp, dtype=jnp.int32)[None, :]).astype(jnp.int32)
    slot_of = jnp.sum(jnp.cumsum(one_hot, axis=0) * one_hot, axis=1) - 1
    target = flat_ids * capacity + slot_of
    token_of_pair = jnp.arange(q_count * TOPK, dtype=jnp.int32) // TOPK
    sending = (
        jnp.zeros((n_mp * capacity, d_model), jnp.bfloat16)
        .at[target]
        .set(jnp.take(normed, token_of_pair, axis=0))
    )
    sending = sending.reshape(n_mp, capacity, d_model)
    ff_width = experts_out.shape[1]
    received = lax.all_to_all(sending, "mp", split_axis=0, concat_axis=0, tiled=True)
    flat_rows = received.reshape(-1, d_model)
    if n_dp == 2:
        half_in = experts_in.shape[1]
        in_other = swap_dp(experts_in)
        out_other = swap_dp(experts_out)
        rows_mine = lax.dynamic_slice_in_dim(flat_rows, row_index * half_in, half_in, axis=1)
        rows_other = lax.dynamic_slice_in_dim(flat_rows, (1 - row_index) * half_in, half_in, axis=1)
        gate_vals = jnp.dot(rows_mine, experts_in[0], preferred_element_type=jnp.float32) + jnp.dot(
            rows_other, in_other[0], preferred_element_type=jnp.float32
        )
        act = (jax.nn.silu(gate_vals[:, :ff_width]) * gate_vals[:, ff_width:]).astype(jnp.bfloat16)
        part_mine = jnp.dot(act, experts_out[0], preferred_element_type=jnp.float32).astype(jnp.bfloat16)
        part_other = jnp.dot(act, out_other[0], preferred_element_type=jnp.float32).astype(jnp.bfloat16)
        outcome = jnp.where(
            row_index == 0,
            jnp.concatenate([part_mine, part_other], axis=1),
            jnp.concatenate([part_other, part_mine], axis=1),
        )
    else:
        gate_up = lax.all_gather(experts_in, "dp", axis=1, tiled=True)
        down = lax.all_gather(experts_out, "dp", axis=2, tiled=True)
        gate_vals = jnp.dot(flat_rows, gate_up[0], preferred_element_type=jnp.float32)
        act = (jax.nn.silu(gate_vals[:, :ff_width]) * gate_vals[:, ff_width:]).astype(jnp.bfloat16)
        outcome = jnp.dot(act, down[0], preferred_element_type=jnp.float32).astype(jnp.bfloat16)
    results = lax.all_to_all(
        outcome.reshape(received.shape), "mp", split_axis=0, concat_axis=0, tiled=True
    )
    picked = jnp.take(results.reshape(-1, d_model), target, axis=0)
    weighted = picked.astype(jnp.float32) * expert_gates.reshape(-1)[:, None]
    expert_sum = jnp.sum(weighted.reshape(q_count, TOPK, d_model), axis=1)
    return (resid_f + expert_sum).astype(jnp.bfloat16)


def solution(mesh):
    in_specs = (
        P(("dp", "mp"), None),
        P(("dp", "mp"), None),
        P(("dp", "mp"), None, None, None),
        P(),
        P(),
        P("dp", None),
        P("dp", "mp"),
        P(),
        P(("dp", "mp"), None),
        P(("dp", "mp"), None),
        P("mp", "dp", None),
        P("mp", None, "dp"),
    )
    out_specs = P(("dp", "mp"), None)
    return jax.shard_map(
        on_device, mesh=mesh, in_specs=in_specs, out_specs=out_specs, check_vma=False
    )
```

time: 352 us -> 270 us (0.77)
  waiting for transfers between devices: 252 us -> 168 us
  starting transfers between devices: 17.9 us -> 34.9 us
  matrix products: 23.3 us -> 15.8 us
  local copies, waits for them, and re-layouts: 16.1 us -> 11.8 us
    all_to_all x1 -> x3, waiting for transfers between devices: 149 us -> 36.9 us  [the longest x1 23.7 us: on_device(): lax.all_to_all(kv_out, 'mp', split_axis=0, concat_axis=0, tiled=True)]
    ppermute x0 -> x2, waiting for transfers between devices: none -> 38.5 us  [swap_dp(): return lax.ppermute(x, 'dp', [(0, 1), (1, 0)])]
    all_gather x2 -> x0, waiting for transfers between devices: 26.7 us -> none  [the longest x1 18.9 us: on_device(): lax.all_gather(experts_in, 'dp', axis=1, tiled=True)]
    all_to_all x1, waiting for transfers between devices: 28.2 us -> 45.6 us  [on_device(): lax.all_to_all(sending, 'mp', split_axis=0, concat_axis=0, tiled=True)]
    all_to_all x1 -> x3, starting transfers between devices: 6.69 us -> 19.3 us  [the longest x1 7.4 us: on_device(): lax.all_to_all(blended.reshape(n_mp, sub, HD), 'mp', split_axis=0, concat...]
    dot_general x4 -> x6, matrix products: 20 us -> 12.6 us  [the longest x1 3.61 us: on_device(): jnp.dot(rows_other, in_other[0], preferred_element_type=jnp.float32)]
  transfers between devices with their start and end apart: 6 -> 8, of which waited for: 5 -> 7; matrix products, arithmetic and copies ran while one was open for 11% -> 7% of each run, Pallas kernels for 0% -> 0%
where the time goes in v1:
time: 270 us; the launch traced here: 269 us
  waiting for transfers between devices  168 us (62%)
  starting transfers between devices  34.9 us (13%)
  other arithmetic  18.1 us (7%)
  matrix products  15.8 us (6%)
  between operations  13.7 us (5%)
  local copies, waits for them, and re-layouts  11.8 us (4%)
  blocking collectives  7.11 us (3%)
    all_to_all x1, waiting for transfers between devices, on_device(): lax.all_to_all(outcome.reshape(received.shape), 'mp', split_axis=0, conca...  47 us
    all_to_all x1, waiting for transfers between devices, on_device(): lax.all_to_all(sending, 'mp', split_axis=0, concat_axis=0, tiled=True)  45.6 us
    ppermute x2, waiting for transfers between devices, swap_dp(): return lax.ppermute(x, 'dp', [(0, 1), (1, 0)])  38.5 us
    all_to_all x1, waiting for transfers between devices, on_device(): lax.all_to_all(kv_out, 'mp', split_axis=0, concat_axis=0, tiled=True)  23.7 us
    scatter x1, other arithmetic, on_device(): sending = jnp.zeros((n_mp * capacity, d_model), jnp.bfloat16).at[target]....  9.46 us
    all_to_all x1, starting transfers between devices, on_device(): lax.all_to_all(blended.reshape(n_mp, sub, HD), 'mp', split_axis=0, concat...  7.4 us
    all_to_all x1, starting transfers between devices, on_device(): lax.all_to_all(kv_out, 'mp', split_axis=0, concat_axis=0, tiled=True)  7.11 us
    all_gather x1, blocking collectives, on_device(): wo_rows = lax.all_gather(out_weight, 'dp', axis=0, tiled=True)  7.11 us
  transfers between devices with their start and end apart: 8, of which 7 were waited for; matrix products, arithmetic and copies ran while one was open for 7% of the time, Pallas kernels for 0%

profile of v1, /device:TPU:11, one launch (start us, length us, event | category | flops | bytes accessed | tf_op | source)
XLA Modules:
  0.0 269.4 jit_solution(10714131633389939585)
XLA Ops:
  6.5 7.1 %all_gather.6 = bf16[1024,128]{1,0:T(8,128)(2,1)} all-gather(bf16[512,128]{1,0:T(8,128)(2,1)} %param.18), channel_id=1, replica_groups=mesh['dp'=2,'mp'=16] {'dp'}, dimensions={0}, use_global_device_ids=true | all-gather | bytes 393216 | tf_op jit(solution)/shard_map/all_gather | solution.py:88
  13.7 1.3 reshape.259
  15.0 0.1 copy.45
  15.1 1.0 tile.4
  16.1 7.1 %all-to-all-start.1 = ((bf16[16,6,16,2,128]{4,2,1,3,0:T(8,128)(2,1)}), bf16[16,6,16,2,128]{4,2,1,3,0:T(8,128)(2,1)S(1)}, u32[]{:S(2)}, u32[]{:S(2)}) async-start(bf16[16,6,16,2,128]{4,2,1,3,0:T(8,128)(2,1)} %bitcast.7), calls=%async_computation.1 | async-start | bytes 1572864 | tf_op jit(solution)/shard_map/all_to_all | solution.py:73
  23.2 0.6 dynamic_slice.13
  23.9 0.7 fusion.36
  24.6 0.1 copy.49
  24.7 0.1 eq.52
  24.9 0.1 reshape.263
  25.1 0.2 select_reduce_fusion
  25.5 0.7 copy.44
  26.2 0.9 reduce-window.6
  27.0 0.2 slice_reduce_fusion
  27.4 23.7 %all-to-all-done.1 = bf16[16,6,16,2,128]{4,2,1,3,0:T(8,128)(2,1)S(1)} async-done(((bf16[16,6,16,2,128]{4,2,1,3,0:T(8,128)(2,1)}), bf16[16,6,16,2,128]{4,2,1,3,0:T(8,128)(2,1)S(1)}, u32[]{:S(2)}, u32[]{:S(2)}) %all-to-all-start.1) | async-done | bytes 786464 | tf_op jit(solution)/shard_map/all_to_all | solution.py:73
  51.1 4.8 %all-to-all-start = ((bf16[16,32,128]{2,1,0:T(8,128)(2,1)}), bf16[16,32,128]{2,1,0:T(8,128)(2,1)S(1)}, u32[]{:S(2)}, u32[]{:S(2)}) async-start(bf16[16,32,128]{2,1,0:T(8,128)(2,1)} %bitcast.4), calls=%async_computation | async-start | bytes 262144 | tf_op jit(solution)/shard_map/all_to_all | solution.py:65
  55.8 0.1 fusion.39
  56.0 7.1 %all-to-all-done = bf16[16,32,128]{2,1,0:T(8,128)(2,1)S(1)} async-done(((bf16[16,32,128]{2,1,0:T(8,128)(2,1)}), bf16[16,32,128]{2,1,0:T(8,128)(2,1)S(1)}, u32[]{:S(2)}, u32[]{:S(2)}) %all-to-all-start) | async-done | bytes 131104 | tf_op jit(solution)/shard_map/all_to_all | solution.py:65
  63.1 0.7 fusion.40
  63.8 0.6 fusion.4
  64.4 1.3 fusion.14
  65.7 7.4 %all-to-all-start.2 = ((bf16[16,32,128]{2,1,0:T(8,128)(2,1)}), bf16[16,32,128]{2,1,0:T(8,128)(2,1)S(1)}, u32[]{:S(2)}, u32[]{:S(2)}) async-start(bf16[16,32,128]{2,1,0:T(8,128)(2,1)} %bitcast.10), calls=%async_computation.2 | async-start | bytes 262144 | tf_op jit(solution)/shard_map/all_to_all | solution.py:85
  73.2 0.1 mul.121
  73.4 6.2 %all-to-all-done.2 = bf16[16,32,128]{2,1,0:T(8,128)(2,1)S(1)} async-done(((bf16[16,32,128]{2,1,0:T(8,128)(2,1)}), bf16[16,32,128]{2,1,0:T(8,128)(2,1)S(1)}, u32[]{:S(2)}, u32[]{:S(2)}) %all-to-all-start.2) | async-done | bytes 131104 | tf_op jit(solution)/shard_map/all_to_all | solution.py:85
  79.7 3.2 %multiply_reduce_fusion.1 = (f32[64]{0:T(128)S(1)}, f32[64,2048]{1,0:T(8,128)S(1)}) fusion(bf16[1024,2048]{1,0:T(8,128)(2,1)} %all-gather.2.cloned.1.call-done, bf16[8,8,8,128]{3,2,1,0:T(8,128)(2,1)S(1)} %bitcast.77, bf16[64,2048]{1,0:T(8,128)(2,1)S(1)} %copy-done.1), kind=kOutput, calls=%fused_computation.34 | convolution fusion | flops 269221824 | bytes 5112064 | tf_op jit(solution)/shard_map/dot_general | solution.py:89
  82.9 0.1 multiply_convert_fusion
  83.0 9.5 %scatter_custom_fusion = bf16[512,2048]{1,0:T(8,128)(2,1)} fusion(s32[384]{0:T(512)S(1)} %fusion.27, pred[384]{0:T(512)(128)(4,1)S(1)} %compare_and_fusion.1, bf16[]{:T(256)} %constant.122.clone.1, bf16[]{:T(256)} %constant.126.clone.1, bf16[64,2048]{1,0:T(8,128)(2,1)S(1)} %multiply_convert_fusion, s32[1024]{0:T(1024)S(1)} %pad_clamp_fusion.1), kind=kCustom, calls=%fused_computation.19 | custom fusion | flops 786432 | bytes 2363908 | tf_op jit(solution)/shard_map/scatter | solution.py:106
  92.5 6.7 %all-to-all-start.3 = ((bf16[16,32,2048]{2,1,0:T(8,128)(2,1)}), bf16[16,32,2048]{2,1,0:T(8,128)(2,1)S(1)}, u32[]{:S(2)}, u32[]{:S(2)}) async-start(bf16[16,32,2048]{2,1,0:T(8,128)(2,1)} %bitcast.14), calls=%async_computation.3 | async-start | bytes 4194304 | tf_op jit(solution)/shard_map/all_to_all | solution.py:110
  99.2 2.1 collective-permute-start
  101.4 45.6 %all-to-all-done.3 = bf16[16,32,2048]{2,1,0:T(8,128)(2,1)S(1)} async-done(((bf16[16,32,2048]{2,1,0:T(8,128)(2,1)}), bf16[16,32,2048]{2,1,0:T(8,128)(2,1)S(1)}, u32[]{:S(2)}, u32[]{:S(2)}) %all-to-all-start.3) | async-done | bytes 2097184 | tf_op jit(solution)/shard_map/all_to_all | solution.py:110
  147.0 3.6 %fusion.2 = f32[512,1408]{1,0:T(8,128)S(1)} fusion(bf16[1,1024,1408]{2,1,0:T(8,128)(2,1)} %param.22, bf16[512,2048]{1,0:T(8,128)(2,1)S(1)} %bitcast.71, s32[]{:T(128)S(6)} %select_n.133), kind=kOutput, calls=%fused_computation.10 | convolution fusion | flops 1476395008 | bytes 6815748 | tf_op jit(solution)/shard_map/dot_general | solution.py:118
  150.6 13.6 %collective-permute-done = bf16[1,1024,1408]{2,1,0:T(8,128)(2,1)} collective-permute-done((bf16[1,1024,1408]{2,1,0:T(8,128)(2,1)}, bf16[1,1024,1408]{2,1,0:T(8,128)(2,1)}, u32[]{:S(2)}, u32[]{:S(2)}) %collective-permute-start) | collective-permute-done | bytes 2883616 | tf_op jit(solution)/shard_map/ppermute | solution.py:29
  164.2 3.6 %convolution_add_fusion = f32[512,1408]{1,0:T(8,128)S(1)} fusion(f32[512,1408]{1,0:T(8,128)S(1)} %fusion.2, bf16[1,1024,1408]{2,1,0:T(8,128)(2,1)} %collective-permute-done, bf16[512,2048]{1,0:T(8,128)(2,1)S(1)} %bitcast.72, s32[]{:T(128)S(6)} %select_n.134), kind=kOutput, calls=%fused_computation.6 | convolution fusion | flops 1477115904 | bytes 9699332 | tf_op jit(solution)/shard_map/dot_general | solution.py:118
  167.8 0.5 fusion.7
  168.3 0.9 copy-done.6
  169.1 1.0 convolution_convert_fusion.1
  170.1 24.9 %collective-permute-done.1 = bf16[1,704,1024]{2,1,0:T(8,128)(2,1)} collective-permute-done((bf16[1,704,1024]{2,1,0:T(8,128)(2,1)}, bf16[1,704,1024]{2,1,0:T(8,128)(2,1)}, u32[]{:S(2)}, u32[]{:S(2)}) %collective-permute-start.1) | collective-permute-done | bytes 1441824 | tf_op jit(solution)/shard_map/ppermute | solution.py:29
  195.1 2.4 convolution_convert_fusion
  197.4 2.2 maximum_select_fusion
  199.6 6.7 %all-to-all-start.4 = ((bf16[16,32,2048]{2,1,0:T(8,128)(2,1)}), bf16[16,32,2048]{2,1,0:T(8,128)(2,1)S(1)}, u32[]{:S(2)}, u32[]{:S(2)}) async-start(bf16[16,32,2048]{2,1,0:T(8,128)(2,1)} %maximum_select_fusion), calls=%async_computation.4 | async-start | bytes 4194304 | tf_op jit(solution)/shard_map/all_to_all | solution.py:135
  206.3 0.1 sub.42
  206.6 0.1 copy.53
  206.7 0.1 copy.55
  206.8 47.0 %all-to-all-done.4 = bf16[16,32,2048]{2,1,0:T(8,128)(2,1)S(1)} async-done(((bf16[16,32,2048]{2,1,0:T(8,128)(2,1)}), bf16[16,32,2048]{2,1,0:T(8,128)(2,1)S(1)}, u32[]{:S(2)}, u32[]{:S(2)}) %all-to-all-start.4) | async-done | bytes 2097184 | tf_op jit(solution)/shard_map/all_to_all | solution.py:135
  253.8 3.1 %gather_fusion = bf16[384,2048]{1,0:T(8,128)(2,1)} fusion(bf16[512,2048]{1,0:T(8,128)(2,1)S(1)} %bitcast.70, s32[1024]{0:T(1024)S(1)} %pad_clamp_fusion), kind=kCustom, calls=%fused_computation.1 | custom fusion | bytes 3147264 | tf_op jit(solution)/shard_map/jit(_take)/gather | solution.py:138
  256.9 2.5 gather.12
  259.4 2.4 multiply_reduce_fusion
  261.8 0.8 add_convert_fusion
  (45 shorter events, 1.0 us)
Async XLA Ops:
  6.5 17.3 %copy-start = (s32[2,96]{1,0:T(2,128)S(1)}, s32[2,96]{1,0:T(2,128)}, u32[]{:S(2)}) copy-start(s32[2,96]{1,0:T(2,128)} %param.15) | copy-start | bytes 2308
  6.5 73.2 %all-gather.2.cloned.1.call-start = ((), (), s32[]{:S(2)}) async-start(), calls=%async_computation.5 | async-start | bytes 4456448 | tf_op jit(solution)/shard_map/all_gather | solution.py:91
  13.7 9.6 %copy-start.7 = (s32[2]{0:T(128)S(1)}, s32[2]{0:T(128)}, u32[]{:S(2)}) copy-start(s32[2]{0:T(128)} %param.16) | copy-start | bytes 28
  13.7 10.2 %copy-start.8 = (s32[1,16]{1,0:T(1,128)S(1)}, s32[1,16]{1,0:T(1,128)}, u32[]{:S(2)}) copy-start(s32[1,16]{1,0:T(1,128)} %param.17) | copy-start | bytes 196
  13.7 10.9 %copy-start.3 = (s32[64,6]{0,1:T(8,128)S(1)}, s32[64,6]{0,1:T(8,128)}, u32[]{:S(2)}) copy-start(s32[64,6]{0,1:T(8,128)} %param.20) | copy-start | bytes 4612
  15.0 10.5 %copy-start.2 = (bf16[64,1024]{1,0:T(8,128)(2,1)S(1)}, bf16[64,1024]{1,0:T(8,128)(2,1)}, u32[]{:S(2)}) copy-start(bf16[64,1024]{1,0:T(8,128)(2,1)} %param.12) | copy-start | bytes 393220
  16.1 34.9 %all-to-all-start.1 = ((bf16[16,6,16,2,128]{4,2,1,3,0:T(8,128)(2,1)}), bf16[16,6,16,2,128]{4,2,1,3,0:T(8,128)(2,1)S(1)}, u32[]{:S(2)}, u32[]{:S(2)}) async-start(bf16[16,6,16,2,128]{4,2,1,3,0:T(8,128)(2,1)} %bitcast.7), calls=%async_computation.1 | async-start | bytes 1572864 | tf_op jit(solution)/shard_map/all_to_all | solution.py:73
  51.1 12.0 %all-to-all-start = ((bf16[16,32,128]{2,1,0:T(8,128)(2,1)}), bf16[16,32,128]{2,1,0:T(8,128)(2,1)S(1)}, u32[]{:S(2)}, u32[]{:S(2)}) async-start(bf16[16,32,128]{2,1,0:T(8,128)(2,1)} %bitcast.4), calls=%async_computation | async-start | bytes 262144 | tf_op jit(solution)/shard_map/all_to_all | solution.py:65
  64.4 15.4 %copy-start.1 = (bf16[64,2048]{1,0:T(8,128)(2,1)S(1)}, bf16[64,2048]{1,0:T(8,128)(2,1)}, u32[]{:S(2)}) copy-start(bf16[64,2048]{1,0:T(8,128)(2,1)} %param.13) | copy-start | bytes 786436
  65.7 13.9 %all-to-all-start.2 = ((bf16[16,32,128]{2,1,0:T(8,128)(2,1)}), bf16[16,32,128]{2,1,0:T(8,128)(2,1)S(1)}, u32[]{:S(2)}, u32[]{:S(2)}) async-start(bf16[16,32,128]{2,1,0:T(8,128)(2,1)} %bitcast.10), calls=%async_computation.2 | async-start | bytes 262144 | tf_op jit(solution)/shard_map/all_to_all | solution.py:85
  79.7 3.2 %copy-start.4 = (f32[2048]{0:T(1024)S(1)}, f32[2048]{0:T(1024)}, u32[]{:S(2)}) copy-start(f32[2048]{0:T(1024)} %param.19) | copy-start | bytes 24580
  92.5 54.5 %all-to-all-start.3 = ((bf16[16,32,2048]{2,1,0:T(8,128)(2,1)}), bf16[16,32,2048]{2,1,0:T(8,128)(2,1)S(1)}, u32[]{:S(2)}, u32[]{:S(2)}) async-start(bf16[16,32,2048]{2,1,0:T(8,128)(2,1)} %bitcast.14), calls=%async_computation.3 | async-start | bytes 4194304 | tf_op jit(solution)/shard_map/all_to_all | solution.py:110
  99.2 65.0 %collective-permute-start = (bf16[1,1024,1408]{2,1,0:T(8,128)(2,1)}, bf16[1,1024,1408]{2,1,0:T(8,128)(2,1)}, u32[]{:S(2)}, u32[]{:S(2)}) collective-permute-start(bf16[1,1024,1408]{2,1,0:T(8,128)(2,1)} %param.22), channel_id=1, source_target_pairs={{0,16},{16,0},{1,17},{17,1},{2,18},{18,2},{3,19},{19,3},{4,20},{20... | collective-permute-start | bytes 8650760 | tf_op jit(solution)/shard_map/ppermute | solution.py:29
  101.3 93.8 %collective-permute-start.1 = (bf16[1,704,1024]{2,1,0:T(8,128)(2,1)}, bf16[1,704,1024]{2,1,0:T(8,128)(2,1)}, u32[]{:S(2)}, u32[]{:S(2)}) collective-permute-start(bf16[1,704,1024]{2,1,0:T(8,128)(2,1)} %param.23), channel_id=1, source_target_pairs={{0,16},{16,0},{1,17},{17,1},{2,18},{18,2},{3,19},{19,3},{4,20},{20... | collective-permute-start | bytes 4325384 | tf_op jit(solution)/shard_map/ppermute | solution.py:29
  167.8 1.4 copy-start.6
  199.6 7.1 %copy-start.5 = (f32[64,6]{0,1:T(8,128)S(1)}, f32[64,6]{0,1:T(8,128)}, u32[]{:S(2)}) copy-start(f32[64,6]{0,1:T(8,128)} %param.21) | copy-start | bytes 4612
  199.6 54.1 %all-to-all-start.4 = ((bf16[16,32,2048]{2,1,0:T(8,128)(2,1)}), bf16[16,32,2048]{2,1,0:T(8,128)(2,1)S(1)}, u32[]{:S(2)}, u32[]{:S(2)}) async-start(bf16[16,32,2048]{2,1,0:T(8,128)(2,1)} %maximum_select_fusion), calls=%async_computation.4 | async-start | bytes 4194304 | tf_op jit(solution)/shard_map/all_to_all | solution.py:135
Sparse Core Ops, SparseCore 0:
  13.8 63.5 all-gather.1

commit v2 on v1

--- a/solution.py
+++ b/solution.py
@@ -62,15 +62,17 @@
     page_count = page_table.shape[1]
 
     q_out = queries.reshape(sub, groups, heads, HD).transpose(1, 2, 0, 3).reshape(n_mp, sub, HD)
-    q_in = lax.all_to_all(q_out, "mp", split_axis=0, concat_axis=0, tiled=True)
+    kv_heads = kv_pages.reshape(pages_dev, PAGE, 2, heads, HD).transpose(3, 0, 1, 2, 4)
+    kv_out = jnp.tile(kv_heads, (groups, 1, 1, 1, 1)).reshape(n_mp, pages_dev * PAGE * 2, HD)
+    both = lax.all_to_all(
+        jnp.concatenate([q_out, kv_out], axis=1), "mp", split_axis=0, concat_axis=0, tiled=True
+    )
+    q_in = both[:, :sub, :]
+    arrived = both[:, sub:, :].reshape(n_mp, pages_dev, PAGE, 2, HD)
     first_pos = cache_len[request] + deal_row % n_mp * q_count
     query_pos = (
         first_pos[:, None] + jnp.arange(sub, dtype=jnp.int32)[None, :] * groups + my_group
     ).reshape(-1)
-
-    kv_heads = kv_pages.reshape(pages_dev, PAGE, 2, heads, HD).transpose(3, 0, 1, 2, 4)
-    kv_out = jnp.tile(kv_heads, (groups, 1, 1, 1, 1))
-    arrived = lax.all_to_all(kv_out, "mp", split_axis=0, concat_axis=0, tiled=True)
     slot_ids = jnp.arange(n_mp * page_share, dtype=jnp.int32)
     physical = (row_index * n_mp + slot_ids // page_share) * pages_dev + slot_ids % page_share
     table_row = page_table[request]
@@ -98,21 +100,24 @@
     flat_ids = expert_ids.reshape(-1)
     one_hot = (flat_ids[:, None] == jnp.arange(n_mp, dtype=jnp.int32)[None, :]).astype(jnp.int32)
     slot_of = jnp.sum(jnp.cumsum(one_hot, axis=0) * one_hot, axis=1) - 1
-    target = flat_ids * capacity + slot_of
-    token_of_pair = jnp.arange(q_count * TOPK, dtype=jnp.int32) // TOPK
-    sending = (
-        jnp.zeros((n_mp * capacity, d_model), jnp.bfloat16)
-        .at[target]
-        .set(jnp.take(normed, token_of_pair, axis=0))
+    target = (flat_ids * capacity + slot_of).reshape(q_count, TOPK)
+    hits = target[:, :, None] == jnp.arange(n_mp * capacity, dtype=jnp.int32)[None, None, :]
+    dispatch = jnp.any(hits, axis=1).astype(jnp.bfloat16)
+    combine = jnp.sum(jnp.where(hits, expert_gates[:, :, None], 0.0), axis=1)
+    ff_width = experts_out.shape[1]
+    if n_dp == 2:
+        in_other = swap_dp(experts_in)
+        out_other = swap_dp(experts_out)
+        normed, in_other, out_other = lax.optimization_barrier((normed, in_other, out_other))
+    sending = lax.dot_general(
+        dispatch, normed, (((0,), (0,)), ((), ())), preferred_element_type=jnp.float32
+    ).astype(jnp.bfloat16)
+    received = lax.all_to_all(
+        sending.reshape(n_mp, capacity, d_model), "mp", split_axis=0, concat_axis=0, tiled=True
     )
-    sending = sending.reshape(n_mp, capacity, d_model)
-    ff_width = experts_out.shape[1]
-    received = lax.all_to_all(sending, "mp", split_axis=0, concat_axis=0, tiled=True)
     flat_rows = received.reshape(-1, d_model)
     if n_dp == 2:
         half_in = experts_in.shape[1]
-        in_other = swap_dp(experts_in)
-        out_other = swap_dp(experts_out)
         rows_mine = lax.dynamic_slice_in_dim(flat_rows, row_index * half_in, half_in, axis=1)
         rows_other = lax.dynamic_slice_in_dim(flat_rows, (1 - row_index) * half_in, half_in, axis=1)
         gate_vals = jnp.dot(rows_mine, experts_in[0], preferred_element_type=jnp.float32) + jnp.dot(
@@ -133,11 +138,14 @@
         act = (jax.nn.silu(gate_vals[:, :ff_width]) * gate_vals[:, ff_width:]).astype(jnp.bfloat16)
         outcome = jnp.dot(act, down[0], preferred_element_type=jnp.float32).astype(jnp.bfloat16)
     results = lax.all_to_all(
-        outcome.reshape(received.shape), "mp", split_axis=0, concat_axis=0, tiled=True
+        outcome.reshape(n_mp, capacity, d_model), "mp", split_axis=0, concat_axis=0, tiled=True
     )
-    picked = jnp.take(results.reshape(-1, d_model), target, axis=0)
-    weighted = picked.astype(jnp.float32) * expert_gates.reshape(-1)[:, None]
-    expert_sum = jnp.sum(weighted.reshape(q_count, TOPK, d_model), axis=1)
+    expert_sum = jnp.dot(
+        combine,
+        results.reshape(-1, d_model).astype(jnp.float32),
+        precision=lax.Precision.HIGHEST,
+        preferred_element_type=jnp.float32,
+    )
     return (resid_f + expert_sum).astype(jnp.bfloat16)
 
 

time: 270 us -> 253 us (0.937)
  other arithmetic: 18.1 us -> 6.79 us
  starting transfers between devices: 34.9 us -> 25.1 us
  local copies, waits for them, and re-layouts: 11.8 us -> 6.72 us
  waiting for transfers between devices: 168 us -> 173 us
  matrix products: 15.8 us -> 19.8 us
    scatter x1 -> x0, other arithmetic: 9.46 us -> none  [on_device(): sending = jnp.zeros((n_mp * capacity, d_model), jnp.bfloat16).at[target]....]
    all_gather x1, waiting for transfers between devices: 0.02 us -> 9.36 us  [on_device(): lax.all_gather(wo_rows, 'mp', axis=1, tiled=True)]
    all_to_all x4 -> x3, starting transfers between devices: 25.3 us -> 19 us  [the longest x1 7.11 us: on_device(): lax.all_to_all(jnp.concatenate([q_out, kv_out], axis=1), 'mp', split_axis...]
    gather x2 -> x0, local copies, waits for them, and re-layouts: 5.61 us -> none  [on_device(): picked = jnp.take(results.reshape(-1, d_model), target, axis=0)]
    all_to_all x4 -> x3, waiting for transfers between devices: 123 us -> 118 us  [the longest x1 47.4 us: on_device(): lax.all_to_all(sending.reshape(n_mp, capacity, d_model), 'mp', split_axis...]
    dot_general x0 -> x2, matrix products: none -> 4.03 us  [the longest x1 2.11 us: on_device(): lax.dot_general(dispatch, normed, (((0,), (0,)), ((), ())), preferred_ele...]
    all_to_all x1, starting transfers between devices: 7.4 us -> 4.59 us  [on_device(): lax.all_to_all(blended.reshape(n_mp, sub, HD), 'mp', split_axis=0, concat...]
  transfers between devices with their start and end apart: 8 -> 7, of which waited for: 7 -> 6; matrix products, arithmetic and copies ran while one was open for 7% -> 6% of each run, Pallas kernels for 0% -> 0%
where the time goes in v2:
time: 253 us; the launch traced here: 252 us
  waiting for transfers between devices  173 us (68%)
  starting transfers between devices  25.1 us (10%)
  matrix products  19.8 us (8%)
  between operations  13.7 us (5%)
  blocking collectives  7.1 us (3%)
  other arithmetic  6.79 us (3%)
  local copies, waits for them, and re-layouts  6.72 us (3%)
    all_to_all x1, waiting for transfers between devices, on_device(): lax.all_to_all(sending.reshape(n_mp, capacity, d_model), 'mp', split_axis...  47.4 us
    all_to_all x1, waiting for transfers between devices, on_device(): lax.all_to_all(outcome.reshape(n_mp, capacity, d_model), 'mp', split_axis...  47.2 us
    ppermute x2, waiting for transfers between devices, swap_dp(): return lax.ppermute(x, 'dp', [(0, 1), (1, 0)])  36.7 us
    all_to_all x1, waiting for transfers between devices, on_device(): lax.all_to_all(jnp.concatenate([q_out, kv_out], axis=1), 'mp', split_axis...  23.7 us
    all_gather x1, waiting for transfers between devices, on_device(): lax.all_gather(wo_rows, 'mp', axis=1, tiled=True)  9.36 us
    all_to_all x1, waiting for transfers between devices, on_device(): lax.all_to_all(blended.reshape(n_mp, sub, HD), 'mp', split_axis=0, concat...  8.19 us
    all_to_all x1, starting transfers between devices, on_device(): lax.all_to_all(jnp.concatenate([q_out, kv_out], axis=1), 'mp', split_axis...  7.11 us
    all_gather x1, blocking collectives, on_device(): wo_rows = lax.all_gather(out_weight, 'dp', axis=0, tiled=True)  7.1 us
  transfers between devices with their start and end apart: 7, of which 6 were waited for; matrix products, arithmetic and copies ran while one was open for 6% of the time, Pallas kernels for 0%

profile of v2, /device:TPU:11, one launch (start us, length us, event | category | flops | bytes accessed | tf_op | source)
XLA Modules:
  0.0 251.8 jit_solution(9382189879674932117)
XLA Ops:
  6.5 7.1 %all_gather.6 = bf16[1024,128]{1,0:T(8,128)(2,1)} all-gather(bf16[512,128]{1,0:T(8,128)(2,1)} %param.18), channel_id=1, replica_groups=mesh['dp'=2,'mp'=16] {'dp'}, dimensions={0}, use_global_device_ids=true | all-gather | bytes 393216 | tf_op jit(solution)/shard_map/all_gather | solution.py:90
  13.7 1.2 reshape.166
  14.9 0.3 copy.60
  15.3 1.0 copy.70
  16.4 0.6 tile.8
  17.0 1.1 pad_maximum_fusion
  18.0 7.1 %all-to-all-start = ((bf16[16,224,128]{2,1,0:T(8,128)(2,1)}), bf16[16,224,128]{2,1,0:T(8,128)(2,1)S(1)}, u32[]{:S(2)}, u32[]{:S(2)}) async-start(bf16[16,224,128]{2,1,0:T(8,128)(2,1)} %pad_maximum_fusion), calls=%async_computation | async-start | bytes 1835008 | tf_op jit(solution)/shard_map/all_to_all | solution.py:67
  25.1 0.2 collective-permute-start
  25.4 1.2 collective-permute-start.1
  26.6 0.6 dynamic_slice.13
  27.2 0.7 fusion.28
  27.9 0.1 copy.65
  28.0 0.1 eq.68
  28.1 0.1 eq.64
  28.5 0.2 select_reduce_fusion.1
  28.8 0.9 reduce-window.6
  29.7 0.2 slice_reduce_fusion
  30.0 0.1 fusion.19
  30.1 0.1 sub.32
  30.3 23.7 %all-to-all-done = bf16[16,224,128]{2,1,0:T(8,128)(2,1)S(1)} async-done(((bf16[16,224,128]{2,1,0:T(8,128)(2,1)}), bf16[16,224,128]{2,1,0:T(8,128)(2,1)S(1)}, u32[]{:S(2)}, u32[]{:S(2)}) %all-to-all-start) | async-done | bytes 917536 | tf_op jit(solution)/shard_map/all_to_all | solution.py:67
  54.0 0.5 copy.61
  54.5 0.2 fusion.30
  54.7 0.1 copy.62
  54.8 0.1 copy.63
  55.0 0.7 fusion.31
  55.7 0.6 fusion.4
  56.3 1.3 fusion.12
  57.6 4.6 %all-to-all-start.1 = ((bf16[16,32,128]{2,1,0:T(8,128)(2,1)}), bf16[16,32,128]{2,1,0:T(8,128)(2,1)S(1)}, u32[]{:S(2)}, u32[]{:S(2)}) async-start(bf16[16,32,128]{2,1,0:T(8,128)(2,1)} %bitcast.11), calls=%async_computation.1 | async-start | bytes 262144 | tf_op jit(solution)/shard_map/all_to_all | solution.py:87
  62.2 0.2 fusion.15
  62.4 8.2 %all-to-all-done.1 = bf16[16,32,128]{2,1,0:T(8,128)(2,1)S(1)} async-done(((bf16[16,32,128]{2,1,0:T(8,128)(2,1)}), bf16[16,32,128]{2,1,0:T(8,128)(2,1)S(1)}, u32[]{:S(2)}, u32[]{:S(2)}) %all-to-all-start.1) | async-done | bytes 131104 | tf_op jit(solution)/shard_map/all_to_all | solution.py:87
  70.6 9.4 %all-gather.2.cloned.1.call-done = bf16[1024,2048]{1,0:T(8,128)(2,1)} async-done(((bf16[1024,128]{1,0:T(8,128)(2,1)}), bf16[1024,2048]{1,0:T(8,128)(2,1)}) %all-gather.2.cloned.1.call-update) | async-done | bytes 4194320 | tf_op jit(solution)/shard_map/all_gather | solution.py:93
  80.0 3.2 %multiply_reduce_fusion = (f32[64]{0:T(128)S(1)}, f32[64,2048]{1,0:T(8,128)S(1)}) fusion(bf16[1024,2048]{1,0:T(8,128)(2,1)} %all-gather.2.cloned.1.call-done, bf16[8,8,8,128]{3,2,1,0:T(8,128)(2,1)S(1)} %bitcast.81, bf16[64,2048]{1,0:T(8,128)(2,1)S(1)} %copy-done.1), kind=kOutput, calls=%fused_computation.31 | convolution fusion | flops 269221824 | bytes 5112064 | tf_op jit(solution)/shard_map/dot_general | solution.py:91
  83.2 0.1 multiply_convert_fusion
  83.3 36.7 %collective-permute-done.1 = bf16[1,704,1024]{2,1,0:T(8,128)(2,1)} collective-permute-done((bf16[1,704,1024]{2,1,0:T(8,128)(2,1)S(1)}, bf16[1,704,1024]{2,1,0:T(8,128)(2,1)}, u32[]{:S(2)}, u32[]{:S(2)}) %collective-permute-start.1) | collective-permute-done | bytes 1441824 | tf_op jit(solution)/shard_map/ppermute | solution.py:29
  120.0 2.1 convolution_convert_fusion
  122.1 6.9 %all-to-all-start.2 = ((bf16[16,32,2048]{2,1,0:T(8,128)(2,1)}), bf16[16,32,2048]{2,1,0:T(8,128)(2,1)S(1)}, u32[]{:S(2)}, u32[]{:S(2)}) async-start(bf16[16,32,2048]{2,1,0:T(8,128)(2,1)} %bitcast.15), calls=%async_computation.2 | async-start | bytes 4194304 | tf_op jit(solution)/shard_map/all_to_all | solution.py:115
  129.0 47.4 %all-to-all-done.2 = bf16[16,32,2048]{2,1,0:T(8,128)(2,1)S(1)} async-done(((bf16[16,32,2048]{2,1,0:T(8,128)(2,1)}), bf16[16,32,2048]{2,1,0:T(8,128)(2,1)S(1)}, u32[]{:S(2)}, u32[]{:S(2)}) %all-to-all-start.2) | async-done | bytes 2097184 | tf_op jit(solution)/shard_map/all_to_all | solution.py:115
  176.4 3.6 %fusion.2 = f32[512,1408]{1,0:T(8,128)S(1)} fusion(bf16[1,1024,1408]{2,1,0:T(8,128)(2,1)} %param.22, bf16[512,2048]{1,0:T(8,128)(2,1)S(1)} %bitcast.74, s32[]{:T(128)S(6)} %select_n.74), kind=kOutput, calls=%fused_computation.7 | convolution fusion | flops 1476395008 | bytes 6815748 | tf_op jit(solution)/shard_map/dot_general | solution.py:123
  180.1 3.6 %convolution_add_fusion = f32[512,1408]{1,0:T(8,128)S(1)} fusion(f32[512,1408]{1,0:T(8,128)S(1)} %fusion.2, bf16[1,1024,1408]{2,1,0:T(8,128)(2,1)} %collective-permute-done, bf16[512,2048]{1,0:T(8,128)(2,1)S(1)} %bitcast.75, s32[]{:T(128)S(6)} %select_n.75), kind=kOutput, calls=%fused_computation.2 | convolution fusion | flops 1477115904 | bytes 9699332 | tf_op jit(solution)/shard_map/dot_general | solution.py:123
  183.7 0.5 fusion.8
  184.2 0.9 copy-done.6
  185.0 1.0 convolution_convert_fusion.2
  186.0 2.4 convolution_convert_fusion.1
  188.4 2.2 maximum_select_fusion
  190.6 5.0 %all-to-all-start.3 = ((bf16[16,32,2048]{2,1,0:T(8,128)(2,1)}), bf16[16,32,2048]{2,1,0:T(8,128)(2,1)S(1)}, u32[]{:S(2)}, u32[]{:S(2)}) async-start(bf16[16,32,2048]{2,1,0:T(8,128)(2,1)} %maximum_select_fusion), calls=%async_computation.3 | async-start | bytes 4194304 | tf_op jit(solution)/shard_map/all_to_all | solution.py:140
  195.7 0.2 select_reduce_fusion
  195.8 47.2 %all-to-all-done.3 = bf16[16,32,2048]{2,1,0:T(8,128)(2,1)S(1)} async-done(((bf16[16,32,2048]{2,1,0:T(8,128)(2,1)}), bf16[16,32,2048]{2,1,0:T(8,128)(2,1)S(1)}, u32[]{:S(2)}, u32[]{:S(2)}) %all-to-all-start.3) | async-done | bytes 2097184 | tf_op jit(solution)/shard_map/all_to_all | solution.py:140
  243.1 1.9 fusion.7
  (38 shorter events, 0.7 us)
Async XLA Ops:
  6.5 21.9 %copy-start = (s32[2,96]{1,0:T(2,128)S(1)}, s32[2,96]{1,0:T(2,128)}, u32[]{:S(2)}) copy-start(s32[2,96]{1,0:T(2,128)} %param.15) | copy-start | bytes 2308
  6.5 73.5 %all-gather.2.cloned.1.call-start = ((), (), s32[]{:S(2)}) async-start(), calls=%async_computation.4 | async-start | bytes 4456448 | tf_op jit(solution)/shard_map/all_gather | solution.py:93
  15.2 10.1 %copy-start.5 = (bf16[1,704,1024]{2,1,0:T(8,128)(2,1)S(1)}, bf16[1,704,1024]{2,1,0:T(8,128)(2,1)}, u32[]{:S(2)}) copy-start(bf16[1,704,1024]{2,1,0:T(8,128)(2,1)} %param.23) | copy-start | bytes 4325380
  15.2 11.4 %copy-start.7 = (s32[2]{0:T(128)S(1)}, s32[2]{0:T(128)}, u32[]{:S(2)}) copy-start(s32[2]{0:T(128)} %param.16) | copy-start | bytes 28
  15.2 11.9 %copy-start.8 = (s32[1,16]{1,0:T(1,128)S(1)}, s32[1,16]{1,0:T(1,128)}, u32[]{:S(2)}) copy-start(s32[1,16]{1,0:T(1,128)} %param.17) | copy-start | bytes 196
  15.3 12.6 %copy-start.2 = (s32[64,6]{0,1:T(8,128)S(1)}, s32[64,6]{0,1:T(8,128)}, u32[]{:S(2)}) copy-start(s32[64,6]{0,1:T(8,128)} %param.20) | copy-start | bytes 4612
  18.0 35.9 %all-to-all-start = ((bf16[16,224,128]{2,1,0:T(8,128)(2,1)}), bf16[16,224,128]{2,1,0:T(8,128)(2,1)S(1)}, u32[]{:S(2)}, u32[]{:S(2)}) async-start(bf16[16,224,128]{2,1,0:T(8,128)(2,1)} %pad_maximum_fusion), calls=%async_computation | async-start | bytes 1835008 | tf_op jit(solution)/shard_map/all_to_all | solution.py:67
  25.1 94.9 %collective-permute-start = (bf16[1,1024,1408]{2,1,0:T(8,128)(2,1)}, bf16[1,1024,1408]{2,1,0:T(8,128)(2,1)}, u32[]{:S(2)}, u32[]{:S(2)}) collective-permute-start(bf16[1,1024,1408]{2,1,0:T(8,128)(2,1)} %param.22), channel_id=1, source_target_pairs={{0,16},{16,0},{1,17},{17,1},{2,18},{18,2},{3,19},{19,3},{4,20},{20... | collective-permute-start | bytes 8650760 | tf_op jit(solution)/shard_map/ppermute | solution.py:29
  25.4 94.7 %collective-permute-start.1 = (bf16[1,704,1024]{2,1,0:T(8,128)(2,1)S(1)}, bf16[1,704,1024]{2,1,0:T(8,128)(2,1)}, u32[]{:S(2)}, u32[]{:S(2)}) collective-permute-start(bf16[1,704,1024]{2,1,0:T(8,128)(2,1)S(1)} %copy-done.5), channel_id=1, source_target_pairs={{0,16},{16,0},{1,17},{17,1},{2,18},{18,2},{3,19},{19,3},{4,20},{20... | collective-permute-start | bytes 4325384 | tf_op jit(solution)/shard_map/ppermute | solution.py:29
  56.3 23.7 %copy-start.1 = (bf16[64,2048]{1,0:T(8,128)(2,1)S(1)}, bf16[64,2048]{1,0:T(8,128)(2,1)}, u32[]{:S(2)}) copy-start(bf16[64,2048]{1,0:T(8,128)(2,1)} %param.13) | copy-start | bytes 786436
  57.6 25.6 %copy-start.3 = (f32[2048]{0:T(1024)S(1)}, f32[2048]{0:T(1024)}, u32[]{:S(2)}) copy-start(f32[2048]{0:T(1024)} %param.19) | copy-start | bytes 24580
  57.6 13.0 %all-to-all-start.1 = ((bf16[16,32,128]{2,1,0:T(8,128)(2,1)}), bf16[16,32,128]{2,1,0:T(8,128)(2,1)S(1)}, u32[]{:S(2)}, u32[]{:S(2)}) async-start(bf16[16,32,128]{2,1,0:T(8,128)(2,1)} %bitcast.11), calls=%async_computation.1 | async-start | bytes 262144 | tf_op jit(solution)/shard_map/all_to_all | solution.py:87
  122.1 54.3 %all-to-all-start.2 = ((bf16[16,32,2048]{2,1,0:T(8,128)(2,1)}), bf16[16,32,2048]{2,1,0:T(8,128)(2,1)S(1)}, u32[]{:S(2)}, u32[]{:S(2)}) async-start(bf16[16,32,2048]{2,1,0:T(8,128)(2,1)} %bitcast.15), calls=%async_computation.2 | async-start | bytes 4194304 | tf_op jit(solution)/shard_map/all_to_all | solution.py:115
  183.7 1.4 copy-start.6
  190.6 5.0 %copy-start.4 = (f32[64,6]{0,1:T(8,128)S(1)}, f32[64,6]{0,1:T(8,128)}, u32[]{:S(2)}) copy-start(f32[64,6]{0,1:T(8,128)} %param.21) | copy-start | bytes 4612
  190.6 52.5 %all-to-all-start.3 = ((bf16[16,32,2048]{2,1,0:T(8,128)(2,1)}), bf16[16,32,2048]{2,1,0:T(8,128)(2,1)S(1)}, u32[]{:S(2)}, u32[]{:S(2)}) async-start(bf16[16,32,2048]{2,1,0:T(8,128)(2,1)} %maximum_select_fusion), calls=%async_computation.3 | async-start | bytes 4194304 | tf_op jit(solution)/shard_map/all_to_all | solution.py:140
Sparse Core Ops, SparseCore 0:
  13.8 66.1 all-gather.1

commit v3 on v2

--- a/solution.py
+++ b/solution.py
@@ -87,12 +87,22 @@
     back = lax.all_to_all(blended.reshape(n_mp, sub, HD), "mp", split_axis=0, concat_axis=0, tiled=True)
     attended = back.reshape(groups, heads, sub, HD).transpose(2, 0, 1, 3).reshape(q_count, width)
 
-    wo_rows = lax.all_gather(out_weight, "dp", axis=0, tiled=True)
-    projected = jnp.dot(
-        attended,
-        lax.all_gather(wo_rows, "mp", axis=1, tiled=True),
-        preferred_element_type=jnp.float32,
-    )
+    if n_dp == 2:
+        half_w = out_weight.shape[0]
+        w_mine = lax.all_gather(out_weight, "mp", axis=1, tiled=True)
+        w_other = lax.all_gather(swap_dp(out_weight), "mp", axis=1, tiled=True)
+        att_mine = lax.dynamic_slice_in_dim(attended, row_index * half_w, half_w, axis=1)
+        att_other = lax.dynamic_slice_in_dim(attended, (1 - row_index) * half_w, half_w, axis=1)
+        projected = jnp.dot(att_mine, w_mine, preferred_element_type=jnp.float32) + jnp.dot(
+            att_other, w_other, preferred_element_type=jnp.float32
+        )
+    else:
+        wo_rows = lax.all_gather(out_weight, "dp", axis=0, tiled=True)
+        projected = jnp.dot(
+            attended,
+            lax.all_gather(wo_rows, "mp", axis=1, tiled=True),
+            preferred_element_type=jnp.float32,
+        )
     resid_f = (hidden.astype(jnp.float32) + projected).astype(jnp.bfloat16).astype(jnp.float32)
     mean_square = jnp.mean(resid_f * resid_f, axis=1, keepdims=True)
     normed = (resid_f * lax.rsqrt(mean_square + epsilon) * norm_gain[None, :]).astype(jnp.bfloat16)
@@ -108,7 +118,7 @@
     if n_dp == 2:
         in_other = swap_dp(experts_in)
         out_other = swap_dp(experts_out)
-        normed, in_other, out_other = lax.optimization_barrier((normed, in_other, out_other))
+        normed, in_other = lax.optimization_barrier((normed, in_other))
     sending = lax.dot_general(
         dispatch, normed, (((0,), (0,)), ((), ())), preferred_element_type=jnp.float32
     ).astype(jnp.bfloat16)
@@ -117,6 +127,7 @@
     )
     flat_rows = received.reshape(-1, d_model)
     if n_dp == 2:
+        flat_rows, out_other = lax.optimization_barrier((flat_rows, out_other))
         half_in = experts_in.shape[1]
         rows_mine = lax.dynamic_slice_in_dim(flat_rows, row_index * half_in, half_in, axis=1)
         rows_other = lax.dynamic_slice_in_dim(flat_rows, (1 - row_index) * half_in, half_in, axis=1)

time: 253 us -> 238 us (0.941)
  blocking collectives: 7.1 us -> 0 us
  waiting for transfers between devices: 173 us -> 166 us
    all_gather x1 -> x2, waiting for transfers between devices: 9.36 us -> 42.9 us  [the longest x1 42.5 us: on_device(): w_other = lax.all_gather(swap_dp(out_weight), 'mp', axis=1, tiled=True)]
    all_to_all x1, waiting for transfers between devices: 47.4 us -> 14.3 us  [on_device(): lax.all_to_all(sending.reshape(n_mp, capacity, d_model), 'mp', split_axis...]
    all_gather x1 -> x0, blocking collectives: 7.1 us -> none  [on_device(): wo_rows = lax.all_gather(out_weight, 'dp', axis=0, tiled=True)]
    ppermute x2 -> x3, waiting for transfers between devices: 36.7 us -> 31.9 us  [swap_dp(): return lax.ppermute(x, 'dp', [(0, 1), (1, 0)])]
  transfers between devices with their start and end apart: 7 -> 9, of which waited for: 6 -> 7; matrix products, arithmetic and copies ran while one was open for 6% -> 7% of each run, Pallas kernels for 0% -> 0%
where the time goes in v3:
time: 238 us; the launch traced here: 237 us
  waiting for transfers between devices  166 us (70%)
  starting transfers between devices  23.9 us (10%)
  matrix products  19.3 us (8%)
  between operations  13.7 us (6%)
  local copies, waits for them, and re-layouts  7.3 us (3%)
  other arithmetic  6.72 us (3%)
    all_to_all x1, waiting for transfers between devices, on_device(): lax.all_to_all(outcome.reshape(n_mp, capacity, d_model), 'mp', split_axis...  47.2 us
    all_gather x1, waiting for transfers between devices, on_device(): w_other = lax.all_gather(swap_dp(out_weight), 'mp', axis=1, tiled=True)  42.5 us
    ppermute x3, waiting for transfers between devices, swap_dp(): return lax.ppermute(x, 'dp', [(0, 1), (1, 0)])  31.9 us
    all_to_all x1, waiting for transfers between devices, on_device(): lax.all_to_all(jnp.concatenate([q_out, kv_out], axis=1), 'mp', split_axis...  21.5 us
    all_to_all x1, waiting for transfers between devices, on_device(): lax.all_to_all(sending.reshape(n_mp, capacity, d_model), 'mp', split_axis...  14.3 us
    all_to_all x1, waiting for transfers between devices, on_device(): lax.all_to_all(blended.reshape(n_mp, sub, HD), 'mp', split_axis=0, concat...  7.43 us
    all_to_all x1, starting transfers between devices, on_device(): lax.all_to_all(jnp.concatenate([q_out, kv_out], axis=1), 'mp', split_axis...  6.83 us
    all_to_all x1, starting transfers between devices, on_device(): lax.all_to_all(outcome.reshape(n_mp, capacity, d_model), 'mp', split_axis...  5.03 us
  transfers between devices with their start and end apart: 9, of which 7 were waited for; matrix products, arithmetic and copies ran while one was open for 7% of the time, Pallas kernels for 0%

profile of v3, /device:TPU:11, one launch (start us, length us, event | category | flops | bytes accessed | tf_op | source)
XLA Modules:
  0.0 236.9 jit_solution(18127600669914010095)
XLA Ops:
  6.5 0.7 all-gather.3.cloned.1.call-update
  7.3 1.3 collective-permute-start
  8.6 1.2 reshape.166
  9.8 0.3 copy.60
  10.1 0.9 copy.70
  11.1 0.6 tile.8
  11.7 1.0 pad_maximum_fusion
  12.7 6.8 %all-to-all-start = ((bf16[16,224,128]{2,1,0:T(8,128)(2,1)}), bf16[16,224,128]{2,1,0:T(8,128)(2,1)S(1)}, u32[]{:S(2)}, u32[]{:S(2)}) async-start(bf16[16,224,128]{2,1,0:T(8,128)(2,1)} %pad_maximum_fusion), calls=%async_computation | async-start | bytes 1835008 | tf_op jit(solution)/shard_map/all_to_all | solution.py:67
  19.6 0.3 collective-permute-start.1
  19.9 0.6 dynamic_slice.19
  20.5 0.7 copy-done.2
  21.2 0.7 fusion.32
  22.0 0.1 eq.68
  22.1 0.1 eq.64
  22.5 0.2 select_reduce_fusion.1
  22.8 0.9 reduce-window.6
  23.7 0.2 slice_reduce_fusion
  24.1 0.1 sub.34
  24.3 21.5 %all-to-all-done = bf16[16,224,128]{2,1,0:T(8,128)(2,1)S(1)} async-done(((bf16[16,224,128]{2,1,0:T(8,128)(2,1)}), bf16[16,224,128]{2,1,0:T(8,128)(2,1)S(1)}, u32[]{:S(2)}, u32[]{:S(2)}) %all-to-all-start) | async-done | bytes 917536 | tf_op jit(solution)/shard_map/all_to_all | solution.py:67
  45.8 0.5 copy.61
  46.3 0.2 fusion.34
  46.7 0.7 fusion.35
  47.5 0.6 fusion.4
  48.0 1.4 fusion.13
  49.4 4.8 %all-to-all-start.1 = ((bf16[16,32,128]{2,1,0:T(8,128)(2,1)}), bf16[16,32,128]{2,1,0:T(8,128)(2,1)S(1)}, u32[]{:S(2)}, u32[]{:S(2)}) async-start(bf16[16,32,128]{2,1,0:T(8,128)(2,1)} %bitcast.11), calls=%async_computation.1 | async-start | bytes 262144 | tf_op jit(solution)/shard_map/all_to_all | solution.py:87
  54.2 0.2 fusion.16
  54.3 7.4 %all-to-all-done.1 = bf16[16,32,128]{2,1,0:T(8,128)(2,1)S(1)} async-done(((bf16[16,32,128]{2,1,0:T(8,128)(2,1)}), bf16[16,32,128]{2,1,0:T(8,128)(2,1)S(1)}, u32[]{:S(2)}, u32[]{:S(2)}) %all-to-all-start.1) | async-done | bytes 131104 | tf_op jit(solution)/shard_map/all_to_all | solution.py:87
  61.8 0.5 all-gather.3.cloned.1.call-done
  62.3 2.1 fusion.18
  64.4 42.5 %all-gather.5.cloned.1.call-done = bf16[512,2048]{1,0:T(8,128)(2,1)} async-done(((bf16[512,128]{1,0:T(8,128)(2,1)}), bf16[512,2048]{1,0:T(8,128)(2,1)}) %all-gather.5.cloned.1.call-update) | async-done | bytes 2097168 | tf_op jit(solution)/shard_map/all_gather | solution.py:93
  106.9 2.2 multiply_reduce_fusion
  109.1 0.1 multiply_convert_fusion
  109.3 2.1 convolution_convert_fusion
  111.4 4.4 %all-to-all-start.2 = ((bf16[16,32,2048]{2,1,0:T(8,128)(2,1)}), bf16[16,32,2048]{2,1,0:T(8,128)(2,1)S(1)}, u32[]{:S(2)}, u32[]{:S(2)}) async-start(bf16[16,32,2048]{2,1,0:T(8,128)(2,1)} %bitcast.15), calls=%async_computation.2 | async-start | bytes 4194304 | tf_op jit(solution)/shard_map/all_to_all | solution.py:125
  115.8 1.3 collective-permute-start.2
  117.1 31.9 %collective-permute-done.2 = bf16[1,704,1024]{2,1,0:T(8,128)(2,1)} collective-permute-done((bf16[1,704,1024]{2,1,0:T(8,128)(2,1)}, bf16[1,704,1024]{2,1,0:T(8,128)(2,1)}, u32[]{:S(2)}, u32[]{:S(2)}) %collective-permute-start.2) | collective-permute-done | bytes 1441824 | tf_op jit(solution)/shard_map/ppermute | solution.py:29
  148.9 14.3 %all-to-all-done.2 = bf16[16,32,2048]{2,1,0:T(8,128)(2,1)S(1)} async-done(((bf16[16,32,2048]{2,1,0:T(8,128)(2,1)}), bf16[16,32,2048]{2,1,0:T(8,128)(2,1)S(1)}, u32[]{:S(2)}, u32[]{:S(2)}) %all-to-all-start.2) | async-done | bytes 2097184 | tf_op jit(solution)/shard_map/all_to_all | solution.py:125
  163.2 3.8 %fusion.1 = f32[512,1408]{1,0:T(8,128)S(1)} fusion(bf16[1,1024,1408]{2,1,0:T(8,128)(2,1)} %collective-permute-done.1, bf16[512,2048]{1,0:T(8,128)(2,1)S(1)} %bitcast.73, s32[]{:T(128)S(6)} %select_n.83), kind=kOutput, calls=%fused_computation.6 | convolution fusion | flops 1476395008 | bytes 6815748 | tf_op jit(solution)/shard_map/dot_general | solution.py:134
  167.0 1.8 convolution_add_fusion
  168.8 0.5 fusion.9
  169.3 0.9 copy-done.7
  170.1 1.0 convolution_convert_fusion.2
  171.1 2.4 convolution_convert_fusion.1
  173.5 2.2 maximum_select_fusion
  175.7 5.0 %all-to-all-start.3 = ((bf16[16,32,2048]{2,1,0:T(8,128)(2,1)}), bf16[16,32,2048]{2,1,0:T(8,128)(2,1)S(1)}, u32[]{:S(2)}, u32[]{:S(2)}) async-start(bf16[16,32,2048]{2,1,0:T(8,128)(2,1)} %maximum_select_fusion), calls=%async_computation.3 | async-start | bytes 4194304 | tf_op jit(solution)/shard_map/all_to_all | solution.py:151
  180.7 0.2 select_reduce_fusion
  180.9 47.2 %all-to-all-done.3 = bf16[16,32,2048]{2,1,0:T(8,128)(2,1)S(1)} async-done(((bf16[16,32,2048]{2,1,0:T(8,128)(2,1)}), bf16[16,32,2048]{2,1,0:T(8,128)(2,1)S(1)}, u32[]{:S(2)}, u32[]{:S(2)}) %all-to-all-start.3) | async-done | bytes 2097184 | tf_op jit(solution)/shard_map/all_to_all | solution.py:151
  228.2 1.9 fusion.8
  (46 shorter events, 1.2 us)
Async XLA Ops:
  6.5 15.9 %copy-start = (s32[2,96]{1,0:T(2,128)S(1)}, s32[2,96]{1,0:T(2,128)}, u32[]{:S(2)}) copy-start(s32[2,96]{1,0:T(2,128)} %param.15) | copy-start | bytes 2308
  6.5 55.8 %all-gather.3.cloned.1.call-start = ((), (), s32[]{:S(2)}) async-start(), calls=%async_computation.4 | async-start | bytes 2228224 | tf_op jit(solution)/shard_map/all_gather | solution.py:92
  7.3 13.2 %collective-permute-start = (bf16[512,128]{1,0:T(8,128)(2,1)}, bf16[512,128]{1,0:T(8,128)(2,1)S(1)}, u32[]{:S(2)}, u32[]{:S(2)}) collective-permute-start(bf16[512,128]{1,0:T(8,128)(2,1)} %param.18), channel_id=1, source_target_pairs={{0,16},{16,0},{1,17},{17,1},{2,18},{18,2},{3,19},{19,3},{4,20},{20... | collective-permute-start | bytes 393224 | tf_op jit(solution)/shard_map/ppermute | solution.py:29
  11.7 8.2 %copy-start.8 = (s32[2]{0:T(128)S(1)}, s32[2]{0:T(128)}, u32[]{:S(2)}) copy-start(s32[2]{0:T(128)} %param.16) | copy-start | bytes 28
  11.7 9.5 %copy-start.9 = (s32[1,16]{1,0:T(1,128)S(1)}, s32[1,16]{1,0:T(1,128)}, u32[]{:S(2)}) copy-start(s32[1,16]{1,0:T(1,128)} %param.17) | copy-start | bytes 196
  11.7 10.1 %copy-start.3 = (s32[64,6]{0,1:T(8,128)S(1)}, s32[64,6]{0,1:T(8,128)}, u32[]{:S(2)}) copy-start(s32[64,6]{0,1:T(8,128)} %param.20) | copy-start | bytes 4612
  12.7 33.0 %all-to-all-start = ((bf16[16,224,128]{2,1,0:T(8,128)(2,1)}), bf16[16,224,128]{2,1,0:T(8,128)(2,1)S(1)}, u32[]{:S(2)}, u32[]{:S(2)}) async-start(bf16[16,224,128]{2,1,0:T(8,128)(2,1)} %pad_maximum_fusion), calls=%async_computation | async-start | bytes 1835008 | tf_op jit(solution)/shard_map/all_to_all | solution.py:67
  19.6 87.3 %all-gather.5.cloned.1.call-start = ((), (), s32[]{:S(2)}) async-start(), calls=%async_computation.5 | async-start | bytes 2228224 | tf_op jit(solution)/shard_map/all_gather | solution.py:93
  19.6 89.7 %collective-permute-start.1 = (bf16[1,1024,1408]{2,1,0:T(8,128)(2,1)}, bf16[1,1024,1408]{2,1,0:T(8,128)(2,1)}, u32[]{:S(2)}, u32[]{:S(2)}) collective-permute-start(bf16[1,1024,1408]{2,1,0:T(8,128)(2,1)} %param.22), channel_id=1, source_target_pairs={{0,16},{16,0},{1,17},{17,1},{2,18},{18,2},{3,19},{19,3},{4,20},{20... | collective-permute-start | bytes 8650760 | tf_op jit(solution)/shard_map/ppermute | solution.py:29
  20.5 0.7 copy-start.2
  49.4 57.5 %copy-start.1 = (bf16[64,2048]{1,0:T(8,128)(2,1)S(1)}, bf16[64,2048]{1,0:T(8,128)(2,1)}, u32[]{:S(2)}) copy-start(bf16[64,2048]{1,0:T(8,128)(2,1)} %param.13) | copy-start | bytes 786436
  49.4 12.4 %all-to-all-start.1 = ((bf16[16,32,128]{2,1,0:T(8,128)(2,1)}), bf16[16,32,128]{2,1,0:T(8,128)(2,1)S(1)}, u32[]{:S(2)}, u32[]{:S(2)}) async-start(bf16[16,32,128]{2,1,0:T(8,128)(2,1)} %bitcast.11), calls=%async_computation.1 | async-start | bytes 262144 | tf_op jit(solution)/shard_map/all_to_all | solution.py:87
  64.4 44.8 %copy-start.4 = (f32[2048]{0:T(1024)S(1)}, f32[2048]{0:T(1024)}, u32[]{:S(2)}) copy-start(f32[2048]{0:T(1024)} %param.19) | copy-start | bytes 24580
  111.4 51.8 %all-to-all-start.2 = ((bf16[16,32,2048]{2,1,0:T(8,128)(2,1)}), bf16[16,32,2048]{2,1,0:T(8,128)(2,1)S(1)}, u32[]{:S(2)}, u32[]{:S(2)}) async-start(bf16[16,32,2048]{2,1,0:T(8,128)(2,1)} %bitcast.15), calls=%async_computation.2 | async-start | bytes 4194304 | tf_op jit(solution)/shard_map/all_to_all | solution.py:125
  115.8 33.2 %collective-permute-start.2 = (bf16[1,704,1024]{2,1,0:T(8,128)(2,1)}, bf16[1,704,1024]{2,1,0:T(8,128)(2,1)}, u32[]{:S(2)}, u32[]{:S(2)}) collective-permute-start(bf16[1,704,1024]{2,1,0:T(8,128)(2,1)} %param.23), channel_id=1, source_target_pairs={{0,16},{16,0},{1,17},{17,1},{2,18},{18,2},{3,19},{19,3},{4,20},{20... | collective-permute-start | bytes 4325384 | tf_op jit(solution)/shard_map/ppermute | solution.py:29
  163.2 3.8 %copy-start.6 = (bf16[1,1024,1408]{2,1,0:T(8,128)(2,1)S(1)}, bf16[1,1024,1408]{2,1,0:T(8,128)(2,1)}, u32[]{:S(2)}) copy-start(bf16[1,1024,1408]{2,1,0:T(8,128)(2,1)} %param.22) | copy-start | bytes 8650756
  168.8 1.4 copy-start.7
  175.7 5.0 %copy-start.5 = (f32[64,6]{0,1:T(8,128)S(1)}, f32[64,6]{0,1:T(8,128)}, u32[]{:S(2)}) copy-start(f32[64,6]{0,1:T(8,128)} %param.21) | copy-start | bytes 4612
  175.7 52.4 %all-to-all-start.3 = ((bf16[16,32,2048]{2,1,0:T(8,128)(2,1)}), bf16[16,32,2048]{2,1,0:T(8,128)(2,1)S(1)}, u32[]{:S(2)}, u32[]{:S(2)}) async-start(bf16[16,32,2048]{2,1,0:T(8,128)(2,1)} %maximum_select_fusion), calls=%async_computation.3 | async-start | bytes 4194304 | tf_op jit(solution)/shard_map/all_to_all | solution.py:151
Sparse Core Ops, SparseCore 0:
  9.5 52.7 all-gather.2
  64.4 42.3 all-gather.4

commit v4 on v2

--- a/solution.py
+++ b/solution.py
@@ -87,7 +87,15 @@
     back = lax.all_to_all(blended.reshape(n_mp, sub, HD), "mp", split_axis=0, concat_axis=0, tiled=True)
     attended = back.reshape(groups, heads, sub, HD).transpose(2, 0, 1, 3).reshape(q_count, width)
 
-    wo_rows = lax.all_gather(out_weight, "dp", axis=0, tiled=True)
+    if n_dp == 2:
+        w_pair = swap_dp(out_weight)
+        wo_rows = jnp.where(
+            row_index == 0,
+            jnp.concatenate([out_weight, w_pair], axis=0),
+            jnp.concatenate([w_pair, out_weight], axis=0),
+        )
+    else:
+        wo_rows = lax.all_gather(out_weight, "dp", axis=0, tiled=True)
     projected = jnp.dot(
         attended,
         lax.all_gather(wo_rows, "mp", axis=1, tiled=True),
@@ -108,7 +116,7 @@
     if n_dp == 2:
         in_other = swap_dp(experts_in)
         out_other = swap_dp(experts_out)
-        normed, in_other, out_other = lax.optimization_barrier((normed, in_other, out_other))
+        normed, in_other = lax.optimization_barrier((normed, in_other))
     sending = lax.dot_general(
         dispatch, normed, (((0,), (0,)), ((), ())), preferred_element_type=jnp.float32
     ).astype(jnp.bfloat16)
@@ -117,6 +125,7 @@
     )
     flat_rows = received.reshape(-1, d_model)
     if n_dp == 2:
+        flat_rows, out_other = lax.optimization_barrier((flat_rows, out_other))
         half_in = experts_in.shape[1]
         rows_mine = lax.dynamic_slice_in_dim(flat_rows, row_index * half_in, half_in, axis=1)
         rows_other = lax.dynamic_slice_in_dim(flat_rows, (1 - row_index) * half_in, half_in, axis=1)

time: 253 us -> 219 us (0.87)
  waiting for transfers between devices: 173 us -> 144 us
  blocking collectives: 7.1 us -> 0 us
  starting transfers between devices: 25.1 us -> 27.9 us
    all_to_all x1, waiting for transfers between devices: 47.4 us -> 14.2 us  [on_device(): lax.all_to_all(sending.reshape(n_mp, capacity, d_model), 'mp', split_axis...]
    all_gather x1 -> x0, blocking collectives: 7.1 us -> none  [on_device(): wo_rows = lax.all_gather(out_weight, 'dp', axis=0, tiled=True)]
    ppermute x2 -> x3, waiting for transfers between devices: 36.7 us -> 39.9 us  [swap_dp(): return lax.ppermute(x, 'dp', [(0, 1), (1, 0)])]
  transfers between devices with their start and end apart: 7 -> 8, of which waited for: 6 -> 8; matrix products, arithmetic and copies ran while one was open for 6% -> 7% of each run, Pallas kernels for 0% -> 0%
where the time goes in v4:
time: 219 us
  waiting for transfers between devices  144 us (66%)
  starting transfers between devices  27.9 us (13%)
  matrix products  18.2 us (8%)
  between operations  13.7 us (6%)
  other arithmetic  8.37 us (4%)
  local copies, waits for them, and re-layouts  6.57 us (3%)
    all_to_all x1, waiting for transfers between devices, on_device(): lax.all_to_all(outcome.reshape(n_mp, capacity, d_model), 'mp', split_axis...  47.2 us
    ppermute x3, waiting for transfers between devices, swap_dp(): return lax.ppermute(x, 'dp', [(0, 1), (1, 0)])  39.9 us
    all_to_all x1, waiting for transfers between devices, on_device(): lax.all_to_all(jnp.concatenate([q_out, kv_out], axis=1), 'mp', split_axis...  25.1 us
    all_to_all x1, waiting for transfers between devices, on_device(): lax.all_to_all(sending.reshape(n_mp, capacity, d_model), 'mp', split_axis...  14.2 us
    all_gather x1, waiting for transfers between devices, on_device(): lax.all_gather(wo_rows, 'mp', axis=1, tiled=True)  9.36 us
    all_to_all x1, waiting for transfers between devices, on_device(): lax.all_to_all(blended.reshape(n_mp, sub, HD), 'mp', split_axis=0, concat...  8.09 us
    all_to_all x1, starting transfers between devices, on_device(): lax.all_to_all(jnp.concatenate([q_out, kv_out], axis=1), 'mp', split_axis...  7.43 us
    all_to_all x1, starting transfers between devices, on_device(): lax.all_to_all(sending.reshape(n_mp, capacity, d_model), 'mp', split_axis...  6.85 us
  transfers between devices with their start and end apart: 8, of which 8 were waited for; matrix products, arithmetic and copies ran while one was open for 7% of the time, Pallas kernels for 0%

profile of v4, /device:TPU:11, one launch (start us, length us, event | category | flops | bytes accessed | tf_op | source)
XLA Modules:
  0.0 218.6 jit_solution(11296519926068575173)
XLA Ops:
  6.5 1.2 collective-permute-start
  7.8 3.3 %collective-permute-done = bf16[512,128]{1,0:T(8,128)(2,1)S(1)} collective-permute-done((bf16[512,128]{1,0:T(8,128)(2,1)}, bf16[512,128]{1,0:T(8,128)(2,1)S(1)}, u32[]{:S(2)}, u32[]{:S(2)}) %collective-permute-start) | collective-permute-done | bytes 131104 | tf_op jit(solution)/shard_map/ppermute | solution.py:29
  11.1 1.8 maximum_select_fusion.1
  12.9 1.2 reshape.166
  14.1 0.3 copy.60
  14.5 0.9 copy.70
  15.5 0.6 tile.8
  16.1 1.0 pad_maximum_fusion
  17.1 7.4 %all-to-all-start = ((bf16[16,224,128]{2,1,0:T(8,128)(2,1)}), bf16[16,224,128]{2,1,0:T(8,128)(2,1)S(1)}, u32[]{:S(2)}, u32[]{:S(2)}) async-start(bf16[16,224,128]{2,1,0:T(8,128)(2,1)} %pad_maximum_fusion), calls=%async_computation | async-start | bytes 1835008 | tf_op jit(solution)/shard_map/all_to_all | solution.py:67
  24.5 1.2 collective-permute-start.1
  25.7 0.6 dynamic_slice.13
  26.3 0.6 fusion.28
  27.0 0.1 eq.70
  27.1 0.1 eq.66
  27.5 0.2 select_reduce_fusion.1
  27.8 0.9 reduce-window.6
  28.7 0.2 slice_reduce_fusion
  29.1 0.1 sub.32
  29.3 25.1 %all-to-all-done = bf16[16,224,128]{2,1,0:T(8,128)(2,1)S(1)} async-done(((bf16[16,224,128]{2,1,0:T(8,128)(2,1)}), bf16[16,224,128]{2,1,0:T(8,128)(2,1)S(1)}, u32[]{:S(2)}, u32[]{:S(2)}) %all-to-all-start) | async-done | bytes 917536 | tf_op jit(solution)/shard_map/all_to_all | solution.py:67
  54.5 0.5 copy.61
  55.0 0.2 fusion.30
  55.2 0.1 copy.62
  55.4 0.7 fusion.31
  56.2 0.6 fusion.4
  56.7 1.4 fusion.12
  58.1 4.8 %all-to-all-start.1 = ((bf16[16,32,128]{2,1,0:T(8,128)(2,1)}), bf16[16,32,128]{2,1,0:T(8,128)(2,1)S(1)}, u32[]{:S(2)}, u32[]{:S(2)}) async-start(bf16[16,32,128]{2,1,0:T(8,128)(2,1)} %bitcast.11), calls=%async_computation.1 | async-start | bytes 262144 | tf_op jit(solution)/shard_map/all_to_all | solution.py:87
  62.9 0.2 fusion.15
  63.0 8.1 %all-to-all-done.1 = bf16[16,32,128]{2,1,0:T(8,128)(2,1)S(1)} async-done(((bf16[16,32,128]{2,1,0:T(8,128)(2,1)}), bf16[16,32,128]{2,1,0:T(8,128)(2,1)S(1)}, u32[]{:S(2)}, u32[]{:S(2)}) %all-to-all-start.1) | async-done | bytes 131104 | tf_op jit(solution)/shard_map/all_to_all | solution.py:87
  71.2 9.4 %all-gather.2.cloned.1.call-done = bf16[1024,2048]{1,0:T(8,128)(2,1)} async-done(((bf16[1024,128]{1,0:T(8,128)(2,1)}), bf16[1024,2048]{1,0:T(8,128)(2,1)}) %all-gather.2.cloned.1.call-update) | async-done | bytes 4194320 | tf_op jit(solution)/shard_map/all_gather | solution.py:101
  80.6 3.2 %multiply_reduce_fusion = (f32[64]{0:T(128)S(1)}, f32[64,2048]{1,0:T(8,128)S(1)}) fusion(bf16[1024,2048]{1,0:T(8,128)(2,1)} %all-gather.2.cloned.1.call-done, bf16[8,8,8,128]{3,2,1,0:T(8,128)(2,1)S(1)} %bitcast.81, bf16[64,2048]{1,0:T(8,128)(2,1)S(1)} %copy-done.1), kind=kOutput, calls=%fused_computation.31 | convolution fusion | flops 269221824 | bytes 5112064 | tf_op jit(solution)/shard_map/dot_general | solution.py:99
  83.7 0.1 multiply_convert_fusion
  83.9 4.7 %collective-permute-done.1 = bf16[1,1024,1408]{2,1,0:T(8,128)(2,1)} collective-permute-done((bf16[1,1024,1408]{2,1,0:T(8,128)(2,1)}, bf16[1,1024,1408]{2,1,0:T(8,128)(2,1)}, u32[]{:S(2)}, u32[]{:S(2)}) %collective-permute-start.1) | collective-permute-done | bytes 2883616 | tf_op jit(solution)/shard_map/ppermute | solution.py:29
  88.5 2.1 convolution_convert_fusion
  90.6 6.8 %all-to-all-start.2 = ((bf16[16,32,2048]{2,1,0:T(8,128)(2,1)}), bf16[16,32,2048]{2,1,0:T(8,128)(2,1)S(1)}, u32[]{:S(2)}, u32[]{:S(2)}) async-start(bf16[16,32,2048]{2,1,0:T(8,128)(2,1)} %bitcast.15), calls=%async_computation.2 | async-start | bytes 4194304 | tf_op jit(solution)/shard_map/all_to_all | solution.py:123
  97.5 1.3 collective-permute-start.2
  98.8 31.9 %collective-permute-done.2 = bf16[1,704,1024]{2,1,0:T(8,128)(2,1)} collective-permute-done((bf16[1,704,1024]{2,1,0:T(8,128)(2,1)}, bf16[1,704,1024]{2,1,0:T(8,128)(2,1)}, u32[]{:S(2)}, u32[]{:S(2)}) %collective-permute-start.2) | collective-permute-done | bytes 1441824 | tf_op jit(solution)/shard_map/ppermute | solution.py:29
  130.7 14.2 %all-to-all-done.2 = bf16[16,32,2048]{2,1,0:T(8,128)(2,1)S(1)} async-done(((bf16[16,32,2048]{2,1,0:T(8,128)(2,1)}), bf16[16,32,2048]{2,1,0:T(8,128)(2,1)S(1)}, u32[]{:S(2)}, u32[]{:S(2)}) %all-to-all-start.2) | async-done | bytes 2097184 | tf_op jit(solution)/shard_map/all_to_all | solution.py:123
  144.9 3.8 %fusion.1 = f32[512,1408]{1,0:T(8,128)S(1)} fusion(bf16[1,1024,1408]{2,1,0:T(8,128)(2,1)} %collective-permute-done.1, bf16[512,2048]{1,0:T(8,128)(2,1)S(1)} %bitcast.74, s32[]{:T(128)S(6)} %select_n.85), kind=kOutput, calls=%fused_computation.6 | convolution fusion | flops 1476395008 | bytes 6815748 | tf_op jit(solution)/shard_map/dot_general | solution.py:132
  148.7 1.8 convolution_add_fusion
  150.5 0.5 fusion.8
  151.0 0.9 copy-done.6
  151.9 1.0 convolution_convert_fusion.2
  152.8 2.3 %convolution_convert_fusion.1 = bf16[512,1024]{1,0:T(8,128)(2,1)S(1)} fusion(bf16[512,704]{1,0:T(8,128)(2,1)S(1)} %fusion.8, bf16[1,704,1024]{2,1,0:T(8,128)(2,1)} %collective-permute-done.2), kind=kOutput, calls=%fused_computation.19 | convolution fusion | flops 738721792 | bytes 3211264 | tf_op jit(solution)/shard_map/dot_general | solution.py:137
  155.2 2.2 %maximum_select_fusion = bf16[16,32,2048]{2,1,0:T(8,128)(2,1)} fusion(bf16[16,32,1024]{2,1,0:T(8,128)(2,1)S(1)} %bitcast.78, bf16[16,32,1024]{2,1,0:T(8,128)(2,1)S(1)} %bitcast.77, pred[]{:T(512)S(6)} %eq.65), kind=kLoop, calls=%fused_computation.15 | loop fusion | flops 9437184 | bytes 4194305 | tf_op jit(solution)/shard_map/jit(_where)/select_n | solution.py:138
  157.4 5.0 %all-to-all-start.3 = ((bf16[16,32,2048]{2,1,0:T(8,128)(2,1)}), bf16[16,32,2048]{2,1,0:T(8,128)(2,1)S(1)}, u32[]{:S(2)}, u32[]{:S(2)}) async-start(bf16[16,32,2048]{2,1,0:T(8,128)(2,1)} %maximum_select_fusion), calls=%async_computation.3 | async-start | bytes 4194304 | tf_op jit(solution)/shard_map/all_to_all | solution.py:149
  162.4 0.2 select_reduce_fusion
  162.6 47.2 %all-to-all-done.3 = bf16[16,32,2048]{2,1,0:T(8,128)(2,1)S(1)} async-done(((bf16[16,32,2048]{2,1,0:T(8,128)(2,1)}), bf16[16,32,2048]{2,1,0:T(8,128)(2,1)S(1)}, u32[]{:S(2)}, u32[]{:S(2)}) %all-to-all-start.3) | async-done | bytes 2097184 | tf_op jit(solution)/shard_map/all_to_all | solution.py:149
  209.9 1.9 fusion.7
  (40 shorter events, 1.0 us)
Async XLA Ops:
  6.5 20.9 %copy-start = (s32[2,96]{1,0:T(2,128)S(1)}, s32[2,96]{1,0:T(2,128)}, u32[]{:S(2)}) copy-start(s32[2,96]{1,0:T(2,128)} %param.15) | copy-start | bytes 2308
  6.5 74.0 %all-gather.2.cloned.1.call-start = ((), (), s32[]{:S(2)}) async-start(), calls=%async_computation.4 | async-start | bytes 4456448 | tf_op jit(solution)/shard_map/all_gather | solution.py:101
  6.5 4.6 %collective-permute-start = (bf16[512,128]{1,0:T(8,128)(2,1)}, bf16[512,128]{1,0:T(8,128)(2,1)S(1)}, u32[]{:S(2)}, u32[]{:S(2)}) collective-permute-start(bf16[512,128]{1,0:T(8,128)(2,1)} %param.18), channel_id=1, source_target_pairs={{0,16},{16,0},{1,17},{17,1},{2,18},{18,2},{3,19},{19,3},{4,20},{20... | collective-permute-start | bytes 393224 | tf_op jit(solution)/shard_map/ppermute | solution.py:29
  14.5 11.3 %copy-start.7 = (s32[2]{0:T(128)S(1)}, s32[2]{0:T(128)}, u32[]{:S(2)}) copy-start(s32[2]{0:T(128)} %param.16) | copy-start | bytes 28
  14.5 11.8 %copy-start.8 = (s32[1,16]{1,0:T(1,128)S(1)}, s32[1,16]{1,0:T(1,128)}, u32[]{:S(2)}) copy-start(s32[1,16]{1,0:T(1,128)} %param.17) | copy-start | bytes 196
  14.5 12.4 %copy-start.2 = (s32[64,6]{0,1:T(8,128)S(1)}, s32[64,6]{0,1:T(8,128)}, u32[]{:S(2)}) copy-start(s32[64,6]{0,1:T(8,128)} %param.20) | copy-start | bytes 4612
  17.1 37.3 %all-to-all-start = ((bf16[16,224,128]{2,1,0:T(8,128)(2,1)}), bf16[16,224,128]{2,1,0:T(8,128)(2,1)S(1)}, u32[]{:S(2)}, u32[]{:S(2)}) async-start(bf16[16,224,128]{2,1,0:T(8,128)(2,1)} %pad_maximum_fusion), calls=%async_computation | async-start | bytes 1835008 | tf_op jit(solution)/shard_map/all_to_all | solution.py:67
  24.5 64.0 %collective-permute-start.1 = (bf16[1,1024,1408]{2,1,0:T(8,128)(2,1)}, bf16[1,1024,1408]{2,1,0:T(8,128)(2,1)}, u32[]{:S(2)}, u32[]{:S(2)}) collective-permute-start(bf16[1,1024,1408]{2,1,0:T(8,128)(2,1)} %param.22), channel_id=1, source_target_pairs={{0,16},{16,0},{1,17},{17,1},{2,18},{18,2},{3,19},{19,3},{4,20},{20... | collective-permute-start | bytes 8650760 | tf_op jit(solution)/shard_map/ppermute | solution.py:29
  56.7 23.8 %copy-start.1 = (bf16[64,2048]{1,0:T(8,128)(2,1)S(1)}, bf16[64,2048]{1,0:T(8,128)(2,1)}, u32[]{:S(2)}) copy-start(bf16[64,2048]{1,0:T(8,128)(2,1)} %param.13) | copy-start | bytes 786436
  58.1 25.6 %copy-start.3 = (f32[2048]{0:T(1024)S(1)}, f32[2048]{0:T(1024)}, u32[]{:S(2)}) copy-start(f32[2048]{0:T(1024)} %param.19) | copy-start | bytes 24580
  58.1 13.0 %all-to-all-start.1 = ((bf16[16,32,128]{2,1,0:T(8,128)(2,1)}), bf16[16,32,128]{2,1,0:T(8,128)(2,1)S(1)}, u32[]{:S(2)}, u32[]{:S(2)}) async-start(bf16[16,32,128]{2,1,0:T(8,128)(2,1)} %bitcast.11), calls=%async_computation.1 | async-start | bytes 262144 | tf_op jit(solution)/shard_map/all_to_all | solution.py:87
  90.6 54.3 %all-to-all-start.2 = ((bf16[16,32,2048]{2,1,0:T(8,128)(2,1)}), bf16[16,32,2048]{2,1,0:T(8,128)(2,1)S(1)}, u32[]{:S(2)}, u32[]{:S(2)}) async-start(bf16[16,32,2048]{2,1,0:T(8,128)(2,1)} %bitcast.15), calls=%async_computation.2 | async-start | bytes 4194304 | tf_op jit(solution)/shard_map/all_to_all | solution.py:123
  97.5 33.2 %collective-permute-start.2 = (bf16[1,704,1024]{2,1,0:T(8,128)(2,1)}, bf16[1,704,1024]{2,1,0:T(8,128)(2,1)}, u32[]{:S(2)}, u32[]{:S(2)}) collective-permute-start(bf16[1,704,1024]{2,1,0:T(8,128)(2,1)} %param.23), channel_id=1, source_target_pairs={{0,16},{16,0},{1,17},{17,1},{2,18},{18,2},{3,19},{19,3},{4,20},{20... | collective-permute-start | bytes 4325384 | tf_op jit(solution)/shard_map/ppermute | solution.py:29
  144.9 3.8 %copy-start.5 = (bf16[1,1024,1408]{2,1,0:T(8,128)(2,1)S(1)}, bf16[1,1024,1408]{2,1,0:T(8,128)(2,1)}, u32[]{:S(2)}) copy-start(bf16[1,1024,1408]{2,1,0:T(8,128)(2,1)} %param.22) | copy-start | bytes 8650756
  150.5 1.4 copy-start.6
  157.4 5.0 %copy-start.4 = (f32[64,6]{0,1:T(8,128)S(1)}, f32[64,6]{0,1:T(8,128)}, u32[]{:S(2)}) copy-start(f32[64,6]{0,1:T(8,128)} %param.21) | copy-start | bytes 4612
  157.4 52.5 %all-to-all-start.3 = ((bf16[16,32,2048]{2,1,0:T(8,128)(2,1)}), bf16[16,32,2048]{2,1,0:T(8,128)(2,1)S(1)}, u32[]{:S(2)}, u32[]{:S(2)}) async-start(bf16[16,32,2048]{2,1,0:T(8,128)(2,1)} %maximum_select_fusion), calls=%async_computation.3 | async-start | bytes 4194304 | tf_op jit(solution)/shard_map/all_to_all | solution.py:149
Sparse Core Ops, SparseCore 0:
  13.0 67.4 all-gather.1

commit v5 on v4

--- a/solution.py
+++ b/solution.py
@@ -96,11 +96,23 @@
         )
     else:
         wo_rows = lax.all_gather(out_weight, "dp", axis=0, tiled=True)
-    projected = jnp.dot(
-        attended,
-        lax.all_gather(wo_rows, "mp", axis=1, tiled=True),
-        preferred_element_type=jnp.float32,
+    half = n_mp // 2
+    mirror = lax.ppermute(wo_rows, "mp", [(m, (m + half) % n_mp) for m in range(n_mp)])
+    sides = [list(range(half)), list(range(half, n_mp))]
+    gathered = lax.all_gather(
+        jnp.stack([wo_rows, mirror]), "mp", axis=1, axis_index_groups=sides
     )
+    near_side = column // half == 0
+    w_stack = jnp.concatenate(
+        [
+            jnp.where(near_side, gathered[0], gathered[1]),
+            jnp.where(near_side, gathered[1], gathered[0]),
+        ],
+        axis=0,
+    )
+    projected = jnp.einsum(
+        "tk,mkc->tmc", attended, w_stack, preferred_element_type=jnp.float32
+    ).reshape(q_count, d_model)
     resid_f = (hidden.astype(jnp.float32) + projected).astype(jnp.bfloat16).astype(jnp.float32)
     mean_square = jnp.mean(resid_f * resid_f, axis=1, keepdims=True)
     normed = (resid_f * lax.rsqrt(mean_square + epsilon) * norm_gain[None, :]).astype(jnp.bfloat16)

time: 219 us -> 231 us (1.055)
  starting transfers between devices: 27.9 us -> 34.9 us
  other arithmetic: 8.37 us -> 14.5 us
  waiting for transfers between devices: 144 us -> 138 us
  local copies, waits for them, and re-layouts: 6.57 us -> 11.2 us
    ppermute x0 -> x1, waiting for transfers between devices: none -> 10.5 us  [on_device(): lax.ppermute(wo_rows, 'mp', [(m, (m + half) % n_mp) for m in range(n_mp)])]
    all_gather x1, waiting for transfers between devices: 9.36 us -> 0.02 us  [on_device(): lax.all_gather(jnp.stack([wo_rows, mirror]), 'mp', axis=1, axis_index_gro...]
    dot_general x0 -> x1, local copies, waits for them, and re-layouts: none -> 6.46 us  [on_device(): jnp.einsum('tk,mkc->tmc', attended, w_stack, preferred_element_type=jnp.f...]
    all_to_all x1, starting transfers between devices: 4.76 us -> 9.63 us  [on_device(): lax.all_to_all(blended.reshape(n_mp, sub, HD), 'mp', split_axis=0, concat...]
    all_to_all x1, waiting for transfers between devices: 8.09 us -> 5.03 us  [on_device(): lax.all_to_all(blended.reshape(n_mp, sub, HD), 'mp', split_axis=0, concat...]
    ppermute x3, waiting for transfers between devices: 39.9 us -> 37.3 us  [swap_dp(): return lax.ppermute(x, 'dp', [(0, 1), (1, 0)])]
    select_n x0 -> x1, other arithmetic: none -> 2.5 us  [on_device(): jnp.where(near_side, gathered[0], gathered[1])]
    ppermute x0 -> x1, starting transfers between devices: none -> 2.37 us  [on_device(): lax.ppermute(wo_rows, 'mp', [(m, (m + half) % n_mp) for m in range(n_mp)])]
  transfers between devices with their start and end apart: 8 -> 9, of which waited for: 8 -> 8; matrix products, arithmetic and copies ran while one was open for 7% -> 11% of each run, Pallas kernels for 0% -> 0%
where the time goes in v5:
time: 231 us
  waiting for transfers between devices  138 us (60%)
  starting transfers between devices  34.9 us (15%)
  matrix products  18.7 us (8%)
  other arithmetic  14.5 us (6%)
  between operations  13.8 us (6%)
  local copies, waits for them, and re-layouts  11.2 us (5%)
    all_to_all x1, waiting for transfers between devices, on_device(): lax.all_to_all(outcome.reshape(n_mp, capacity, d_model), 'mp', split_axis...  47.2 us
    ppermute x3, waiting for transfers between devices, swap_dp(): return lax.ppermute(x, 'dp', [(0, 1), (1, 0)])  37.3 us
    all_to_all x1, waiting for transfers between devices, on_device(): lax.all_to_all(jnp.concatenate([q_out, kv_out], axis=1), 'mp', split_axis...  23.3 us
    all_to_all x1, waiting for transfers between devices, on_device(): lax.all_to_all(sending.reshape(n_mp, capacity, d_model), 'mp', split_axis...  14.2 us
    ppermute x1, waiting for transfers between devices, on_device(): lax.ppermute(wo_rows, 'mp', [(m, (m + half) % n_mp) for m in range(n_mp)])  10.5 us
    all_to_all x1, starting transfers between devices, on_device(): lax.all_to_all(blended.reshape(n_mp, sub, HD), 'mp', split_axis=0, concat...  9.63 us
    all_to_all x1, starting transfers between devices, on_device(): lax.all_to_all(jnp.concatenate([q_out, kv_out], axis=1), 'mp', split_axis...  7.16 us
    all_to_all x1, starting transfers between devices, on_device(): lax.all_to_all(sending.reshape(n_mp, capacity, d_model), 'mp', split_axis...  6.84 us
  transfers between devices with their start and end apart: 9, of which 8 were waited for; matrix products, arithmetic and copies ran while one was open for 11% of the time, Pallas kernels for 0%

profile of v5, /device:TPU:11, one launch (start us, length us, event | category | flops | bytes accessed | tf_op | source)
XLA Modules:
  0.0 230.6 jit_solution(4421318348075619837)
XLA Ops:
  6.5 1.3 collective-permute-start
  7.9 3.3 %collective-permute-done = bf16[512,128]{1,0:T(8,128)(2,1)S(1)} collective-permute-done((bf16[512,128]{1,0:T(8,128)(2,1)}, bf16[512,128]{1,0:T(8,128)(2,1)S(1)}, u32[]{:S(2)}, u32[]{:S(2)}) %collective-permute-start) | collective-permute-done | bytes 131104 | tf_op jit(solution)/shard_map/ppermute | solution.py:29
  11.2 1.1 maximum_select_fusion.2
  12.2 2.4 %collective-permute-start.1 = (bf16[1024,128]{1,0:T(8,128)(2,1)S(1)}, bf16[1024,128]{1,0:T(8,128)(2,1)S(1)}, u32[]{:S(2)}, u32[]{:S(2)}) collective-permute-start(bf16[1024,128]{1,0:T(8,128)(2,1)S(1)} %maximum_select_fusion.2), channel_id=1, source_target_pairs={{0,8},{1,9},{2,10},{3,11},{4,12},{5,13},{6,14},{7,15},{8,0},{9,1},... | collective-permute-start | bytes 786440 | tf_op jit(solution)/shard_map/ppermute | solution.py:100
  14.6 1.1 maximum_select_fusion.1
  15.7 10.5 %collective-permute-done.1 = bf16[1024,128]{1,0:T(8,128)(2,1)S(1)} collective-permute-done((bf16[1024,128]{1,0:T(8,128)(2,1)S(1)}, bf16[1024,128]{1,0:T(8,128)(2,1)S(1)}, u32[]{:S(2)}, u32[]{:S(2)}) %collective-permute-start.1) | collective-permute-done | bytes 262176 | tf_op jit(solution)/shard_map/ppermute | solution.py:100
  26.2 0.9 pad_maximum_fusion.1
  27.0 0.3 reshape.227
  27.3 0.3 copy.63
  27.7 0.6 tile.8
  28.3 1.0 pad_maximum_fusion
  29.3 7.2 %all-to-all-start = ((bf16[16,224,128]{2,1,0:T(8,128)(2,1)}), bf16[16,224,128]{2,1,0:T(8,128)(2,1)S(1)}, u32[]{:S(2)}, u32[]{:S(2)}) async-start(bf16[16,224,128]{2,1,0:T(8,128)(2,1)} %pad_maximum_fusion), calls=%async_computation | async-start | bytes 1835008 | tf_op jit(solution)/shard_map/all_to_all | solution.py:67
  36.5 1.2 collective-permute-start.2
  37.7 0.6 dynamic_slice.13
  38.3 0.7 fusion.28
  39.6 0.2 select_reduce_fusion.1
  40.0 0.9 reduce-window.6
  40.8 0.2 slice_reduce_fusion
  41.4 23.3 %all-to-all-done = bf16[16,224,128]{2,1,0:T(8,128)(2,1)S(1)} async-done(((bf16[16,224,128]{2,1,0:T(8,128)(2,1)}), bf16[16,224,128]{2,1,0:T(8,128)(2,1)S(1)}, u32[]{:S(2)}, u32[]{:S(2)}) %all-to-all-start) | async-done | bytes 917536 | tf_op jit(solution)/shard_map/all_to_all | solution.py:67
  64.8 0.5 copy.64
  65.4 0.2 fusion.30
  65.8 0.7 fusion.31
  66.5 0.6 fusion.4
  67.1 1.4 fusion.12
  68.5 9.6 %all-to-all-start.1 = ((bf16[16,32,128]{2,1,0:T(8,128)(2,1)}), bf16[16,32,128]{2,1,0:T(8,128)(2,1)S(1)}, u32[]{:S(2)}, u32[]{:S(2)}) async-start(bf16[16,32,128]{2,1,0:T(8,128)(2,1)} %bitcast.11), calls=%async_computation.1 | async-start | bytes 262144 | tf_op jit(solution)/shard_map/all_to_all | solution.py:87
  78.1 0.2 fusion.15
  78.3 5.0 %all-to-all-done.1 = bf16[16,32,128]{2,1,0:T(8,128)(2,1)S(1)} async-done(((bf16[16,32,128]{2,1,0:T(8,128)(2,1)}), bf16[16,32,128]{2,1,0:T(8,128)(2,1)S(1)}, u32[]{:S(2)}, u32[]{:S(2)}) %all-to-all-start.1) | async-done | bytes 131104 | tf_op jit(solution)/shard_map/all_to_all | solution.py:87
  83.4 2.5 %broadcast_select_fusion.1 = (bf16[1,8192,128]{2,1,0:T(8,128)(2,1)S(1)}, bf16[1,8192,128]{2,1,0:T(8,128)(2,1)S(1)}) fusion(pred[]{:T(512)S(6)} %eq.68, bf16[2,8192,128]{2,1,0:T(8,128)(2,1)} %all-gather.3.cloned.1.call-done), kind=kLoop, calls=%fused_computation.18 | loop fusion | flops 2097152 | bytes 8388609 | tf_op jit(solution)/shard_map/jit(_where)/select_n | solution.py:108
  85.9 2.3 maximum_bitcast_fusion
  88.2 6.5 %copy.68 = bf16[16,128,1024]{2,1,0:T(8,128)(2,1)} copy(bf16[16,128,1024]{1,2,0:T(8,128)(2,1)} %maximum_bitcast_fusion) | data formatting | bytes 8388608 | tf_op jit(solution)/shard_map/tk,mkc->tmc/dot_general | solution.py:113
  94.6 3.7 %multiply_reduce_fusion = (f32[64]{0:T(128)S(1)}, f32[64,2048]{1,0:T(8,128)S(1)}) fusion(bf16[2048,1024]{1,0:T(8,128)(2,1)} %bitcast.79, bf16[8,8,8,128]{3,2,1,0:T(8,128)(2,1)S(1)} %bitcast.94, bf16[64,2048]{1,0:T(8,128)(2,1)S(1)} %copy-done.2), kind=kOutput, calls=%fused_computation.35 | convolution fusion | flops 269221824 | bytes 5112064 | tf_op jit(solution)/shard_map/tk,mkc->tmc/dot_general | solution.py:113
  98.5 2.0 collective-permute-done.2
  100.5 2.1 convolution_convert_fusion
  102.6 6.8 %all-to-all-start.2 = ((bf16[16,32,2048]{2,1,0:T(8,128)(2,1)}), bf16[16,32,2048]{2,1,0:T(8,128)(2,1)S(1)}, u32[]{:S(2)}, u32[]{:S(2)}) async-start(bf16[16,32,2048]{2,1,0:T(8,128)(2,1)} %bitcast.22), calls=%async_computation.2 | async-start | bytes 4194304 | tf_op jit(solution)/shard_map/all_to_all | solution.py:135
  109.5 1.3 collective-permute-start.3
  110.8 31.9 %collective-permute-done.3 = bf16[1,704,1024]{2,1,0:T(8,128)(2,1)} collective-permute-done((bf16[1,704,1024]{2,1,0:T(8,128)(2,1)}, bf16[1,704,1024]{2,1,0:T(8,128)(2,1)}, u32[]{:S(2)}, u32[]{:S(2)}) %collective-permute-start.3) | collective-permute-done | bytes 1441824 | tf_op jit(solution)/shard_map/ppermute | solution.py:29
  142.7 14.2 %all-to-all-done.2 = bf16[16,32,2048]{2,1,0:T(8,128)(2,1)S(1)} async-done(((bf16[16,32,2048]{2,1,0:T(8,128)(2,1)}), bf16[16,32,2048]{2,1,0:T(8,128)(2,1)S(1)}, u32[]{:S(2)}, u32[]{:S(2)}) %all-to-all-start.2) | async-done | bytes 2097184 | tf_op jit(solution)/shard_map/all_to_all | solution.py:135
  156.9 3.8 %fusion.1 = f32[512,1408]{1,0:T(8,128)S(1)} fusion(bf16[1,1024,1408]{2,1,0:T(8,128)(2,1)} %collective-permute-done.2, bf16[512,2048]{1,0:T(8,128)(2,1)S(1)} %bitcast.85, s32[]{:T(128)S(6)} %select_n.122), kind=kOutput, calls=%fused_computation.7 | convolution fusion | flops 1476395008 | bytes 6815748 | tf_op jit(solution)/shard_map/dot_general | solution.py:144
  160.7 1.8 convolution_add_fusion
  162.5 0.5 fusion.8
  163.0 0.9 copy-done.8
  163.9 1.0 convolution_convert_fusion.2
  164.9 2.3 %convolution_convert_fusion.1 = bf16[512,1024]{1,0:T(8,128)(2,1)S(1)} fusion(bf16[512,704]{1,0:T(8,128)(2,1)S(1)} %fusion.8, bf16[1,704,1024]{2,1,0:T(8,128)(2,1)} %collective-permute-done.3), kind=kOutput, calls=%fused_computation.22 | convolution fusion | flops 738721792 | bytes 3211264 | tf_op jit(solution)/shard_map/dot_general | solution.py:149
  167.2 2.2 maximum_select_fusion
  169.4 5.0 %all-to-all-start.3 = ((bf16[16,32,2048]{2,1,0:T(8,128)(2,1)}), bf16[16,32,2048]{2,1,0:T(8,128)(2,1)S(1)}, u32[]{:S(2)}, u32[]{:S(2)}) async-start(bf16[16,32,2048]{2,1,0:T(8,128)(2,1)} %maximum_select_fusion), calls=%async_computation.3 | async-start | bytes 4194304 | tf_op jit(solution)/shard_map/all_to_all | solution.py:161
  174.4 0.2 select_reduce_fusion
  174.6 47.2 %all-to-all-done.3 = bf16[16,32,2048]{2,1,0:T(8,128)(2,1)S(1)} async-done(((bf16[16,32,2048]{2,1,0:T(8,128)(2,1)}), bf16[16,32,2048]{2,1,0:T(8,128)(2,1)S(1)}, u32[]{:S(2)}, u32[]{:S(2)}) %all-to-all-start.3) | async-done | bytes 2097184 | tf_op jit(solution)/shard_map/all_to_all | solution.py:161
  221.9 1.9 fusion.7
  (51 shorter events, 1.7 us)
Async XLA Ops:
  6.5 33.0 %copy-start = (s32[2,96]{1,0:T(2,128)S(1)}, s32[2,96]{1,0:T(2,128)}, u32[]{:S(2)}) copy-start(s32[2,96]{1,0:T(2,128)} %param.15) | copy-start | bytes 2308
  6.5 20.5 %copy-start.1 = (bf16[6,16,2,1024]{3,2,1,0:T(2,128)(2,1)S(1)}, bf16[6,16,2,1024]{3,2,1,0:T(2,128)(2,1)}, u32[]{:S(2)}) copy-start(bf16[6,16,2,1024]{3,2,1,0:T(2,128)(2,1)} %param.14) | copy-start | bytes 1179652
  6.5 21.1 %copy-start.3 = (bf16[64,1024]{1,0:T(8,128)(2,1)S(1)}, bf16[64,1024]{1,0:T(8,128)(2,1)}, u32[]{:S(2)}) copy-start(bf16[64,1024]{1,0:T(8,128)(2,1)} %param.12) | copy-start | bytes 393220
  6.5 76.8 %all-gather.3.cloned.1.call-start = ((), (), s32[]{:S(2)}) async-start(), calls=%async_computation.4 | async-start | bytes 4718592 | tf_op jit(solution)/shard_map/all_gather | solution.py:102
  6.5 4.6 %collective-permute-start = (bf16[512,128]{1,0:T(8,128)(2,1)}, bf16[512,128]{1,0:T(8,128)(2,1)S(1)}, u32[]{:S(2)}, u32[]{:S(2)}) collective-permute-start(bf16[512,128]{1,0:T(8,128)(2,1)} %param.18), channel_id=1, source_target_pairs={{0,16},{16,0},{1,17},{17,1},{2,18},{18,2},{3,19},{19,3},{4,20},{20... | collective-permute-start | bytes 393224 | tf_op jit(solution)/shard_map/ppermute | solution.py:29
  12.2 13.9 %collective-permute-start.1 = (bf16[1024,128]{1,0:T(8,128)(2,1)S(1)}, bf16[1024,128]{1,0:T(8,128)(2,1)S(1)}, u32[]{:S(2)}, u32[]{:S(2)}) collective-permute-start(bf16[1024,128]{1,0:T(8,128)(2,1)S(1)} %maximum_select_fusion.2), channel_id=1, source_target_pairs={{0,8},{1,9},{2,10},{3,11},{4,12},{5,13},{6,14},{7,15},{8,0},{9,1},... | collective-permute-start | bytes 786440 | tf_op jit(solution)/shard_map/ppermute | solution.py:100
  27.6 10.1 %copy-start.9 = (s32[2]{0:T(128)S(1)}, s32[2]{0:T(128)}, u32[]{:S(2)}) copy-start(s32[2]{0:T(128)} %param.16) | copy-start | bytes 28
  27.6 10.7 %copy-start.10 = (s32[1,16]{1,0:T(1,128)S(1)}, s32[1,16]{1,0:T(1,128)}, u32[]{:S(2)}) copy-start(s32[1,16]{1,0:T(1,128)} %param.17) | copy-start | bytes 196
  27.6 11.4 %copy-start.4 = (s32[64,6]{0,1:T(8,128)S(1)}, s32[64,6]{0,1:T(8,128)}, u32[]{:S(2)}) copy-start(s32[64,6]{0,1:T(8,128)} %param.20) | copy-start | bytes 4612
  29.3 35.4 %all-to-all-start = ((bf16[16,224,128]{2,1,0:T(8,128)(2,1)}), bf16[16,224,128]{2,1,0:T(8,128)(2,1)S(1)}, u32[]{:S(2)}, u32[]{:S(2)}) async-start(bf16[16,224,128]{2,1,0:T(8,128)(2,1)} %pad_maximum_fusion), calls=%async_computation | async-start | bytes 1835008 | tf_op jit(solution)/shard_map/all_to_all | solution.py:67
  36.5 64.0 %collective-permute-start.2 = (bf16[1,1024,1408]{2,1,0:T(8,128)(2,1)}, bf16[1,1024,1408]{2,1,0:T(8,128)(2,1)}, u32[]{:S(2)}, u32[]{:S(2)}) collective-permute-start(bf16[1,1024,1408]{2,1,0:T(8,128)(2,1)} %param.22), channel_id=1, source_target_pairs={{0,16},{16,0},{1,17},{17,1},{2,18},{18,2},{3,19},{19,3},{4,20},{20... | collective-permute-start | bytes 8650760 | tf_op jit(solution)/shard_map/ppermute | solution.py:29
  68.5 14.8 %all-to-all-start.1 = ((bf16[16,32,128]{2,1,0:T(8,128)(2,1)}), bf16[16,32,128]{2,1,0:T(8,128)(2,1)S(1)}, u32[]{:S(2)}, u32[]{:S(2)}) async-start(bf16[16,32,128]{2,1,0:T(8,128)(2,1)} %bitcast.11), calls=%async_computation.1 | async-start | bytes 262144 | tf_op jit(solution)/shard_map/all_to_all | solution.py:87
  88.2 6.5 %copy-start.2 = (bf16[64,2048]{1,0:T(8,128)(2,1)S(1)}, bf16[64,2048]{1,0:T(8,128)(2,1)}, u32[]{:S(2)}) copy-start(bf16[64,2048]{1,0:T(8,128)(2,1)} %param.13) | copy-start | bytes 786436
  94.6 3.7 %copy-start.5 = (f32[2048]{0:T(1024)S(1)}, f32[2048]{0:T(1024)}, u32[]{:S(2)}) copy-start(f32[2048]{0:T(1024)} %param.19) | copy-start | bytes 24580
  102.6 54.3 %all-to-all-start.2 = ((bf16[16,32,2048]{2,1,0:T(8,128)(2,1)}), bf16[16,32,2048]{2,1,0:T(8,128)(2,1)S(1)}, u32[]{:S(2)}, u32[]{:S(2)}) async-start(bf16[16,32,2048]{2,1,0:T(8,128)(2,1)} %bitcast.22), calls=%async_computation.2 | async-start | bytes 4194304 | tf_op jit(solution)/shard_map/all_to_all | solution.py:135
  109.5 33.2 %collective-permute-start.3 = (bf16[1,704,1024]{2,1,0:T(8,128)(2,1)}, bf16[1,704,1024]{2,1,0:T(8,128)(2,1)}, u32[]{:S(2)}, u32[]{:S(2)}) collective-permute-start(bf16[1,704,1024]{2,1,0:T(8,128)(2,1)} %param.23), channel_id=1, source_target_pairs={{0,16},{16,0},{1,17},{17,1},{2,18},{18,2},{3,19},{19,3},{4,20},{20... | collective-permute-start | bytes 4325384 | tf_op jit(solution)/shard_map/ppermute | solution.py:29
  156.9 3.8 %copy-start.7 = (bf16[1,1024,1408]{2,1,0:T(8,128)(2,1)S(1)}, bf16[1,1024,1408]{2,1,0:T(8,128)(2,1)}, u32[]{:S(2)}) copy-start(bf16[1,1024,1408]{2,1,0:T(8,128)(2,1)} %param.22) | copy-start | bytes 8650756
  162.5 1.4 copy-start.8
  169.4 5.0 %copy-start.6 = (f32[64,6]{0,1:T(8,128)S(1)}, f32[64,6]{0,1:T(8,128)}, u32[]{:S(2)}) copy-start(f32[64,6]{0,1:T(8,128)} %param.21) | copy-start | bytes 4612
  169.4 52.5 %all-to-all-start.3 = ((bf16[16,32,2048]{2,1,0:T(8,128)(2,1)}), bf16[16,32,2048]{2,1,0:T(8,128)(2,1)S(1)}, u32[]{:S(2)}, u32[]{:S(2)}) async-start(bf16[16,32,2048]{2,1,0:T(8,128)(2,1)} %maximum_select_fusion), calls=%async_computation.3 | async-start | bytes 4194304 | tf_op jit(solution)/shard_map/all_to_all | solution.py:161
Sparse Core Ops, SparseCore 0:
  27.2 44.4 all-gather.2

commit v6 on v4

--- a/solution.py
+++ b/solution.py
@@ -125,27 +125,24 @@
     )
     flat_rows = received.reshape(-1, d_model)
     if n_dp == 2:
+        first = row_index == 0
+        gate_up = jnp.where(
+            first,
+            jnp.concatenate([experts_in[0], in_other[0]], axis=0),
+            jnp.concatenate([in_other[0], experts_in[0]], axis=0),
+        )
         flat_rows, out_other = lax.optimization_barrier((flat_rows, out_other))
-        half_in = experts_in.shape[1]
-        rows_mine = lax.dynamic_slice_in_dim(flat_rows, row_index * half_in, half_in, axis=1)
-        rows_other = lax.dynamic_slice_in_dim(flat_rows, (1 - row_index) * half_in, half_in, axis=1)
-        gate_vals = jnp.dot(rows_mine, experts_in[0], preferred_element_type=jnp.float32) + jnp.dot(
-            rows_other, in_other[0], preferred_element_type=jnp.float32
-        )
-        act = (jax.nn.silu(gate_vals[:, :ff_width]) * gate_vals[:, ff_width:]).astype(jnp.bfloat16)
-        part_mine = jnp.dot(act, experts_out[0], preferred_element_type=jnp.float32).astype(jnp.bfloat16)
-        part_other = jnp.dot(act, out_other[0], preferred_element_type=jnp.float32).astype(jnp.bfloat16)
-        outcome = jnp.where(
-            row_index == 0,
-            jnp.concatenate([part_mine, part_other], axis=1),
-            jnp.concatenate([part_other, part_mine], axis=1),
+        down = jnp.where(
+            first,
+            jnp.concatenate([experts_out[0], out_other[0]], axis=1),
+            jnp.concatenate([out_other[0], experts_out[0]], axis=1),
         )
     else:
-        gate_up = lax.all_gather(experts_in, "dp", axis=1, tiled=True)
-        down = lax.all_gather(experts_out, "dp", axis=2, tiled=True)
-        gate_vals = jnp.dot(flat_rows, gate_up[0], preferred_element_type=jnp.float32)
-        act = (jax.nn.silu(gate_vals[:, :ff_width]) * gate_vals[:, ff_width:]).astype(jnp.bfloat16)
-        outcome = jnp.dot(act, down[0], preferred_element_type=jnp.float32).astype(jnp.bfloat16)
+        gate_up = lax.all_gather(experts_in, "dp", axis=1, tiled=True)[0]
+        down = lax.all_gather(experts_out, "dp", axis=2, tiled=True)[0]
+    gate_vals = jnp.dot(flat_rows, gate_up, preferred_element_type=jnp.float32)
+    act = (jax.nn.silu(gate_vals[:, :ff_width]) * gate_vals[:, ff_width:]).astype(jnp.bfloat16)
+    outcome = jnp.dot(act, down, preferred_element_type=jnp.float32).astype(jnp.bfloat16)
     results = lax.all_to_all(
         outcome.reshape(n_mp, capacity, d_model), "mp", split_axis=0, concat_axis=0, tiled=True
     )

time: 219 us -> 219 us (level)
  matrix products: 18.2 us -> 21.6 us
  other arithmetic: 8.37 us -> 5.68 us
    dot_general x4 -> x2, matrix products: 8.89 us -> 12.4 us  [the longest x1 7.04 us: on_device(): gate_vals = jnp.dot(flat_rows, gate_up, preferred_element_type=jnp.float32)]
    select_n x1 -> x0, other arithmetic: 2.2 us -> none  [on_device(): jnp.where(row_index == 0, jnp.concatenate([part_mine, part_other], axis=1...]
where the time goes in v6:
time: 219 us
  waiting for transfers between devices  144 us (66%)
  starting transfers between devices  27.8 us (13%)
  matrix products  21.6 us (10%)
  between operations  13.7 us (6%)
  local copies, waits for them, and re-layouts  5.72 us (3%)
  other arithmetic  5.68 us (3%)
    all_to_all x1, waiting for transfers between devices, on_device(): lax.all_to_all(outcome.reshape(n_mp, capacity, d_model), 'mp', split_axis...  47.2 us
    ppermute x3, waiting for transfers between devices, swap_dp(): return lax.ppermute(x, 'dp', [(0, 1), (1, 0)])  39.9 us
    all_to_all x1, waiting for transfers between devices, on_device(): lax.all_to_all(jnp.concatenate([q_out, kv_out], axis=1), 'mp', split_axis...  25.1 us
    all_to_all x1, waiting for transfers between devices, on_device(): lax.all_to_all(sending.reshape(n_mp, capacity, d_model), 'mp', split_axis...  14.3 us
    all_gather x1, waiting for transfers between devices, on_device(): lax.all_gather(wo_rows, 'mp', axis=1, tiled=True)  9.36 us
    all_to_all x1, waiting for transfers between devices, on_device(): lax.all_to_all(blended.reshape(n_mp, sub, HD), 'mp', split_axis=0, concat...  8.11 us
    all_to_all x1, starting transfers between devices, on_device(): lax.all_to_all(jnp.concatenate([q_out, kv_out], axis=1), 'mp', split_axis...  7.43 us
    dot_general x1, matrix products, on_device(): gate_vals = jnp.dot(flat_rows, gate_up, preferred_element_type=jnp.float32)  7.04 us
  transfers between devices with their start and end apart: 8, of which 8 were waited for; matrix products, arithmetic and copies ran while one was open for 7% of the time, Pallas kernels for 0%

profile of v6, /device:TPU:11, one launch (start us, length us, event | category | flops | bytes accessed | tf_op | source)
XLA Modules:
  0.0 218.5 jit_solution(3411971738480546132)
XLA Ops:
  6.5 1.2 collective-permute-start
  7.8 3.3 %collective-permute-done = bf16[512,128]{1,0:T(8,128)(2,1)S(1)} collective-permute-done((bf16[512,128]{1,0:T(8,128)(2,1)}, bf16[512,128]{1,0:T(8,128)(2,1)S(1)}, u32[]{:S(2)}, u32[]{:S(2)}) %collective-permute-start) | collective-permute-done | bytes 131104 | tf_op jit(solution)/shard_map/ppermute | solution.py:29
  11.1 1.8 maximum_select_fusion.4
  12.9 1.2 reshape.164
  14.1 0.3 copy.60
  14.5 0.9 copy.70
  15.5 0.6 tile.8
  16.1 1.0 pad_maximum_fusion
  17.1 7.4 %all-to-all-start = ((bf16[16,224,128]{2,1,0:T(8,128)(2,1)}), bf16[16,224,128]{2,1,0:T(8,128)(2,1)S(1)}, u32[]{:S(2)}, u32[]{:S(2)}) async-start(bf16[16,224,128]{2,1,0:T(8,128)(2,1)} %pad_maximum_fusion), calls=%async_computation | async-start | bytes 1835008 | tf_op jit(solution)/shard_map/all_to_all | solution.py:67
  24.5 1.2 collective-permute-start.1
  25.7 0.6 dynamic_slice.7
  26.3 0.6 fusion.33
  26.9 0.1 copy.65
  27.0 0.1 eq.70
  27.1 0.1 eq.66
  27.4 0.1 add.155
  27.5 0.2 select_reduce_fusion.1
  27.7 0.1 add.146
  27.8 0.9 reduce-window.6
  28.7 0.2 slice_reduce_fusion
  29.0 0.1 fusion.27
  29.1 0.1 sub.29
  29.3 25.1 %all-to-all-done = bf16[16,224,128]{2,1,0:T(8,128)(2,1)S(1)} async-done(((bf16[16,224,128]{2,1,0:T(8,128)(2,1)}), bf16[16,224,128]{2,1,0:T(8,128)(2,1)S(1)}, u32[]{:S(2)}, u32[]{:S(2)}) %all-to-all-start) | async-done | bytes 917536 | tf_op jit(solution)/shard_map/all_to_all | solution.py:67
  54.5 0.5 copy.61
  55.0 0.2 fusion.38
  55.2 0.1 copy.62
  55.3 0.1 copy.63
  55.4 0.7 fusion.39
  56.2 0.6 fusion.14
  56.7 1.3 fusion.20
  58.1 4.8 %all-to-all-start.1 = ((bf16[16,32,128]{2,1,0:T(8,128)(2,1)}), bf16[16,32,128]{2,1,0:T(8,128)(2,1)S(1)}, u32[]{:S(2)}, u32[]{:S(2)}) async-start(bf16[16,32,128]{2,1,0:T(8,128)(2,1)} %bitcast.11), calls=%async_computation.1 | async-start | bytes 262144 | tf_op jit(solution)/shard_map/all_to_all | solution.py:87
  62.8 0.2 fusion.23
  63.0 8.1 %all-to-all-done.1 = bf16[16,32,128]{2,1,0:T(8,128)(2,1)S(1)} async-done(((bf16[16,32,128]{2,1,0:T(8,128)(2,1)}), bf16[16,32,128]{2,1,0:T(8,128)(2,1)S(1)}, u32[]{:S(2)}, u32[]{:S(2)}) %all-to-all-start.1) | async-done | bytes 131104 | tf_op jit(solution)/shard_map/all_to_all | solution.py:87
  71.2 9.4 %all-gather.2.cloned.1.call-done = bf16[1024,2048]{1,0:T(8,128)(2,1)} async-done(((bf16[1024,128]{1,0:T(8,128)(2,1)}), bf16[1024,2048]{1,0:T(8,128)(2,1)}) %all-gather.2.cloned.1.call-update) | async-done | bytes 4194320 | tf_op jit(solution)/shard_map/all_gather | solution.py:101
  80.6 3.2 %multiply_reduce_fusion = (f32[64]{0:T(128)S(1)}, f32[64,2048]{1,0:T(8,128)S(1)}) fusion(bf16[1024,2048]{1,0:T(8,128)(2,1)} %all-gather.2.cloned.1.call-done, bf16[8,8,8,128]{3,2,1,0:T(8,128)(2,1)S(1)} %bitcast.69, bf16[64,2048]{1,0:T(8,128)(2,1)S(1)} %copy-done.1), kind=kOutput, calls=%fused_computation.37 | convolution fusion | flops 269221824 | bytes 5112064 | tf_op jit(solution)/shard_map/dot_general | solution.py:99
  83.7 0.1 multiply_convert_fusion
  83.9 4.7 %collective-permute-done.1 = bf16[1,1024,1408]{2,1,0:T(8,128)(2,1)} collective-permute-done((bf16[1,1024,1408]{2,1,0:T(8,128)(2,1)}, bf16[1,1024,1408]{2,1,0:T(8,128)(2,1)}, u32[]{:S(2)}, u32[]{:S(2)}) %collective-permute-start.1) | collective-permute-done | bytes 2883616 | tf_op jit(solution)/shard_map/ppermute | solution.py:29
  88.5 2.1 convolution_convert_fusion.1
  90.6 6.8 %all-to-all-start.2 = ((bf16[16,32,2048]{2,1,0:T(8,128)(2,1)}), bf16[16,32,2048]{2,1,0:T(8,128)(2,1)S(1)}, u32[]{:S(2)}, u32[]{:S(2)}) async-start(bf16[16,32,2048]{2,1,0:T(8,128)(2,1)} %bitcast.15), calls=%async_computation.2 | async-start | bytes 4194304 | tf_op jit(solution)/shard_map/all_to_all | solution.py:123
  97.5 1.2 collective-permute-start.2
  98.7 31.9 %collective-permute-done.2 = bf16[1,704,1024]{2,1,0:T(8,128)(2,1)} collective-permute-done((bf16[1,704,1024]{2,1,0:T(8,128)(2,1)}, bf16[1,704,1024]{2,1,0:T(8,128)(2,1)}, u32[]{:S(2)}, u32[]{:S(2)}) %collective-permute-start.2) | collective-permute-done | bytes 1441824 | tf_op jit(solution)/shard_map/ppermute | solution.py:29
  130.6 14.3 %all-to-all-done.2 = bf16[16,32,2048]{2,1,0:T(8,128)(2,1)S(1)} async-done(((bf16[16,32,2048]{2,1,0:T(8,128)(2,1)}), bf16[16,32,2048]{2,1,0:T(8,128)(2,1)S(1)}, u32[]{:S(2)}, u32[]{:S(2)}) %all-to-all-start.2) | async-done | bytes 2097184 | tf_op jit(solution)/shard_map/all_to_all | solution.py:123
  144.9 7.0 %fusion = f32[512,1408]{1,0:T(8,128)S(1)} fusion(bf16[512,2048]{1,0:T(8,128)(2,1)S(1)} %bitcast.64, bf16[1024,1408]{1,0:T(8,128)(2,1)} %bitcast.18, bf16[1024,1408]{1,0:T(8,128)(2,1)} %bitcast.75, pred[]{:T(512)S(6)} %eq.65), kind=kOutput, calls=%fused_computation.1 | convolution fusion | flops 2978742272 | bytes 10747905 | tf_op jit(solution)/shard_map/dot_general | solution.py:143
  152.0 5.3 %convolution_convert_fusion = bf16[512,2048]{1,0:T(8,128)(2,1)} fusion(bf16[704,1024]{1,0:T(8,128)(2,1)} %bitcast.20, bf16[704,1024]{1,0:T(8,128)(2,1)S(1)} %bitcast.76, pred[]{:T(512)S(6)} %eq.65, f32[512,1408]{1,0:T(8,128)S(1)} %fusion), kind=kOutput, calls=%fused_computation.12 | convolution fusion | flops 1492582400 | bytes 8126465 | tf_op jit(solution)/shard_map/dot_general | solution.py:145
  157.3 5.0 %all-to-all-start.3 = ((bf16[16,32,2048]{2,1,0:T(8,128)(2,1)}), bf16[16,32,2048]{2,1,0:T(8,128)(2,1)S(1)}, u32[]{:S(2)}, u32[]{:S(2)}) async-start(bf16[16,32,2048]{2,1,0:T(8,128)(2,1)} %bitcast.65), calls=%async_computation.3 | async-start | bytes 4194304 | tf_op jit(solution)/shard_map/all_to_all | solution.py:146
  162.3 0.2 select_reduce_fusion
  162.5 47.2 %all-to-all-done.3 = bf16[16,32,2048]{2,1,0:T(8,128)(2,1)S(1)} async-done(((bf16[16,32,2048]{2,1,0:T(8,128)(2,1)}), bf16[16,32,2048]{2,1,0:T(8,128)(2,1)S(1)}, u32[]{:S(2)}, u32[]{:S(2)}) %all-to-all-start.3) | async-done | bytes 2097184 | tf_op jit(solution)/shard_map/all_to_all | solution.py:146
  209.7 1.9 fusion.17
  (34 shorter events, 0.5 us)
Async XLA Ops:
  6.5 20.9 %copy-start = (s32[2,96]{1,0:T(2,128)S(1)}, s32[2,96]{1,0:T(2,128)}, u32[]{:S(2)}) copy-start(s32[2,96]{1,0:T(2,128)} %param.15) | copy-start | bytes 2308
  6.5 74.0 %all-gather.2.cloned.1.call-start = ((), (), s32[]{:S(2)}) async-start(), calls=%async_computation.4 | async-start | bytes 4456448 | tf_op jit(solution)/shard_map/all_gather | solution.py:101
  6.5 4.6 %collective-permute-start = (bf16[512,128]{1,0:T(8,128)(2,1)}, bf16[512,128]{1,0:T(8,128)(2,1)S(1)}, u32[]{:S(2)}, u32[]{:S(2)}) collective-permute-start(bf16[512,128]{1,0:T(8,128)(2,1)} %param.18), channel_id=1, source_target_pairs={{0,16},{16,0},{1,17},{17,1},{2,18},{18,2},{3,19},{19,3},{4,20},{20... | collective-permute-start | bytes 393224 | tf_op jit(solution)/shard_map/ppermute | solution.py:29
  14.5 11.3 %copy-start.6 = (s32[2]{0:T(128)S(1)}, s32[2]{0:T(128)}, u32[]{:S(2)}) copy-start(s32[2]{0:T(128)} %param.16) | copy-start | bytes 28
  14.5 11.8 %copy-start.7 = (s32[1,16]{1,0:T(1,128)S(1)}, s32[1,16]{1,0:T(1,128)}, u32[]{:S(2)}) copy-start(s32[1,16]{1,0:T(1,128)} %param.17) | copy-start | bytes 196
  14.5 12.4 %copy-start.2 = (s32[64,6]{0,1:T(8,128)S(1)}, s32[64,6]{0,1:T(8,128)}, u32[]{:S(2)}) copy-start(s32[64,6]{0,1:T(8,128)} %param.20) | copy-start | bytes 4612
  17.1 37.3 %all-to-all-start = ((bf16[16,224,128]{2,1,0:T(8,128)(2,1)}), bf16[16,224,128]{2,1,0:T(8,128)(2,1)S(1)}, u32[]{:S(2)}, u32[]{:S(2)}) async-start(bf16[16,224,128]{2,1,0:T(8,128)(2,1)} %pad_maximum_fusion), calls=%async_computation | async-start | bytes 1835008 | tf_op jit(solution)/shard_map/all_to_all | solution.py:67
  24.5 64.0 %collective-permute-start.1 = (bf16[1,1024,1408]{2,1,0:T(8,128)(2,1)}, bf16[1,1024,1408]{2,1,0:T(8,128)(2,1)}, u32[]{:S(2)}, u32[]{:S(2)}) collective-permute-start(bf16[1,1024,1408]{2,1,0:T(8,128)(2,1)} %param.22), channel_id=1, source_target_pairs={{0,16},{16,0},{1,17},{17,1},{2,18},{18,2},{3,19},{19,3},{4,20},{20... | collective-permute-start | bytes 8650760 | tf_op jit(solution)/shard_map/ppermute | solution.py:29
  56.7 23.8 %copy-start.1 = (bf16[64,2048]{1,0:T(8,128)(2,1)S(1)}, bf16[64,2048]{1,0:T(8,128)(2,1)}, u32[]{:S(2)}) copy-start(bf16[64,2048]{1,0:T(8,128)(2,1)} %param.13) | copy-start | bytes 786436
  58.1 25.6 %copy-start.3 = (f32[2048]{0:T(1024)S(1)}, f32[2048]{0:T(1024)}, u32[]{:S(2)}) copy-start(f32[2048]{0:T(1024)} %param.19) | copy-start | bytes 24580
  58.1 13.0 %all-to-all-start.1 = ((bf16[16,32,128]{2,1,0:T(8,128)(2,1)}), bf16[16,32,128]{2,1,0:T(8,128)(2,1)S(1)}, u32[]{:S(2)}, u32[]{:S(2)}) async-start(bf16[16,32,128]{2,1,0:T(8,128)(2,1)} %bitcast.11), calls=%async_computation.1 | async-start | bytes 262144 | tf_op jit(solution)/shard_map/all_to_all | solution.py:87
  90.6 54.3 %all-to-all-start.2 = ((bf16[16,32,2048]{2,1,0:T(8,128)(2,1)}), bf16[16,32,2048]{2,1,0:T(8,128)(2,1)S(1)}, u32[]{:S(2)}, u32[]{:S(2)}) async-start(bf16[16,32,2048]{2,1,0:T(8,128)(2,1)} %bitcast.15), calls=%async_computation.2 | async-start | bytes 4194304 | tf_op jit(solution)/shard_map/all_to_all | solution.py:123
  97.5 33.1 %collective-permute-start.2 = (bf16[1,704,1024]{2,1,0:T(8,128)(2,1)}, bf16[1,704,1024]{2,1,0:T(8,128)(2,1)}, u32[]{:S(2)}, u32[]{:S(2)}) collective-permute-start(bf16[1,704,1024]{2,1,0:T(8,128)(2,1)} %param.23), channel_id=1, source_target_pairs={{0,16},{16,0},{1,17},{17,1},{2,18},{18,2},{3,19},{19,3},{4,20},{20... | collective-permute-start | bytes 4325384 | tf_op jit(solution)/shard_map/ppermute | solution.py:29
  144.9 7.0 %copy-start.5 = (bf16[1,704,1024]{2,1,0:T(8,128)(2,1)S(1)}, bf16[1,704,1024]{2,1,0:T(8,128)(2,1)}, u32[]{:S(2)}) copy-start(bf16[1,704,1024]{2,1,0:T(8,128)(2,1)} %param.23) | copy-start | bytes 4325380
  157.3 5.0 %copy-start.4 = (f32[64,6]{0,1:T(8,128)S(1)}, f32[64,6]{0,1:T(8,128)}, u32[]{:S(2)}) copy-start(f32[64,6]{0,1:T(8,128)} %param.21) | copy-start | bytes 4612
  157.3 52.5 %all-to-all-start.3 = ((bf16[16,32,2048]{2,1,0:T(8,128)(2,1)}), bf16[16,32,2048]{2,1,0:T(8,128)(2,1)S(1)}, u32[]{:S(2)}, u32[]{:S(2)}) async-start(bf16[16,32,2048]{2,1,0:T(8,128)(2,1)} %bitcast.65), calls=%async_computation.3 | async-start | bytes 4194304 | tf_op jit(solution)/shard_map/all_to_all | solution.py:146
Sparse Core Ops, SparseCore 0:
  13.0 67.4 all-gather.1

commit v7 on v6

--- a/solution.py
+++ b/solution.py
@@ -96,11 +96,29 @@
         )
     else:
         wo_rows = lax.all_gather(out_weight, "dp", axis=0, tiled=True)
-    projected = jnp.dot(
-        attended,
-        lax.all_gather(wo_rows, "mp", axis=1, tiled=True),
-        preferred_element_type=jnp.float32,
-    )
+    bits = n_mp.bit_length() - 1
+    if n_mp == 1 << bits:
+        block = wo_rows[None]
+        for b in reversed(range(bits)):
+            pair = lax.ppermute(block, "mp", [(m, m ^ (1 << b)) for m in range(n_mp)])
+            low = (column >> b) % 2 == 0
+            block = jnp.concatenate(
+                [jnp.where(low, block, pair), jnp.where(low, pair, block)], axis=0
+            )
+        by_shard = jnp.einsum("tk,jkc->tjc", attended, block, preferred_element_type=jnp.float32)
+        order = (0,) + tuple(range(bits, 0, -1)) + (bits + 1,)
+        shard_w = wo_rows.shape[1]
+        projected = (
+            by_shard.reshape((q_count,) + (2,) * bits + (shard_w,))
+            .transpose(order)
+            .reshape(q_count, d_model)
+        )
+    else:
+        projected = jnp.dot(
+            attended,
+            lax.all_gather(wo_rows, "mp", axis=1, tiled=True),
+            preferred_element_type=jnp.float32,
+        )
     resid_f = (hidden.astype(jnp.float32) + projected).astype(jnp.bfloat16).astype(jnp.float32)
     mean_square = jnp.mean(resid_f * resid_f, axis=1, keepdims=True)
     normed = (resid_f * lax.rsqrt(mean_square + epsilon) * norm_gain[None, :]).astype(jnp.bfloat16)

time: 219 us -> 217 us (level)
  between operations: 13.7 us -> 0.37 us
  starting transfers between devices: 27.8 us -> 37.5 us
  other arithmetic: 5.68 us -> 11.1 us
  waiting for transfers between devices: 144 us -> 140 us
  local copies, waits for them, and re-layouts: 5.72 us -> 8.62 us
    ppermute x0 -> x4, waiting for transfers between devices: none -> 37.5 us  [on_device(): pair = lax.ppermute(block, 'mp', [(m, m ^ 1 << b) for m in range(n_mp)])]
    all_to_all x1, waiting for transfers between devices: 25.1 us -> 0.01 us  [on_device(): lax.all_to_all(jnp.concatenate([q_out, kv_out], axis=1), 'mp', split_axis...]
    all_gather x1 -> x0, waiting for transfers between devices: 9.36 us -> none  [on_device(): lax.all_gather(wo_rows, 'mp', axis=1, tiled=True)]
    ppermute x0 -> x4, starting transfers between devices: none -> 5.96 us  [on_device(): pair = lax.ppermute(block, 'mp', [(m, m ^ 1 << b) for m in range(n_mp)])]
    ppermute x3, waiting for transfers between devices: 39.9 us -> 35.6 us  [swap_dp(): return lax.ppermute(x, 'dp', [(0, 1), (1, 0)])]
    select_n x0 -> x4, other arithmetic: none -> 3.74 us  [on_device(): jnp.where(low, block, pair)]
    all_to_all x1, starting transfers between devices: 4.75 us -> 7.98 us  [on_device(): lax.all_to_all(blended.reshape(n_mp, sub, HD), 'mp', split_axis=0, concat...]
    all_to_all x1, waiting for transfers between devices: 8.11 us -> 4.99 us  [on_device(): lax.all_to_all(blended.reshape(n_mp, sub, HD), 'mp', split_axis=0, concat...]
  transfers between devices with their start and end apart: 8 -> 11, of which waited for: 8 -> 9; matrix products, arithmetic and copies ran while one was open for 7% -> 10% of each run, Pallas kernels for 0% -> 0%
where the time goes in v7:
time: 217 us
  waiting for transfers between devices  140 us (65%)
  starting transfers between devices  37.5 us (17%)
  matrix products  19.5 us (9%)
  other arithmetic  11.1 us (5%)
  local copies, waits for them, and re-layouts  8.62 us (4%)
    all_to_all x1, waiting for transfers between devices, on_device(): lax.all_to_all(outcome.reshape(n_mp, capacity, d_model), 'mp', split_axis...  47.2 us
    ppermute x4, waiting for transfers between devices, on_device(): pair = lax.ppermute(block, 'mp', [(m, m ^ 1 << b) for m in range(n_mp)])  37.5 us
    ppermute x3, waiting for transfers between devices, swap_dp(): return lax.ppermute(x, 'dp', [(0, 1), (1, 0)])  35.6 us
    all_to_all x1, waiting for transfers between devices, on_device(): lax.all_to_all(sending.reshape(n_mp, capacity, d_model), 'mp', split_axis...  14.2 us
    all_to_all x1, starting transfers between devices, on_device(): lax.all_to_all(blended.reshape(n_mp, sub, HD), 'mp', split_axis=0, concat...  7.98 us
    all_to_all x1, starting transfers between devices, on_device(): lax.all_to_all(jnp.concatenate([q_out, kv_out], axis=1), 'mp', split_axis...  7.84 us
    dot_general x1, matrix products, on_device(): gate_vals = jnp.dot(flat_rows, gate_up, preferred_element_type=jnp.float32)  7.2 us
    all_to_all x1, starting transfers between devices, on_device(): lax.all_to_all(sending.reshape(n_mp, capacity, d_model), 'mp', split_axis...  6.85 us
  transfers between devices with their start and end apart: 11, of which 9 were waited for; matrix products, arithmetic and copies ran while one was open for 10% of the time, Pallas kernels for 0%

profile of v7, /device:TPU:11, one launch (start us, length us, event | category | flops | bytes accessed | tf_op | source)
XLA Modules:
  0.0 216.6 jit_solution(3733477040740844269)
XLA Ops:
  0.0 1.2 collective-permute-start
  1.2 3.3 %collective-permute-done = bf16[512,128]{1,0:T(8,128)(2,1)S(1)} collective-permute-done((bf16[512,128]{1,0:T(8,128)(2,1)}, bf16[512,128]{1,0:T(8,128)(2,1)S(1)}, u32[]{:S(2)}, u32[]{:S(2)}) %collective-permute-start) | collective-permute-done | bytes 131104 | tf_op jit(solution)/shard_map/ppermute | solution.py:29
  4.6 1.1 maximum_select_fusion.4
  5.6 2.4 %collective-permute-start.1 = (bf16[1,1024,128]{2,1,0:T(8,128)(2,1)S(1)}, bf16[1,1024,128]{2,1,0:T(8,128)(2,1)S(1)}, u32[]{:S(2)}, u32[]{:S(2)}) collective-permute-start(bf16[1,1024,128]{2,1,0:T(8,128)(2,1)S(1)} %maximum_select_fusion.4), channel_id=1, source_target_pairs={{0,8},{1,9},{2,10},{3,11},{4,12},{5,13},{6,14},{7,15},{8,0},{9,1},... | collective-permute-start | bytes 786440 | tf_op jit(solution)/shard_map/ppermute | solution.py:103
  8.0 1.2 reshape.224
  9.3 0.3 copy.70
  9.6 0.9 copy.83
  10.6 9.0 %collective-permute-done.1 = bf16[1,1024,128]{2,1,0:T(8,128)(2,1)S(1)} collective-permute-done((bf16[1,1024,128]{2,1,0:T(8,128)(2,1)S(1)}, bf16[1,1024,128]{2,1,0:T(8,128)(2,1)S(1)}, u32[]{:S(2)}, u32[]{:S(2)}) %collective-permute-start.1) | collective-permute-done | bytes 262176 | tf_op jit(solution)/shard_map/ppermute | solution.py:103
  19.7 0.6 tile.8
  20.3 1.1 pad_maximum_fusion.3
  21.4 7.8 %all-to-all-start = ((bf16[16,224,128]{2,1,0:T(8,128)(2,1)}), bf16[16,224,128]{2,1,0:T(8,128)(2,1)}, u32[]{:S(2)}, u32[]{:S(2)}) async-start(bf16[16,224,128]{2,1,0:T(8,128)(2,1)} %pad_maximum_fusion.3), calls=%async_computation | async-start | bytes 1835008 | tf_op jit(solution)/shard_map/all_to_all | solution.py:67
  29.3 1.2 collective-permute-start.5
  30.8 2.0 collective-permute-done.2
  33.0 0.3 collective-permute-start.3
  33.3 0.2 select_reduce_fusion.1
  33.5 0.6 dynamic_slice.7
  34.1 0.8 reduce-window.6
  35.0 0.7 fusion.33
  35.8 26.5 %collective-permute-done.3 = bf16[4,1024,128]{2,1,0:T(8,128)(2,1)} collective-permute-done((bf16[4,1024,128]{2,1,0:T(8,128)(2,1)S(1)}, bf16[4,1024,128]{2,1,0:T(8,128)(2,1)}, u32[]{:S(2)}, u32[]{:S(2)}) %collective-permute-start.3) | collective-permute-done | bytes 1048608 | tf_op jit(solution)/shard_map/ppermute | solution.py:103
  62.3 1.5 broadcast_select_fusion.3
  63.8 1.5 pad_maximum_fusion.1
  65.3 3.2 %collective-permute-start.4 = (bf16[8,1024,128]{2,1,0:T(8,128)(2,1)}, bf16[8,1024,128]{2,1,0:T(8,128)(2,1)}, u32[]{:S(2)}, u32[]{:S(2)}) collective-permute-start(bf16[8,1024,128]{2,1,0:T(8,128)(2,1)} %pad_maximum_fusion.1), channel_id=1, source_target_pairs={{0,1},{1,0},{2,3},{3,2},{4,5},{5,4},{6,7},{7,6},{8,9},{9,8},{10,11... | collective-permute-start | bytes 6291464 | tf_op jit(solution)/shard_map/ppermute | solution.py:103
  68.5 0.2 slice_reduce_fusion
  69.4 1.2 slice.33
  70.6 0.5 copy.71
  71.4 0.9 slice.32
  72.3 0.7 fusion.39
  73.0 0.6 fusion.14
  73.7 1.4 fusion.18
  75.0 8.0 %all-to-all-start.1 = ((bf16[16,32,128]{2,1,0:T(8,128)(2,1)}), bf16[16,32,128]{2,1,0:T(8,128)(2,1)S(1)}, u32[]{:S(2)}, u32[]{:S(2)}) async-start(bf16[16,32,128]{2,1,0:T(8,128)(2,1)} %bitcast.11), calls=%async_computation.1 | async-start | bytes 262144 | tf_op jit(solution)/shard_map/all_to_all | solution.py:87
  83.2 5.0 %all-to-all-done.1 = bf16[16,32,128]{2,1,0:T(8,128)(2,1)S(1)} async-done(((bf16[16,32,128]{2,1,0:T(8,128)(2,1)}), bf16[16,32,128]{2,1,0:T(8,128)(2,1)S(1)}, u32[]{:S(2)}, u32[]{:S(2)}) %all-to-all-start.1) | async-done | bytes 131104 | tf_op jit(solution)/shard_map/all_to_all | solution.py:87
  88.3 2.1 broadcast_select_fusion.1
  90.5 0.4 pad_maximum_fusion
  90.9 0.8 convolution_bitcast_fusion
  91.7 0.4 copy.76
  92.1 0.4 reshape.230
  92.6 0.2 fusion.22
  92.9 0.4 collective-permute-done.5
  93.3 2.1 convolution_convert_fusion.1
  95.4 6.8 %all-to-all-start.2 = ((bf16[16,32,2048]{2,1,0:T(8,128)(2,1)}), bf16[16,32,2048]{2,1,0:T(8,128)(2,1)S(1)}, u32[]{:S(2)}, u32[]{:S(2)}) async-start(bf16[16,32,2048]{2,1,0:T(8,128)(2,1)} %bitcast.21), calls=%async_computation.2 | async-start | bytes 4194304 | tf_op jit(solution)/shard_map/all_to_all | solution.py:141
  102.2 1.3 collective-permute-start.6
  103.5 31.9 %collective-permute-done.6 = bf16[1,704,1024]{2,1,0:T(8,128)(2,1)} collective-permute-done((bf16[1,704,1024]{2,1,0:T(8,128)(2,1)}, bf16[1,704,1024]{2,1,0:T(8,128)(2,1)}, u32[]{:S(2)}, u32[]{:S(2)}) %collective-permute-start.6) | collective-permute-done | bytes 1441824 | tf_op jit(solution)/shard_map/ppermute | solution.py:29
  135.4 14.2 %all-to-all-done.2 = bf16[16,32,2048]{2,1,0:T(8,128)(2,1)S(1)} async-done(((bf16[16,32,2048]{2,1,0:T(8,128)(2,1)}), bf16[16,32,2048]{2,1,0:T(8,128)(2,1)S(1)}, u32[]{:S(2)}, u32[]{:S(2)}) %all-to-all-start.2) | async-done | bytes 2097184 | tf_op jit(solution)/shard_map/all_to_all | solution.py:141
  149.7 7.2 %fusion = f32[512,1408]{1,0:T(8,128)S(1)} fusion(bf16[512,2048]{1,0:T(8,128)(2,1)S(1)} %bitcast.72, bf16[1024,1408]{1,0:T(8,128)(2,1)} %bitcast.24, bf16[1024,1408]{1,0:T(8,128)(2,1)} %bitcast.86, pred[]{:T(512)S(6)} %eq.86), kind=kOutput, calls=%fused_computation.1 | convolution fusion | flops 2978742272 | bytes 10747905 | tf_op jit(solution)/shard_map/dot_general | solution.py:161
  156.9 5.3 %convolution_convert_fusion = bf16[512,2048]{1,0:T(8,128)(2,1)} fusion(bf16[704,1024]{1,0:T(8,128)(2,1)} %bitcast.26, bf16[704,1024]{1,0:T(8,128)(2,1)S(1)} %bitcast.87, pred[]{:T(512)S(6)} %eq.86, f32[512,1408]{1,0:T(8,128)S(1)} %fusion), kind=kOutput, calls=%fused_computation.13 | convolution fusion | flops 1492582400 | bytes 8126465 | tf_op jit(solution)/shard_map/dot_general | solution.py:163
  162.2 5.0 %all-to-all-start.3 = ((bf16[16,32,2048]{2,1,0:T(8,128)(2,1)}), bf16[16,32,2048]{2,1,0:T(8,128)(2,1)S(1)}, u32[]{:S(2)}, u32[]{:S(2)}) async-start(bf16[16,32,2048]{2,1,0:T(8,128)(2,1)} %bitcast.73), calls=%async_computation.3 | async-start | bytes 4194304 | tf_op jit(solution)/shard_map/all_to_all | solution.py:164
  167.4 47.2 %all-to-all-done.3 = bf16[16,32,2048]{2,1,0:T(8,128)(2,1)S(1)} async-done(((bf16[16,32,2048]{2,1,0:T(8,128)(2,1)}), bf16[16,32,2048]{2,1,0:T(8,128)(2,1)S(1)}, u32[]{:S(2)}, u32[]{:S(2)}) %all-to-all-start.3) | async-done | bytes 2097184 | tf_op jit(solution)/shard_map/all_to_all | solution.py:164
  214.7 1.9 fusion.15
  (51 shorter events, 2.4 us)
Async XLA Ops:
  0.0 30.8 %copy-start = (s32[2,96]{1,0:T(2,128)S(1)}, s32[2,96]{1,0:T(2,128)}, u32[]{:S(2)}) copy-start(s32[2,96]{1,0:T(2,128)} %param.15) | copy-start | bytes 2308
  0.0 4.6 %collective-permute-start = (bf16[512,128]{1,0:T(8,128)(2,1)}, bf16[512,128]{1,0:T(8,128)(2,1)S(1)}, u32[]{:S(2)}, u32[]{:S(2)}) collective-permute-start(bf16[512,128]{1,0:T(8,128)(2,1)} %param.18), channel_id=1, source_target_pairs={{0,16},{16,0},{1,17},{17,1},{2,18},{18,2},{3,19},{19,3},{4,20},{20... | collective-permute-start | bytes 393224 | tf_op jit(solution)/shard_map/ppermute | solution.py:29
  5.6 13.9 %collective-permute-start.1 = (bf16[1,1024,128]{2,1,0:T(8,128)(2,1)S(1)}, bf16[1,1024,128]{2,1,0:T(8,128)(2,1)S(1)}, u32[]{:S(2)}, u32[]{:S(2)}) collective-permute-start(bf16[1,1024,128]{2,1,0:T(8,128)(2,1)S(1)} %maximum_select_fusion.4), channel_id=1, source_target_pairs={{0,8},{1,9},{2,10},{3,11},{4,12},{5,13},{6,14},{7,15},{8,0},{9,1},... | collective-permute-start | bytes 786440 | tf_op jit(solution)/shard_map/ppermute | solution.py:103
  19.6 10.9 %copy-start.2 = (s32[64,6]{0,1:T(8,128)S(1)}, s32[64,6]{0,1:T(8,128)}, u32[]{:S(2)}) copy-start(s32[64,6]{0,1:T(8,128)} %param.20) | copy-start | bytes 4612
  19.7 13.2 %collective-permute-start.2 = (bf16[2,1024,128]{2,1,0:T(8,128)(2,1)S(1)}, bf16[2,1024,128]{2,1,0:T(8,128)(2,1)S(1)}, u32[]{:S(2)}, u32[]{:S(2)}) collective-permute-start(bf16[2,1024,128]{2,1,0:T(8,128)(2,1)S(1)} %pad_maximum_fusion.4), channel_id=1, source_target_pairs={{0,4},{1,5},{2,6},{3,7},{4,0},{5,1},{6,2},{7,3},{8,12},{9,13},{10,... | collective-permute-start | bytes 1572872 | tf_op jit(solution)/shard_map/ppermute | solution.py:103
  21.4 12.1 %copy-start.6 = (s32[2]{0:T(128)S(1)}, s32[2]{0:T(128)}, u32[]{:S(2)}) copy-start(s32[2]{0:T(128)} %param.16) | copy-start | bytes 28
  21.4 13.5 %copy-start.7 = (s32[1,16]{1,0:T(1,128)S(1)}, s32[1,16]{1,0:T(1,128)}, u32[]{:S(2)}) copy-start(s32[1,16]{1,0:T(1,128)} %param.17) | copy-start | bytes 196
  21.4 47.9 %all-to-all-start = ((bf16[16,224,128]{2,1,0:T(8,128)(2,1)}), bf16[16,224,128]{2,1,0:T(8,128)(2,1)}, u32[]{:S(2)}, u32[]{:S(2)}) async-start(bf16[16,224,128]{2,1,0:T(8,128)(2,1)} %pad_maximum_fusion.3), calls=%async_computation | async-start | bytes 1835008 | tf_op jit(solution)/shard_map/all_to_all | solution.py:67
  29.3 64.0 %collective-permute-start.5 = (bf16[1,1024,1408]{2,1,0:T(8,128)(2,1)}, bf16[1,1024,1408]{2,1,0:T(8,128)(2,1)}, u32[]{:S(2)}, u32[]{:S(2)}) collective-permute-start(bf16[1,1024,1408]{2,1,0:T(8,128)(2,1)} %param.22), channel_id=1, source_target_pairs={{0,16},{16,0},{1,17},{17,1},{2,18},{18,2},{3,19},{19,3},{4,20},{20... | collective-permute-start | bytes 8650760 | tf_op jit(solution)/shard_map/ppermute | solution.py:29
  33.0 29.3 %collective-permute-start.3 = (bf16[4,1024,128]{2,1,0:T(8,128)(2,1)S(1)}, bf16[4,1024,128]{2,1,0:T(8,128)(2,1)}, u32[]{:S(2)}, u32[]{:S(2)}) collective-permute-start(bf16[4,1024,128]{2,1,0:T(8,128)(2,1)S(1)} %pad_maximum_fusion.2), channel_id=1, source_target_pairs={{0,2},{1,3},{2,0},{3,1},{4,6},{5,7},{6,4},{7,5},{8,10},{9,11},{10,... | collective-permute-start | bytes 3145736 | tf_op jit(solution)/shard_map/ppermute | solution.py:103
  65.3 23.0 %collective-permute-start.4 = (bf16[8,1024,128]{2,1,0:T(8,128)(2,1)}, bf16[8,1024,128]{2,1,0:T(8,128)(2,1)}, u32[]{:S(2)}, u32[]{:S(2)}) collective-permute-start(bf16[8,1024,128]{2,1,0:T(8,128)(2,1)} %pad_maximum_fusion.1), channel_id=1, source_target_pairs={{0,1},{1,0},{2,3},{3,2},{4,5},{5,4},{6,7},{7,6},{8,9},{9,8},{10,11... | collective-permute-start | bytes 6291464 | tf_op jit(solution)/shard_map/ppermute | solution.py:103
  75.0 13.2 %all-to-all-start.1 = ((bf16[16,32,128]{2,1,0:T(8,128)(2,1)}), bf16[16,32,128]{2,1,0:T(8,128)(2,1)S(1)}, u32[]{:S(2)}, u32[]{:S(2)}) async-start(bf16[16,32,128]{2,1,0:T(8,128)(2,1)} %bitcast.11), calls=%async_computation.1 | async-start | bytes 262144 | tf_op jit(solution)/shard_map/all_to_all | solution.py:87
  90.8 1.7 copy-start.1
  90.9 1.9 copy-start.3
  95.4 54.3 %all-to-all-start.2 = ((bf16[16,32,2048]{2,1,0:T(8,128)(2,1)}), bf16[16,32,2048]{2,1,0:T(8,128)(2,1)S(1)}, u32[]{:S(2)}, u32[]{:S(2)}) async-start(bf16[16,32,2048]{2,1,0:T(8,128)(2,1)} %bitcast.21), calls=%async_computation.2 | async-start | bytes 4194304 | tf_op jit(solution)/shard_map/all_to_all | solution.py:141
  102.2 33.2 %collective-permute-start.6 = (bf16[1,704,1024]{2,1,0:T(8,128)(2,1)}, bf16[1,704,1024]{2,1,0:T(8,128)(2,1)}, u32[]{:S(2)}, u32[]{:S(2)}) collective-permute-start(bf16[1,704,1024]{2,1,0:T(8,128)(2,1)} %param.23), channel_id=1, source_target_pairs={{0,16},{16,0},{1,17},{17,1},{2,18},{18,2},{3,19},{19,3},{4,20},{20... | collective-permute-start | bytes 4325384 | tf_op jit(solution)/shard_map/ppermute | solution.py:29
  149.7 7.2 %copy-start.5 = (bf16[1,704,1024]{2,1,0:T(8,128)(2,1)S(1)}, bf16[1,704,1024]{2,1,0:T(8,128)(2,1)}, u32[]{:S(2)}) copy-start(bf16[1,704,1024]{2,1,0:T(8,128)(2,1)} %param.23) | copy-start | bytes 4325380
  162.2 5.0 %copy-start.4 = (f32[64,6]{0,1:T(8,128)S(1)}, f32[64,6]{0,1:T(8,128)}, u32[]{:S(2)}) copy-start(f32[64,6]{0,1:T(8,128)} %param.21) | copy-start | bytes 4612
  162.2 52.5 %all-to-all-start.3 = ((bf16[16,32,2048]{2,1,0:T(8,128)(2,1)}), bf16[16,32,2048]{2,1,0:T(8,128)(2,1)S(1)}, u32[]{:S(2)}, u32[]{:S(2)}) async-start(bf16[16,32,2048]{2,1,0:T(8,128)(2,1)} %bitcast.73), calls=%async_computation.3 | async-start | bytes 4194304 | tf_op jit(solution)/shard_map/all_to_all | solution.py:164

commit v8 on v7

--- a/solution.py
+++ b/solution.py
@@ -84,8 +84,10 @@
     key_rows = arrived[:, :, :, 0, :].reshape(-1, HD)
     value_rows = arrived[:, :, :, 1, :].reshape(-1, HD)
     blended = attend_head(q_in.reshape(-1, HD), key_rows, value_rows, key_pos, query_pos)
-    back = lax.all_to_all(blended.reshape(n_mp, sub, HD), "mp", split_axis=0, concat_axis=0, tiled=True)
-    attended = back.reshape(groups, heads, sub, HD).transpose(2, 0, 1, 3).reshape(q_count, width)
+
+    def gather_heads(rows):
+        back = lax.all_to_all(rows.reshape(n_mp, sub, HD), "mp", split_axis=0, concat_axis=0, tiled=True)
+        return back.reshape(groups, heads, sub, HD).transpose(2, 0, 1, 3).reshape(q_count, width)
 
     if n_dp == 2:
         w_pair = swap_dp(out_weight)
@@ -100,11 +102,14 @@
     if n_mp == 1 << bits:
         block = wo_rows[None]
         for b in reversed(range(bits)):
+            if b == 1:
+                block, blended = lax.optimization_barrier((block, blended))
             pair = lax.ppermute(block, "mp", [(m, m ^ (1 << b)) for m in range(n_mp)])
             low = (column >> b) % 2 == 0
             block = jnp.concatenate(
                 [jnp.where(low, block, pair), jnp.where(low, pair, block)], axis=0
             )
+        attended = gather_heads(blended)
         by_shard = jnp.einsum("tk,jkc->tjc", attended, block, preferred_element_type=jnp.float32)
         order = (0,) + tuple(range(bits, 0, -1)) + (bits + 1,)
         shard_w = wo_rows.shape[1]
@@ -114,6 +119,7 @@
             .reshape(q_count, d_model)
         )
     else:
+        attended = gather_heads(blended)
         projected = jnp.dot(
             attended,
             lax.all_gather(wo_rows, "mp", axis=1, tiled=True),
@@ -149,7 +155,7 @@
             jnp.concatenate([experts_in[0], in_other[0]], axis=0),
             jnp.concatenate([in_other[0], experts_in[0]], axis=0),
         )
-        flat_rows, out_other = lax.optimization_barrier((flat_rows, out_other))
+        flat_rows, out_other, gate_up = lax.optimization_barrier((flat_rows, out_other, gate_up))
         down = jnp.where(
             first,
             jnp.concatenate([experts_out[0], out_other[0]], axis=1),

time: 217 us -> 275 us (1.27)
  waiting for transfers between devices: 140 us -> 196 us
  other arithmetic: 11.1 us -> 18.6 us
  starting transfers between devices: 37.5 us -> 33.9 us
    ppermute x3, waiting for transfers between devices: 35.6 us -> 71.9 us  [swap_dp(): return lax.ppermute(x, 'dp', [(0, 1), (1, 0)])]
    ppermute x4, waiting for transfers between devices: 37.5 us -> 58.1 us  [on_device(): pair = lax.ppermute(block, 'mp', [(m, m ^ 1 << b) for m in range(n_mp)])]
    select_n x0 -> x1, other arithmetic: none -> 8.7 us  [on_device(): jnp.where(first, jnp.concatenate([experts_in[0], in_other[0]], axis=0), j...]
    all_to_all x1, starting transfers between devices: 7.98 us -> 5 us  [gather_heads(): lax.all_to_all(rows.reshape(n_mp, sub, HD), 'mp', split_axis=0, concat_ax...]
  transfers between devices with their start and end apart: 11 -> 11, of which waited for: 9 -> 9; matrix products, arithmetic and copies ran while one was open for 10% -> 6% of each run, Pallas kernels for 0% -> 0%
where the time goes in v8:
time: 275 us; the launch traced here: 274 us
  waiting for transfers between devices  196 us (71%)
  starting transfers between devices  33.9 us (12%)
  other arithmetic  18.6 us (7%)
  matrix products  18 us (7%)
  local copies, waits for them, and re-layouts  6.7 us (2%)
    ppermute x3, waiting for transfers between devices, swap_dp(): return lax.ppermute(x, 'dp', [(0, 1), (1, 0)])  71.9 us
    ppermute x4, waiting for transfers between devices, on_device(): pair = lax.ppermute(block, 'mp', [(m, m ^ 1 << b) for m in range(n_mp)])  58.1 us
    all_to_all x1, waiting for transfers between devices, on_device(): lax.all_to_all(outcome.reshape(n_mp, capacity, d_model), 'mp', split_axis...  47.2 us
    all_to_all x1, waiting for transfers between devices, on_device(): lax.all_to_all(sending.reshape(n_mp, capacity, d_model), 'mp', split_axis...  14.2 us
    select_n x1, other arithmetic, on_device(): jnp.where(first, jnp.concatenate([experts_in[0], in_other[0]], axis=0), j...  8.7 us
    ppermute x4, starting transfers between devices, on_device(): pair = lax.ppermute(block, 'mp', [(m, m ^ 1 << b) for m in range(n_mp)])  7.99 us
    all_to_all x1, starting transfers between devices, on_device(): lax.all_to_all(jnp.concatenate([q_out, kv_out], axis=1), 'mp', split_axis...  6.55 us
    dot_general x1, matrix products, on_device(): gate_vals = jnp.dot(flat_rows, gate_up, preferred_element_type=jnp.float32)  5.86 us
  transfers between devices with their start and end apart: 11, of which 9 were waited for; matrix products, arithmetic and copies ran while one was open for 6% of the time, Pallas kernels for 0%

profile of v8, /device:TPU:11, one launch (start us, length us, event | category | flops | bytes accessed | tf_op | source)
XLA Modules:
  0.0 274.0 jit_solution(13388281242652996593)
XLA Ops:
  0.0 1.3 reshape.224
  1.3 0.3 copy.70
  1.6 1.0 copy.83
  2.6 0.6 tile.8
  3.3 1.0 pad_maximum_fusion.3
  4.2 6.6 %all-to-all-start = ((bf16[16,224,128]{2,1,0:T(8,128)(2,1)}), bf16[16,224,128]{2,1,0:T(8,128)(2,1)S(1)}, u32[]{:S(2)}, u32[]{:S(2)}) async-start(bf16[16,224,128]{2,1,0:T(8,128)(2,1)} %pad_maximum_fusion.3), calls=%async_computation | async-start | bytes 1835008 | tf_op jit(solution)/shard_map/all_to_all | solution.py:67
  10.8 1.3 collective-permute-start
  12.1 0.6 dynamic_slice.7
  12.7 0.7 fusion.26
  13.4 2.2 collective-permute-done
  15.7 2.2 collective-permute-start.1
  18.0 24.0 %collective-permute-done.1 = bf16[1,1024,128]{2,1,0:T(8,128)(2,1)S(1)} collective-permute-done((bf16[1,1024,128]{2,1,0:T(8,128)(2,1)S(1)}, bf16[1,1024,128]{2,1,0:T(8,128)(2,1)S(1)}, u32[]{:S(2)}, u32[]{:S(2)}) %collective-permute-start.1) | collective-permute-done | bytes 262176 | tf_op jit(solution)/shard_map/ppermute | solution.py:107
  42.1 3.2 %collective-permute-start.2 = (bf16[2,1024,128]{2,1,0:T(8,128)(2,1)S(1)}, bf16[2,1024,128]{2,1,0:T(8,128)(2,1)S(1)}, u32[]{:S(2)}, u32[]{:S(2)}) collective-permute-start(bf16[2,1024,128]{2,1,0:T(8,128)(2,1)S(1)} %pad_maximum_fusion.4), channel_id=1, source_target_pairs={{0,4},{1,5},{2,6},{3,7},{4,0},{5,1},{6,2},{7,3},{8,12},{9,13},{10,... | collective-permute-start | bytes 1572872 | tf_op jit(solution)/shard_map/ppermute | solution.py:107
  45.2 0.2 select_reduce_fusion.1
  45.6 11.1 %collective-permute-done.2 = bf16[2,1024,128]{2,1,0:T(8,128)(2,1)S(1)} collective-permute-done((bf16[2,1024,128]{2,1,0:T(8,128)(2,1)S(1)}, bf16[2,1024,128]{2,1,0:T(8,128)(2,1)S(1)}, u32[]{:S(2)}, u32[]{:S(2)}) %collective-permute-start.2) | collective-permute-done | bytes 524320 | tf_op jit(solution)/shard_map/ppermute | solution.py:107
  56.9 0.5 copy.71
  57.5 0.2 fusion.30
  57.9 0.7 fusion.31
  58.6 0.6 fusion.7
  59.2 1.4 fusion.11
  60.6 0.3 collective-permute-start.3
  60.9 23.0 %collective-permute-done.3 = bf16[4,1024,128]{2,1,0:T(8,128)(2,1)} collective-permute-done((bf16[4,1024,128]{2,1,0:T(8,128)(2,1)S(1)}, bf16[4,1024,128]{2,1,0:T(8,128)(2,1)}, u32[]{:S(2)}, u32[]{:S(2)}) %collective-permute-start.3) | collective-permute-done | bytes 1048608 | tf_op jit(solution)/shard_map/ppermute | solution.py:107
  83.9 1.4 broadcast_select_fusion.3
  85.2 1.5 pad_maximum_fusion.1
  86.8 2.4 collective-permute-start.4
  89.2 1.2 collective-permute-start.5
  90.8 0.9 reduce-window.6
  91.7 0.2 slice_reduce_fusion
  92.2 5.0 %all-to-all-start.1 = ((bf16[16,32,128]{2,1,0:T(8,128)(2,1)}), bf16[16,32,128]{2,1,0:T(8,128)(2,1)S(1)}, u32[]{:S(2)}, u32[]{:S(2)}) async-start(bf16[16,32,128]{2,1,0:T(8,128)(2,1)} %bitcast.13), calls=%async_computation.1 | async-start | bytes 262144 | tf_op jit(solution)/shard_map/all_to_all | solution.py:89
  97.4 5.0 %all-to-all-done.1 = bf16[16,32,128]{2,1,0:T(8,128)(2,1)S(1)} async-done(((bf16[16,32,128]{2,1,0:T(8,128)(2,1)}), bf16[16,32,128]{2,1,0:T(8,128)(2,1)S(1)}, u32[]{:S(2)}, u32[]{:S(2)}) %all-to-all-start.1) | async-done | bytes 131104 | tf_op jit(solution)/shard_map/all_to_all | solution.py:89
  102.5 2.1 broadcast_select_fusion.1
  104.7 0.4 pad_maximum_fusion
  105.1 0.8 convolution_bitcast_fusion
  105.9 0.4 copy.76
  106.3 0.4 reshape.230
  106.8 0.2 fusion.15
  107.1 46.5 %collective-permute-done.5 = bf16[1,1024,1408]{2,1,0:T(8,128)(2,1)} collective-permute-done((bf16[1,1024,1408]{2,1,0:T(8,128)(2,1)}, bf16[1,1024,1408]{2,1,0:T(8,128)(2,1)}, u32[]{:S(2)}, u32[]{:S(2)}) %collective-permute-start.5) | collective-permute-done | bytes 2883616 | tf_op jit(solution)/shard_map/ppermute | solution.py:29
  153.6 2.1 convolution_convert_fusion.1
  155.7 5.5 %all-to-all-start.2 = ((bf16[16,32,2048]{2,1,0:T(8,128)(2,1)}), bf16[16,32,2048]{2,1,0:T(8,128)(2,1)S(1)}, u32[]{:S(2)}, u32[]{:S(2)}) async-start(bf16[16,32,2048]{2,1,0:T(8,128)(2,1)} %bitcast.21), calls=%async_computation.2 | async-start | bytes 4194304 | tf_op jit(solution)/shard_map/all_to_all | solution.py:147
  161.2 1.3 collective-permute-start.6
  162.5 8.7 %maximum_select_fusion = bf16[2048,1408]{1,0:T(8,128)(2,1)} fusion(bf16[1024,1408]{1,0:T(8,128)(2,1)} %bitcast.24, bf16[1024,1408]{1,0:T(8,128)(2,1)} %bitcast.23, pred[]{:T(512)S(6)} %eq.80), kind=kLoop, calls=%fused_computation | loop fusion | flops 25952256 | bytes 11534337 | tf_op jit(solution)/shard_map/jit(_where)/select_n | solution.py:153
  171.2 23.2 %collective-permute-done.6 = bf16[1,704,1024]{2,1,0:T(8,128)(2,1)} collective-permute-done((bf16[1,704,1024]{2,1,0:T(8,128)(2,1)}, bf16[1,704,1024]{2,1,0:T(8,128)(2,1)}, u32[]{:S(2)}, u32[]{:S(2)}) %collective-permute-start.6) | collective-permute-done | bytes 1441824 | tf_op jit(solution)/shard_map/ppermute | solution.py:29
  194.4 14.2 %all-to-all-done.2 = bf16[16,32,2048]{2,1,0:T(8,128)(2,1)S(1)} async-done(((bf16[16,32,2048]{2,1,0:T(8,128)(2,1)}), bf16[16,32,2048]{2,1,0:T(8,128)(2,1)S(1)}, u32[]{:S(2)}, u32[]{:S(2)}) %all-to-all-start.2) | async-done | bytes 2097184 | tf_op jit(solution)/shard_map/all_to_all | solution.py:147
  208.6 5.9 %fusion.32 = f32[512,1408]{1,0:T(8,128)S(1)} fusion(bf16[512,2048]{1,0:T(8,128)(2,1)S(1)} %bitcast.73, bf16[2048,1408]{1,0:T(8,128)(2,1)} %maximum_select_fusion), kind=kOutput, calls=%fused_computation.83 | convolution fusion | flops 2952790016 | bytes 10747904 | tf_op jit(solution)/shard_map/dot_general | solution.py:167
  214.5 5.2 %convolution_convert_fusion = bf16[512,2048]{1,0:T(8,128)(2,1)} fusion(bf16[704,1024]{1,0:T(8,128)(2,1)} %bitcast.26, bf16[704,1024]{1,0:T(8,128)(2,1)S(1)} %bitcast.87, pred[]{:T(512)S(6)} %eq.80, f32[512,1408]{1,0:T(8,128)S(1)} %fusion.32), kind=kOutput, calls=%fused_computation.6 | convolution fusion | flops 1492582400 | bytes 8126465 | tf_op jit(solution)/shard_map/dot_general | solution.py:169
  219.7 5.0 %all-to-all-start.3 = ((bf16[16,32,2048]{2,1,0:T(8,128)(2,1)}), bf16[16,32,2048]{2,1,0:T(8,128)(2,1)S(1)}, u32[]{:S(2)}, u32[]{:S(2)}) async-start(bf16[16,32,2048]{2,1,0:T(8,128)(2,1)} %bitcast.74), calls=%async_computation.3 | async-start | bytes 4194304 | tf_op jit(solution)/shard_map/all_to_all | solution.py:170
  224.9 47.2 %all-to-all-done.3 = bf16[16,32,2048]{2,1,0:T(8,128)(2,1)S(1)} async-done(((bf16[16,32,2048]{2,1,0:T(8,128)(2,1)}), bf16[16,32,2048]{2,1,0:T(8,128)(2,1)S(1)}, u32[]{:S(2)}, u32[]{:S(2)}) %all-to-all-start.3) | async-done | bytes 2097184 | tf_op jit(solution)/shard_map/all_to_all | solution.py:170
  272.1 1.9 fusion.8
  (54 shorter events, 2.4 us)
Async XLA Ops:
  0.0 18.0 %copy-start = (s32[2,96]{1,0:T(2,128)S(1)}, s32[2,96]{1,0:T(2,128)}, u32[]{:S(2)}) copy-start(s32[2,96]{1,0:T(2,128)} %param.15) | copy-start | bytes 2308
  1.6 9.2 %copy-start.2 = (bf16[512,128]{1,0:T(8,128)(2,1)S(1)}, bf16[512,128]{1,0:T(8,128)(2,1)}, u32[]{:S(2)}) copy-start(bf16[512,128]{1,0:T(8,128)(2,1)} %param.18) | copy-start | bytes 393220
  1.6 10.5 %copy-start.7 = (s32[2]{0:T(128)S(1)}, s32[2]{0:T(128)}, u32[]{:S(2)}) copy-start(s32[2]{0:T(128)} %param.16) | copy-start | bytes 28
  1.6 11.1 %copy-start.8 = (s32[1,16]{1,0:T(1,128)S(1)}, s32[1,16]{1,0:T(1,128)}, u32[]{:S(2)}) copy-start(s32[1,16]{1,0:T(1,128)} %param.17) | copy-start | bytes 196
  4.2 52.6 %all-to-all-start = ((bf16[16,224,128]{2,1,0:T(8,128)(2,1)}), bf16[16,224,128]{2,1,0:T(8,128)(2,1)S(1)}, u32[]{:S(2)}, u32[]{:S(2)}) async-start(bf16[16,224,128]{2,1,0:T(8,128)(2,1)} %pad_maximum_fusion.3), calls=%async_computation | async-start | bytes 1835008 | tf_op jit(solution)/shard_map/all_to_all | solution.py:67
  10.8 4.8 %collective-permute-start = (bf16[512,128]{1,0:T(8,128)(2,1)S(1)}, bf16[512,128]{1,0:T(8,128)(2,1)S(1)}, u32[]{:S(2)}, u32[]{:S(2)}) collective-permute-start(bf16[512,128]{1,0:T(8,128)(2,1)S(1)} %copy-done.2), channel_id=1, source_target_pairs={{0,16},{16,0},{1,17},{17,1},{2,18},{18,2},{3,19},{19,3},{4,20},{20... | collective-permute-start | bytes 393224 | tf_op jit(solution)/shard_map/ppermute | solution.py:29
  15.7 26.3 %collective-permute-start.1 = (bf16[1,1024,128]{2,1,0:T(8,128)(2,1)S(1)}, bf16[1,1024,128]{2,1,0:T(8,128)(2,1)S(1)}, u32[]{:S(2)}, u32[]{:S(2)}) collective-permute-start(bf16[1,1024,128]{2,1,0:T(8,128)(2,1)S(1)} %maximum_select_fusion.3), channel_id=1, source_target_pairs={{0,8},{1,9},{2,10},{3,11},{4,12},{5,13},{6,14},{7,15},{8,0},{9,1},... | collective-permute-start | bytes 786440 | tf_op jit(solution)/shard_map/ppermute | solution.py:107
  42.1 14.6 %collective-permute-start.2 = (bf16[2,1024,128]{2,1,0:T(8,128)(2,1)S(1)}, bf16[2,1024,128]{2,1,0:T(8,128)(2,1)S(1)}, u32[]{:S(2)}, u32[]{:S(2)}) collective-permute-start(bf16[2,1024,128]{2,1,0:T(8,128)(2,1)S(1)} %pad_maximum_fusion.4), channel_id=1, source_target_pairs={{0,4},{1,5},{2,6},{3,7},{4,0},{5,1},{6,2},{7,3},{8,12},{9,13},{10,... | collective-permute-start | bytes 1572872 | tf_op jit(solution)/shard_map/ppermute | solution.py:107
  60.6 23.3 %collective-permute-start.3 = (bf16[4,1024,128]{2,1,0:T(8,128)(2,1)S(1)}, bf16[4,1024,128]{2,1,0:T(8,128)(2,1)}, u32[]{:S(2)}, u32[]{:S(2)}) collective-permute-start(bf16[4,1024,128]{2,1,0:T(8,128)(2,1)S(1)} %pad_maximum_fusion.2), channel_id=1, source_target_pairs={{0,2},{1,3},{2,0},{3,1},{4,6},{5,7},{6,4},{7,5},{8,10},{9,11},{10,... | collective-permute-start | bytes 3145736 | tf_op jit(solution)/shard_map/ppermute | solution.py:107
  85.2 5.2 %copy-start.3 = (s32[64,6]{0,1:T(8,128)S(1)}, s32[64,6]{0,1:T(8,128)}, u32[]{:S(2)}) copy-start(s32[64,6]{0,1:T(8,128)} %param.20) | copy-start | bytes 4612
  86.8 15.8 %collective-permute-start.4 = (bf16[8,1024,128]{2,1,0:T(8,128)(2,1)}, bf16[8,1024,128]{2,1,0:T(8,128)(2,1)}, u32[]{:S(2)}, u32[]{:S(2)}) collective-permute-start(bf16[8,1024,128]{2,1,0:T(8,128)(2,1)} %pad_maximum_fusion.1), channel_id=1, source_target_pairs={{0,1},{1,0},{2,3},{3,2},{4,5},{5,4},{6,7},{7,6},{8,9},{9,8},{10,11... | collective-permute-start | bytes 6291464 | tf_op jit(solution)/shard_map/ppermute | solution.py:107
  89.2 64.4 %collective-permute-start.5 = (bf16[1,1024,1408]{2,1,0:T(8,128)(2,1)}, bf16[1,1024,1408]{2,1,0:T(8,128)(2,1)}, u32[]{:S(2)}, u32[]{:S(2)}) collective-permute-start(bf16[1,1024,1408]{2,1,0:T(8,128)(2,1)} %param.22), channel_id=1, source_target_pairs={{0,16},{16,0},{1,17},{17,1},{2,18},{18,2},{3,19},{19,3},{4,20},{20... | collective-permute-start | bytes 8650760 | tf_op jit(solution)/shard_map/ppermute | solution.py:29
  92.2 10.2 %all-to-all-start.1 = ((bf16[16,32,128]{2,1,0:T(8,128)(2,1)}), bf16[16,32,128]{2,1,0:T(8,128)(2,1)S(1)}, u32[]{:S(2)}, u32[]{:S(2)}) async-start(bf16[16,32,128]{2,1,0:T(8,128)(2,1)} %bitcast.13), calls=%async_computation.1 | async-start | bytes 262144 | tf_op jit(solution)/shard_map/all_to_all | solution.py:89
  105.1 1.7 copy-start.1
  105.1 1.9 copy-start.4
  155.7 52.9 %all-to-all-start.2 = ((bf16[16,32,2048]{2,1,0:T(8,128)(2,1)}), bf16[16,32,2048]{2,1,0:T(8,128)(2,1)S(1)}, u32[]{:S(2)}, u32[]{:S(2)}) async-start(bf16[16,32,2048]{2,1,0:T(8,128)(2,1)} %bitcast.21), calls=%async_computation.2 | async-start | bytes 4194304 | tf_op jit(solution)/shard_map/all_to_all | solution.py:147
  161.2 33.2 %collective-permute-start.6 = (bf16[1,704,1024]{2,1,0:T(8,128)(2,1)}, bf16[1,704,1024]{2,1,0:T(8,128)(2,1)}, u32[]{:S(2)}, u32[]{:S(2)}) collective-permute-start(bf16[1,704,1024]{2,1,0:T(8,128)(2,1)} %param.23), channel_id=1, source_target_pairs={{0,16},{16,0},{1,17},{17,1},{2,18},{18,2},{3,19},{19,3},{4,20},{20... | collective-permute-start | bytes 4325384 | tf_op jit(solution)/shard_map/ppermute | solution.py:29
  208.6 5.9 %copy-start.6 = (bf16[1,704,1024]{2,1,0:T(8,128)(2,1)S(1)}, bf16[1,704,1024]{2,1,0:T(8,128)(2,1)}, u32[]{:S(2)}) copy-start(bf16[1,704,1024]{2,1,0:T(8,128)(2,1)} %param.23) | copy-start | bytes 4325380
  219.7 5.0 %copy-start.5 = (f32[64,6]{0,1:T(8,128)S(1)}, f32[64,6]{0,1:T(8,128)}, u32[]{:S(2)}) copy-start(f32[64,6]{0,1:T(8,128)} %param.21) | copy-start | bytes 4612
  219.7 52.5 %all-to-all-start.3 = ((bf16[16,32,2048]{2,1,0:T(8,128)(2,1)}), bf16[16,32,2048]{2,1,0:T(8,128)(2,1)S(1)}, u32[]{:S(2)}, u32[]{:S(2)}) async-start(bf16[16,32,2048]{2,1,0:T(8,128)(2,1)} %bitcast.74), calls=%async_computation.3 | async-start | bytes 4194304 | tf_op jit(solution)/shard_map/all_to_all | solution.py:170

commit v9 on v7

--- a/solution.py
+++ b/solution.py
@@ -149,7 +149,7 @@
             jnp.concatenate([experts_in[0], in_other[0]], axis=0),
             jnp.concatenate([in_other[0], experts_in[0]], axis=0),
         )
-        flat_rows, out_other = lax.optimization_barrier((flat_rows, out_other))
+        flat_rows, out_other, gate_up = lax.optimization_barrier((flat_rows, out_other, gate_up))
         down = jnp.where(
             first,
             jnp.concatenate([experts_out[0], out_other[0]], axis=1),

time: 217 us -> 216 us (level)
  waiting for transfers between devices: 140 us -> 131 us
  other arithmetic: 11.1 us -> 19.9 us
    ppermute x3, waiting for transfers between devices: 35.6 us -> 26.8 us  [swap_dp(): return lax.ppermute(x, 'dp', [(0, 1), (1, 0)])]
    select_n x0 -> x1, other arithmetic: none -> 8.78 us  [on_device(): jnp.where(first, jnp.concatenate([experts_in[0], in_other[0]], axis=0), j...]
  transfers between devices with their start and end apart: 11 -> 11, of which waited for: 9 -> 9; matrix products, arithmetic and copies ran while one was open for 10% -> 14% of each run, Pallas kernels for 0% -> 0%
where the time goes in v9:
time: 216 us; the launch traced here: 215 us
  waiting for transfers between devices  131 us (61%)
  starting transfers between devices  37.5 us (17%)
  other arithmetic  19.9 us (9%)
  matrix products  18.1 us (8%)
  local copies, waits for them, and re-layouts  8.62 us (4%)
    all_to_all x1, waiting for transfers between devices, on_device(): lax.all_to_all(outcome.reshape(n_mp, capacity, d_model), 'mp', split_axis...  47.2 us
    ppermute x4, waiting for transfers between devices, on_device(): pair = lax.ppermute(block, 'mp', [(m, m ^ 1 << b) for m in range(n_mp)])  37.5 us
    ppermute x3, waiting for transfers between devices, swap_dp(): return lax.ppermute(x, 'dp', [(0, 1), (1, 0)])  26.8 us
    all_to_all x1, waiting for transfers between devices, on_device(): lax.all_to_all(sending.reshape(n_mp, capacity, d_model), 'mp', split_axis...  14.2 us
    select_n x1, other arithmetic, on_device(): jnp.where(first, jnp.concatenate([experts_in[0], in_other[0]], axis=0), j...  8.78 us
    all_to_all x1, starting transfers between devices, on_device(): lax.all_to_all(blended.reshape(n_mp, sub, HD), 'mp', split_axis=0, concat...  7.99 us
    all_to_all x1, starting transfers between devices, on_device(): lax.all_to_all(jnp.concatenate([q_out, kv_out], axis=1), 'mp', split_axis...  7.84 us
    all_to_all x1, starting transfers between devices, on_device(): lax.all_to_all(sending.reshape(n_mp, capacity, d_model), 'mp', split_axis...  6.85 us
  transfers between devices with their start and end apart: 11, of which 9 were waited for; matrix products, arithmetic and copies ran while one was open for 14% of the time, Pallas kernels for 0%

profile of v9, /device:TPU:11, one launch (start us, length us, event | category | flops | bytes accessed | tf_op | source)
XLA Modules:
  0.0 215.2 jit_solution(3806974715702381291)
XLA Ops:
  0.0 1.2 collective-permute-start
  1.2 3.3 %collective-permute-done = bf16[512,128]{1,0:T(8,128)(2,1)S(1)} collective-permute-done((bf16[512,128]{1,0:T(8,128)(2,1)}, bf16[512,128]{1,0:T(8,128)(2,1)S(1)}, u32[]{:S(2)}, u32[]{:S(2)}) %collective-permute-start) | collective-permute-done | bytes 131104 | tf_op jit(solution)/shard_map/ppermute | solution.py:29
  4.6 1.1 maximum_select_fusion.3
  5.6 2.4 %collective-permute-start.1 = (bf16[1,1024,128]{2,1,0:T(8,128)(2,1)S(1)}, bf16[1,1024,128]{2,1,0:T(8,128)(2,1)S(1)}, u32[]{:S(2)}, u32[]{:S(2)}) collective-permute-start(bf16[1,1024,128]{2,1,0:T(8,128)(2,1)S(1)} %maximum_select_fusion.3), channel_id=1, source_target_pairs={{0,8},{1,9},{2,10},{3,11},{4,12},{5,13},{6,14},{7,15},{8,0},{9,1},... | collective-permute-start | bytes 786440 | tf_op jit(solution)/shard_map/ppermute | solution.py:103
  8.0 1.2 reshape.224
  9.3 0.3 copy.70
  9.6 0.9 copy.83
  10.6 9.0 %collective-permute-done.1 = bf16[1,1024,128]{2,1,0:T(8,128)(2,1)S(1)} collective-permute-done((bf16[1,1024,128]{2,1,0:T(8,128)(2,1)S(1)}, bf16[1,1024,128]{2,1,0:T(8,128)(2,1)S(1)}, u32[]{:S(2)}, u32[]{:S(2)}) %collective-permute-start.1) | collective-permute-done | bytes 262176 | tf_op jit(solution)/shard_map/ppermute | solution.py:103
  19.7 0.6 tile.8
  20.3 1.1 pad_maximum_fusion.3
  21.4 7.8 %all-to-all-start = ((bf16[16,224,128]{2,1,0:T(8,128)(2,1)}), bf16[16,224,128]{2,1,0:T(8,128)(2,1)}, u32[]{:S(2)}, u32[]{:S(2)}) async-start(bf16[16,224,128]{2,1,0:T(8,128)(2,1)} %pad_maximum_fusion.3), calls=%async_computation | async-start | bytes 1835008 | tf_op jit(solution)/shard_map/all_to_all | solution.py:67
  29.3 1.2 collective-permute-start.5
  30.8 2.0 collective-permute-done.2
  33.0 0.3 collective-permute-start.3
  33.5 0.6 dynamic_slice.7
  34.1 0.8 reduce-window.6
  35.0 0.7 fusion.26
  35.8 26.5 %collective-permute-done.3 = bf16[4,1024,128]{2,1,0:T(8,128)(2,1)} collective-permute-done((bf16[4,1024,128]{2,1,0:T(8,128)(2,1)S(1)}, bf16[4,1024,128]{2,1,0:T(8,128)(2,1)}, u32[]{:S(2)}, u32[]{:S(2)}) %collective-permute-start.3) | collective-permute-done | bytes 1048608 | tf_op jit(solution)/shard_map/ppermute | solution.py:103
  62.3 1.5 broadcast_select_fusion.3
  63.8 1.5 pad_maximum_fusion.1
  65.3 3.2 %collective-permute-start.4 = (bf16[8,1024,128]{2,1,0:T(8,128)(2,1)}, bf16[8,1024,128]{2,1,0:T(8,128)(2,1)}, u32[]{:S(2)}, u32[]{:S(2)}) collective-permute-start(bf16[8,1024,128]{2,1,0:T(8,128)(2,1)} %pad_maximum_fusion.1), channel_id=1, source_target_pairs={{0,1},{1,0},{2,3},{3,2},{4,5},{5,4},{6,7},{7,6},{8,9},{9,8},{10,11... | collective-permute-start | bytes 6291464 | tf_op jit(solution)/shard_map/ppermute | solution.py:103
  68.5 0.2 slice_reduce_fusion
  69.4 1.2 slice.33
  70.6 0.5 copy.71
  71.4 0.9 slice.32
  72.3 0.7 fusion.31
  73.0 0.6 fusion.7
  73.7 1.4 fusion.11
  75.1 8.0 %all-to-all-start.1 = ((bf16[16,32,128]{2,1,0:T(8,128)(2,1)}), bf16[16,32,128]{2,1,0:T(8,128)(2,1)S(1)}, u32[]{:S(2)}, u32[]{:S(2)}) async-start(bf16[16,32,128]{2,1,0:T(8,128)(2,1)} %bitcast.11), calls=%async_computation.1 | async-start | bytes 262144 | tf_op jit(solution)/shard_map/all_to_all | solution.py:87
  83.2 5.0 %all-to-all-done.1 = bf16[16,32,128]{2,1,0:T(8,128)(2,1)S(1)} async-done(((bf16[16,32,128]{2,1,0:T(8,128)(2,1)}), bf16[16,32,128]{2,1,0:T(8,128)(2,1)S(1)}, u32[]{:S(2)}, u32[]{:S(2)}) %all-to-all-start.1) | async-done | bytes 131104 | tf_op jit(solution)/shard_map/all_to_all | solution.py:87
  88.3 2.1 broadcast_select_fusion.1
  90.5 0.4 pad_maximum_fusion
  90.9 0.8 convolution_bitcast_fusion
  91.7 0.4 copy.76
  92.1 0.4 reshape.230
  92.6 0.2 fusion.15
  92.9 0.4 collective-permute-done.5
  93.3 2.1 convolution_convert_fusion.1
  95.4 6.8 %all-to-all-start.2 = ((bf16[16,32,2048]{2,1,0:T(8,128)(2,1)}), bf16[16,32,2048]{2,1,0:T(8,128)(2,1)S(1)}, u32[]{:S(2)}, u32[]{:S(2)}) async-start(bf16[16,32,2048]{2,1,0:T(8,128)(2,1)} %bitcast.21), calls=%async_computation.2 | async-start | bytes 4194304 | tf_op jit(solution)/shard_map/all_to_all | solution.py:141
  102.3 1.3 collective-permute-start.6
  103.6 8.8 %maximum_select_fusion = bf16[2048,1408]{1,0:T(8,128)(2,1)} fusion(bf16[1024,1408]{1,0:T(8,128)(2,1)} %bitcast.24, bf16[1024,1408]{1,0:T(8,128)(2,1)} %bitcast.23, pred[]{:T(512)S(6)} %eq.86), kind=kLoop, calls=%fused_computation | loop fusion | flops 25952256 | bytes 11534337 | tf_op jit(solution)/shard_map/jit(_where)/select_n | solution.py:147
  112.4 23.1 %collective-permute-done.6 = bf16[1,704,1024]{2,1,0:T(8,128)(2,1)} collective-permute-done((bf16[1,704,1024]{2,1,0:T(8,128)(2,1)}, bf16[1,704,1024]{2,1,0:T(8,128)(2,1)}, u32[]{:S(2)}, u32[]{:S(2)}) %collective-permute-start.6) | collective-permute-done | bytes 1441824 | tf_op jit(solution)/shard_map/ppermute | solution.py:29
  135.5 14.2 %all-to-all-done.2 = bf16[16,32,2048]{2,1,0:T(8,128)(2,1)S(1)} async-done(((bf16[16,32,2048]{2,1,0:T(8,128)(2,1)}), bf16[16,32,2048]{2,1,0:T(8,128)(2,1)S(1)}, u32[]{:S(2)}, u32[]{:S(2)}) %all-to-all-start.2) | async-done | bytes 2097184 | tf_op jit(solution)/shard_map/all_to_all | solution.py:141
  149.7 5.9 %fusion.32 = f32[512,1408]{1,0:T(8,128)S(1)} fusion(bf16[512,2048]{1,0:T(8,128)(2,1)S(1)} %bitcast.73, bf16[2048,1408]{1,0:T(8,128)(2,1)} %maximum_select_fusion), kind=kOutput, calls=%fused_computation.83 | convolution fusion | flops 2952790016 | bytes 10747904 | tf_op jit(solution)/shard_map/dot_general | solution.py:161
  155.6 5.2 %convolution_convert_fusion = bf16[512,2048]{1,0:T(8,128)(2,1)} fusion(bf16[704,1024]{1,0:T(8,128)(2,1)} %bitcast.26, bf16[704,1024]{1,0:T(8,128)(2,1)S(1)} %bitcast.87, pred[]{:T(512)S(6)} %eq.86, f32[512,1408]{1,0:T(8,128)S(1)} %fusion.32), kind=kOutput, calls=%fused_computation.6 | convolution fusion | flops 1492582400 | bytes 8126465 | tf_op jit(solution)/shard_map/dot_general | solution.py:163
  160.8 5.0 %all-to-all-start.3 = ((bf16[16,32,2048]{2,1,0:T(8,128)(2,1)}), bf16[16,32,2048]{2,1,0:T(8,128)(2,1)S(1)}, u32[]{:S(2)}, u32[]{:S(2)}) async-start(bf16[16,32,2048]{2,1,0:T(8,128)(2,1)} %bitcast.74), calls=%async_computation.3 | async-start | bytes 4194304 | tf_op jit(solution)/shard_map/all_to_all | solution.py:164
  166.1 47.2 %all-to-all-done.3 = bf16[16,32,2048]{2,1,0:T(8,128)(2,1)S(1)} async-done(((bf16[16,32,2048]{2,1,0:T(8,128)(2,1)}), bf16[16,32,2048]{2,1,0:T(8,128)(2,1)S(1)}, u32[]{:S(2)}, u32[]{:S(2)}) %all-to-all-start.3) | async-done | bytes 2097184 | tf_op jit(solution)/shard_map/all_to_all | solution.py:164
  213.3 1.9 fusion.8
  (52 shorter events, 2.6 us)
Async XLA Ops:
  0.0 30.8 %copy-start = (s32[2,96]{1,0:T(2,128)S(1)}, s32[2,96]{1,0:T(2,128)}, u32[]{:S(2)}) copy-start(s32[2,96]{1,0:T(2,128)} %param.15) | copy-start | bytes 2308
  0.0 4.6 %collective-permute-start = (bf16[512,128]{1,0:T(8,128)(2,1)}, bf16[512,128]{1,0:T(8,128)(2,1)S(1)}, u32[]{:S(2)}, u32[]{:S(2)}) collective-permute-start(bf16[512,128]{1,0:T(8,128)(2,1)} %param.18), channel_id=1, source_target_pairs={{0,16},{16,0},{1,17},{17,1},{2,18},{18,2},{3,19},{19,3},{4,20},{20... | collective-permute-start | bytes 393224 | tf_op jit(solution)/shard_map/ppermute | solution.py:29
  5.6 13.9 %collective-permute-start.1 = (bf16[1,1024,128]{2,1,0:T(8,128)(2,1)S(1)}, bf16[1,1024,128]{2,1,0:T(8,128)(2,1)S(1)}, u32[]{:S(2)}, u32[]{:S(2)}) collective-permute-start(bf16[1,1024,128]{2,1,0:T(8,128)(2,1)S(1)} %maximum_select_fusion.3), channel_id=1, source_target_pairs={{0,8},{1,9},{2,10},{3,11},{4,12},{5,13},{6,14},{7,15},{8,0},{9,1},... | collective-permute-start | bytes 786440 | tf_op jit(solution)/shard_map/ppermute | solution.py:103
  19.6 10.9 %copy-start.2 = (s32[64,6]{0,1:T(8,128)S(1)}, s32[64,6]{0,1:T(8,128)}, u32[]{:S(2)}) copy-start(s32[64,6]{0,1:T(8,128)} %param.20) | copy-start | bytes 4612
  19.7 13.2 %collective-permute-start.2 = (bf16[2,1024,128]{2,1,0:T(8,128)(2,1)S(1)}, bf16[2,1024,128]{2,1,0:T(8,128)(2,1)S(1)}, u32[]{:S(2)}, u32[]{:S(2)}) collective-permute-start(bf16[2,1024,128]{2,1,0:T(8,128)(2,1)S(1)} %pad_maximum_fusion.4), channel_id=1, source_target_pairs={{0,4},{1,5},{2,6},{3,7},{4,0},{5,1},{6,2},{7,3},{8,12},{9,13},{10,... | collective-permute-start | bytes 1572872 | tf_op jit(solution)/shard_map/ppermute | solution.py:103
  21.4 12.1 %copy-start.6 = (s32[2]{0:T(128)S(1)}, s32[2]{0:T(128)}, u32[]{:S(2)}) copy-start(s32[2]{0:T(128)} %param.16) | copy-start | bytes 28
  21.4 13.5 %copy-start.7 = (s32[1,16]{1,0:T(1,128)S(1)}, s32[1,16]{1,0:T(1,128)}, u32[]{:S(2)}) copy-start(s32[1,16]{1,0:T(1,128)} %param.17) | copy-start | bytes 196
  21.4 47.9 %all-to-all-start = ((bf16[16,224,128]{2,1,0:T(8,128)(2,1)}), bf16[16,224,128]{2,1,0:T(8,128)(2,1)}, u32[]{:S(2)}, u32[]{:S(2)}) async-start(bf16[16,224,128]{2,1,0:T(8,128)(2,1)} %pad_maximum_fusion.3), calls=%async_computation | async-start | bytes 1835008 | tf_op jit(solution)/shard_map/all_to_all | solution.py:67
  29.3 64.0 %collective-permute-start.5 = (bf16[1,1024,1408]{2,1,0:T(8,128)(2,1)}, bf16[1,1024,1408]{2,1,0:T(8,128)(2,1)}, u32[]{:S(2)}, u32[]{:S(2)}) collective-permute-start(bf16[1,1024,1408]{2,1,0:T(8,128)(2,1)} %param.22), channel_id=1, source_target_pairs={{0,16},{16,0},{1,17},{17,1},{2,18},{18,2},{3,19},{19,3},{4,20},{20... | collective-permute-start | bytes 8650760 | tf_op jit(solution)/shard_map/ppermute | solution.py:29
  33.0 29.3 %collective-permute-start.3 = (bf16[4,1024,128]{2,1,0:T(8,128)(2,1)S(1)}, bf16[4,1024,128]{2,1,0:T(8,128)(2,1)}, u32[]{:S(2)}, u32[]{:S(2)}) collective-permute-start(bf16[4,1024,128]{2,1,0:T(8,128)(2,1)S(1)} %pad_maximum_fusion.2), channel_id=1, source_target_pairs={{0,2},{1,3},{2,0},{3,1},{4,6},{5,7},{6,4},{7,5},{8,10},{9,11},{10,... | collective-permute-start | bytes 3145736 | tf_op jit(solution)/shard_map/ppermute | solution.py:103
  65.3 23.0 %collective-permute-start.4 = (bf16[8,1024,128]{2,1,0:T(8,128)(2,1)}, bf16[8,1024,128]{2,1,0:T(8,128)(2,1)}, u32[]{:S(2)}, u32[]{:S(2)}) collective-permute-start(bf16[8,1024,128]{2,1,0:T(8,128)(2,1)} %pad_maximum_fusion.1), channel_id=1, source_target_pairs={{0,1},{1,0},{2,3},{3,2},{4,5},{5,4},{6,7},{7,6},{8,9},{9,8},{10,11... | collective-permute-start | bytes 6291464 | tf_op jit(solution)/shard_map/ppermute | solution.py:103
  75.1 13.2 %all-to-all-start.1 = ((bf16[16,32,128]{2,1,0:T(8,128)(2,1)}), bf16[16,32,128]{2,1,0:T(8,128)(2,1)S(1)}, u32[]{:S(2)}, u32[]{:S(2)}) async-start(bf16[16,32,128]{2,1,0:T(8,128)(2,1)} %bitcast.11), calls=%async_computation.1 | async-start | bytes 262144 | tf_op jit(solution)/shard_map/all_to_all | solution.py:87
  90.8 1.7 copy-start.1
  90.9 1.9 copy-start.3
  95.4 54.3 %all-to-all-start.2 = ((bf16[16,32,2048]{2,1,0:T(8,128)(2,1)}), bf16[16,32,2048]{2,1,0:T(8,128)(2,1)S(1)}, u32[]{:S(2)}, u32[]{:S(2)}) async-start(bf16[16,32,2048]{2,1,0:T(8,128)(2,1)} %bitcast.21), calls=%async_computation.2 | async-start | bytes 4194304 | tf_op jit(solution)/shard_map/all_to_all | solution.py:141
  102.3 33.2 %collective-permute-start.6 = (bf16[1,704,1024]{2,1,0:T(8,128)(2,1)}, bf16[1,704,1024]{2,1,0:T(8,128)(2,1)}, u32[]{:S(2)}, u32[]{:S(2)}) collective-permute-start(bf16[1,704,1024]{2,1,0:T(8,128)(2,1)} %param.23), channel_id=1, source_target_pairs={{0,16},{16,0},{1,17},{17,1},{2,18},{18,2},{3,19},{19,3},{4,20},{20... | collective-permute-start | bytes 4325384 | tf_op jit(solution)/shard_map/ppermute | solution.py:29
  149.7 5.9 %copy-start.5 = (bf16[1,704,1024]{2,1,0:T(8,128)(2,1)S(1)}, bf16[1,704,1024]{2,1,0:T(8,128)(2,1)}, u32[]{:S(2)}) copy-start(bf16[1,704,1024]{2,1,0:T(8,128)(2,1)} %param.23) | copy-start | bytes 4325380
  160.8 5.0 %copy-start.4 = (f32[64,6]{0,1:T(8,128)S(1)}, f32[64,6]{0,1:T(8,128)}, u32[]{:S(2)}) copy-start(f32[64,6]{0,1:T(8,128)} %param.21) | copy-start | bytes 4612
  160.8 52.5 %all-to-all-start.3 = ((bf16[16,32,2048]{2,1,0:T(8,128)(2,1)}), bf16[16,32,2048]{2,1,0:T(8,128)(2,1)S(1)}, u32[]{:S(2)}, u32[]{:S(2)}) async-start(bf16[16,32,2048]{2,1,0:T(8,128)(2,1)} %bitcast.74), calls=%async_computation.3 | async-start | bytes 4194304 | tf_op jit(solution)/shard_map/all_to_all | solution.py:164

commit v10 on v9

--- a/solution.py
+++ b/solution.py
@@ -99,13 +99,21 @@
     bits = n_mp.bit_length() - 1
     if n_mp == 1 << bits:
         block = wo_rows[None]
-        for b in reversed(range(bits)):
+        for b in reversed(range(1, bits)):
             pair = lax.ppermute(block, "mp", [(m, m ^ (1 << b)) for m in range(n_mp)])
             low = (column >> b) % 2 == 0
             block = jnp.concatenate(
                 [jnp.where(low, block, pair), jnp.where(low, pair, block)], axis=0
             )
-        by_shard = jnp.einsum("tk,jkc->tjc", attended, block, preferred_element_type=jnp.float32)
+        pair = lax.ppermute(block, "mp", [(m, m ^ 1) for m in range(n_mp)])
+        own_part = jnp.einsum("tk,jkc->tjc", attended, block, preferred_element_type=jnp.float32)
+        pair_part = jnp.einsum("tk,jkc->tjc", attended, pair, preferred_element_type=jnp.float32)
+        low = column % 2 == 0
+        by_shard = jnp.where(
+            low,
+            jnp.concatenate([own_part, pair_part], axis=1),
+            jnp.concatenate([pair_part, own_part], axis=1),
+        )
         order = (0,) + tuple(range(bits, 0, -1)) + (bits + 1,)
         shard_w = wo_rows.shape[1]
         projected = (
@@ -149,12 +157,12 @@
             jnp.concatenate([experts_in[0], in_other[0]], axis=0),
             jnp.concatenate([in_other[0], experts_in[0]], axis=0),
         )
-        flat_rows, out_other, gate_up = lax.optimization_barrier((flat_rows, out_other, gate_up))
         down = jnp.where(
             first,
             jnp.concatenate([experts_out[0], out_other[0]], axis=1),
             jnp.concatenate([out_other[0], experts_out[0]], axis=1),
         )
+        flat_rows, down, gate_up = lax.optimization_barrier((flat_rows, down, gate_up))
     else:
         gate_up = lax.all_gather(experts_in, "dp", axis=1, tiled=True)[0]
         down = lax.all_gather(experts_out, "dp", axis=2, tiled=True)[0]

time: 216 us -> 214 us (level)
  waiting for transfers between devices: 131 us -> 138 us
  starting transfers between devices: 37.5 us -> 33.4 us
  other arithmetic: 19.9 us -> 17 us
    all_to_all x1, waiting for transfers between devices: 14.2 us -> 4.38 us  [on_device(): lax.all_to_all(sending.reshape(n_mp, capacity, d_model), 'mp', split_axis...]
    ppermute x4 -> x3, waiting for transfers between devices: 37.5 us -> 46.4 us  [on_device(): pair = lax.ppermute(block, 'mp', [(m, m ^ 1 << b) for m in range(n_mp)])]
    ppermute x3, waiting for transfers between devices: 26.8 us -> 35 us  [swap_dp(): return lax.ppermute(x, 'dp', [(0, 1), (1, 0)])]
    select_n x4 -> x3, other arithmetic: 3.74 us -> 0.25 us  [on_device(): jnp.where(low, block, pair)]
    ppermute x4 -> x3, starting transfers between devices: 5.96 us -> 3 us  [on_device(): pair = lax.ppermute(block, 'mp', [(m, m ^ 1 << b) for m in range(n_mp)])]
    select_n x0 -> x2, other arithmetic: none -> 2.75 us  [the longest x1 2.7 us: on_device(): jnp.where(first, jnp.concatenate([experts_out[0], out_other[0]], axis=1),...]
    all_to_all x1, starting transfers between devices: 7.84 us -> 5.68 us  [on_device(): lax.all_to_all(jnp.concatenate([q_out, kv_out], axis=1), 'mp', split_axis...]
  transfers between devices with their start and end apart: 11 -> 11, of which waited for: 9 -> 8; matrix products, arithmetic and copies ran while one was open for 14% -> 13% of each run, Pallas kernels for 0% -> 0%
where the time goes in v10:
time: 214 us
  waiting for transfers between devices  138 us (64%)
  starting transfers between devices  33.4 us (16%)
  matrix products  18.3 us (9%)
  other arithmetic  17 us (8%)
  local copies, waits for them, and re-layouts  6.64 us (3%)
    all_to_all x1, waiting for transfers between devices, on_device(): lax.all_to_all(outcome.reshape(n_mp, capacity, d_model), 'mp', split_axis...  47.2 us
    ppermute x3, waiting for transfers between devices, on_device(): pair = lax.ppermute(block, 'mp', [(m, m ^ 1 << b) for m in range(n_mp)])  46.4 us
    ppermute x3, waiting for transfers between devices, swap_dp(): return lax.ppermute(x, 'dp', [(0, 1), (1, 0)])  35 us
    select_n x1, other arithmetic, on_device(): jnp.where(first, jnp.concatenate([experts_in[0], in_other[0]], axis=0), j...  7.45 us
    all_to_all x1, starting transfers between devices, on_device(): lax.all_to_all(blended.reshape(n_mp, sub, HD), 'mp', split_axis=0, concat...  7.23 us
    all_to_all x1, starting transfers between devices, on_device(): lax.all_to_all(sending.reshape(n_mp, capacity, d_model), 'mp', split_axis...  7.05 us
    dot_general x1, matrix products, on_device(): gate_vals = jnp.dot(flat_rows, gate_up, preferred_element_type=jnp.float32)  6.38 us
    all_to_all x1, starting transfers between devices, on_device(): lax.all_to_all(jnp.concatenate([q_out, kv_out], axis=1), 'mp', split_axis...  5.68 us
  transfers between devices with their start and end apart: 11, of which 8 were waited for; matrix products, arithmetic and copies ran while one was open for 13% of the time, Pallas kernels for 0%

profile of v10, /device:TPU:11, one launch (start us, length us, event | category | flops | bytes accessed | tf_op | source)
XLA Modules:
  0.0 213.8 jit_solution(6720175783507945723)
XLA Ops:
  0.0 1.2 collective-permute-start
  1.2 3.3 %collective-permute-done = bf16[512,128]{1,0:T(8,128)(2,1)S(1)} collective-permute-done((bf16[512,128]{1,0:T(8,128)(2,1)}, bf16[512,128]{1,0:T(8,128)(2,1)S(1)}, u32[]{:S(2)}, u32[]{:S(2)}) %collective-permute-start) | collective-permute-done | bytes 131104 | tf_op jit(solution)/shard_map/ppermute | solution.py:29
  4.6 1.1 maximum_select_fusion.3
  5.6 2.4 %collective-permute-start.1 = (bf16[1,1024,128]{2,1,0:T(8,128)(2,1)S(1)}, bf16[1,1024,128]{2,1,0:T(8,128)(2,1)S(1)}, u32[]{:S(2)}, u32[]{:S(2)}) collective-permute-start(bf16[1,1024,128]{2,1,0:T(8,128)(2,1)S(1)} %maximum_select_fusion.3), channel_id=1, source_target_pairs={{0,8},{1,9},{2,10},{3,11},{4,12},{5,13},{6,14},{7,15},{8,0},{9,1},... | collective-permute-start | bytes 786440 | tf_op jit(solution)/shard_map/ppermute | solution.py:103
  8.0 1.2 reshape.227
  9.3 0.3 copy.66
  9.6 0.9 copy.77
  10.6 0.6 tile.8
  11.2 1.0 pad_maximum_fusion.2
  12.2 5.7 %all-to-all-start = ((bf16[16,224,128]{2,1,0:T(8,128)(2,1)}), bf16[16,224,128]{2,1,0:T(8,128)(2,1)S(1)}, u32[]{:S(2)}, u32[]{:S(2)}) async-start(bf16[16,224,128]{2,1,0:T(8,128)(2,1)} %pad_maximum_fusion.2), calls=%async_computation | async-start | bytes 1835008 | tf_op jit(solution)/shard_map/all_to_all | solution.py:67
  17.9 1.2 collective-permute-start.5
  19.3 0.2 collective-permute-done.1
  19.8 0.9 reduce-window.6
  20.7 0.2 slice_reduce_fusion
  20.9 0.2 select_reduce_fusion.1
  21.1 24.2 %collective-permute-done.2 = bf16[2,1024,128]{2,1,0:T(8,128)(2,1)S(1)} collective-permute-done((bf16[2,1024,128]{2,1,0:T(8,128)(2,1)S(1)}, bf16[2,1024,128]{2,1,0:T(8,128)(2,1)S(1)}, u32[]{:S(2)}, u32[]{:S(2)}) %collective-permute-start.2) | collective-permute-done | bytes 524320 | tf_op jit(solution)/shard_map/ppermute | solution.py:103
  45.4 1.1 pad_maximum_fusion.1
  46.4 0.5 collective-permute-start.3
  47.1 0.6 dynamic_slice.7
  47.8 0.7 fusion.19
  48.6 22.1 %collective-permute-done.3 = bf16[4,1024,128]{2,1,0:T(8,128)(2,1)S(1)} collective-permute-done((bf16[4,1024,128]{2,1,0:T(8,128)(2,1)}, bf16[4,1024,128]{2,1,0:T(8,128)(2,1)S(1)}, u32[]{:S(2)}, u32[]{:S(2)}) %collective-permute-start.3) | collective-permute-done | bytes 1048608 | tf_op jit(solution)/shard_map/ppermute | solution.py:103
  70.8 0.2 pad_maximum_fusion
  71.0 1.6 collective-permute-start.4
  73.1 0.5 copy.67
  73.6 0.2 fusion.22
  73.9 0.7 fusion.23
  74.8 0.6 fusion.1
  75.3 1.4 fusion.5
  76.7 7.2 %all-to-all-start.1 = ((bf16[16,32,128]{2,1,0:T(8,128)(2,1)}), bf16[16,32,128]{2,1,0:T(8,128)(2,1)S(1)}, u32[]{:S(2)}, u32[]{:S(2)}) async-start(bf16[16,32,128]{2,1,0:T(8,128)(2,1)} %bitcast.11), calls=%async_computation.1 | async-start | bytes 262144 | tf_op jit(solution)/shard_map/all_to_all | solution.py:87
  84.1 5.0 %all-to-all-done.1 = bf16[16,32,128]{2,1,0:T(8,128)(2,1)S(1)} async-done(((bf16[16,32,128]{2,1,0:T(8,128)(2,1)}), bf16[16,32,128]{2,1,0:T(8,128)(2,1)S(1)}, u32[]{:S(2)}, u32[]{:S(2)}) %all-to-all-start.1) | async-done | bytes 131104 | tf_op jit(solution)/shard_map/all_to_all | solution.py:87
  89.2 0.5 fusion.24
  89.8 2.1 fusion.25
  91.9 0.4 copy.71
  92.3 0.4 reshape.233
  92.8 0.2 fusion.9
  93.1 2.1 convolution_convert_fusion.1
  95.2 7.1 %all-to-all-start.2 = ((bf16[16,32,2048]{2,1,0:T(8,128)(2,1)}), bf16[16,32,2048]{2,1,0:T(8,128)(2,1)}, u32[]{:S(2)}, u32[]{:S(2)}) async-start(bf16[16,32,2048]{2,1,0:T(8,128)(2,1)} %bitcast.19), calls=%async_computation.2 | async-start | bytes 4194304 | tf_op jit(solution)/shard_map/all_to_all | solution.py:149
  102.3 1.3 collective-permute-start.6
  103.6 31.7 %collective-permute-done.6 = bf16[1,704,1024]{2,1,0:T(8,128)(2,1)S(1)} collective-permute-done((bf16[1,704,1024]{2,1,0:T(8,128)(2,1)S(1)}, bf16[1,704,1024]{2,1,0:T(8,128)(2,1)S(1)}, u32[]{:S(2)}, u32[]{:S(2)}) %collective-permute-start.6) | collective-permute-done | bytes 1441824 | tf_op jit(solution)/shard_map/ppermute | solution.py:29
  135.3 2.7 %maximum_select_fusion.1 = bf16[704,2048]{1,0:T(8,128)(2,1)S(1)} fusion(bf16[704,1024]{1,0:T(8,128)(2,1)S(1)} %bitcast.75, bf16[704,1024]{1,0:T(8,128)(2,1)} %bitcast.74, pred[]{:T(512)S(6)} %eq.86), kind=kLoop, calls=%fused_computation.7 | loop fusion | flops 12976128 | bytes 5767169 | tf_op jit(solution)/shard_map/jit(_where)/select_n | solution.py:160
  138.0 7.5 %maximum_select_fusion = bf16[2048,1408]{1,0:T(8,128)(2,1)} fusion(bf16[1024,1408]{1,0:T(8,128)(2,1)} %bitcast.24, bf16[1024,1408]{1,0:T(8,128)(2,1)S(1)} %bitcast.70, pred[]{:T(512)S(6)} %eq.86), kind=kLoop, calls=%fused_computation | loop fusion | flops 25952256 | bytes 11534337 | tf_op jit(solution)/shard_map/jit(_where)/select_n | solution.py:155
  145.4 4.4 %all-to-all-done.2 = bf16[16,32,2048]{2,1,0:T(8,128)(2,1)} async-done(((bf16[16,32,2048]{2,1,0:T(8,128)(2,1)}), bf16[16,32,2048]{2,1,0:T(8,128)(2,1)}, u32[]{:S(2)}, u32[]{:S(2)}) %all-to-all-start.2) | async-done | bytes 2097184 | tf_op jit(solution)/shard_map/all_to_all | solution.py:149
  149.8 6.4 %fusion.26 = f32[512,1408]{1,0:T(8,128)S(1)} fusion(bf16[512,2048]{1,0:T(8,128)(2,1)} %bitcast.20, bf16[2048,1408]{1,0:T(8,128)(2,1)} %maximum_select_fusion), kind=kOutput, calls=%fused_computation.74 | convolution fusion | flops 2952790016 | bytes 10747904 | tf_op jit(solution)/shard_map/dot_general | solution.py:169
  156.2 3.3 %convolution_convert_fusion = bf16[512,2048]{1,0:T(8,128)(2,1)} fusion(bf16[704,2048]{1,0:T(8,128)(2,1)S(1)} %maximum_select_fusion.1, f32[512,1408]{1,0:T(8,128)S(1)} %fusion.26), kind=kOutput, calls=%fused_computation.5 | convolution fusion | flops 1479606272 | bytes 8126464 | tf_op jit(solution)/shard_map/dot_general | solution.py:171
  159.5 5.0 %all-to-all-start.3 = ((bf16[16,32,2048]{2,1,0:T(8,128)(2,1)}), bf16[16,32,2048]{2,1,0:T(8,128)(2,1)S(1)}, u32[]{:S(2)}, u32[]{:S(2)}) async-start(bf16[16,32,2048]{2,1,0:T(8,128)(2,1)} %bitcast.71), calls=%async_computation.3 | async-start | bytes 4194304 | tf_op jit(solution)/shard_map/all_to_all | solution.py:172
  164.5 0.2 select_reduce_fusion
  164.7 47.2 %all-to-all-done.3 = bf16[16,32,2048]{2,1,0:T(8,128)(2,1)S(1)} async-done(((bf16[16,32,2048]{2,1,0:T(8,128)(2,1)}), bf16[16,32,2048]{2,1,0:T(8,128)(2,1)S(1)}, u32[]{:S(2)}, u32[]{:S(2)}) %all-to-all-start.3) | async-done | bytes 2097184 | tf_op jit(solution)/shard_map/all_to_all | solution.py:172
  211.9 1.9 fusion.2
  (55 shorter events, 2.4 us)
Async XLA Ops:
  0.0 20.7 %copy-start = (s32[2,96]{1,0:T(2,128)S(1)}, s32[2,96]{1,0:T(2,128)}, u32[]{:S(2)}) copy-start(s32[2,96]{1,0:T(2,128)} %param.15) | copy-start | bytes 2308
  0.0 4.6 %collective-permute-start = (bf16[512,128]{1,0:T(8,128)(2,1)}, bf16[512,128]{1,0:T(8,128)(2,1)S(1)}, u32[]{:S(2)}, u32[]{:S(2)}) collective-permute-start(bf16[512,128]{1,0:T(8,128)(2,1)} %param.18), channel_id=1, source_target_pairs={{0,16},{16,0},{1,17},{17,1},{2,18},{18,2},{3,19},{19,3},{4,20},{20... | collective-permute-start | bytes 393224 | tf_op jit(solution)/shard_map/ppermute | solution.py:29
  5.6 13.9 %collective-permute-start.1 = (bf16[1,1024,128]{2,1,0:T(8,128)(2,1)S(1)}, bf16[1,1024,128]{2,1,0:T(8,128)(2,1)S(1)}, u32[]{:S(2)}, u32[]{:S(2)}) collective-permute-start(bf16[1,1024,128]{2,1,0:T(8,128)(2,1)S(1)} %maximum_select_fusion.3), channel_id=1, source_target_pairs={{0,8},{1,9},{2,10},{3,11},{4,12},{5,13},{6,14},{7,15},{8,0},{9,1},... | collective-permute-start | bytes 786440 | tf_op jit(solution)/shard_map/ppermute | solution.py:103
  9.6 9.5 %copy-start.4 = (s32[64,6]{0,1:T(8,128)S(1)}, s32[64,6]{0,1:T(8,128)}, u32[]{:S(2)}) copy-start(s32[64,6]{0,1:T(8,128)} %param.20) | copy-start | bytes 4612
  12.2 60.8 %all-to-all-start = ((bf16[16,224,128]{2,1,0:T(8,128)(2,1)}), bf16[16,224,128]{2,1,0:T(8,128)(2,1)S(1)}, u32[]{:S(2)}, u32[]{:S(2)}) async-start(bf16[16,224,128]{2,1,0:T(8,128)(2,1)} %pad_maximum_fusion.2), calls=%async_computation | async-start | bytes 1835008 | tf_op jit(solution)/shard_map/all_to_all | solution.py:67
  17.9 75.3 %collective-permute-start.5 = (bf16[1,1024,1408]{2,1,0:T(8,128)(2,1)}, bf16[1,1024,1408]{2,1,0:T(8,128)(2,1)}, u32[]{:S(2)}, u32[]{:S(2)}) collective-permute-start(bf16[1,1024,1408]{2,1,0:T(8,128)(2,1)} %param.22), channel_id=1, source_target_pairs={{0,16},{16,0},{1,17},{17,1},{2,18},{18,2},{3,19},{19,3},{4,20},{20... | collective-permute-start | bytes 8650760 | tf_op jit(solution)/shard_map/ppermute | solution.py:29
  19.6 27.5 %copy-start.7 = (s32[2]{0:T(128)S(1)}, s32[2]{0:T(128)}, u32[]{:S(2)}) copy-start(s32[2]{0:T(128)} %param.16) | copy-start | bytes 28
  19.6 28.2 %copy-start.8 = (s32[1,16]{1,0:T(1,128)S(1)}, s32[1,16]{1,0:T(1,128)}, u32[]{:S(2)}) copy-start(s32[1,16]{1,0:T(1,128)} %param.17) | copy-start | bytes 196
  19.7 25.6 %collective-permute-start.2 = (bf16[2,1024,128]{2,1,0:T(8,128)(2,1)S(1)}, bf16[2,1024,128]{2,1,0:T(8,128)(2,1)S(1)}, u32[]{:S(2)}, u32[]{:S(2)}) collective-permute-start(bf16[2,1024,128]{2,1,0:T(8,128)(2,1)S(1)} %pad_maximum_fusion.3), channel_id=1, source_target_pairs={{0,4},{1,5},{2,6},{3,7},{4,0},{5,1},{6,2},{7,3},{8,12},{9,13},{10,... | collective-permute-start | bytes 1572872 | tf_op jit(solution)/shard_map/ppermute | solution.py:103
  46.4 24.2 %collective-permute-start.3 = (bf16[4,1024,128]{2,1,0:T(8,128)(2,1)}, bf16[4,1024,128]{2,1,0:T(8,128)(2,1)S(1)}, u32[]{:S(2)}, u32[]{:S(2)}) collective-permute-start(bf16[4,1024,128]{2,1,0:T(8,128)(2,1)} %pad_maximum_fusion.1), channel_id=1, source_target_pairs={{0,2},{1,3},{2,0},{3,1},{4,6},{5,7},{6,4},{7,5},{8,10},{9,11},{10,... | collective-permute-start | bytes 3145736 | tf_op jit(solution)/shard_map/ppermute | solution.py:103
  71.0 18.7 %collective-permute-start.4 = (bf16[8,1024,128]{2,1,0:T(8,128)(2,1)S(1)}, bf16[8,1024,128]{2,1,0:T(8,128)(2,1)}, u32[]{:S(2)}, u32[]{:S(2)}) collective-permute-start(bf16[8,1024,128]{2,1,0:T(8,128)(2,1)S(1)} %pad_maximum_fusion), channel_id=1, source_target_pairs={{0,1},{1,0},{2,3},{3,2},{4,5},{5,4},{6,7},{7,6},{8,9},{9,8},{10,11... | collective-permute-start | bytes 6291464 | tf_op jit(solution)/shard_map/ppermute | solution.py:108
  76.7 12.4 %all-to-all-start.1 = ((bf16[16,32,128]{2,1,0:T(8,128)(2,1)}), bf16[16,32,128]{2,1,0:T(8,128)(2,1)S(1)}, u32[]{:S(2)}, u32[]{:S(2)}) async-start(bf16[16,32,128]{2,1,0:T(8,128)(2,1)} %bitcast.11), calls=%async_computation.1 | async-start | bytes 262144 | tf_op jit(solution)/shard_map/all_to_all | solution.py:87
  89.7 3.0 %copy-start.3 = (bf16[64,2048]{1,0:T(8,128)(2,1)S(1)}, bf16[64,2048]{1,0:T(8,128)(2,1)}, u32[]{:S(2)}) copy-start(bf16[64,2048]{1,0:T(8,128)(2,1)} %param.13) | copy-start | bytes 786436
  89.7 3.2 %copy-start.5 = (f32[2048]{0:T(1024)S(1)}, f32[2048]{0:T(1024)}, u32[]{:S(2)}) copy-start(f32[2048]{0:T(1024)} %param.19) | copy-start | bytes 24580
  93.1 9.2 %copy-start.2 = (bf16[1,704,1024]{2,1,0:T(8,128)(2,1)S(1)}, bf16[1,704,1024]{2,1,0:T(8,128)(2,1)}, u32[]{:S(2)}) copy-start(bf16[1,704,1024]{2,1,0:T(8,128)(2,1)} %param.23) | copy-start | bytes 4325380
  95.2 54.6 %all-to-all-start.2 = ((bf16[16,32,2048]{2,1,0:T(8,128)(2,1)}), bf16[16,32,2048]{2,1,0:T(8,128)(2,1)}, u32[]{:S(2)}, u32[]{:S(2)}) async-start(bf16[16,32,2048]{2,1,0:T(8,128)(2,1)} %bitcast.19), calls=%async_computation.2 | async-start | bytes 4194304 | tf_op jit(solution)/shard_map/all_to_all | solution.py:149
  102.3 33.0 %collective-permute-start.6 = (bf16[1,704,1024]{2,1,0:T(8,128)(2,1)S(1)}, bf16[1,704,1024]{2,1,0:T(8,128)(2,1)S(1)}, u32[]{:S(2)}, u32[]{:S(2)}) collective-permute-start(bf16[1,704,1024]{2,1,0:T(8,128)(2,1)S(1)} %copy-done.2), channel_id=1, source_target_pairs={{0,16},{16,0},{1,17},{17,1},{2,18},{18,2},{3,19},{19,3},{4,20},{20... | collective-permute-start | bytes 4325384 | tf_op jit(solution)/shard_map/ppermute | solution.py:29
  135.3 2.7 %copy-start.1 = (bf16[1,1024,1408]{2,1,0:T(8,128)(2,1)S(1)}, bf16[1,1024,1408]{2,1,0:T(8,128)(2,1)}, u32[]{:S(2)}) copy-start(bf16[1,1024,1408]{2,1,0:T(8,128)(2,1)} %param.22) | copy-start | bytes 8650756
  159.5 5.0 %copy-start.6 = (f32[64,6]{0,1:T(8,128)S(1)}, f32[64,6]{0,1:T(8,128)}, u32[]{:S(2)}) copy-start(f32[64,6]{0,1:T(8,128)} %param.21) | copy-start | bytes 4612
  159.5 52.4 %all-to-all-start.3 = ((bf16[16,32,2048]{2,1,0:T(8,128)(2,1)}), bf16[16,32,2048]{2,1,0:T(8,128)(2,1)S(1)}, u32[]{:S(2)}, u32[]{:S(2)}) async-start(bf16[16,32,2048]{2,1,0:T(8,128)(2,1)} %bitcast.71), calls=%async_computation.3 | async-start | bytes 4194304 | tf_op jit(solution)/shard_map/all_to_all | solution.py:172

commit v11 on v10

--- a/solution.py
+++ b/solution.py
@@ -157,12 +157,12 @@
             jnp.concatenate([experts_in[0], in_other[0]], axis=0),
             jnp.concatenate([in_other[0], experts_in[0]], axis=0),
         )
+        flat_rows, out_other, gate_up = lax.optimization_barrier((flat_rows, out_other, gate_up))
         down = jnp.where(
             first,
             jnp.concatenate([experts_out[0], out_other[0]], axis=1),
             jnp.concatenate([out_other[0], experts_out[0]], axis=1),
         )
-        flat_rows, down, gate_up = lax.optimization_barrier((flat_rows, down, gate_up))
     else:
         gate_up = lax.all_gather(experts_in, "dp", axis=1, tiled=True)[0]
         down = lax.all_gather(experts_out, "dp", axis=2, tiled=True)[0]

time: 214 us -> 215 us (level)
    all_to_all x1, waiting for transfers between devices: 4.38 us -> 14.2 us  [on_device(): lax.all_to_all(sending.reshape(n_mp, capacity, d_model), 'mp', split_axis...]
    ppermute x3, waiting for transfers between devices: 35 us -> 26.5 us  [swap_dp(): return lax.ppermute(x, 'dp', [(0, 1), (1, 0)])]
    select_n x1 -> x0, other arithmetic: 2.7 us -> none  [on_device(): jnp.where(first, jnp.concatenate([experts_out[0], out_other[0]], axis=1),...]
  transfers between devices with their start and end apart: 11 -> 11, of which waited for: 8 -> 8; matrix products, arithmetic and copies ran while one was open for 13% -> 12% of each run, Pallas kernels for 0% -> 0%
where the time goes in v11:
time: 215 us
  waiting for transfers between devices  139 us (65%)
  starting transfers between devices  32.6 us (15%)
  matrix products  19.9 us (9%)
  other arithmetic  15.6 us (7%)
  local copies, waits for them, and re-layouts  6.64 us (3%)
    all_to_all x1, waiting for transfers between devices, on_device(): lax.all_to_all(outcome.reshape(n_mp, capacity, d_model), 'mp', split_axis...  47.2 us
    ppermute x3, waiting for transfers between devices, on_device(): pair = lax.ppermute(block, 'mp', [(m, m ^ 1 << b) for m in range(n_mp)])  46.5 us
    ppermute x3, waiting for transfers between devices, swap_dp(): return lax.ppermute(x, 'dp', [(0, 1), (1, 0)])  26.5 us
    all_to_all x1, waiting for transfers between devices, on_device(): lax.all_to_all(sending.reshape(n_mp, capacity, d_model), 'mp', split_axis...  14.2 us
    select_n x1, other arithmetic, on_device(): jnp.where(first, jnp.concatenate([experts_in[0], in_other[0]], axis=0), j...  8.74 us
    all_to_all x1, starting transfers between devices, on_device(): lax.all_to_all(blended.reshape(n_mp, sub, HD), 'mp', split_axis=0, concat...  7.23 us
    all_to_all x1, starting transfers between devices, on_device(): lax.all_to_all(sending.reshape(n_mp, capacity, d_model), 'mp', split_axis...  6.41 us
    dot_general x1, matrix products, on_device(): gate_vals = jnp.dot(flat_rows, gate_up, preferred_element_type=jnp.float32)  5.89 us
  transfers between devices with their start and end apart: 11, of which 8 were waited for; matrix products, arithmetic and copies ran while one was open for 12% of the time, Pallas kernels for 0%

profile of v11, /device:TPU:11, one launch (start us, length us, event | category | flops | bytes accessed | tf_op | source)
XLA Modules:
  0.0 214.6 jit_solution(10470509081362449767)
XLA Ops:
  0.0 1.2 collective-permute-start
  1.2 3.3 %collective-permute-done = bf16[512,128]{1,0:T(8,128)(2,1)S(1)} collective-permute-done((bf16[512,128]{1,0:T(8,128)(2,1)}, bf16[512,128]{1,0:T(8,128)(2,1)S(1)}, u32[]{:S(2)}, u32[]{:S(2)}) %collective-permute-start) | collective-permute-done | bytes 131104 | tf_op jit(solution)/shard_map/ppermute | solution.py:29
  4.6 1.0 maximum_select_fusion.4
  5.6 2.4 %collective-permute-start.1 = (bf16[1,1024,128]{2,1,0:T(8,128)(2,1)S(1)}, bf16[1,1024,128]{2,1,0:T(8,128)(2,1)S(1)}, u32[]{:S(2)}, u32[]{:S(2)}) collective-permute-start(bf16[1,1024,128]{2,1,0:T(8,128)(2,1)S(1)} %maximum_select_fusion.4), channel_id=1, source_target_pairs={{0,8},{1,9},{2,10},{3,11},{4,12},{5,13},{6,14},{7,15},{8,0},{9,1},... | collective-permute-start | bytes 786440 | tf_op jit(solution)/shard_map/ppermute | solution.py:103
  8.0 1.2 reshape.227
  9.3 0.3 copy.66
  9.6 0.9 copy.77
  10.6 0.6 tile.8
  11.2 1.0 pad_maximum_fusion.2
  12.2 5.7 %all-to-all-start = ((bf16[16,224,128]{2,1,0:T(8,128)(2,1)}), bf16[16,224,128]{2,1,0:T(8,128)(2,1)S(1)}, u32[]{:S(2)}, u32[]{:S(2)}) async-start(bf16[16,224,128]{2,1,0:T(8,128)(2,1)} %pad_maximum_fusion.2), calls=%async_computation | async-start | bytes 1835008 | tf_op jit(solution)/shard_map/all_to_all | solution.py:67
  17.8 1.2 collective-permute-start.5
  19.3 0.2 collective-permute-done.1
  19.6 0.2 collective-permute-start.2
  19.8 0.9 reduce-window.6
  20.7 0.2 slice_reduce_fusion
  20.9 0.2 select_reduce_fusion.1
  21.1 24.2 %collective-permute-done.2 = bf16[2,1024,128]{2,1,0:T(8,128)(2,1)S(1)} collective-permute-done((bf16[2,1024,128]{2,1,0:T(8,128)(2,1)S(1)}, bf16[2,1024,128]{2,1,0:T(8,128)(2,1)S(1)}, u32[]{:S(2)}, u32[]{:S(2)}) %collective-permute-start.2) | collective-permute-done | bytes 524320 | tf_op jit(solution)/shard_map/ppermute | solution.py:103
  45.3 1.1 pad_maximum_fusion.1
  46.4 0.4 collective-permute-start.3
  47.0 0.6 dynamic_slice.7
  47.7 0.7 fusion.25
  48.5 22.2 %collective-permute-done.3 = bf16[4,1024,128]{2,1,0:T(8,128)(2,1)S(1)} collective-permute-done((bf16[4,1024,128]{2,1,0:T(8,128)(2,1)}, bf16[4,1024,128]{2,1,0:T(8,128)(2,1)S(1)}, u32[]{:S(2)}, u32[]{:S(2)}) %collective-permute-start.3) | collective-permute-done | bytes 1048608 | tf_op jit(solution)/shard_map/ppermute | solution.py:103
  70.8 0.2 pad_maximum_fusion
  71.0 1.6 collective-permute-start.4
  73.1 0.5 copy.67
  73.6 0.2 fusion.29
  73.9 0.7 fusion.30
  74.8 0.6 fusion.7
  75.3 1.4 fusion.11
  76.7 7.2 %all-to-all-start.1 = ((bf16[16,32,128]{2,1,0:T(8,128)(2,1)}), bf16[16,32,128]{2,1,0:T(8,128)(2,1)S(1)}, u32[]{:S(2)}, u32[]{:S(2)}) async-start(bf16[16,32,128]{2,1,0:T(8,128)(2,1)} %bitcast.11), calls=%async_computation.1 | async-start | bytes 262144 | tf_op jit(solution)/shard_map/all_to_all | solution.py:87
  84.1 5.0 %all-to-all-done.1 = bf16[16,32,128]{2,1,0:T(8,128)(2,1)S(1)} async-done(((bf16[16,32,128]{2,1,0:T(8,128)(2,1)}), bf16[16,32,128]{2,1,0:T(8,128)(2,1)S(1)}, u32[]{:S(2)}, u32[]{:S(2)}) %all-to-all-start.1) | async-done | bytes 131104 | tf_op jit(solution)/shard_map/all_to_all | solution.py:87
  89.2 0.5 fusion.31
  89.7 2.1 fusion.32
  91.9 0.4 copy.71
  92.3 0.4 reshape.233
  92.7 0.2 fusion.15
  93.1 2.1 convolution_convert_fusion.1
  95.2 6.4 %all-to-all-start.2 = ((bf16[16,32,2048]{2,1,0:T(8,128)(2,1)}), bf16[16,32,2048]{2,1,0:T(8,128)(2,1)S(1)}, u32[]{:S(2)}, u32[]{:S(2)}) async-start(bf16[16,32,2048]{2,1,0:T(8,128)(2,1)} %bitcast.19), calls=%async_computation.2 | async-start | bytes 4194304 | tf_op jit(solution)/shard_map/all_to_all | solution.py:149
  101.6 1.3 collective-permute-start.6
  102.9 8.7 %maximum_select_fusion = bf16[2048,1408]{1,0:T(8,128)(2,1)} fusion(bf16[1024,1408]{1,0:T(8,128)(2,1)} %bitcast.22, bf16[1024,1408]{1,0:T(8,128)(2,1)} %bitcast.69, pred[]{:T(512)S(6)} %eq.86), kind=kLoop, calls=%fused_computation | loop fusion | flops 25952256 | bytes 11534337 | tf_op jit(solution)/shard_map/jit(_where)/select_n | solution.py:155
  111.7 23.1 %collective-permute-done.6 = bf16[1,704,1024]{2,1,0:T(8,128)(2,1)} collective-permute-done((bf16[1,704,1024]{2,1,0:T(8,128)(2,1)}, bf16[1,704,1024]{2,1,0:T(8,128)(2,1)}, u32[]{:S(2)}, u32[]{:S(2)}) %collective-permute-start.6) | collective-permute-done | bytes 1441824 | tf_op jit(solution)/shard_map/ppermute | solution.py:29
  134.8 14.2 %all-to-all-done.2 = bf16[16,32,2048]{2,1,0:T(8,128)(2,1)S(1)} async-done(((bf16[16,32,2048]{2,1,0:T(8,128)(2,1)}), bf16[16,32,2048]{2,1,0:T(8,128)(2,1)S(1)}, u32[]{:S(2)}, u32[]{:S(2)}) %all-to-all-start.2) | async-done | bytes 2097184 | tf_op jit(solution)/shard_map/all_to_all | solution.py:149
  149.1 5.9 %fusion.33 = f32[512,1408]{1,0:T(8,128)S(1)} fusion(bf16[512,2048]{1,0:T(8,128)(2,1)S(1)} %bitcast.70, bf16[2048,1408]{1,0:T(8,128)(2,1)} %maximum_select_fusion), kind=kOutput, calls=%fused_computation.81 | convolution fusion | flops 2952790016 | bytes 10747904 | tf_op jit(solution)/shard_map/dot_general | solution.py:169
  155.0 5.2 %convolution_convert_fusion = bf16[512,2048]{1,0:T(8,128)(2,1)} fusion(bf16[704,1024]{1,0:T(8,128)(2,1)} %bitcast.24, bf16[704,1024]{1,0:T(8,128)(2,1)S(1)} %bitcast.85, pred[]{:T(512)S(6)} %eq.86, f32[512,1408]{1,0:T(8,128)S(1)} %fusion.33), kind=kOutput, calls=%fused_computation.5 | convolution fusion | flops 1492582400 | bytes 8126465 | tf_op jit(solution)/shard_map/dot_general | solution.py:171
  160.2 5.0 %all-to-all-start.3 = ((bf16[16,32,2048]{2,1,0:T(8,128)(2,1)}), bf16[16,32,2048]{2,1,0:T(8,128)(2,1)S(1)}, u32[]{:S(2)}, u32[]{:S(2)}) async-start(bf16[16,32,2048]{2,1,0:T(8,128)(2,1)} %bitcast.71), calls=%async_computation.3 | async-start | bytes 4194304 | tf_op jit(solution)/shard_map/all_to_all | solution.py:172
  165.3 0.2 select_reduce_fusion
  165.4 47.2 %all-to-all-done.3 = bf16[16,32,2048]{2,1,0:T(8,128)(2,1)S(1)} async-done(((bf16[16,32,2048]{2,1,0:T(8,128)(2,1)}), bf16[16,32,2048]{2,1,0:T(8,128)(2,1)S(1)}, u32[]{:S(2)}, u32[]{:S(2)}) %all-to-all-start.3) | async-done | bytes 2097184 | tf_op jit(solution)/shard_map/all_to_all | solution.py:172
  212.7 1.9 fusion.8
  (52 shorter events, 2.2 us)
Async XLA Ops:
  0.0 20.7 %copy-start = (s32[2,96]{1,0:T(2,128)S(1)}, s32[2,96]{1,0:T(2,128)}, u32[]{:S(2)}) copy-start(s32[2,96]{1,0:T(2,128)} %param.15) | copy-start | bytes 2308
  0.0 4.6 %collective-permute-start = (bf16[512,128]{1,0:T(8,128)(2,1)}, bf16[512,128]{1,0:T(8,128)(2,1)S(1)}, u32[]{:S(2)}, u32[]{:S(2)}) collective-permute-start(bf16[512,128]{1,0:T(8,128)(2,1)} %param.18), channel_id=1, source_target_pairs={{0,16},{16,0},{1,17},{17,1},{2,18},{18,2},{3,19},{19,3},{4,20},{20... | collective-permute-start | bytes 393224 | tf_op jit(solution)/shard_map/ppermute | solution.py:29
  5.6 13.9 %collective-permute-start.1 = (bf16[1,1024,128]{2,1,0:T(8,128)(2,1)S(1)}, bf16[1,1024,128]{2,1,0:T(8,128)(2,1)S(1)}, u32[]{:S(2)}, u32[]{:S(2)}) collective-permute-start(bf16[1,1024,128]{2,1,0:T(8,128)(2,1)S(1)} %maximum_select_fusion.4), channel_id=1, source_target_pairs={{0,8},{1,9},{2,10},{3,11},{4,12},{5,13},{6,14},{7,15},{8,0},{9,1},... | collective-permute-start | bytes 786440 | tf_op jit(solution)/shard_map/ppermute | solution.py:103
  9.6 9.5 %copy-start.2 = (s32[64,6]{0,1:T(8,128)S(1)}, s32[64,6]{0,1:T(8,128)}, u32[]{:S(2)}) copy-start(s32[64,6]{0,1:T(8,128)} %param.20) | copy-start | bytes 4612
  12.2 60.8 %all-to-all-start = ((bf16[16,224,128]{2,1,0:T(8,128)(2,1)}), bf16[16,224,128]{2,1,0:T(8,128)(2,1)S(1)}, u32[]{:S(2)}, u32[]{:S(2)}) async-start(bf16[16,224,128]{2,1,0:T(8,128)(2,1)} %pad_maximum_fusion.2), calls=%async_computation | async-start | bytes 1835008 | tf_op jit(solution)/shard_map/all_to_all | solution.py:67
  17.8 75.3 %collective-permute-start.5 = (bf16[1,1024,1408]{2,1,0:T(8,128)(2,1)}, bf16[1,1024,1408]{2,1,0:T(8,128)(2,1)}, u32[]{:S(2)}, u32[]{:S(2)}) collective-permute-start(bf16[1,1024,1408]{2,1,0:T(8,128)(2,1)} %param.22), channel_id=1, source_target_pairs={{0,16},{16,0},{1,17},{17,1},{2,18},{18,2},{3,19},{19,3},{4,20},{20... | collective-permute-start | bytes 8650760 | tf_op jit(solution)/shard_map/ppermute | solution.py:29
  19.6 27.4 %copy-start.6 = (s32[2]{0:T(128)S(1)}, s32[2]{0:T(128)}, u32[]{:S(2)}) copy-start(s32[2]{0:T(128)} %param.16) | copy-start | bytes 28
  19.6 28.1 %copy-start.7 = (s32[1,16]{1,0:T(1,128)S(1)}, s32[1,16]{1,0:T(1,128)}, u32[]{:S(2)}) copy-start(s32[1,16]{1,0:T(1,128)} %param.17) | copy-start | bytes 196
  19.6 25.6 %collective-permute-start.2 = (bf16[2,1024,128]{2,1,0:T(8,128)(2,1)S(1)}, bf16[2,1024,128]{2,1,0:T(8,128)(2,1)S(1)}, u32[]{:S(2)}, u32[]{:S(2)}) collective-permute-start(bf16[2,1024,128]{2,1,0:T(8,128)(2,1)S(1)} %pad_maximum_fusion.3), channel_id=1, source_target_pairs={{0,4},{1,5},{2,6},{3,7},{4,0},{5,1},{6,2},{7,3},{8,12},{9,13},{10,... | collective-permute-start | bytes 1572872 | tf_op jit(solution)/shard_map/ppermute | solution.py:103
  46.4 24.2 %collective-permute-start.3 = (bf16[4,1024,128]{2,1,0:T(8,128)(2,1)}, bf16[4,1024,128]{2,1,0:T(8,128)(2,1)S(1)}, u32[]{:S(2)}, u32[]{:S(2)}) collective-permute-start(bf16[4,1024,128]{2,1,0:T(8,128)(2,1)} %pad_maximum_fusion.1), channel_id=1, source_target_pairs={{0,2},{1,3},{2,0},{3,1},{4,6},{5,7},{6,4},{7,5},{8,10},{9,11},{10,... | collective-permute-start | bytes 3145736 | tf_op jit(solution)/shard_map/ppermute | solution.py:103
  71.0 18.7 %collective-permute-start.4 = (bf16[8,1024,128]{2,1,0:T(8,128)(2,1)S(1)}, bf16[8,1024,128]{2,1,0:T(8,128)(2,1)}, u32[]{:S(2)}, u32[]{:S(2)}) collective-permute-start(bf16[8,1024,128]{2,1,0:T(8,128)(2,1)S(1)} %pad_maximum_fusion), channel_id=1, source_target_pairs={{0,1},{1,0},{2,3},{3,2},{4,5},{5,4},{6,7},{7,6},{8,9},{9,8},{10,11... | collective-permute-start | bytes 6291464 | tf_op jit(solution)/shard_map/ppermute | solution.py:108
  76.7 12.4 %all-to-all-start.1 = ((bf16[16,32,128]{2,1,0:T(8,128)(2,1)}), bf16[16,32,128]{2,1,0:T(8,128)(2,1)S(1)}, u32[]{:S(2)}, u32[]{:S(2)}) async-start(bf16[16,32,128]{2,1,0:T(8,128)(2,1)} %bitcast.11), calls=%async_computation.1 | async-start | bytes 262144 | tf_op jit(solution)/shard_map/all_to_all | solution.py:87
  89.7 3.0 %copy-start.1 = (bf16[64,2048]{1,0:T(8,128)(2,1)S(1)}, bf16[64,2048]{1,0:T(8,128)(2,1)}, u32[]{:S(2)}) copy-start(bf16[64,2048]{1,0:T(8,128)(2,1)} %param.13) | copy-start | bytes 786436
  89.7 3.2 %copy-start.3 = (f32[2048]{0:T(1024)S(1)}, f32[2048]{0:T(1024)}, u32[]{:S(2)}) copy-start(f32[2048]{0:T(1024)} %param.19) | copy-start | bytes 24580
  95.2 53.8 %all-to-all-start.2 = ((bf16[16,32,2048]{2,1,0:T(8,128)(2,1)}), bf16[16,32,2048]{2,1,0:T(8,128)(2,1)S(1)}, u32[]{:S(2)}, u32[]{:S(2)}) async-start(bf16[16,32,2048]{2,1,0:T(8,128)(2,1)} %bitcast.19), calls=%async_computation.2 | async-start | bytes 4194304 | tf_op jit(solution)/shard_map/all_to_all | solution.py:149
  101.6 33.2 %collective-permute-start.6 = (bf16[1,704,1024]{2,1,0:T(8,128)(2,1)}, bf16[1,704,1024]{2,1,0:T(8,128)(2,1)}, u32[]{:S(2)}, u32[]{:S(2)}) collective-permute-start(bf16[1,704,1024]{2,1,0:T(8,128)(2,1)} %param.23), channel_id=1, source_target_pairs={{0,16},{16,0},{1,17},{17,1},{2,18},{18,2},{3,19},{19,3},{4,20},{20... | collective-permute-start | bytes 4325384 | tf_op jit(solution)/shard_map/ppermute | solution.py:29
  149.1 5.9 %copy-start.5 = (bf16[1,704,1024]{2,1,0:T(8,128)(2,1)S(1)}, bf16[1,704,1024]{2,1,0:T(8,128)(2,1)}, u32[]{:S(2)}) copy-start(bf16[1,704,1024]{2,1,0:T(8,128)(2,1)} %param.23) | copy-start | bytes 4325380
  160.2 5.0 %copy-start.4 = (f32[64,6]{0,1:T(8,128)S(1)}, f32[64,6]{0,1:T(8,128)}, u32[]{:S(2)}) copy-start(f32[64,6]{0,1:T(8,128)} %param.21) | copy-start | bytes 4612
  160.2 52.4 %all-to-all-start.3 = ((bf16[16,32,2048]{2,1,0:T(8,128)(2,1)}), bf16[16,32,2048]{2,1,0:T(8,128)(2,1)S(1)}, u32[]{:S(2)}, u32[]{:S(2)}) async-start(bf16[16,32,2048]{2,1,0:T(8,128)(2,1)} %bitcast.71), calls=%async_computation.3 | async-start | bytes 4194304 | tf_op jit(solution)/shard_map/all_to_all | solution.py:172

commit v12 on v11

--- a/solution.py
+++ b/solution.py
@@ -67,6 +67,26 @@
     both = lax.all_to_all(
         jnp.concatenate([q_out, kv_out], axis=1), "mp", split_axis=0, concat_axis=0, tiled=True
     )
+    if n_dp == 2:
+        w_pair = swap_dp(out_weight)
+        wo_rows = jnp.where(
+            row_index == 0,
+            jnp.concatenate([out_weight, w_pair], axis=0),
+            jnp.concatenate([w_pair, out_weight], axis=0),
+        )
+    else:
+        wo_rows = lax.all_gather(out_weight, "dp", axis=0, tiled=True)
+    bits = n_mp.bit_length() - 1
+    if n_mp == 1 << bits:
+        block = wo_rows[None]
+        if bits > 1:
+            b = bits - 1
+            pair = lax.ppermute(block, "mp", [(m, m ^ (1 << b)) for m in range(n_mp)])
+            low = (column >> b) % 2 == 0
+            block = jnp.concatenate(
+                [jnp.where(low, block, pair), jnp.where(low, pair, block)], axis=0
+            )
+        block, both = lax.optimization_barrier((block, both))
     q_in = both[:, :sub, :]
     arrived = both[:, sub:, :].reshape(n_mp, pages_dev, PAGE, 2, HD)
     first_pos = cache_len[request] + deal_row % n_mp * q_count
@@ -84,28 +104,19 @@
     key_rows = arrived[:, :, :, 0, :].reshape(-1, HD)
     value_rows = arrived[:, :, :, 1, :].reshape(-1, HD)
     blended = attend_head(q_in.reshape(-1, HD), key_rows, value_rows, key_pos, query_pos)
-    back = lax.all_to_all(blended.reshape(n_mp, sub, HD), "mp", split_axis=0, concat_axis=0, tiled=True)
-    attended = back.reshape(groups, heads, sub, HD).transpose(2, 0, 1, 3).reshape(q_count, width)
-
-    if n_dp == 2:
-        w_pair = swap_dp(out_weight)
-        wo_rows = jnp.where(
-            row_index == 0,
-            jnp.concatenate([out_weight, w_pair], axis=0),
-            jnp.concatenate([w_pair, out_weight], axis=0),
-        )
-    else:
-        wo_rows = lax.all_gather(out_weight, "dp", axis=0, tiled=True)
-    bits = n_mp.bit_length() - 1
+
     if n_mp == 1 << bits:
-        block = wo_rows[None]
-        for b in reversed(range(1, bits)):
+        back = lax.all_to_all(
+            blended.reshape(n_mp, sub, HD), "mp", split_axis=0, concat_axis=0, tiled=True
+        )
+        for b in reversed(range(1, bits - 1)):
             pair = lax.ppermute(block, "mp", [(m, m ^ (1 << b)) for m in range(n_mp)])
             low = (column >> b) % 2 == 0
             block = jnp.concatenate(
                 [jnp.where(low, block, pair), jnp.where(low, pair, block)], axis=0
             )
         pair = lax.ppermute(block, "mp", [(m, m ^ 1) for m in range(n_mp)])
+        attended = back.reshape(groups, heads, sub, HD).transpose(2, 0, 1, 3).reshape(q_count, width)
         own_part = jnp.einsum("tk,jkc->tjc", attended, block, preferred_element_type=jnp.float32)
         pair_part = jnp.einsum("tk,jkc->tjc", attended, pair, preferred_element_type=jnp.float32)
         low = column % 2 == 0
@@ -122,6 +133,10 @@
             .reshape(q_count, d_model)
         )
     else:
+        back = lax.all_to_all(
+            blended.reshape(n_mp, sub, HD), "mp", split_axis=0, concat_axis=0, tiled=True
+        )
+        attended = back.reshape(groups, heads, sub, HD).transpose(2, 0, 1, 3).reshape(q_count, width)
         projected = jnp.dot(
             attended,
             lax.all_gather(wo_rows, "mp", axis=1, tiled=True),

time: 215 us -> 226 us (1.051)
  waiting for transfers between devices: 139 us -> 149 us
  starting transfers between devices: 32.6 us -> 35.1 us
  other arithmetic: 15.6 us -> 13.3 us
    ppermute x3, waiting for transfers between devices: 46.5 us -> 54.5 us  [on_device(): pair = lax.ppermute(block, 'mp', [(m, m ^ 1 << b) for m in range(n_mp)])]
    ppermute x3, starting transfers between devices: 2.91 us -> 5.6 us  [on_device(): pair = lax.ppermute(block, 'mp', [(m, m ^ 1 << b) for m in range(n_mp)])]
    all_to_all x1, starting transfers between devices: 7.23 us -> 4.81 us  [on_device(): lax.all_to_all(blended.reshape(n_mp, sub, HD), 'mp', split_axis=0, concat...]
  transfers between devices with their start and end apart: 11 -> 11, of which waited for: 8 -> 8; matrix products, arithmetic and copies ran while one was open for 12% -> 9% of each run, Pallas kernels for 0% -> 0%
where the time goes in v12:
time: 226 us; the launch traced here: 225 us
  waiting for transfers between devices  149 us (66%)
  starting transfers between devices  35.1 us (16%)
  matrix products  20.3 us (9%)
  other arithmetic  13.3 us (6%)
  local copies, waits for them, and re-layouts  6.77 us (3%)
    ppermute x3, waiting for transfers between devices, on_device(): pair = lax.ppermute(block, 'mp', [(m, m ^ 1 << b) for m in range(n_mp)])  54.5 us
    all_to_all x1, waiting for transfers between devices, on_device(): lax.all_to_all(outcome.reshape(n_mp, capacity, d_model), 'mp', split_axis...  47.2 us
    ppermute x3, waiting for transfers between devices, swap_dp(): return lax.ppermute(x, 'dp', [(0, 1), (1, 0)])  27.9 us
    all_to_all x1, waiting for transfers between devices, on_device(): lax.all_to_all(sending.reshape(n_mp, capacity, d_model), 'mp', split_axis...  14.4 us
    select_n x1, other arithmetic, on_device(): jnp.where(first, jnp.concatenate([experts_in[0], in_other[0]], axis=0), j...  7.44 us
    all_to_all x1, starting transfers between devices, on_device(): lax.all_to_all(sending.reshape(n_mp, capacity, d_model), 'mp', split_axis...  7.07 us
    all_to_all x1, starting transfers between devices, on_device(): lax.all_to_all(jnp.concatenate([q_out, kv_out], axis=1), 'mp', split_axis...  6.55 us
    dot_general x1, matrix products, on_device(): gate_vals = jnp.dot(flat_rows, gate_up, preferred_element_type=jnp.float32)  6.49 us
  transfers between devices with their start and end apart: 11, of which 8 were waited for; matrix products, arithmetic and copies ran while one was open for 9% of the time, Pallas kernels for 0%

profile of v12, /device:TPU:11, one launch (start us, length us, event | category | flops | bytes accessed | tf_op | source)
XLA Modules:
  0.0 225.0 jit_solution(4066310505164831993)
XLA Ops:
  0.0 1.3 reshape.227
  1.3 0.3 copy.66
  1.6 1.0 copy.77
  2.6 0.6 tile.8
  3.2 1.0 pad_maximum_fusion.2
  4.2 6.6 %all-to-all-start = ((bf16[16,224,128]{2,1,0:T(8,128)(2,1)}), bf16[16,224,128]{2,1,0:T(8,128)(2,1)S(1)}, u32[]{:S(2)}, u32[]{:S(2)}) async-start(bf16[16,224,128]{2,1,0:T(8,128)(2,1)} %pad_maximum_fusion.2), calls=%async_computation | async-start | bytes 1835008 | tf_op jit(solution)/shard_map/all_to_all | solution.py:67
  10.8 1.3 collective-permute-start
  12.1 3.5 %collective-permute-done = bf16[512,128]{1,0:T(8,128)(2,1)S(1)} collective-permute-done((bf16[512,128]{1,0:T(8,128)(2,1)S(1)}, bf16[512,128]{1,0:T(8,128)(2,1)S(1)}, u32[]{:S(2)}, u32[]{:S(2)}) %collective-permute-start) | collective-permute-done | bytes 131104 | tf_op jit(solution)/shard_map/ppermute | solution.py:29
  15.6 2.2 collective-permute-start.1
  17.8 1.2 collective-permute-start.5
  19.3 22.7 %collective-permute-done.1 = bf16[1,1024,128]{2,1,0:T(8,128)(2,1)S(1)} collective-permute-done((bf16[1,1024,128]{2,1,0:T(8,128)(2,1)S(1)}, bf16[1,1024,128]{2,1,0:T(8,128)(2,1)S(1)}, u32[]{:S(2)}, u32[]{:S(2)}) %collective-permute-start.1) | collective-permute-done | bytes 262176 | tf_op jit(solution)/shard_map/ppermute | solution.py:84
  42.1 3.2 %collective-permute-start.2 = (bf16[2,1024,128]{2,1,0:T(8,128)(2,1)S(1)}, bf16[2,1024,128]{2,1,0:T(8,128)(2,1)S(1)}, u32[]{:S(2)}, u32[]{:S(2)}) collective-permute-start(bf16[2,1024,128]{2,1,0:T(8,128)(2,1)S(1)} %pad_maximum_fusion.3), channel_id=1, source_target_pairs={{0,4},{1,5},{2,6},{3,7},{4,0},{5,1},{6,2},{7,3},{8,12},{9,13},{10,... | collective-permute-start | bytes 1572872 | tf_op jit(solution)/shard_map/ppermute | solution.py:113
  45.3 0.9 reduce-window.6
  46.2 0.2 slice_reduce_fusion
  46.4 0.2 select_reduce_fusion.1
  46.6 10.2 %collective-permute-done.2 = bf16[2,1024,128]{2,1,0:T(8,128)(2,1)S(1)} collective-permute-done((bf16[2,1024,128]{2,1,0:T(8,128)(2,1)S(1)}, bf16[2,1024,128]{2,1,0:T(8,128)(2,1)S(1)}, u32[]{:S(2)}, u32[]{:S(2)}) %collective-permute-start.2) | collective-permute-done | bytes 524320 | tf_op jit(solution)/shard_map/ppermute | solution.py:113
  56.9 1.1 pad_maximum_fusion.1
  57.9 0.3 collective-permute-start.3
  58.4 0.6 dynamic_slice.7
  59.1 0.7 fusion.25
  59.9 21.6 %collective-permute-done.3 = bf16[4,1024,128]{2,1,0:T(8,128)(2,1)S(1)} collective-permute-done((bf16[4,1024,128]{2,1,0:T(8,128)(2,1)}, bf16[4,1024,128]{2,1,0:T(8,128)(2,1)S(1)}, u32[]{:S(2)}, u32[]{:S(2)}) %collective-permute-start.3) | collective-permute-done | bytes 1048608 | tf_op jit(solution)/shard_map/ppermute | solution.py:113
  81.7 0.2 pad_maximum_fusion
  81.9 2.2 collective-permute-start.4
  84.6 0.5 copy.67
  85.1 0.2 fusion.29
  85.5 0.7 fusion.30
  86.3 0.6 fusion.7
  86.9 1.4 fusion.11
  88.3 4.8 %all-to-all-start.1 = ((bf16[16,32,128]{2,1,0:T(8,128)(2,1)}), bf16[16,32,128]{2,1,0:T(8,128)(2,1)S(1)}, u32[]{:S(2)}, u32[]{:S(2)}) async-start(bf16[16,32,128]{2,1,0:T(8,128)(2,1)} %bitcast.13), calls=%async_computation.1 | async-start | bytes 262144 | tf_op jit(solution)/shard_map/all_to_all | solution.py:109
  93.1 0.2 fusion.14
  93.3 5.0 %all-to-all-done.1 = bf16[16,32,128]{2,1,0:T(8,128)(2,1)S(1)} async-done(((bf16[16,32,128]{2,1,0:T(8,128)(2,1)}), bf16[16,32,128]{2,1,0:T(8,128)(2,1)S(1)}, u32[]{:S(2)}, u32[]{:S(2)}) %all-to-all-start.1) | async-done | bytes 131104 | tf_op jit(solution)/shard_map/all_to_all | solution.py:109
  98.4 0.5 fusion.31
  98.9 2.1 fusion.32
  101.1 0.4 copy.71
  101.5 0.4 reshape.233
  101.9 0.2 fusion.15
  102.3 2.1 convolution_convert_fusion.1
  104.4 7.1 %all-to-all-start.2 = ((bf16[16,32,2048]{2,1,0:T(8,128)(2,1)}), bf16[16,32,2048]{2,1,0:T(8,128)(2,1)}, u32[]{:S(2)}, u32[]{:S(2)}) async-start(bf16[16,32,2048]{2,1,0:T(8,128)(2,1)} %bitcast.19), calls=%async_computation.2 | async-start | bytes 4194304 | tf_op jit(solution)/shard_map/all_to_all | solution.py:164
  111.4 1.3 collective-permute-start.6
  112.8 7.4 %maximum_select_fusion = bf16[2048,1408]{1,0:T(8,128)(2,1)} fusion(bf16[1024,1408]{1,0:T(8,128)(2,1)} %bitcast.22, bf16[1024,1408]{1,0:T(8,128)(2,1)S(1)} %bitcast.70, pred[]{:T(512)S(6)} %eq.84), kind=kLoop, calls=%fused_computation | loop fusion | flops 25952256 | bytes 11534337 | tf_op jit(solution)/shard_map/jit(_where)/select_n | solution.py:170
  120.2 24.4 %collective-permute-done.6 = bf16[1,704,1024]{2,1,0:T(8,128)(2,1)} collective-permute-done((bf16[1,704,1024]{2,1,0:T(8,128)(2,1)}, bf16[1,704,1024]{2,1,0:T(8,128)(2,1)}, u32[]{:S(2)}, u32[]{:S(2)}) %collective-permute-start.6) | collective-permute-done | bytes 1441824 | tf_op jit(solution)/shard_map/ppermute | solution.py:29
  144.6 14.4 %all-to-all-done.2 = bf16[16,32,2048]{2,1,0:T(8,128)(2,1)} async-done(((bf16[16,32,2048]{2,1,0:T(8,128)(2,1)}), bf16[16,32,2048]{2,1,0:T(8,128)(2,1)}, u32[]{:S(2)}, u32[]{:S(2)}) %all-to-all-start.2) | async-done | bytes 2097184 | tf_op jit(solution)/shard_map/all_to_all | solution.py:164
  159.0 6.5 %fusion.33 = f32[512,1408]{1,0:T(8,128)S(1)} fusion(bf16[512,2048]{1,0:T(8,128)(2,1)} %bitcast.20, bf16[2048,1408]{1,0:T(8,128)(2,1)} %maximum_select_fusion), kind=kOutput, calls=%fused_computation.81 | convolution fusion | flops 2952790016 | bytes 10747904 | tf_op jit(solution)/shard_map/dot_general | solution.py:184
  165.5 5.1 %convolution_convert_fusion = bf16[512,2048]{1,0:T(8,128)(2,1)} fusion(bf16[704,1024]{1,0:T(8,128)(2,1)} %bitcast.24, bf16[704,1024]{1,0:T(8,128)(2,1)S(1)} %bitcast.84, pred[]{:T(512)S(6)} %eq.84, f32[512,1408]{1,0:T(8,128)S(1)} %fusion.33), kind=kOutput, calls=%fused_computation.5 | convolution fusion | flops 1492582400 | bytes 8126465 | tf_op jit(solution)/shard_map/dot_general | solution.py:186
  170.6 5.0 %all-to-all-start.3 = ((bf16[16,32,2048]{2,1,0:T(8,128)(2,1)}), bf16[16,32,2048]{2,1,0:T(8,128)(2,1)S(1)}, u32[]{:S(2)}, u32[]{:S(2)}) async-start(bf16[16,32,2048]{2,1,0:T(8,128)(2,1)} %bitcast.71), calls=%async_computation.3 | async-start | bytes 4194304 | tf_op jit(solution)/shard_map/all_to_all | solution.py:187
  175.7 0.2 select_reduce_fusion
  175.8 47.2 %all-to-all-done.3 = bf16[16,32,2048]{2,1,0:T(8,128)(2,1)S(1)} async-done(((bf16[16,32,2048]{2,1,0:T(8,128)(2,1)}), bf16[16,32,2048]{2,1,0:T(8,128)(2,1)S(1)}, u32[]{:S(2)}, u32[]{:S(2)}) %all-to-all-start.3) | async-done | bytes 2097184 | tf_op jit(solution)/shard_map/all_to_all | solution.py:187
  223.1 1.9 fusion.8
  (59 shorter events, 2.2 us)
Async XLA Ops:
  0.0 46.1 %copy-start = (s32[2,96]{1,0:T(2,128)S(1)}, s32[2,96]{1,0:T(2,128)}, u32[]{:S(2)}) copy-start(s32[2,96]{1,0:T(2,128)} %param.15) | copy-start | bytes 2308
  1.6 9.2 %copy-start.4 = (bf16[512,128]{1,0:T(8,128)(2,1)S(1)}, bf16[512,128]{1,0:T(8,128)(2,1)}, u32[]{:S(2)}) copy-start(bf16[512,128]{1,0:T(8,128)(2,1)} %param.18) | copy-start | bytes 393220
  2.6 16.5 %copy-start.5 = (s32[64,6]{0,1:T(8,128)S(1)}, s32[64,6]{0,1:T(8,128)}, u32[]{:S(2)}) copy-start(s32[64,6]{0,1:T(8,128)} %param.20) | copy-start | bytes 4612
  4.2 37.9 %all-to-all-start = ((bf16[16,224,128]{2,1,0:T(8,128)(2,1)}), bf16[16,224,128]{2,1,0:T(8,128)(2,1)S(1)}, u32[]{:S(2)}, u32[]{:S(2)}) async-start(bf16[16,224,128]{2,1,0:T(8,128)(2,1)} %pad_maximum_fusion.2), calls=%async_computation | async-start | bytes 1835008 | tf_op jit(solution)/shard_map/all_to_all | solution.py:67
  10.8 4.8 %collective-permute-start = (bf16[512,128]{1,0:T(8,128)(2,1)S(1)}, bf16[512,128]{1,0:T(8,128)(2,1)S(1)}, u32[]{:S(2)}, u32[]{:S(2)}) collective-permute-start(bf16[512,128]{1,0:T(8,128)(2,1)S(1)} %copy-done.4), channel_id=1, source_target_pairs={{0,16},{16,0},{1,17},{17,1},{2,18},{18,2},{3,19},{19,3},{4,20},{20... | collective-permute-start | bytes 393224 | tf_op jit(solution)/shard_map/ppermute | solution.py:29
  15.6 26.3 %collective-permute-start.1 = (bf16[1,1024,128]{2,1,0:T(8,128)(2,1)S(1)}, bf16[1,1024,128]{2,1,0:T(8,128)(2,1)S(1)}, u32[]{:S(2)}, u32[]{:S(2)}) collective-permute-start(bf16[1,1024,128]{2,1,0:T(8,128)(2,1)S(1)} %maximum_select_fusion.4), channel_id=1, source_target_pairs={{0,8},{1,9},{2,10},{3,11},{4,12},{5,13},{6,14},{7,15},{8,0},{9,1},... | collective-permute-start | bytes 786440 | tf_op jit(solution)/shard_map/ppermute | solution.py:84
  17.8 84.5 %collective-permute-start.5 = (bf16[1,1024,1408]{2,1,0:T(8,128)(2,1)}, bf16[1,1024,1408]{2,1,0:T(8,128)(2,1)}, u32[]{:S(2)}, u32[]{:S(2)}) collective-permute-start(bf16[1,1024,1408]{2,1,0:T(8,128)(2,1)} %param.22), channel_id=1, source_target_pairs={{0,16},{16,0},{1,17},{17,1},{2,18},{18,2},{3,19},{19,3},{4,20},{20... | collective-permute-start | bytes 8650760 | tf_op jit(solution)/shard_map/ppermute | solution.py:29
  42.0 16.4 %copy-start.9 = (s32[2]{0:T(128)S(1)}, s32[2]{0:T(128)}, u32[]{:S(2)}) copy-start(s32[2]{0:T(128)} %param.16) | copy-start | bytes 28
  42.0 17.1 %copy-start.10 = (s32[1,16]{1,0:T(1,128)S(1)}, s32[1,16]{1,0:T(1,128)}, u32[]{:S(2)}) copy-start(s32[1,16]{1,0:T(1,128)} %param.17) | copy-start | bytes 196
  42.1 42.5 %copy-start.1 = (bf16[16,224,128]{2,1,0:T(8,128)(2,1)}, bf16[16,224,128]{2,1,0:T(8,128)(2,1)S(1)}, u32[]{:S(2)}) copy-start(bf16[16,224,128]{2,1,0:T(8,128)(2,1)S(1)} %all-to-all-done) | copy-start | bytes 2752516
  42.1 14.7 %collective-permute-start.2 = (bf16[2,1024,128]{2,1,0:T(8,128)(2,1)S(1)}, bf16[2,1024,128]{2,1,0:T(8,128)(2,1)S(1)}, u32[]{:S(2)}, u32[]{:S(2)}) collective-permute-start(bf16[2,1024,128]{2,1,0:T(8,128)(2,1)S(1)} %pad_maximum_fusion.3), channel_id=1, source_target_pairs={{0,4},{1,5},{2,6},{3,7},{4,0},{5,1},{6,2},{7,3},{8,12},{9,13},{10,... | collective-permute-start | bytes 1572872 | tf_op jit(solution)/shard_map/ppermute | solution.py:113
  57.9 23.6 %collective-permute-start.3 = (bf16[4,1024,128]{2,1,0:T(8,128)(2,1)}, bf16[4,1024,128]{2,1,0:T(8,128)(2,1)S(1)}, u32[]{:S(2)}, u32[]{:S(2)}) collective-permute-start(bf16[4,1024,128]{2,1,0:T(8,128)(2,1)} %pad_maximum_fusion.1), channel_id=1, source_target_pairs={{0,2},{1,3},{2,0},{3,1},{4,6},{5,7},{6,4},{7,5},{8,10},{9,11},{10,... | collective-permute-start | bytes 3145736 | tf_op jit(solution)/shard_map/ppermute | solution.py:113
  81.9 17.0 %collective-permute-start.4 = (bf16[8,1024,128]{2,1,0:T(8,128)(2,1)S(1)}, bf16[8,1024,128]{2,1,0:T(8,128)(2,1)}, u32[]{:S(2)}, u32[]{:S(2)}) collective-permute-start(bf16[8,1024,128]{2,1,0:T(8,128)(2,1)S(1)} %pad_maximum_fusion), channel_id=1, source_target_pairs={{0,1},{1,0},{2,3},{3,2},{4,5},{5,4},{6,7},{7,6},{8,9},{9,8},{10,11... | collective-permute-start | bytes 6291464 | tf_op jit(solution)/shard_map/ppermute | solution.py:118
  84.6 0.9 slice-start
  88.3 10.0 %all-to-all-start.1 = ((bf16[16,32,128]{2,1,0:T(8,128)(2,1)}), bf16[16,32,128]{2,1,0:T(8,128)(2,1)S(1)}, u32[]{:S(2)}, u32[]{:S(2)}) async-start(bf16[16,32,128]{2,1,0:T(8,128)(2,1)} %bitcast.13), calls=%async_computation.1 | async-start | bytes 262144 | tf_op jit(solution)/shard_map/all_to_all | solution.py:109
  98.9 3.0 %copy-start.3 = (bf16[64,2048]{1,0:T(8,128)(2,1)S(1)}, bf16[64,2048]{1,0:T(8,128)(2,1)}, u32[]{:S(2)}) copy-start(bf16[64,2048]{1,0:T(8,128)(2,1)} %param.13) | copy-start | bytes 786436
  98.9 3.2 %copy-start.6 = (f32[2048]{0:T(1024)S(1)}, f32[2048]{0:T(1024)}, u32[]{:S(2)}) copy-start(f32[2048]{0:T(1024)} %param.19) | copy-start | bytes 24580
  102.3 10.5 %copy-start.2 = (bf16[1,1024,1408]{2,1,0:T(8,128)(2,1)S(1)}, bf16[1,1024,1408]{2,1,0:T(8,128)(2,1)}, u32[]{:S(2)}) copy-start(bf16[1,1024,1408]{2,1,0:T(8,128)(2,1)} %param.22) | copy-start | bytes 8650756
  104.4 54.6 %all-to-all-start.2 = ((bf16[16,32,2048]{2,1,0:T(8,128)(2,1)}), bf16[16,32,2048]{2,1,0:T(8,128)(2,1)}, u32[]{:S(2)}, u32[]{:S(2)}) async-start(bf16[16,32,2048]{2,1,0:T(8,128)(2,1)} %bitcast.19), calls=%async_computation.2 | async-start | bytes 4194304 | tf_op jit(solution)/shard_map/all_to_all | solution.py:164
  111.4 33.2 %collective-permute-start.6 = (bf16[1,704,1024]{2,1,0:T(8,128)(2,1)}, bf16[1,704,1024]{2,1,0:T(8,128)(2,1)}, u32[]{:S(2)}, u32[]{:S(2)}) collective-permute-start(bf16[1,704,1024]{2,1,0:T(8,128)(2,1)} %param.23), channel_id=1, source_target_pairs={{0,16},{16,0},{1,17},{17,1},{2,18},{18,2},{3,19},{19,3},{4,20},{20... | collective-permute-start | bytes 4325384 | tf_op jit(solution)/shard_map/ppermute | solution.py:29
  159.0 6.5 %copy-start.8 = (bf16[1,704,1024]{2,1,0:T(8,128)(2,1)S(1)}, bf16[1,704,1024]{2,1,0:T(8,128)(2,1)}, u32[]{:S(2)}) copy-start(bf16[1,704,1024]{2,1,0:T(8,128)(2,1)} %param.23) | copy-start | bytes 4325380
  170.6 5.0 %copy-start.7 = (f32[64,6]{0,1:T(8,128)S(1)}, f32[64,6]{0,1:T(8,128)}, u32[]{:S(2)}) copy-start(f32[64,6]{0,1:T(8,128)} %param.21) | copy-start | bytes 4612
  170.6 52.4 %all-to-all-start.3 = ((bf16[16,32,2048]{2,1,0:T(8,128)(2,1)}), bf16[16,32,2048]{2,1,0:T(8,128)(2,1)S(1)}, u32[]{:S(2)}, u32[]{:S(2)}) async-start(bf16[16,32,2048]{2,1,0:T(8,128)(2,1)} %bitcast.71), calls=%async_computation.3 | async-start | bytes 4194304 | tf_op jit(solution)/shard_map/all_to_all | solution.py:187

commit v13 on v10

--- a/solution.py
+++ b/solution.py
@@ -87,18 +87,10 @@
     back = lax.all_to_all(blended.reshape(n_mp, sub, HD), "mp", split_axis=0, concat_axis=0, tiled=True)
     attended = back.reshape(groups, heads, sub, HD).transpose(2, 0, 1, 3).reshape(q_count, width)
 
-    if n_dp == 2:
-        w_pair = swap_dp(out_weight)
-        wo_rows = jnp.where(
-            row_index == 0,
-            jnp.concatenate([out_weight, w_pair], axis=0),
-            jnp.concatenate([w_pair, out_weight], axis=0),
-        )
-    else:
-        wo_rows = lax.all_gather(out_weight, "dp", axis=0, tiled=True)
     bits = n_mp.bit_length() - 1
-    if n_mp == 1 << bits:
-        block = wo_rows[None]
+    if n_dp == 2 and n_mp == 1 << bits:
+        w_other = lax.all_gather(swap_dp(out_weight), "mp", axis=1, tiled=True)
+        block = out_weight[None]
         for b in reversed(range(1, bits)):
             pair = lax.ppermute(block, "mp", [(m, m ^ (1 << b)) for m in range(n_mp)])
             low = (column >> b) % 2 == 0
@@ -106,8 +98,11 @@
                 [jnp.where(low, block, pair), jnp.where(low, pair, block)], axis=0
             )
         pair = lax.ppermute(block, "mp", [(m, m ^ 1) for m in range(n_mp)])
-        own_part = jnp.einsum("tk,jkc->tjc", attended, block, preferred_element_type=jnp.float32)
-        pair_part = jnp.einsum("tk,jkc->tjc", attended, pair, preferred_element_type=jnp.float32)
+        half_w = out_weight.shape[0]
+        att_mine = lax.dynamic_slice_in_dim(attended, row_index * half_w, half_w, axis=1)
+        att_other = lax.dynamic_slice_in_dim(attended, (1 - row_index) * half_w, half_w, axis=1)
+        own_part = jnp.einsum("tk,jkc->tjc", att_mine, block, preferred_element_type=jnp.float32)
+        pair_part = jnp.einsum("tk,jkc->tjc", att_mine, pair, preferred_element_type=jnp.float32)
         low = column % 2 == 0
         by_shard = jnp.where(
             low,
@@ -115,13 +110,12 @@
             jnp.concatenate([pair_part, own_part], axis=1),
         )
         order = (0,) + tuple(range(bits, 0, -1)) + (bits + 1,)
-        shard_w = wo_rows.shape[1]
-        projected = (
-            by_shard.reshape((q_count,) + (2,) * bits + (shard_w,))
-            .transpose(order)
-            .reshape(q_count, d_model)
-        )
+        shard_w = out_weight.shape[1]
+        projected = by_shard.reshape((q_count,) + (2,) * bits + (shard_w,)).transpose(order).reshape(
+            q_count, d_model
+        ) + jnp.dot(att_other, w_other, preferred_element_type=jnp.float32)
     else:
+        wo_rows = lax.all_gather(out_weight, "dp", axis=0, tiled=True)
         projected = jnp.dot(
             attended,
             lax.all_gather(wo_rows, "mp", axis=1, tiled=True),

time: 214 us -> 221 us (1.033)
  between operations: 0.38 us -> 13.8 us
  waiting for transfers between devices: 138 us -> 130 us
    ppermute x3, waiting for transfers between devices: 46.4 us -> 35.8 us  [on_device(): pair = lax.ppermute(block, 'mp', [(m, m ^ 1 << b) for m in range(n_mp)])]
    all_gather x0 -> x1, waiting for transfers between devices: none -> 4.91 us  [on_device(): w_other = lax.all_gather(swap_dp(out_weight), 'mp', axis=1, tiled=True)]
    ppermute x3, waiting for transfers between devices: 35 us -> 32 us  [swap_dp(): return lax.ppermute(x, 'dp', [(0, 1), (1, 0)])]
    all_to_all x1, waiting for transfers between devices: 4.99 us -> 7.85 us  [on_device(): lax.all_to_all(blended.reshape(n_mp, sub, HD), 'mp', split_axis=0, concat...]
    all_to_all x1, waiting for transfers between devices: 4.38 us -> 1.67 us  [on_device(): lax.all_to_all(sending.reshape(n_mp, capacity, d_model), 'mp', split_axis...]
    ppermute x3, starting transfers between devices: 3 us -> 5.6 us  [on_device(): pair = lax.ppermute(block, 'mp', [(m, m ^ 1 << b) for m in range(n_mp)])]
    all_to_all x1, starting transfers between devices: 7.23 us -> 4.82 us  [on_device(): lax.all_to_all(blended.reshape(n_mp, sub, HD), 'mp', split_axis=0, concat...]
    select_n x1, other arithmetic: 2.7 us -> 4.96 us  [on_device(): jnp.where(first, jnp.concatenate([experts_out[0], out_other[0]], axis=1),...]
  transfers between devices with their start and end apart: 11 -> 12, of which waited for: 8 -> 8; matrix products, arithmetic and copies ran while one was open for 13% -> 12% of each run, Pallas kernels for 0% -> 0%
where the time goes in v13:
time: 221 us; the launch traced here: 220 us
  waiting for transfers between devices  130 us (59%)
  starting transfers between devices  31.8 us (14%)
  other arithmetic  18.5 us (8%)
  matrix products  18.2 us (8%)
  between operations  13.8 us (6%)
  local copies, waits for them, and re-layouts  8.42 us (4%)
    all_to_all x1, waiting for transfers between devices, on_device(): lax.all_to_all(outcome.reshape(n_mp, capacity, d_model), 'mp', split_axis...  47.2 us
    ppermute x3, waiting for transfers between devices, on_device(): pair = lax.ppermute(block, 'mp', [(m, m ^ 1 << b) for m in range(n_mp)])  35.8 us
    ppermute x3, waiting for transfers between devices, swap_dp(): return lax.ppermute(x, 'dp', [(0, 1), (1, 0)])  32 us
    all_to_all x1, waiting for transfers between devices, on_device(): lax.all_to_all(blended.reshape(n_mp, sub, HD), 'mp', split_axis=0, concat...  7.85 us
    select_n x1, other arithmetic, on_device(): jnp.where(first, jnp.concatenate([experts_in[0], in_other[0]], axis=0), j...  7.6 us
    all_to_all x1, starting transfers between devices, on_device(): lax.all_to_all(jnp.concatenate([q_out, kv_out], axis=1), 'mp', split_axis...  6.55 us
    dot_general x1, matrix products, on_device(): gate_vals = jnp.dot(flat_rows, gate_up, preferred_element_type=jnp.float32)  5.9 us
    ppermute x3, starting transfers between devices, on_device(): pair = lax.ppermute(block, 'mp', [(m, m ^ 1 << b) for m in range(n_mp)])  5.6 us
  transfers between devices with their start and end apart: 12, of which 8 were waited for; matrix products, arithmetic and copies ran while one was open for 12% of the time, Pallas kernels for 0%

profile of v13, /device:TPU:11, one launch (start us, length us, event | category | flops | bytes accessed | tf_op | source)
XLA Modules:
  0.0 220.3 jit_solution(16293648697630678157)
XLA Ops:
  6.5 1.3 reshape.172
  7.8 0.3 copy.66
  8.2 1.0 copy.77
  9.2 0.6 tile.8
  9.8 1.0 pad_maximum_fusion.1
  10.8 6.6 %all-to-all-start = ((bf16[16,224,128]{2,1,0:T(8,128)(2,1)}), bf16[16,224,128]{2,1,0:T(8,128)(2,1)S(1)}, u32[]{:S(2)}, u32[]{:S(2)}) async-start(bf16[16,224,128]{2,1,0:T(8,128)(2,1)} %pad_maximum_fusion.1), calls=%async_computation | async-start | bytes 1835008 | tf_op jit(solution)/shard_map/all_to_all | solution.py:67
  17.4 1.3 collective-permute-start.4
  18.7 2.1 collective-permute-start
  20.8 0.2 collective-permute-start.5
  21.0 0.6 dynamic_slice.13
  22.1 0.7 fusion.30
  22.7 20.1 %collective-permute-done = bf16[1,512,128]{2,1,0:T(8,128)(2,1)S(1)} collective-permute-done((bf16[1,512,128]{2,1,0:T(8,128)(2,1)S(1)}, bf16[1,512,128]{2,1,0:T(8,128)(2,1)S(1)}, u32[]{:S(2)}, u32[]{:S(2)}) %collective-permute-start) | collective-permute-done | bytes 131104 | tf_op jit(solution)/shard_map/ppermute | solution.py:95
  43.0 3.2 %collective-permute-start.1 = (bf16[2,512,128]{2,1,0:T(8,128)(2,1)S(1)}, bf16[2,512,128]{2,1,0:T(8,128)(2,1)S(1)}, u32[]{:S(2)}, u32[]{:S(2)}) collective-permute-start(bf16[2,512,128]{2,1,0:T(8,128)(2,1)S(1)} %pad_maximum_fusion.3), channel_id=1, source_target_pairs={{0,4},{1,5},{2,6},{3,7},{4,0},{5,1},{6,2},{7,3},{8,12},{9,13},{10,... | collective-permute-start | bytes 786440 | tf_op jit(solution)/shard_map/ppermute | solution.py:95
  46.1 0.7 copy-done.6
  46.9 5.1 %collective-permute-done.1 = bf16[2,512,128]{2,1,0:T(8,128)(2,1)S(1)} collective-permute-done((bf16[2,512,128]{2,1,0:T(8,128)(2,1)S(1)}, bf16[2,512,128]{2,1,0:T(8,128)(2,1)S(1)}, u32[]{:S(2)}, u32[]{:S(2)}) %collective-permute-start.1) | collective-permute-done | bytes 262176 | tf_op jit(solution)/shard_map/ppermute | solution.py:95
  52.1 0.3 collective-permute-start.2
  52.7 0.6 add.178
  53.3 0.7 add.169
  54.0 0.8 reduce-window.6
  54.9 0.2 slice_reduce_fusion
  55.4 10.5 %collective-permute-done.2 = bf16[4,512,128]{2,1,0:T(8,128)(2,1)S(1)} collective-permute-done((bf16[4,512,128]{2,1,0:T(8,128)(2,1)S(1)}, bf16[4,512,128]{2,1,0:T(8,128)(2,1)S(1)}, u32[]{:S(2)}, u32[]{:S(2)}) %collective-permute-start.2) | collective-permute-done | bytes 524320 | tf_op jit(solution)/shard_map/ppermute | solution.py:95
  66.1 1.1 pad_maximum_fusion
  67.1 2.0 collective-permute-start.3
  69.2 0.5 copy.67
  70.0 0.7 fusion.34
  70.7 0.6 fusion.1
  71.4 1.4 fusion.8
  72.8 4.8 %all-to-all-start.1 = ((bf16[16,32,128]{2,1,0:T(8,128)(2,1)}), bf16[16,32,128]{2,1,0:T(8,128)(2,1)S(1)}, u32[]{:S(2)}, u32[]{:S(2)}) async-start(bf16[16,32,128]{2,1,0:T(8,128)(2,1)} %bitcast.11), calls=%async_computation.1 | async-start | bytes 262144 | tf_op jit(solution)/shard_map/all_to_all | solution.py:87
  77.6 0.8 fusion.11
  78.4 7.8 %all-to-all-done.1 = bf16[16,32,128]{2,1,0:T(8,128)(2,1)S(1)} async-done(((bf16[16,32,128]{2,1,0:T(8,128)(2,1)}), bf16[16,32,128]{2,1,0:T(8,128)(2,1)S(1)}, u32[]{:S(2)}, u32[]{:S(2)}) %all-to-all-start.1) | async-done | bytes 131104 | tf_op jit(solution)/shard_map/all_to_all | solution.py:87
  86.3 0.3 fusion.14
  86.7 0.3 fusion.12
  87.0 0.4 copy.71
  87.5 0.4 reshape.178
  87.9 4.9 %all-gather.2.cloned.1.call-done = bf16[512,2048]{1,0:T(8,128)(2,1)} async-done(((bf16[512,128]{1,0:T(8,128)(2,1)}), bf16[512,2048]{1,0:T(8,128)(2,1)}) %all-gather.2.cloned.1.call-update) | async-done | bytes 2097168 | tf_op jit(solution)/shard_map/all_gather | solution.py:92
  92.8 2.2 %multiply_reduce_fusion = (f32[64]{0:T(128)S(1)}, f32[64,2048]{1,0:T(8,128)S(1)}) fusion(f32[64,2048]{1,0:T(8,128)S(1)} %reshape.178, bf16[512,2048]{1,0:T(8,128)(2,1)} %all-gather.2.cloned.1.call-done, bf16[64,1024]{1,0:T(8,128)(2,1)S(1)} %bitcast.84, s32[]{:T(128)S(6)} %select_n.162, bf16[64,2048]{1,0:T(8,128)(2,1)S(1)} %copy-done.3), kind=kOutput, calls=%fused_computation.28 | convolution fusion | flops 135135168 | bytes 3473668 | tf_op jit(solution)/shard_map/dot_general | solution.py:116
  95.2 2.2 convolution_convert_fusion.1
  97.4 4.8 %all-to-all-start.2 = ((bf16[16,32,2048]{2,1,0:T(8,128)(2,1)}), bf16[16,32,2048]{2,1,0:T(8,128)(2,1)S(1)}, u32[]{:S(2)}, u32[]{:S(2)}) async-start(bf16[16,32,2048]{2,1,0:T(8,128)(2,1)} %bitcast.19), calls=%async_computation.2 | async-start | bytes 4194304 | tf_op jit(solution)/shard_map/all_to_all | solution.py:143
  102.2 1.2 collective-permute-start.6
  103.4 32.0 %collective-permute-done.6 = bf16[1,704,1024]{2,1,0:T(8,128)(2,1)} collective-permute-done((bf16[1,704,1024]{2,1,0:T(8,128)(2,1)}, bf16[1,704,1024]{2,1,0:T(8,128)(2,1)}, u32[]{:S(2)}, u32[]{:S(2)}) %collective-permute-start.6) | collective-permute-done | bytes 1441824 | tf_op jit(solution)/shard_map/ppermute | solution.py:29
  135.4 5.0 %maximum_select_fusion.1 = bf16[704,2048]{1,0:T(8,128)(2,1)} fusion(bf16[704,1024]{1,0:T(8,128)(2,1)} %bitcast.22, bf16[704,1024]{1,0:T(8,128)(2,1)} %bitcast.80, pred[]{:T(512)S(6)} %eq.96), kind=kLoop, calls=%fused_computation.7 | loop fusion | flops 12976128 | bytes 5767169 | tf_op jit(solution)/shard_map/jit(_where)/select_n | solution.py:154
  140.4 7.6 %maximum_select_fusion = bf16[2048,1408]{1,0:T(8,128)(2,1)} fusion(bf16[1024,1408]{1,0:T(8,128)(2,1)} %bitcast.24, bf16[1024,1408]{1,0:T(8,128)(2,1)S(1)} %bitcast.75, pred[]{:T(512)S(6)} %eq.96), kind=kLoop, calls=%fused_computation | loop fusion | flops 25952256 | bytes 11534337 | tf_op jit(solution)/shard_map/jit(_where)/select_n | solution.py:149
  148.0 1.7 all-to-all-done.2
  149.6 5.9 %fusion.35 = f32[512,1408]{1,0:T(8,128)S(1)} fusion(bf16[512,2048]{1,0:T(8,128)(2,1)S(1)} %bitcast.76, bf16[2048,1408]{1,0:T(8,128)(2,1)} %maximum_select_fusion), kind=kOutput, calls=%fused_computation.82 | convolution fusion | flops 2952790016 | bytes 10747904 | tf_op jit(solution)/shard_map/dot_general | solution.py:163
  155.6 3.2 %convolution_convert_fusion = bf16[512,2048]{1,0:T(8,128)(2,1)} fusion(bf16[704,2048]{1,0:T(8,128)(2,1)S(1)} %copy-done.1, f32[512,1408]{1,0:T(8,128)S(1)} %fusion.35), kind=kOutput, calls=%fused_computation.5 | convolution fusion | flops 1479606272 | bytes 8126464 | tf_op jit(solution)/shard_map/dot_general | solution.py:165
  158.8 5.3 %all-to-all-start.3 = ((bf16[16,32,2048]{2,1,0:T(8,128)(2,1)}), bf16[16,32,2048]{2,1,0:T(8,128)(2,1)S(1)}, u32[]{:S(2)}, u32[]{:S(2)}) async-start(bf16[16,32,2048]{2,1,0:T(8,128)(2,1)} %bitcast.77), calls=%async_computation.3 | async-start | bytes 4194304 | tf_op jit(solution)/shard_map/all_to_all | solution.py:166
  164.3 47.2 %all-to-all-done.3 = bf16[16,32,2048]{2,1,0:T(8,128)(2,1)S(1)} async-done(((bf16[16,32,2048]{2,1,0:T(8,128)(2,1)}), bf16[16,32,2048]{2,1,0:T(8,128)(2,1)S(1)}, u32[]{:S(2)}, u32[]{:S(2)}) %all-to-all-start.3) | async-done | bytes 2097184 | tf_op jit(solution)/shard_map/all_to_all | solution.py:166
  211.5 1.9 fusion.5
  (67 shorter events, 2.3 us)
Async XLA Ops:
  6.5 15.1 %copy-start = (s32[2,96]{1,0:T(2,128)S(1)}, s32[2,96]{1,0:T(2,128)}, u32[]{:S(2)}) copy-start(s32[2,96]{1,0:T(2,128)} %param.15) | copy-start | bytes 2308
  8.1 9.3 %copy-start.5 = (bf16[512,128]{1,0:T(8,128)(2,1)S(1)}, bf16[512,128]{1,0:T(8,128)(2,1)}, u32[]{:S(2)}) copy-start(bf16[512,128]{1,0:T(8,128)(2,1)} %param.18) | copy-start | bytes 393220
  8.1 12.9 %copy-start.12 = (s32[2]{0:T(128)S(1)}, s32[2]{0:T(128)}, u32[]{:S(2)}) copy-start(s32[2]{0:T(128)} %param.16) | copy-start | bytes 28
  8.1 13.7 %copy-start.7 = (s32[64,6]{0,1:T(8,128)S(1)}, s32[64,6]{0,1:T(8,128)}, u32[]{:S(2)}) copy-start(s32[64,6]{0,1:T(8,128)} %param.20) | copy-start | bytes 4612
  8.1 13.9 %copy-start.13 = (s32[1,16]{1,0:T(1,128)S(1)}, s32[1,16]{1,0:T(1,128)}, u32[]{:S(2)}) copy-start(s32[1,16]{1,0:T(1,128)} %param.17) | copy-start | bytes 196
  10.8 58.3 %all-to-all-start = ((bf16[16,224,128]{2,1,0:T(8,128)(2,1)}), bf16[16,224,128]{2,1,0:T(8,128)(2,1)S(1)}, u32[]{:S(2)}, u32[]{:S(2)}) async-start(bf16[16,224,128]{2,1,0:T(8,128)(2,1)} %pad_maximum_fusion.1), calls=%async_computation | async-start | bytes 1835008 | tf_op jit(solution)/shard_map/all_to_all | solution.py:67
  17.3 75.5 %all-gather.2.cloned.1.call-start = ((), (), s32[]{:S(2)}) async-start(), calls=%async_computation.4 | async-start | bytes 2228224 | tf_op jit(solution)/shard_map/all_gather | solution.py:92
  17.4 28.7 %collective-permute-start.4 = (bf16[512,128]{1,0:T(8,128)(2,1)S(1)}, bf16[512,128]{1,0:T(8,128)(2,1)S(1)}, u32[]{:S(2)}, u32[]{:S(2)}) collective-permute-start(bf16[512,128]{1,0:T(8,128)(2,1)S(1)} %copy-done.5), channel_id=1, source_target_pairs={{0,16},{16,0},{1,17},{17,1},{2,18},{18,2},{3,19},{19,3},{4,20},{20... | collective-permute-start | bytes 393224 | tf_op jit(solution)/shard_map/ppermute | solution.py:29
  18.7 24.2 %collective-permute-start = (bf16[1,512,128]{2,1,0:T(8,128)(2,1)S(1)}, bf16[1,512,128]{2,1,0:T(8,128)(2,1)S(1)}, u32[]{:S(2)}, u32[]{:S(2)}) collective-permute-start(bf16[1,512,128]{2,1,0:T(8,128)(2,1)S(1)} %bitcast.90), channel_id=1, source_target_pairs={{0,8},{1,9},{2,10},{3,11},{4,12},{5,13},{6,14},{7,15},{8,0},{9,1},... | collective-permute-start | bytes 393224 | tf_op jit(solution)/shard_map/ppermute | solution.py:95
  20.8 74.4 %collective-permute-start.5 = (bf16[1,1024,1408]{2,1,0:T(8,128)(2,1)}, bf16[1,1024,1408]{2,1,0:T(8,128)(2,1)}, u32[]{:S(2)}, u32[]{:S(2)}) collective-permute-start(bf16[1,1024,1408]{2,1,0:T(8,128)(2,1)} %param.22), channel_id=1, source_target_pairs={{0,16},{16,0},{1,17},{17,1},{2,18},{18,2},{3,19},{19,3},{4,20},{20... | collective-permute-start | bytes 8650760 | tf_op jit(solution)/shard_map/ppermute | solution.py:29
  43.0 9.1 %collective-permute-start.1 = (bf16[2,512,128]{2,1,0:T(8,128)(2,1)S(1)}, bf16[2,512,128]{2,1,0:T(8,128)(2,1)S(1)}, u32[]{:S(2)}, u32[]{:S(2)}) collective-permute-start(bf16[2,512,128]{2,1,0:T(8,128)(2,1)S(1)} %pad_maximum_fusion.3), channel_id=1, source_target_pairs={{0,4},{1,5},{2,6},{3,7},{4,0},{5,1},{6,2},{7,3},{8,12},{9,13},{10,... | collective-permute-start | bytes 786440 | tf_op jit(solution)/shard_map/ppermute | solution.py:95
  46.1 0.7 copy-start.6
  52.1 13.8 %collective-permute-start.2 = (bf16[4,512,128]{2,1,0:T(8,128)(2,1)S(1)}, bf16[4,512,128]{2,1,0:T(8,128)(2,1)S(1)}, u32[]{:S(2)}, u32[]{:S(2)}) collective-permute-start(bf16[4,512,128]{2,1,0:T(8,128)(2,1)S(1)} %pad_maximum_fusion.2), channel_id=1, source_target_pairs={{0,2},{1,3},{2,0},{3,1},{4,6},{5,7},{6,4},{7,5},{8,10},{9,11},{10,... | collective-permute-start | bytes 1572872 | tf_op jit(solution)/shard_map/ppermute | solution.py:95
  67.1 2.9 %copy-start.9 = (s32[1536]{0:T(1024)S(1)}, s32[1536]{0:T(1024)}, u32[]{:S(2)}) copy-start(s32[1536]{0:T(1024)} %add.169) | copy-start | bytes 18436
  67.1 2.9 %copy-start.11 = (s32[512]{0:T(512)S(1)}, s32[512]{0:T(512)}, u32[]{:S(2)}) copy-start(s32[512]{0:T(512)} %add.178) | copy-start | bytes 6148
  67.1 19.5 %collective-permute-start.3 = (bf16[8,512,128]{2,1,0:T(8,128)(2,1)}, bf16[8,512,128]{2,1,0:T(8,128)(2,1)S(1)}, u32[]{:S(2)}, u32[]{:S(2)}) collective-permute-start(bf16[8,512,128]{2,1,0:T(8,128)(2,1)} %pad_maximum_fusion), channel_id=1, source_target_pairs={{0,1},{1,0},{2,3},{3,2},{4,5},{5,4},{6,7},{7,6},{8,9},{9,8},{10,11... | collective-permute-start | bytes 3145736 | tf_op jit(solution)/shard_map/ppermute | solution.py:100
  72.8 13.5 %all-to-all-start.1 = ((bf16[16,32,128]{2,1,0:T(8,128)(2,1)}), bf16[16,32,128]{2,1,0:T(8,128)(2,1)S(1)}, u32[]{:S(2)}, u32[]{:S(2)}) async-start(bf16[16,32,128]{2,1,0:T(8,128)(2,1)} %bitcast.11), calls=%async_computation.1 | async-start | bytes 262144 | tf_op jit(solution)/shard_map/all_to_all | solution.py:87
  86.6 6.2 %copy-start.3 = (bf16[64,2048]{1,0:T(8,128)(2,1)S(1)}, bf16[64,2048]{1,0:T(8,128)(2,1)}, u32[]{:S(2)}) copy-start(bf16[64,2048]{1,0:T(8,128)(2,1)} %param.13) | copy-start | bytes 786436
  87.0 8.0 %copy-start.8 = (f32[2048]{0:T(1024)S(1)}, f32[2048]{0:T(1024)}, u32[]{:S(2)}) copy-start(f32[2048]{0:T(1024)} %param.19) | copy-start | bytes 24580
  87.5 7.7 %copy-start.4 = (pred[64,512]{1,0:T(8,128)(4,1)S(1)}, pred[64,512]{1,0:T(8,128)(4,1)}, u32[]{:S(2)}) copy-start(pred[64,512]{1,0:T(8,128)(4,1)} %fusion.11) | copy-start | bytes 98308
  97.4 52.3 %all-to-all-start.2 = ((bf16[16,32,2048]{2,1,0:T(8,128)(2,1)}), bf16[16,32,2048]{2,1,0:T(8,128)(2,1)S(1)}, u32[]{:S(2)}, u32[]{:S(2)}) async-start(bf16[16,32,2048]{2,1,0:T(8,128)(2,1)} %bitcast.19), calls=%async_computation.2 | async-start | bytes 4194304 | tf_op jit(solution)/shard_map/all_to_all | solution.py:143
  102.2 33.2 %collective-permute-start.6 = (bf16[1,704,1024]{2,1,0:T(8,128)(2,1)}, bf16[1,704,1024]{2,1,0:T(8,128)(2,1)}, u32[]{:S(2)}, u32[]{:S(2)}) collective-permute-start(bf16[1,704,1024]{2,1,0:T(8,128)(2,1)} %param.23), channel_id=1, source_target_pairs={{0,16},{16,0},{1,17},{17,1},{2,18},{18,2},{3,19},{19,3},{4,20},{20... | collective-permute-start | bytes 4325384 | tf_op jit(solution)/shard_map/ppermute | solution.py:29
  135.4 5.0 %copy-start.2 = (bf16[1,1024,1408]{2,1,0:T(8,128)(2,1)S(1)}, bf16[1,1024,1408]{2,1,0:T(8,128)(2,1)}, u32[]{:S(2)}) copy-start(bf16[1,1024,1408]{2,1,0:T(8,128)(2,1)} %param.22) | copy-start | bytes 8650756
  149.6 5.9 %copy-start.1 = (bf16[704,2048]{1,0:T(8,128)(2,1)S(1)}, bf16[704,2048]{1,0:T(8,128)(2,1)}, u32[]{:S(2)}) copy-start(bf16[704,2048]{1,0:T(8,128)(2,1)} %maximum_select_fusion.1) | copy-start | bytes 8650756
  158.8 5.3 %copy-start.10 = (f32[64,6]{0,1:T(8,128)S(1)}, f32[64,6]{0,1:T(8,128)}, u32[]{:S(2)}) copy-start(f32[64,6]{0,1:T(8,128)} %param.21) | copy-start | bytes 4612
  158.8 52.7 %all-to-all-start.3 = ((bf16[16,32,2048]{2,1,0:T(8,128)(2,1)}), bf16[16,32,2048]{2,1,0:T(8,128)(2,1)S(1)}, u32[]{:S(2)}, u32[]{:S(2)}) async-start(bf16[16,32,2048]{2,1,0:T(8,128)(2,1)} %bitcast.77), calls=%async_computation.3 | async-start | bytes 4194304 | tf_op jit(solution)/shard_map/all_to_all | solution.py:166
Sparse Core Ops, SparseCore 0:
  46.9 45.8 all-gather.1

commit v14 on v10

--- a/solution.py
+++ b/solution.py
@@ -140,9 +140,9 @@
     combine = jnp.sum(jnp.where(hits, expert_gates[:, :, None], 0.0), axis=1)
     ff_width = experts_out.shape[1]
     if n_dp == 2:
+        out_other = swap_dp(experts_out)
         in_other = swap_dp(experts_in)
-        out_other = swap_dp(experts_out)
-        normed, in_other = lax.optimization_barrier((normed, in_other))
+        normed, out_other = lax.optimization_barrier((normed, out_other))
     sending = lax.dot_general(
         dispatch, normed, (((0,), (0,)), ((), ())), preferred_element_type=jnp.float32
     ).astype(jnp.bfloat16)

time: 214 us -> 214 us (level)
    all_to_all x1, waiting for transfers between devices: 4.38 us -> 26.2 us  [on_device(): lax.all_to_all(sending.reshape(n_mp, capacity, d_model), 'mp', split_axis...]
    ppermute x3, waiting for transfers between devices: 35 us -> 13.7 us  [swap_dp(): return lax.ppermute(x, 'dp', [(0, 1), (1, 0)])]
  transfers between devices with their start and end apart: 11 -> 11, of which waited for: 8 -> 7; matrix products, arithmetic and copies ran while one was open for 13% -> 14% of each run, Pallas kernels for 0% -> 0%
where the time goes in v14:
time: 214 us
  waiting for transfers between devices  138 us (64%)
  starting transfers between devices  32.4 us (15%)
  matrix products  18.3 us (9%)
  other arithmetic  17.9 us (8%)
  local copies, waits for them, and re-layouts  6.64 us (3%)
    all_to_all x1, waiting for transfers between devices, on_device(): lax.all_to_all(outcome.reshape(n_mp, capacity, d_model), 'mp', split_axis...  47.2 us
    ppermute x3, waiting for transfers between devices, on_device(): pair = lax.ppermute(block, 'mp', [(m, m ^ 1 << b) for m in range(n_mp)])  46.1 us
    all_to_all x1, waiting for transfers between devices, on_device(): lax.all_to_all(sending.reshape(n_mp, capacity, d_model), 'mp', split_axis...  26.2 us
    ppermute x3, waiting for transfers between devices, swap_dp(): return lax.ppermute(x, 'dp', [(0, 1), (1, 0)])  13.7 us
    select_n x1, other arithmetic, on_device(): jnp.where(first, jnp.concatenate([experts_in[0], in_other[0]], axis=0), j...  7.46 us
    all_to_all x1, starting transfers between devices, on_device(): lax.all_to_all(blended.reshape(n_mp, sub, HD), 'mp', split_axis=0, concat...  7.25 us
    all_to_all x1, starting transfers between devices, on_device(): lax.all_to_all(sending.reshape(n_mp, capacity, d_model), 'mp', split_axis...  7.06 us
    dot_general x1, matrix products, on_device(): gate_vals = jnp.dot(flat_rows, gate_up, preferred_element_type=jnp.float32)  6.38 us
  transfers between devices with their start and end apart: 11, of which 7 were waited for; matrix products, arithmetic and copies ran while one was open for 14% of the time, Pallas kernels for 0%

profile of v14, /device:TPU:11, one launch (start us, length us, event | category | flops | bytes accessed | tf_op | source)
XLA Modules:
  0.0 213.9 jit_solution(10027619122510501409)
XLA Ops:
  0.0 1.2 collective-permute-start
  1.2 3.3 %collective-permute-done = bf16[512,128]{1,0:T(8,128)(2,1)S(1)} collective-permute-done((bf16[512,128]{1,0:T(8,128)(2,1)}, bf16[512,128]{1,0:T(8,128)(2,1)S(1)}, u32[]{:S(2)}, u32[]{:S(2)}) %collective-permute-start) | collective-permute-done | bytes 131104 | tf_op jit(solution)/shard_map/ppermute | solution.py:29
  4.6 1.1 maximum_select_fusion.3
  5.6 2.4 %collective-permute-start.1 = (bf16[1,1024,128]{2,1,0:T(8,128)(2,1)S(1)}, bf16[1,1024,128]{2,1,0:T(8,128)(2,1)S(1)}, u32[]{:S(2)}, u32[]{:S(2)}) collective-permute-start(bf16[1,1024,128]{2,1,0:T(8,128)(2,1)S(1)} %maximum_select_fusion.3), channel_id=1, source_target_pairs={{0,8},{1,9},{2,10},{3,11},{4,12},{5,13},{6,14},{7,15},{8,0},{9,1},... | collective-permute-start | bytes 786440 | tf_op jit(solution)/shard_map/ppermute | solution.py:103
  8.0 1.2 reshape.227
  9.3 0.3 copy.66
  9.6 0.9 copy.77
  10.6 0.6 tile.8
  11.2 1.0 pad_maximum_fusion.2
  12.2 5.7 %all-to-all-start = ((bf16[16,224,128]{2,1,0:T(8,128)(2,1)}), bf16[16,224,128]{2,1,0:T(8,128)(2,1)S(1)}, u32[]{:S(2)}, u32[]{:S(2)}) async-start(bf16[16,224,128]{2,1,0:T(8,128)(2,1)} %pad_maximum_fusion.2), calls=%async_computation | async-start | bytes 1835008 | tf_op jit(solution)/shard_map/all_to_all | solution.py:67
  17.8 1.2 collective-permute-start.5
  19.1 0.2 collective-permute-start.6
  19.7 0.3 collective-permute-start.2
  20.0 0.9 reduce-window.6
  20.9 0.2 slice_reduce_fusion
  21.1 0.2 select_reduce_fusion.1
  21.3 23.9 %collective-permute-done.2 = bf16[2,1024,128]{2,1,0:T(8,128)(2,1)S(1)} collective-permute-done((bf16[2,1024,128]{2,1,0:T(8,128)(2,1)S(1)}, bf16[2,1024,128]{2,1,0:T(8,128)(2,1)S(1)}, u32[]{:S(2)}, u32[]{:S(2)}) %collective-permute-start.2) | collective-permute-done | bytes 524320 | tf_op jit(solution)/shard_map/ppermute | solution.py:103
  45.3 1.2 pad_maximum_fusion.1
  46.5 0.4 collective-permute-start.3
  47.0 0.6 dynamic_slice.7
  47.8 0.7 fusion.19
  48.6 22.2 %collective-permute-done.3 = bf16[4,1024,128]{2,1,0:T(8,128)(2,1)S(1)} collective-permute-done((bf16[4,1024,128]{2,1,0:T(8,128)(2,1)}, bf16[4,1024,128]{2,1,0:T(8,128)(2,1)S(1)}, u32[]{:S(2)}, u32[]{:S(2)}) %collective-permute-start.3) | collective-permute-done | bytes 1048608 | tf_op jit(solution)/shard_map/ppermute | solution.py:103
  70.9 0.2 pad_maximum_fusion
  71.1 1.6 collective-permute-start.4
  73.2 0.5 copy.67
  73.7 0.2 fusion.22
  74.1 0.7 fusion.23
  74.8 0.6 fusion.1
  75.4 1.4 fusion.5
  76.8 7.2 %all-to-all-start.1 = ((bf16[16,32,128]{2,1,0:T(8,128)(2,1)}), bf16[16,32,128]{2,1,0:T(8,128)(2,1)S(1)}, u32[]{:S(2)}, u32[]{:S(2)}) async-start(bf16[16,32,128]{2,1,0:T(8,128)(2,1)} %bitcast.11), calls=%async_computation.1 | async-start | bytes 262144 | tf_op jit(solution)/shard_map/all_to_all | solution.py:87
  84.2 5.0 %all-to-all-done.1 = bf16[16,32,128]{2,1,0:T(8,128)(2,1)S(1)} async-done(((bf16[16,32,128]{2,1,0:T(8,128)(2,1)}), bf16[16,32,128]{2,1,0:T(8,128)(2,1)S(1)}, u32[]{:S(2)}, u32[]{:S(2)}) %all-to-all-start.1) | async-done | bytes 131104 | tf_op jit(solution)/shard_map/all_to_all | solution.py:87
  89.3 0.5 fusion.24
  89.8 2.1 fusion.25
  92.0 0.4 copy.71
  92.4 0.4 reshape.233
  92.9 0.2 fusion.9
  93.2 2.1 convolution_convert_fusion.1
  95.3 7.1 %all-to-all-start.2 = ((bf16[16,32,2048]{2,1,0:T(8,128)(2,1)}), bf16[16,32,2048]{2,1,0:T(8,128)(2,1)}, u32[]{:S(2)}, u32[]{:S(2)}) async-start(bf16[16,32,2048]{2,1,0:T(8,128)(2,1)} %bitcast.19), calls=%async_computation.2 | async-start | bytes 4194304 | tf_op jit(solution)/shard_map/all_to_all | solution.py:149
  102.4 10.4 %collective-permute-done.6 = bf16[1,1024,1408]{2,1,0:T(8,128)(2,1)} collective-permute-done((bf16[1,1024,1408]{2,1,0:T(8,128)(2,1)}, bf16[1,1024,1408]{2,1,0:T(8,128)(2,1)}, u32[]{:S(2)}, u32[]{:S(2)}) %collective-permute-start.6) | collective-permute-done | bytes 2883616 | tf_op jit(solution)/shard_map/ppermute | solution.py:29
  112.8 7.5 %maximum_select_fusion = bf16[2048,1408]{1,0:T(8,128)(2,1)} fusion(bf16[1024,1408]{1,0:T(8,128)(2,1)} %bitcast.24, bf16[1024,1408]{1,0:T(8,128)(2,1)S(1)} %bitcast.70, pred[]{:T(512)S(6)} %eq.86), kind=kLoop, calls=%fused_computation | loop fusion | flops 25952256 | bytes 11534337 | tf_op jit(solution)/shard_map/jit(_where)/select_n | solution.py:155
  120.2 3.5 %maximum_select_fusion.1 = bf16[704,2048]{1,0:T(8,128)(2,1)S(1)} fusion(bf16[704,1024]{1,0:T(8,128)(2,1)} %bitcast.22, bf16[704,1024]{1,0:T(8,128)(2,1)} %bitcast.21, pred[]{:T(512)S(6)} %eq.86), kind=kLoop, calls=%fused_computation.7 | loop fusion | flops 12976128 | bytes 5767169 | tf_op jit(solution)/shard_map/jit(_where)/select_n | solution.py:160
  123.7 26.2 %all-to-all-done.2 = bf16[16,32,2048]{2,1,0:T(8,128)(2,1)} async-done(((bf16[16,32,2048]{2,1,0:T(8,128)(2,1)}), bf16[16,32,2048]{2,1,0:T(8,128)(2,1)}, u32[]{:S(2)}, u32[]{:S(2)}) %all-to-all-start.2) | async-done | bytes 2097184 | tf_op jit(solution)/shard_map/all_to_all | solution.py:149
  149.9 6.4 %fusion.26 = f32[512,1408]{1,0:T(8,128)S(1)} fusion(bf16[512,2048]{1,0:T(8,128)(2,1)} %bitcast.20, bf16[2048,1408]{1,0:T(8,128)(2,1)} %maximum_select_fusion), kind=kOutput, calls=%fused_computation.74 | convolution fusion | flops 2952790016 | bytes 10747904 | tf_op jit(solution)/shard_map/dot_general | solution.py:169
  156.3 3.3 %convolution_convert_fusion = bf16[512,2048]{1,0:T(8,128)(2,1)} fusion(bf16[704,2048]{1,0:T(8,128)(2,1)S(1)} %maximum_select_fusion.1, f32[512,1408]{1,0:T(8,128)S(1)} %fusion.26), kind=kOutput, calls=%fused_computation.5 | convolution fusion | flops 1479606272 | bytes 8126464 | tf_op jit(solution)/shard_map/dot_general | solution.py:171
  159.6 5.0 %all-to-all-start.3 = ((bf16[16,32,2048]{2,1,0:T(8,128)(2,1)}), bf16[16,32,2048]{2,1,0:T(8,128)(2,1)S(1)}, u32[]{:S(2)}, u32[]{:S(2)}) async-start(bf16[16,32,2048]{2,1,0:T(8,128)(2,1)} %bitcast.71), calls=%async_computation.3 | async-start | bytes 4194304 | tf_op jit(solution)/shard_map/all_to_all | solution.py:172
  164.6 0.2 select_reduce_fusion
  164.8 47.2 %all-to-all-done.3 = bf16[16,32,2048]{2,1,0:T(8,128)(2,1)S(1)} async-done(((bf16[16,32,2048]{2,1,0:T(8,128)(2,1)}), bf16[16,32,2048]{2,1,0:T(8,128)(2,1)S(1)}, u32[]{:S(2)}, u32[]{:S(2)}) %all-to-all-start.3) | async-done | bytes 2097184 | tf_op jit(solution)/shard_map/all_to_all | solution.py:172
  212.0 1.9 fusion.2
  (53 shorter events, 2.2 us)
Async XLA Ops:
  0.0 20.9 %copy-start = (s32[2,96]{1,0:T(2,128)S(1)}, s32[2,96]{1,0:T(2,128)}, u32[]{:S(2)}) copy-start(s32[2,96]{1,0:T(2,128)} %param.15) | copy-start | bytes 2308
  0.0 4.6 %collective-permute-start = (bf16[512,128]{1,0:T(8,128)(2,1)}, bf16[512,128]{1,0:T(8,128)(2,1)S(1)}, u32[]{:S(2)}, u32[]{:S(2)}) collective-permute-start(bf16[512,128]{1,0:T(8,128)(2,1)} %param.18), channel_id=1, source_target_pairs={{0,16},{16,0},{1,17},{17,1},{2,18},{18,2},{3,19},{19,3},{4,20},{20... | collective-permute-start | bytes 393224 | tf_op jit(solution)/shard_map/ppermute | solution.py:29
  5.6 13.9 %collective-permute-start.1 = (bf16[1,1024,128]{2,1,0:T(8,128)(2,1)S(1)}, bf16[1,1024,128]{2,1,0:T(8,128)(2,1)S(1)}, u32[]{:S(2)}, u32[]{:S(2)}) collective-permute-start(bf16[1,1024,128]{2,1,0:T(8,128)(2,1)S(1)} %maximum_select_fusion.3), channel_id=1, source_target_pairs={{0,8},{1,9},{2,10},{3,11},{4,12},{5,13},{6,14},{7,15},{8,0},{9,1},... | collective-permute-start | bytes 786440 | tf_op jit(solution)/shard_map/ppermute | solution.py:103
  9.6 9.7 %copy-start.3 = (s32[64,6]{0,1:T(8,128)S(1)}, s32[64,6]{0,1:T(8,128)}, u32[]{:S(2)}) copy-start(s32[64,6]{0,1:T(8,128)} %param.20) | copy-start | bytes 4612
  12.2 60.9 %all-to-all-start = ((bf16[16,224,128]{2,1,0:T(8,128)(2,1)}), bf16[16,224,128]{2,1,0:T(8,128)(2,1)S(1)}, u32[]{:S(2)}, u32[]{:S(2)}) async-start(bf16[16,224,128]{2,1,0:T(8,128)(2,1)} %pad_maximum_fusion.2), calls=%async_computation | async-start | bytes 1835008 | tf_op jit(solution)/shard_map/all_to_all | solution.py:67
  17.8 75.4 %collective-permute-start.5 = (bf16[1,704,1024]{2,1,0:T(8,128)(2,1)}, bf16[1,704,1024]{2,1,0:T(8,128)(2,1)}, u32[]{:S(2)}, u32[]{:S(2)}) collective-permute-start(bf16[1,704,1024]{2,1,0:T(8,128)(2,1)} %param.23), channel_id=1, source_target_pairs={{0,16},{16,0},{1,17},{17,1},{2,18},{18,2},{3,19},{19,3},{4,20},{20... | collective-permute-start | bytes 4325384 | tf_op jit(solution)/shard_map/ppermute | solution.py:29
  19.1 93.7 %collective-permute-start.6 = (bf16[1,1024,1408]{2,1,0:T(8,128)(2,1)}, bf16[1,1024,1408]{2,1,0:T(8,128)(2,1)}, u32[]{:S(2)}, u32[]{:S(2)}) collective-permute-start(bf16[1,1024,1408]{2,1,0:T(8,128)(2,1)} %param.22), channel_id=1, source_target_pairs={{0,16},{16,0},{1,17},{17,1},{2,18},{18,2},{3,19},{19,3},{4,20},{20... | collective-permute-start | bytes 8650760 | tf_op jit(solution)/shard_map/ppermute | solution.py:29
  19.6 27.4 %copy-start.6 = (s32[2]{0:T(128)S(1)}, s32[2]{0:T(128)}, u32[]{:S(2)}) copy-start(s32[2]{0:T(128)} %param.16) | copy-start | bytes 28
  19.6 28.1 %copy-start.7 = (s32[1,16]{1,0:T(1,128)S(1)}, s32[1,16]{1,0:T(1,128)}, u32[]{:S(2)}) copy-start(s32[1,16]{1,0:T(1,128)} %param.17) | copy-start | bytes 196
  19.7 25.6 %collective-permute-start.2 = (bf16[2,1024,128]{2,1,0:T(8,128)(2,1)S(1)}, bf16[2,1024,128]{2,1,0:T(8,128)(2,1)S(1)}, u32[]{:S(2)}, u32[]{:S(2)}) collective-permute-start(bf16[2,1024,128]{2,1,0:T(8,128)(2,1)S(1)} %pad_maximum_fusion.3), channel_id=1, source_target_pairs={{0,4},{1,5},{2,6},{3,7},{4,0},{5,1},{6,2},{7,3},{8,12},{9,13},{10,... | collective-permute-start | bytes 1572872 | tf_op jit(solution)/shard_map/ppermute | solution.py:103
  46.5 24.2 %collective-permute-start.3 = (bf16[4,1024,128]{2,1,0:T(8,128)(2,1)}, bf16[4,1024,128]{2,1,0:T(8,128)(2,1)S(1)}, u32[]{:S(2)}, u32[]{:S(2)}) collective-permute-start(bf16[4,1024,128]{2,1,0:T(8,128)(2,1)} %pad_maximum_fusion.1), channel_id=1, source_target_pairs={{0,2},{1,3},{2,0},{3,1},{4,6},{5,7},{6,4},{7,5},{8,10},{9,11},{10,... | collective-permute-start | bytes 3145736 | tf_op jit(solution)/shard_map/ppermute | solution.py:103
  71.1 18.8 %collective-permute-start.4 = (bf16[8,1024,128]{2,1,0:T(8,128)(2,1)S(1)}, bf16[8,1024,128]{2,1,0:T(8,128)(2,1)}, u32[]{:S(2)}, u32[]{:S(2)}) collective-permute-start(bf16[8,1024,128]{2,1,0:T(8,128)(2,1)S(1)} %pad_maximum_fusion), channel_id=1, source_target_pairs={{0,1},{1,0},{2,3},{3,2},{4,5},{5,4},{6,7},{7,6},{8,9},{9,8},{10,11... | collective-permute-start | bytes 6291464 | tf_op jit(solution)/shard_map/ppermute | solution.py:108
  76.8 12.4 %all-to-all-start.1 = ((bf16[16,32,128]{2,1,0:T(8,128)(2,1)}), bf16[16,32,128]{2,1,0:T(8,128)(2,1)S(1)}, u32[]{:S(2)}, u32[]{:S(2)}) async-start(bf16[16,32,128]{2,1,0:T(8,128)(2,1)} %bitcast.11), calls=%async_computation.1 | async-start | bytes 262144 | tf_op jit(solution)/shard_map/all_to_all | solution.py:87
  89.8 3.0 %copy-start.2 = (bf16[64,2048]{1,0:T(8,128)(2,1)S(1)}, bf16[64,2048]{1,0:T(8,128)(2,1)}, u32[]{:S(2)}) copy-start(bf16[64,2048]{1,0:T(8,128)(2,1)} %param.13) | copy-start | bytes 786436
  89.8 3.2 %copy-start.4 = (f32[2048]{0:T(1024)S(1)}, f32[2048]{0:T(1024)}, u32[]{:S(2)}) copy-start(f32[2048]{0:T(1024)} %param.19) | copy-start | bytes 24580
  93.2 19.6 %copy-start.1 = (bf16[1,1024,1408]{2,1,0:T(8,128)(2,1)S(1)}, bf16[1,1024,1408]{2,1,0:T(8,128)(2,1)}, u32[]{:S(2)}) copy-start(bf16[1,1024,1408]{2,1,0:T(8,128)(2,1)} %param.22) | copy-start | bytes 8650756
  95.3 54.6 %all-to-all-start.2 = ((bf16[16,32,2048]{2,1,0:T(8,128)(2,1)}), bf16[16,32,2048]{2,1,0:T(8,128)(2,1)}, u32[]{:S(2)}, u32[]{:S(2)}) async-start(bf16[16,32,2048]{2,1,0:T(8,128)(2,1)} %bitcast.19), calls=%async_computation.2 | async-start | bytes 4194304 | tf_op jit(solution)/shard_map/all_to_all | solution.py:149
  159.6 5.0 %copy-start.5 = (f32[64,6]{0,1:T(8,128)S(1)}, f32[64,6]{0,1:T(8,128)}, u32[]{:S(2)}) copy-start(f32[64,6]{0,1:T(8,128)} %param.21) | copy-start | bytes 4612
  159.6 52.4 %all-to-all-start.3 = ((bf16[16,32,2048]{2,1,0:T(8,128)(2,1)}), bf16[16,32,2048]{2,1,0:T(8,128)(2,1)S(1)}, u32[]{:S(2)}, u32[]{:S(2)}) async-start(bf16[16,32,2048]{2,1,0:T(8,128)(2,1)} %bitcast.71), calls=%async_computation.3 | async-start | bytes 4194304 | tf_op jit(solution)/shard_map/all_to_all | solution.py:172

commit v15 on v14

--- a/solution.py
+++ b/solution.py
@@ -146,10 +146,15 @@
     sending = lax.dot_general(
         dispatch, normed, (((0,), (0,)), ((), ())), preferred_element_type=jnp.float32
     ).astype(jnp.bfloat16)
-    received = lax.all_to_all(
-        sending.reshape(n_mp, capacity, d_model), "mp", split_axis=0, concat_axis=0, tiled=True
-    )
-    flat_rows = received.reshape(-1, d_model)
+    chunks = 2 if capacity % 2 == 0 else 1
+    part = capacity // chunks
+    by_slot = sending.reshape(n_mp, capacity, d_model)
+    arrivals = [
+        lax.all_to_all(
+            by_slot[:, k * part : (k + 1) * part], "mp", split_axis=0, concat_axis=0, tiled=True
+        )
+        for k in range(chunks)
+    ]
     if n_dp == 2:
         first = row_index == 0
         gate_up = jnp.where(
@@ -162,16 +167,23 @@
             jnp.concatenate([experts_out[0], out_other[0]], axis=1),
             jnp.concatenate([out_other[0], experts_out[0]], axis=1),
         )
-        flat_rows, down, gate_up = lax.optimization_barrier((flat_rows, down, gate_up))
+        arrivals[0], down, gate_up = lax.optimization_barrier((arrivals[0], down, gate_up))
     else:
         gate_up = lax.all_gather(experts_in, "dp", axis=1, tiled=True)[0]
         down = lax.all_gather(experts_out, "dp", axis=2, tiled=True)[0]
-    gate_vals = jnp.dot(flat_rows, gate_up, preferred_element_type=jnp.float32)
-    act = (jax.nn.silu(gate_vals[:, :ff_width]) * gate_vals[:, ff_width:]).astype(jnp.bfloat16)
-    outcome = jnp.dot(act, down, preferred_element_type=jnp.float32).astype(jnp.bfloat16)
-    results = lax.all_to_all(
-        outcome.reshape(n_mp, capacity, d_model), "mp", split_axis=0, concat_axis=0, tiled=True
-    )
+    returned = []
+    for arrived_rows in arrivals:
+        gate_vals = jnp.dot(
+            arrived_rows.reshape(-1, d_model), gate_up, preferred_element_type=jnp.float32
+        )
+        act = (jax.nn.silu(gate_vals[:, :ff_width]) * gate_vals[:, ff_width:]).astype(jnp.bfloat16)
+        outcome = jnp.dot(act, down, preferred_element_type=jnp.float32).astype(jnp.bfloat16)
+        returned.append(
+            lax.all_to_all(
+                outcome.reshape(n_mp, part, d_model), "mp", split_axis=0, concat_axis=0, tiled=True
+            )
+        )
+    results = jnp.concatenate(returned, axis=1)
     expert_sum = jnp.dot(
         combine,
         results.reshape(-1, d_model).astype(jnp.float32),

time: 214 us -> 218 us (1.019)
  waiting for transfers between devices: 138 us -> 107 us
  blocking collectives: 0 us -> 30.2 us
  starting transfers between devices: 32.4 us -> 35.1 us
    all_to_all x0 -> x1, blocking collectives: none -> 30.2 us  [on_device(): lax.all_to_all(by_slot[:, k * part:(k + 1) * part], 'mp', split_axis=0, c...]
    all_to_all x2 -> x3, waiting for transfers between devices: 73.4 us -> 52.4 us  [the longest x2 42.9 us: on_device(): lax.all_to_all(outcome.reshape(n_mp, part, d_model), 'mp', split_axis=0,...]
    ppermute x3, waiting for transfers between devices: 13.7 us -> 3.34 us  [swap_dp(): return lax.ppermute(x, 'dp', [(0, 1), (1, 0)])]
    all_to_all x2 -> x3, starting transfers between devices: 12.1 us -> 14.8 us  [the longest x2 9.88 us: on_device(): lax.all_to_all(outcome.reshape(n_mp, part, d_model), 'mp', split_axis=0,...]
    dot_general x1 -> x2, matrix products: 6.38 us -> 6.42 us  [on_device(): jnp.dot(arrived_rows.reshape(-1, d_model), gate_up, preferred_element_typ...]
  transfers between devices with their start and end apart: 11 -> 12, of which waited for: 7 -> 7; matrix products, arithmetic and copies ran while one was open for 14% -> 19% of each run, Pallas kernels for 0% -> 0%
where the time goes in v15:
time: 218 us; the launch traced here: 217 us
  waiting for transfers between devices  107 us (49%)
  starting transfers between devices  35.1 us (16%)
  blocking collectives  30.2 us (14%)
  other arithmetic  18.5 us (8%)
  matrix products  17.9 us (8%)
  local copies, waits for them, and re-layouts  7.91 us (4%)
    ppermute x3, waiting for transfers between devices, on_device(): pair = lax.ppermute(block, 'mp', [(m, m ^ 1 << b) for m in range(n_mp)])  46.1 us
    all_to_all x2, waiting for transfers between devices, on_device(): lax.all_to_all(outcome.reshape(n_mp, part, d_model), 'mp', split_axis=0,...  42.9 us
    all_to_all x1, blocking collectives, on_device(): lax.all_to_all(by_slot[:, k * part:(k + 1) * part], 'mp', split_axis=0, c...  30.2 us
    all_to_all x2, starting transfers between devices, on_device(): lax.all_to_all(outcome.reshape(n_mp, part, d_model), 'mp', split_axis=0,...  9.88 us
    all_to_all x1, waiting for transfers between devices, on_device(): lax.all_to_all(by_slot[:, k * part:(k + 1) * part], 'mp', split_axis=0, c...  9.48 us
    all_to_all x1, starting transfers between devices, on_device(): lax.all_to_all(blended.reshape(n_mp, sub, HD), 'mp', split_axis=0, concat...  7.22 us
    dot_general x2, matrix products, on_device(): jnp.dot(arrived_rows.reshape(-1, d_model), gate_up, preferred_element_typ...  6.42 us
    select_n x1, other arithmetic, on_device(): jnp.where(first, jnp.concatenate([experts_in[0], in_other[0]], axis=0), j...  6.14 us
  transfers between devices with their start and end apart: 12, of which 7 were waited for; matrix products, arithmetic and copies ran while one was open for 19% of the time, Pallas kernels for 0%

profile of v15, /device:TPU:11, one launch (start us, length us, event | category | flops | bytes accessed | tf_op | source)
XLA Modules:
  0.0 216.8 jit_solution(1541348487652252512)
XLA Ops:
  0.0 1.2 collective-permute-start
  1.2 3.3 %collective-permute-done = bf16[512,128]{1,0:T(8,128)(2,1)S(1)} collective-permute-done((bf16[512,128]{1,0:T(8,128)(2,1)}, bf16[512,128]{1,0:T(8,128)(2,1)S(1)}, u32[]{:S(2)}, u32[]{:S(2)}) %collective-permute-start) | collective-permute-done | bytes 131104 | tf_op jit(solution)/shard_map/ppermute | solution.py:29
  4.6 1.1 maximum_select_fusion.3
  5.6 2.4 %collective-permute-start.1 = (bf16[1,1024,128]{2,1,0:T(8,128)(2,1)S(1)}, bf16[1,1024,128]{2,1,0:T(8,128)(2,1)S(1)}, u32[]{:S(2)}, u32[]{:S(2)}) collective-permute-start(bf16[1,1024,128]{2,1,0:T(8,128)(2,1)S(1)} %maximum_select_fusion.3), channel_id=1, source_target_pairs={{0,8},{1,9},{2,10},{3,11},{4,12},{5,13},{6,14},{7,15},{8,0},{9,1},... | collective-permute-start | bytes 786440 | tf_op jit(solution)/shard_map/ppermute | solution.py:103
  8.0 1.2 reshape.233
  9.3 0.3 copy.66
  9.6 0.9 copy.77
  10.6 0.6 tile.8
  11.2 1.0 pad_maximum_fusion.3
  12.2 5.7 %all-to-all-start = ((bf16[16,224,128]{2,1,0:T(8,128)(2,1)}), bf16[16,224,128]{2,1,0:T(8,128)(2,1)S(1)}, u32[]{:S(2)}, u32[]{:S(2)}) async-start(bf16[16,224,128]{2,1,0:T(8,128)(2,1)} %pad_maximum_fusion.3), calls=%async_computation | async-start | bytes 1835008 | tf_op jit(solution)/shard_map/all_to_all | solution.py:67
  17.9 1.2 collective-permute-start.5
  19.1 0.2 collective-permute-start.6
  19.7 0.3 collective-permute-start.2
  20.1 0.9 reduce-window.6
  20.9 0.2 slice_reduce_fusion
  21.3 23.9 %collective-permute-done.2 = bf16[2,1024,128]{2,1,0:T(8,128)(2,1)S(1)} collective-permute-done((bf16[2,1024,128]{2,1,0:T(8,128)(2,1)S(1)}, bf16[2,1024,128]{2,1,0:T(8,128)(2,1)S(1)}, u32[]{:S(2)}, u32[]{:S(2)}) %collective-permute-start.2) | collective-permute-done | bytes 524320 | tf_op jit(solution)/shard_map/ppermute | solution.py:103
  45.4 1.1 pad_maximum_fusion.2
  46.4 0.4 collective-permute-start.3
  47.0 0.6 dynamic_slice.7
  47.7 0.7 fusion.22
  48.5 22.2 %collective-permute-done.3 = bf16[4,1024,128]{2,1,0:T(8,128)(2,1)S(1)} collective-permute-done((bf16[4,1024,128]{2,1,0:T(8,128)(2,1)}, bf16[4,1024,128]{2,1,0:T(8,128)(2,1)S(1)}, u32[]{:S(2)}, u32[]{:S(2)}) %collective-permute-start.3) | collective-permute-done | bytes 1048608 | tf_op jit(solution)/shard_map/ppermute | solution.py:103
  71.0 1.6 collective-permute-start.4
  73.1 0.5 copy.67
  74.0 0.7 fusion.28
  74.8 0.6 fusion.1
  75.3 1.4 fusion.4
  76.7 7.2 %all-to-all-start.1 = ((bf16[16,32,128]{2,1,0:T(8,128)(2,1)}), bf16[16,32,128]{2,1,0:T(8,128)(2,1)S(1)}, u32[]{:S(2)}, u32[]{:S(2)}) async-start(bf16[16,32,128]{2,1,0:T(8,128)(2,1)} %bitcast.11), calls=%async_computation.1 | async-start | bytes 262144 | tf_op jit(solution)/shard_map/all_to_all | solution.py:87
  84.1 5.0 %all-to-all-done.1 = bf16[16,32,128]{2,1,0:T(8,128)(2,1)S(1)} async-done(((bf16[16,32,128]{2,1,0:T(8,128)(2,1)}), bf16[16,32,128]{2,1,0:T(8,128)(2,1)S(1)}, u32[]{:S(2)}, u32[]{:S(2)}) %all-to-all-start.1) | async-done | bytes 131104 | tf_op jit(solution)/shard_map/all_to_all | solution.py:87
  89.2 0.5 fusion.29
  89.7 2.1 fusion.30
  91.9 0.4 copy.71
  92.3 0.4 reshape.239
  93.1 0.8 convolution_convert_fusion
  93.9 1.3 fusion.26
  95.1 30.2 %all_to_all.30 = bf16[16,16,2048]{2,1,0:T(8,128)(2,1)S(1)} all-to-all(bf16[16,16,2048]{2,1,0:T(8,128)(2,1)S(1)} %get-tuple-element.18), channel_id=1, replica_groups=mesh['dp'=2,'mp'=16] {'mp'}, dimensions={0} | all-to-all | bytes 2097152 | tf_op jit(solution)/shard_map/all_to_all | solution.py:153
  125.3 4.9 %all-to-all-start.4 = ((bf16[16,16,2048]{2,1,0:T(8,128)(2,1)}), bf16[16,16,2048]{2,1,0:T(8,128)(2,1)S(1)}, u32[]{:S(2)}, u32[]{:S(2)}) async-start(bf16[16,16,2048]{2,1,0:T(8,128)(2,1)} %get-tuple-element.17), calls=%async_computation.4 | async-start | bytes 2097152 | tf_op jit(solution)/shard_map/all_to_all | solution.py:153
  130.2 6.1 %maximum_select_fusion = bf16[2048,1408]{1,0:T(8,128)(2,1)S(1)} fusion(bf16[1024,1408]{1,0:T(8,128)(2,1)} %bitcast.23, bf16[1024,1408]{1,0:T(8,128)(2,1)} %bitcast.76, pred[]{:T(512)S(6)} %eq.86), kind=kLoop, calls=%fused_computation | loop fusion | flops 25952256 | bytes 11534337 | tf_op jit(solution)/shard_map/jit(_where)/select_n | solution.py:160
  136.4 5.3 %maximum_select_fusion.1 = bf16[704,2048]{1,0:T(8,128)(2,1)S(1)} fusion(bf16[704,1024]{1,0:T(8,128)(2,1)} %bitcast.21, bf16[704,1024]{1,0:T(8,128)(2,1)} %bitcast.20, pred[]{:T(512)S(6)} %eq.86), kind=kLoop, calls=%fused_computation.6 | loop fusion | flops 12976128 | bytes 5767169 | tf_op jit(solution)/shard_map/jit(_where)/select_n | solution.py:165
  141.8 1.8 fusion.31
  143.6 2.1 convolution_convert_fusion.2
  145.6 9.5 %all-to-all-done.4 = bf16[16,16,2048]{2,1,0:T(8,128)(2,1)S(1)} async-done(((bf16[16,16,2048]{2,1,0:T(8,128)(2,1)}), bf16[16,16,2048]{2,1,0:T(8,128)(2,1)S(1)}, u32[]{:S(2)}, u32[]{:S(2)}) %all-to-all-start.4) | async-done | bytes 1048608 | tf_op jit(solution)/shard_map/all_to_all | solution.py:153
  155.1 4.9 %all-to-all-start.3 = ((bf16[16,16,2048]{2,1,0:T(8,128)(2,1)}), bf16[16,16,2048]{2,1,0:T(8,128)(2,1)S(1)}, u32[]{:S(2)}, u32[]{:S(2)}) async-start(bf16[16,16,2048]{2,1,0:T(8,128)(2,1)} %bitcast.80), calls=%async_computation.3 | async-start | bytes 2097152 | tf_op jit(solution)/shard_map/all_to_all | solution.py:182
  160.1 4.6 %fusion.32 = f32[256,1408]{1,0:T(8,128)S(1)} fusion(bf16[256,2048]{1,0:T(8,128)(2,1)S(1)} %bitcast.79, bf16[2048,1408]{1,0:T(8,128)(2,1)} %copy-done.1), kind=kOutput, calls=%fused_computation.82 | convolution fusion | flops 1476395008 | bytes 8257536 | tf_op jit(solution)/shard_map/dot_general | solution.py:176
  164.7 2.0 convolution_convert_fusion.1
  166.7 18.2 %all-to-all-done.3 = bf16[16,16,2048]{2,1,0:T(8,128)(2,1)S(1)} async-done(((bf16[16,16,2048]{2,1,0:T(8,128)(2,1)}), bf16[16,16,2048]{2,1,0:T(8,128)(2,1)S(1)}, u32[]{:S(2)}, u32[]{:S(2)}) %all-to-all-start.3) | async-done | bytes 1048608 | tf_op jit(solution)/shard_map/all_to_all | solution.py:182
  184.9 4.9 %all-to-all-start.5 = ((bf16[16,16,2048]{2,1,0:T(8,128)(2,1)}), bf16[16,16,2048]{2,1,0:T(8,128)(2,1)S(1)}, u32[]{:S(2)}, u32[]{:S(2)}) async-start(bf16[16,16,2048]{2,1,0:T(8,128)(2,1)} %bitcast.82), calls=%async_computation.5 | async-start | bytes 2097152 | tf_op jit(solution)/shard_map/all_to_all | solution.py:182
  190.1 24.7 %all-to-all-done.5 = bf16[16,16,2048]{2,1,0:T(8,128)(2,1)S(1)} async-done(((bf16[16,16,2048]{2,1,0:T(8,128)(2,1)}), bf16[16,16,2048]{2,1,0:T(8,128)(2,1)S(1)}, u32[]{:S(2)}, u32[]{:S(2)}) %all-to-all-start.5) | async-done | bytes 1048608 | tf_op jit(solution)/shard_map/all_to_all | solution.py:182
  214.9 1.9 fusion.2
  (64 shorter events, 3.3 us)
Async XLA Ops:
  0.0 20.9 %copy-start = (s32[2,96]{1,0:T(2,128)S(1)}, s32[2,96]{1,0:T(2,128)}, u32[]{:S(2)}) copy-start(s32[2,96]{1,0:T(2,128)} %param.15) | copy-start | bytes 2308
  0.0 4.6 %collective-permute-start = (bf16[512,128]{1,0:T(8,128)(2,1)}, bf16[512,128]{1,0:T(8,128)(2,1)S(1)}, u32[]{:S(2)}, u32[]{:S(2)}) collective-permute-start(bf16[512,128]{1,0:T(8,128)(2,1)} %param.18), channel_id=1, source_target_pairs={{0,16},{16,0},{1,17},{17,1},{2,18},{18,2},{3,19},{19,3},{4,20},{20... | collective-permute-start | bytes 393224 | tf_op jit(solution)/shard_map/ppermute | solution.py:29
  5.6 13.9 %collective-permute-start.1 = (bf16[1,1024,128]{2,1,0:T(8,128)(2,1)S(1)}, bf16[1,1024,128]{2,1,0:T(8,128)(2,1)S(1)}, u32[]{:S(2)}, u32[]{:S(2)}) collective-permute-start(bf16[1,1024,128]{2,1,0:T(8,128)(2,1)S(1)} %maximum_select_fusion.3), channel_id=1, source_target_pairs={{0,8},{1,9},{2,10},{3,11},{4,12},{5,13},{6,14},{7,15},{8,0},{9,1},... | collective-permute-start | bytes 786440 | tf_op jit(solution)/shard_map/ppermute | solution.py:103
  9.6 9.7 %copy-start.5 = (s32[64,6]{0,1:T(8,128)S(1)}, s32[64,6]{0,1:T(8,128)}, u32[]{:S(2)}) copy-start(s32[64,6]{0,1:T(8,128)} %param.20) | copy-start | bytes 4612
  12.2 60.8 %all-to-all-start = ((bf16[16,224,128]{2,1,0:T(8,128)(2,1)}), bf16[16,224,128]{2,1,0:T(8,128)(2,1)S(1)}, u32[]{:S(2)}, u32[]{:S(2)}) async-start(bf16[16,224,128]{2,1,0:T(8,128)(2,1)} %pad_maximum_fusion.3), calls=%async_computation | async-start | bytes 1835008 | tf_op jit(solution)/shard_map/all_to_all | solution.py:67
  17.9 75.2 %collective-permute-start.5 = (bf16[1,704,1024]{2,1,0:T(8,128)(2,1)}, bf16[1,704,1024]{2,1,0:T(8,128)(2,1)}, u32[]{:S(2)}, u32[]{:S(2)}) collective-permute-start(bf16[1,704,1024]{2,1,0:T(8,128)(2,1)} %param.23), channel_id=1, source_target_pairs={{0,16},{16,0},{1,17},{17,1},{2,18},{18,2},{3,19},{19,3},{4,20},{20... | collective-permute-start | bytes 4325384 | tf_op jit(solution)/shard_map/ppermute | solution.py:29
  19.1 111.2 %collective-permute-start.6 = (bf16[1,1024,1408]{2,1,0:T(8,128)(2,1)}, bf16[1,1024,1408]{2,1,0:T(8,128)(2,1)}, u32[]{:S(2)}, u32[]{:S(2)}) collective-permute-start(bf16[1,1024,1408]{2,1,0:T(8,128)(2,1)} %param.22), channel_id=1, source_target_pairs={{0,16},{16,0},{1,17},{17,1},{2,18},{18,2},{3,19},{19,3},{4,20},{20... | collective-permute-start | bytes 8650760 | tf_op jit(solution)/shard_map/ppermute | solution.py:29
  19.6 27.3 %copy-start.8 = (s32[2]{0:T(128)S(1)}, s32[2]{0:T(128)}, u32[]{:S(2)}) copy-start(s32[2]{0:T(128)} %param.16) | copy-start | bytes 28
  19.6 28.1 %copy-start.9 = (s32[1,16]{1,0:T(1,128)S(1)}, s32[1,16]{1,0:T(1,128)}, u32[]{:S(2)}) copy-start(s32[1,16]{1,0:T(1,128)} %param.17) | copy-start | bytes 196
  19.7 25.6 %collective-permute-start.2 = (bf16[2,1024,128]{2,1,0:T(8,128)(2,1)S(1)}, bf16[2,1024,128]{2,1,0:T(8,128)(2,1)S(1)}, u32[]{:S(2)}, u32[]{:S(2)}) collective-permute-start(bf16[2,1024,128]{2,1,0:T(8,128)(2,1)S(1)} %pad_maximum_fusion.4), channel_id=1, source_target_pairs={{0,4},{1,5},{2,6},{3,7},{4,0},{5,1},{6,2},{7,3},{8,12},{9,13},{10,... | collective-permute-start | bytes 1572872 | tf_op jit(solution)/shard_map/ppermute | solution.py:103
  46.4 24.2 %collective-permute-start.3 = (bf16[4,1024,128]{2,1,0:T(8,128)(2,1)}, bf16[4,1024,128]{2,1,0:T(8,128)(2,1)S(1)}, u32[]{:S(2)}, u32[]{:S(2)}) collective-permute-start(bf16[4,1024,128]{2,1,0:T(8,128)(2,1)} %pad_maximum_fusion.2), channel_id=1, source_target_pairs={{0,2},{1,3},{2,0},{3,1},{4,6},{5,7},{6,4},{7,5},{8,10},{9,11},{10,... | collective-permute-start | bytes 3145736 | tf_op jit(solution)/shard_map/ppermute | solution.py:103
  71.0 18.7 %collective-permute-start.4 = (bf16[8,1024,128]{2,1,0:T(8,128)(2,1)S(1)}, bf16[8,1024,128]{2,1,0:T(8,128)(2,1)}, u32[]{:S(2)}, u32[]{:S(2)}) collective-permute-start(bf16[8,1024,128]{2,1,0:T(8,128)(2,1)S(1)} %pad_maximum_fusion), channel_id=1, source_target_pairs={{0,1},{1,0},{2,3},{3,2},{4,5},{5,4},{6,7},{7,6},{8,9},{9,8},{10,11... | collective-permute-start | bytes 6291464 | tf_op jit(solution)/shard_map/ppermute | solution.py:108
  76.7 12.4 %all-to-all-start.1 = ((bf16[16,32,128]{2,1,0:T(8,128)(2,1)}), bf16[16,32,128]{2,1,0:T(8,128)(2,1)S(1)}, u32[]{:S(2)}, u32[]{:S(2)}) async-start(bf16[16,32,128]{2,1,0:T(8,128)(2,1)} %bitcast.11), calls=%async_computation.1 | async-start | bytes 262144 | tf_op jit(solution)/shard_map/all_to_all | solution.py:87
  89.7 3.0 %copy-start.4 = (bf16[64,2048]{1,0:T(8,128)(2,1)S(1)}, bf16[64,2048]{1,0:T(8,128)(2,1)}, u32[]{:S(2)}) copy-start(bf16[64,2048]{1,0:T(8,128)(2,1)} %param.13) | copy-start | bytes 786436
  89.7 3.2 %copy-start.6 = (f32[2048]{0:T(1024)S(1)}, f32[2048]{0:T(1024)}, u32[]{:S(2)}) copy-start(f32[2048]{0:T(1024)} %param.19) | copy-start | bytes 24580
  125.3 29.8 %all-to-all-start.4 = ((bf16[16,16,2048]{2,1,0:T(8,128)(2,1)}), bf16[16,16,2048]{2,1,0:T(8,128)(2,1)S(1)}, u32[]{:S(2)}, u32[]{:S(2)}) async-start(bf16[16,16,2048]{2,1,0:T(8,128)(2,1)} %get-tuple-element.17), calls=%async_computation.4 | async-start | bytes 2097152 | tf_op jit(solution)/shard_map/all_to_all | solution.py:153
  136.4 5.3 %copy-start.1 = (bf16[2048,1408]{1,0:T(8,128)(2,1)}, bf16[2048,1408]{1,0:T(8,128)(2,1)S(1)}, u32[]{:S(2)}) copy-start(bf16[2048,1408]{1,0:T(8,128)(2,1)S(1)} %maximum_select_fusion) | copy-start | bytes 17301508
  141.7 1.8 copy-start.2
  155.1 29.8 %all-to-all-start.3 = ((bf16[16,16,2048]{2,1,0:T(8,128)(2,1)}), bf16[16,16,2048]{2,1,0:T(8,128)(2,1)S(1)}, u32[]{:S(2)}, u32[]{:S(2)}) async-start(bf16[16,16,2048]{2,1,0:T(8,128)(2,1)} %bitcast.80), calls=%async_computation.3 | async-start | bytes 2097152 | tf_op jit(solution)/shard_map/all_to_all | solution.py:182
  160.1 4.6 %copy-start.3 = (bf16[704,2048]{1,0:T(8,128)(2,1)S(1)}, bf16[704,2048]{1,0:T(8,128)(2,1)}, u32[]{:S(2)}) copy-start(bf16[704,2048]{1,0:T(8,128)(2,1)} %copy-done.2) | copy-start | bytes 8650756
  164.7 25.2 %copy-start.7 = (f32[64,6]{0,1:T(8,128)S(1)}, f32[64,6]{0,1:T(8,128)}, u32[]{:S(2)}) copy-start(f32[64,6]{0,1:T(8,128)} %param.21) | copy-start | bytes 4612
  184.9 29.8 %all-to-all-start.5 = ((bf16[16,16,2048]{2,1,0:T(8,128)(2,1)}), bf16[16,16,2048]{2,1,0:T(8,128)(2,1)S(1)}, u32[]{:S(2)}, u32[]{:S(2)}) async-start(bf16[16,16,2048]{2,1,0:T(8,128)(2,1)} %bitcast.82), calls=%async_computation.5 | async-start | bytes 2097152 | tf_op jit(solution)/shard_map/all_to_all | solution.py:182

commit v16 on v12

--- a/solution.py
+++ b/solution.py
@@ -64,9 +64,6 @@
     q_out = queries.reshape(sub, groups, heads, HD).transpose(1, 2, 0, 3).reshape(n_mp, sub, HD)
     kv_heads = kv_pages.reshape(pages_dev, PAGE, 2, heads, HD).transpose(3, 0, 1, 2, 4)
     kv_out = jnp.tile(kv_heads, (groups, 1, 1, 1, 1)).reshape(n_mp, pages_dev * PAGE * 2, HD)
-    both = lax.all_to_all(
-        jnp.concatenate([q_out, kv_out], axis=1), "mp", split_axis=0, concat_axis=0, tiled=True
-    )
     if n_dp == 2:
         w_pair = swap_dp(out_weight)
         wo_rows = jnp.where(
@@ -77,6 +74,7 @@
     else:
         wo_rows = lax.all_gather(out_weight, "dp", axis=0, tiled=True)
     bits = n_mp.bit_length() - 1
+    kv_send = jnp.concatenate([q_out, kv_out], axis=1)
     if n_mp == 1 << bits:
         block = wo_rows[None]
         if bits > 1:
@@ -86,7 +84,8 @@
             block = jnp.concatenate(
                 [jnp.where(low, block, pair), jnp.where(low, pair, block)], axis=0
             )
-        block, both = lax.optimization_barrier((block, both))
+        block, kv_send = lax.optimization_barrier((block, kv_send))
+    both = lax.all_to_all(kv_send, "mp", split_axis=0, concat_axis=0, tiled=True)
     q_in = both[:, :sub, :]
     arrived = both[:, sub:, :].reshape(n_mp, pages_dev, PAGE, 2, HD)
     first_pos = cache_len[request] + deal_row % n_mp * q_count
@@ -104,11 +103,11 @@
     key_rows = arrived[:, :, :, 0, :].reshape(-1, HD)
     value_rows = arrived[:, :, :, 1, :].reshape(-1, HD)
     blended = attend_head(q_in.reshape(-1, HD), key_rows, value_rows, key_pos, query_pos)
-
+    back = lax.all_to_all(blended.reshape(n_mp, sub, HD), "mp", split_axis=0, concat_axis=0, tiled=True)
+    attended = back.reshape(groups, heads, sub, HD).transpose(2, 0, 1, 3).reshape(q_count, width)
+
+    bits = n_mp.bit_length() - 1
     if n_mp == 1 << bits:
-        back = lax.all_to_all(
-            blended.reshape(n_mp, sub, HD), "mp", split_axis=0, concat_axis=0, tiled=True
-        )
         for b in reversed(range(1, bits - 1)):
             pair = lax.ppermute(block, "mp", [(m, m ^ (1 << b)) for m in range(n_mp)])
             low = (column >> b) % 2 == 0
@@ -116,7 +115,6 @@
                 [jnp.where(low, block, pair), jnp.where(low, pair, block)], axis=0
             )
         pair = lax.ppermute(block, "mp", [(m, m ^ 1) for m in range(n_mp)])
-        attended = back.reshape(groups, heads, sub, HD).transpose(2, 0, 1, 3).reshape(q_count, width)
         own_part = jnp.einsum("tk,jkc->tjc", attended, block, preferred_element_type=jnp.float32)
         pair_part = jnp.einsum("tk,jkc->tjc", attended, pair, preferred_element_type=jnp.float32)
         low = column % 2 == 0
@@ -133,10 +131,6 @@
             .reshape(q_count, d_model)
         )
     else:
-        back = lax.all_to_all(
-            blended.reshape(n_mp, sub, HD), "mp", split_axis=0, concat_axis=0, tiled=True
-        )
-        attended = back.reshape(groups, heads, sub, HD).transpose(2, 0, 1, 3).reshape(q_count, width)
         projected = jnp.dot(
             attended,
             lax.all_gather(wo_rows, "mp", axis=1, tiled=True),
@@ -155,9 +149,9 @@
     combine = jnp.sum(jnp.where(hits, expert_gates[:, :, None], 0.0), axis=1)
     ff_width = experts_out.shape[1]
     if n_dp == 2:
+        out_other = swap_dp(experts_out)
         in_other = swap_dp(experts_in)
-        out_other = swap_dp(experts_out)
-        normed, in_other = lax.optimization_barrier((normed, in_other))
+        normed, out_other = lax.optimization_barrier((normed, out_other))
     sending = lax.dot_general(
         dispatch, normed, (((0,), (0,)), ((), ())), preferred_element_type=jnp.float32
     ).astype(jnp.bfloat16)
@@ -172,12 +166,12 @@
             jnp.concatenate([experts_in[0], in_other[0]], axis=0),
             jnp.concatenate([in_other[0], experts_in[0]], axis=0),
         )
-        flat_rows, out_other, gate_up = lax.optimization_barrier((flat_rows, out_other, gate_up))
         down = jnp.where(
             first,
             jnp.concatenate([experts_out[0], out_other[0]], axis=1),
             jnp.concatenate([out_other[0], experts_out[0]], axis=1),
         )
+        flat_rows, down, gate_up = lax.optimization_barrier((flat_rows, down, gate_up))
     else:
         gate_up = lax.all_gather(experts_in, "dp", axis=1, tiled=True)[0]
         down = lax.all_gather(experts_out, "dp", axis=2, tiled=True)[0]

time: 226 us -> 209 us (0.925)
  waiting for transfers between devices: 149 us -> 129 us
  other arithmetic: 13.3 us -> 17 us
    ppermute x3, waiting for transfers between devices: 27.9 us -> 7.89 us  [swap_dp(): return lax.ppermute(x, 'dp', [(0, 1), (1, 0)])]
    ppermute x3, waiting for transfers between devices: 54.5 us -> 35.8 us  [on_device(): pair = lax.ppermute(block, 'mp', [(m, m ^ 1 << b) for m in range(n_mp)])]
    all_to_all x1, waiting for transfers between devices: 14.4 us -> 32.9 us  [on_device(): lax.all_to_all(sending.reshape(n_mp, capacity, d_model), 'mp', split_axis...]
    all_to_all x1, starting transfers between devices: 4.81 us -> 8.27 us  [on_device(): lax.all_to_all(blended.reshape(n_mp, sub, HD), 'mp', split_axis=0, concat...]
    ppermute x3, starting transfers between devices: 5.6 us -> 2.7 us  [on_device(): pair = lax.ppermute(block, 'mp', [(m, m ^ 1 << b) for m in range(n_mp)])]
    select_n x0 -> x1, other arithmetic: none -> 2.58 us  [on_device(): jnp.where(first, jnp.concatenate([experts_out[0], out_other[0]], axis=1),...]
  transfers between devices with their start and end apart: 11 -> 11, of which waited for: 8 -> 8; matrix products, arithmetic and copies ran while one was open for 9% -> 14% of each run, Pallas kernels for 0% -> 0%
where the time goes in v16:
time: 209 us; the launch traced here: 208 us
  waiting for transfers between devices  129 us (62%)
  starting transfers between devices  36.5 us (17%)
  matrix products  18.4 us (9%)
  other arithmetic  17 us (8%)
  local copies, waits for them, and re-layouts  7.32 us (4%)
    all_to_all x1, waiting for transfers between devices, on_device(): lax.all_to_all(outcome.reshape(n_mp, capacity, d_model), 'mp', split_axis...  47.2 us
    ppermute x3, waiting for transfers between devices, on_device(): pair = lax.ppermute(block, 'mp', [(m, m ^ 1 << b) for m in range(n_mp)])  35.8 us
    all_to_all x1, waiting for transfers between devices, on_device(): lax.all_to_all(sending.reshape(n_mp, capacity, d_model), 'mp', split_axis...  32.9 us
    all_to_all x1, starting transfers between devices, on_device(): lax.all_to_all(blended.reshape(n_mp, sub, HD), 'mp', split_axis=0, concat...  8.27 us
    ppermute x3, waiting for transfers between devices, swap_dp(): return lax.ppermute(x, 'dp', [(0, 1), (1, 0)])  7.89 us
    all_to_all x1, starting transfers between devices, on_device(): lax.all_to_all(kv_send, 'mp', split_axis=0, concat_axis=0, tiled=True)  7.82 us
    select_n x1, other arithmetic, on_device(): jnp.where(first, jnp.concatenate([experts_in[0], in_other[0]], axis=0), j...  7.49 us
    all_to_all x1, starting transfers between devices, on_device(): lax.all_to_all(sending.reshape(n_mp, capacity, d_model), 'mp', split_axis...  7.06 us
  transfers between devices with their start and end apart: 11, of which 8 were waited for; matrix products, arithmetic and copies ran while one was open for 14% of the time, Pallas kernels for 0%

profile of v16, /device:TPU:11, one launch (start us, length us, event | category | flops | bytes accessed | tf_op | source)
XLA Modules:
  0.0 208.4 jit_solution(14057756334592925119)
XLA Ops:
  0.0 1.2 collective-permute-start
  1.2 3.3 %collective-permute-done = bf16[512,128]{1,0:T(8,128)(2,1)S(1)} collective-permute-done((bf16[512,128]{1,0:T(8,128)(2,1)}, bf16[512,128]{1,0:T(8,128)(2,1)S(1)}, u32[]{:S(2)}, u32[]{:S(2)}) %collective-permute-start) | collective-permute-done | bytes 131104 | tf_op jit(solution)/shard_map/ppermute | solution.py:29
  4.6 1.1 maximum_select_fusion.3
  5.6 2.4 %collective-permute-start.1 = (bf16[1,1024,128]{2,1,0:T(8,128)(2,1)S(1)}, bf16[1,1024,128]{2,1,0:T(8,128)(2,1)S(1)}, u32[]{:S(2)}, u32[]{:S(2)}) collective-permute-start(bf16[1,1024,128]{2,1,0:T(8,128)(2,1)S(1)} %maximum_select_fusion.3), channel_id=1, source_target_pairs={{0,8},{1,9},{2,10},{3,11},{4,12},{5,13},{6,14},{7,15},{8,0},{9,1},... | collective-permute-start | bytes 786440 | tf_op jit(solution)/shard_map/ppermute | solution.py:82
  8.0 1.2 collective-permute-start.5
  9.3 0.2 collective-permute-start.6
  9.5 1.2 reshape.227
  10.7 0.3 copy.66
  11.0 0.9 copy.77
  12.0 0.8 copy.72
  12.9 0.6 tile.8
  13.5 1.0 pad_maximum_fusion.2
  14.5 5.0 %collective-permute-done.1 = bf16[1,1024,128]{2,1,0:T(8,128)(2,1)S(1)} collective-permute-done((bf16[1,1024,128]{2,1,0:T(8,128)(2,1)S(1)}, bf16[1,1024,128]{2,1,0:T(8,128)(2,1)S(1)}, u32[]{:S(2)}, u32[]{:S(2)}) %collective-permute-start.1) | collective-permute-done | bytes 262176 | tf_op jit(solution)/shard_map/ppermute | solution.py:82
  19.8 0.9 reduce-window.6
  20.7 0.2 slice_reduce_fusion
  20.9 0.2 select_reduce_fusion.1
  21.1 7.8 %all-to-all-start = ((bf16[16,224,128]{2,1,0:T(8,128)(2,1)}), bf16[16,224,128]{2,1,0:T(8,128)(2,1)S(1)}, u32[]{:S(2)}, u32[]{:S(2)}) async-start(bf16[16,224,128]{2,1,0:T(8,128)(2,1)} %pad_maximum_fusion.2), calls=%async_computation | async-start | bytes 1835008 | tf_op jit(solution)/shard_map/all_to_all | solution.py:88
  28.9 3.9 %collective-permute-done.2 = bf16[2,1024,128]{2,1,0:T(8,128)(2,1)S(1)} collective-permute-done((bf16[2,1024,128]{2,1,0:T(8,128)(2,1)S(1)}, bf16[2,1024,128]{2,1,0:T(8,128)(2,1)S(1)}, u32[]{:S(2)}, u32[]{:S(2)}) %collective-permute-start.2) | collective-permute-done | bytes 524320 | tf_op jit(solution)/shard_map/ppermute | solution.py:112
  32.9 1.2 pad_maximum_fusion.1
  34.0 0.3 collective-permute-start.3
  34.5 0.6 dynamic_slice.7
  35.2 0.7 fusion.19
  36.0 26.8 %collective-permute-done.3 = bf16[4,1024,128]{2,1,0:T(8,128)(2,1)S(1)} collective-permute-done((bf16[4,1024,128]{2,1,0:T(8,128)(2,1)}, bf16[4,1024,128]{2,1,0:T(8,128)(2,1)S(1)}, u32[]{:S(2)}, u32[]{:S(2)}) %collective-permute-start.3) | collective-permute-done | bytes 1048608 | tf_op jit(solution)/shard_map/ppermute | solution.py:112
  63.0 0.2 pad_maximum_fusion
  63.2 2.9 %collective-permute-start.4 = (bf16[8,1024,128]{2,1,0:T(8,128)(2,1)S(1)}, bf16[8,1024,128]{2,1,0:T(8,128)(2,1)}, u32[]{:S(2)}, u32[]{:S(2)}) collective-permute-start(bf16[8,1024,128]{2,1,0:T(8,128)(2,1)S(1)} %pad_maximum_fusion), channel_id=1, source_target_pairs={{0,1},{1,0},{2,3},{3,2},{4,5},{5,4},{6,7},{7,6},{8,9},{9,8},{10,11... | collective-permute-start | bytes 6291464 | tf_op jit(solution)/shard_map/ppermute | solution.py:117
  66.6 0.5 copy.67
  67.1 0.2 fusion.22
  67.5 0.7 fusion.23
  68.3 0.6 fusion.1
  68.8 1.4 fusion.5
  70.2 8.3 %all-to-all-start.1 = ((bf16[16,32,128]{2,1,0:T(8,128)(2,1)}), bf16[16,32,128]{2,1,0:T(8,128)(2,1)S(1)}, u32[]{:S(2)}, u32[]{:S(2)}) async-start(bf16[16,32,128]{2,1,0:T(8,128)(2,1)} %bitcast.13), calls=%async_computation.1 | async-start | bytes 262144 | tf_op jit(solution)/shard_map/all_to_all | solution.py:106
  78.7 5.0 %all-to-all-done.1 = bf16[16,32,128]{2,1,0:T(8,128)(2,1)S(1)} async-done(((bf16[16,32,128]{2,1,0:T(8,128)(2,1)}), bf16[16,32,128]{2,1,0:T(8,128)(2,1)S(1)}, u32[]{:S(2)}, u32[]{:S(2)}) %all-to-all-start.1) | async-done | bytes 131104 | tf_op jit(solution)/shard_map/all_to_all | solution.py:106
  83.8 0.5 fusion.24
  84.3 2.1 %fusion.25 = f32[64,8,128]{2,0,1:T(8,128)S(1)} fusion(bf16[64,1024,1]{1,0,2:T(8,128)(2,1)S(1)} %reshape.239, bf16[8,1024,128]{2,1,0:T(8,128)(2,1)} %collective-permute-done.4), kind=kOutput, calls=%fused_computation.73 | convolution fusion | flops 134217728 | bytes 2490368 | tf_op jit(solution)/shard_map/tk,jkc->tjc/dot_general | solution.py:119
  86.5 0.4 copy.71
  86.9 0.4 reshape.233
  87.3 0.2 fusion.9
  87.7 2.1 %convolution_convert_fusion.1 = bf16[512,2048]{1,0:T(8,128)(2,1)} fusion(pred[64,512]{1,0:T(8,128)(4,1)S(1)} %fusion.8, bf16[64,2048]{1,0:T(8,128)(2,1)S(1)} %fusion.11), kind=kOutput, calls=%fused_computation.6 | convolution fusion | flops 135266304 | bytes 2392064 | tf_op jit(solution)/shard_map/dot_general | solution.py:155
  89.8 7.1 %all-to-all-start.2 = ((bf16[16,32,2048]{2,1,0:T(8,128)(2,1)}), bf16[16,32,2048]{2,1,0:T(8,128)(2,1)}, u32[]{:S(2)}, u32[]{:S(2)}) async-start(bf16[16,32,2048]{2,1,0:T(8,128)(2,1)} %bitcast.19), calls=%async_computation.2 | async-start | bytes 4194304 | tf_op jit(solution)/shard_map/all_to_all | solution.py:158
  96.8 4.5 %collective-permute-done.6 = bf16[1,1024,1408]{2,1,0:T(8,128)(2,1)} collective-permute-done((bf16[1,1024,1408]{2,1,0:T(8,128)(2,1)}, bf16[1,1024,1408]{2,1,0:T(8,128)(2,1)}, u32[]{:S(2)}, u32[]{:S(2)}) %collective-permute-start.6) | collective-permute-done | bytes 2883616 | tf_op jit(solution)/shard_map/ppermute | solution.py:29
  101.4 7.5 %maximum_select_fusion = bf16[2048,1408]{1,0:T(8,128)(2,1)} fusion(bf16[1024,1408]{1,0:T(8,128)(2,1)} %bitcast.24, bf16[1024,1408]{1,0:T(8,128)(2,1)S(1)} %bitcast.70, pred[]{:T(512)S(6)} %eq.84), kind=kLoop, calls=%fused_computation | loop fusion | flops 25952256 | bytes 11534337 | tf_op jit(solution)/shard_map/jit(_where)/select_n | solution.py:164
  108.9 2.6 %maximum_select_fusion.1 = bf16[704,2048]{1,0:T(8,128)(2,1)S(1)} fusion(bf16[704,1024]{1,0:T(8,128)(2,1)} %bitcast.22, bf16[704,1024]{1,0:T(8,128)(2,1)S(1)} %bitcast.74, pred[]{:T(512)S(6)} %eq.84), kind=kLoop, calls=%fused_computation.7 | loop fusion | flops 12976128 | bytes 5767169 | tf_op jit(solution)/shard_map/jit(_where)/select_n | solution.py:169
  111.5 32.9 %all-to-all-done.2 = bf16[16,32,2048]{2,1,0:T(8,128)(2,1)} async-done(((bf16[16,32,2048]{2,1,0:T(8,128)(2,1)}), bf16[16,32,2048]{2,1,0:T(8,128)(2,1)}, u32[]{:S(2)}, u32[]{:S(2)}) %all-to-all-start.2) | async-done | bytes 2097184 | tf_op jit(solution)/shard_map/all_to_all | solution.py:158
  144.4 6.4 %fusion.26 = f32[512,1408]{1,0:T(8,128)S(1)} fusion(bf16[512,2048]{1,0:T(8,128)(2,1)} %bitcast.20, bf16[2048,1408]{1,0:T(8,128)(2,1)} %maximum_select_fusion), kind=kOutput, calls=%fused_computation.74 | convolution fusion | flops 2952790016 | bytes 10747904 | tf_op jit(solution)/shard_map/dot_general | solution.py:178
  150.8 3.3 %convolution_convert_fusion = bf16[512,2048]{1,0:T(8,128)(2,1)} fusion(bf16[704,2048]{1,0:T(8,128)(2,1)S(1)} %maximum_select_fusion.1, f32[512,1408]{1,0:T(8,128)S(1)} %fusion.26), kind=kOutput, calls=%fused_computation.5 | convolution fusion | flops 1479606272 | bytes 8126464 | tf_op jit(solution)/shard_map/dot_general | solution.py:180
  154.0 5.0 %all-to-all-start.3 = ((bf16[16,32,2048]{2,1,0:T(8,128)(2,1)}), bf16[16,32,2048]{2,1,0:T(8,128)(2,1)S(1)}, u32[]{:S(2)}, u32[]{:S(2)}) async-start(bf16[16,32,2048]{2,1,0:T(8,128)(2,1)} %bitcast.71), calls=%async_computation.3 | async-start | bytes 4194304 | tf_op jit(solution)/shard_map/all_to_all | solution.py:181
  159.2 47.2 %all-to-all-done.3 = bf16[16,32,2048]{2,1,0:T(8,128)(2,1)S(1)} async-done(((bf16[16,32,2048]{2,1,0:T(8,128)(2,1)}), bf16[16,32,2048]{2,1,0:T(8,128)(2,1)S(1)}, u32[]{:S(2)}, u32[]{:S(2)}) %all-to-all-start.3) | async-done | bytes 2097184 | tf_op jit(solution)/shard_map/all_to_all | solution.py:181
  206.5 1.9 fusion.2
  (55 shorter events, 2.4 us)
Async XLA Ops:
  0.0 20.6 %copy-start = (s32[2,96]{1,0:T(2,128)S(1)}, s32[2,96]{1,0:T(2,128)}, u32[]{:S(2)}) copy-start(s32[2,96]{1,0:T(2,128)} %param.15) | copy-start | bytes 2308
  0.0 4.6 %collective-permute-start = (bf16[512,128]{1,0:T(8,128)(2,1)}, bf16[512,128]{1,0:T(8,128)(2,1)S(1)}, u32[]{:S(2)}, u32[]{:S(2)}) collective-permute-start(bf16[512,128]{1,0:T(8,128)(2,1)} %param.18), channel_id=1, source_target_pairs={{0,16},{16,0},{1,17},{17,1},{2,18},{18,2},{3,19},{19,3},{4,20},{20... | collective-permute-start | bytes 393224 | tf_op jit(solution)/shard_map/ppermute | solution.py:29
  5.6 13.9 %collective-permute-start.1 = (bf16[1,1024,128]{2,1,0:T(8,128)(2,1)S(1)}, bf16[1,1024,128]{2,1,0:T(8,128)(2,1)S(1)}, u32[]{:S(2)}, u32[]{:S(2)}) collective-permute-start(bf16[1,1024,128]{2,1,0:T(8,128)(2,1)S(1)} %maximum_select_fusion.3), channel_id=1, source_target_pairs={{0,8},{1,9},{2,10},{3,11},{4,12},{5,13},{6,14},{7,15},{8,0},{9,1},... | collective-permute-start | bytes 786440 | tf_op jit(solution)/shard_map/ppermute | solution.py:82
  8.0 79.7 %collective-permute-start.5 = (bf16[1,704,1024]{2,1,0:T(8,128)(2,1)}, bf16[1,704,1024]{2,1,0:T(8,128)(2,1)}, u32[]{:S(2)}, u32[]{:S(2)}) collective-permute-start(bf16[1,704,1024]{2,1,0:T(8,128)(2,1)} %param.23), channel_id=1, source_target_pairs={{0,16},{16,0},{1,17},{17,1},{2,18},{18,2},{3,19},{19,3},{4,20},{20... | collective-permute-start | bytes 4325384 | tf_op jit(solution)/shard_map/ppermute | solution.py:29
  9.3 92.1 %collective-permute-start.6 = (bf16[1,1024,1408]{2,1,0:T(8,128)(2,1)}, bf16[1,1024,1408]{2,1,0:T(8,128)(2,1)}, u32[]{:S(2)}, u32[]{:S(2)}) collective-permute-start(bf16[1,1024,1408]{2,1,0:T(8,128)(2,1)} %param.22), channel_id=1, source_target_pairs={{0,16},{16,0},{1,17},{17,1},{2,18},{18,2},{3,19},{19,3},{4,20},{20... | collective-permute-start | bytes 8650760 | tf_op jit(solution)/shard_map/ppermute | solution.py:29
  19.6 13.2 %collective-permute-start.2 = (bf16[2,1024,128]{2,1,0:T(8,128)(2,1)S(1)}, bf16[2,1024,128]{2,1,0:T(8,128)(2,1)S(1)}, u32[]{:S(2)}, u32[]{:S(2)}) collective-permute-start(bf16[2,1024,128]{2,1,0:T(8,128)(2,1)S(1)} %pad_maximum_fusion.3), channel_id=1, source_target_pairs={{0,4},{1,5},{2,6},{3,7},{4,0},{5,1},{6,2},{7,3},{8,12},{9,13},{10,... | collective-permute-start | bytes 1572872 | tf_op jit(solution)/shard_map/ppermute | solution.py:112
  21.1 13.4 %copy-start.7 = (s32[2]{0:T(128)S(1)}, s32[2]{0:T(128)}, u32[]{:S(2)}) copy-start(s32[2]{0:T(128)} %param.16) | copy-start | bytes 28
  21.1 14.1 %copy-start.8 = (s32[1,16]{1,0:T(1,128)S(1)}, s32[1,16]{1,0:T(1,128)}, u32[]{:S(2)}) copy-start(s32[1,16]{1,0:T(1,128)} %param.17) | copy-start | bytes 196
  21.1 45.4 %all-to-all-start = ((bf16[16,224,128]{2,1,0:T(8,128)(2,1)}), bf16[16,224,128]{2,1,0:T(8,128)(2,1)S(1)}, u32[]{:S(2)}, u32[]{:S(2)}) async-start(bf16[16,224,128]{2,1,0:T(8,128)(2,1)} %pad_maximum_fusion.2), calls=%async_computation | async-start | bytes 1835008 | tf_op jit(solution)/shard_map/all_to_all | solution.py:88
  34.0 28.8 %collective-permute-start.3 = (bf16[4,1024,128]{2,1,0:T(8,128)(2,1)}, bf16[4,1024,128]{2,1,0:T(8,128)(2,1)S(1)}, u32[]{:S(2)}, u32[]{:S(2)}) collective-permute-start(bf16[4,1024,128]{2,1,0:T(8,128)(2,1)} %pad_maximum_fusion.1), channel_id=1, source_target_pairs={{0,2},{1,3},{2,0},{3,1},{4,6},{5,7},{6,4},{7,5},{8,10},{9,11},{10,... | collective-permute-start | bytes 3145736 | tf_op jit(solution)/shard_map/ppermute | solution.py:112
  63.2 21.1 %collective-permute-start.4 = (bf16[8,1024,128]{2,1,0:T(8,128)(2,1)S(1)}, bf16[8,1024,128]{2,1,0:T(8,128)(2,1)}, u32[]{:S(2)}, u32[]{:S(2)}) collective-permute-start(bf16[8,1024,128]{2,1,0:T(8,128)(2,1)S(1)} %pad_maximum_fusion), channel_id=1, source_target_pairs={{0,1},{1,0},{2,3},{3,2},{4,5},{5,4},{6,7},{7,6},{8,9},{9,8},{10,11... | collective-permute-start | bytes 6291464 | tf_op jit(solution)/shard_map/ppermute | solution.py:117
  68.8 9.7 %copy-start.4 = (s32[64,6]{0,1:T(8,128)S(1)}, s32[64,6]{0,1:T(8,128)}, u32[]{:S(2)}) copy-start(s32[64,6]{0,1:T(8,128)} %param.20) | copy-start | bytes 4612
  70.2 13.4 %all-to-all-start.1 = ((bf16[16,32,128]{2,1,0:T(8,128)(2,1)}), bf16[16,32,128]{2,1,0:T(8,128)(2,1)S(1)}, u32[]{:S(2)}, u32[]{:S(2)}) async-start(bf16[16,32,128]{2,1,0:T(8,128)(2,1)} %bitcast.13), calls=%async_computation.1 | async-start | bytes 262144 | tf_op jit(solution)/shard_map/all_to_all | solution.py:106
  84.3 3.0 %copy-start.3 = (bf16[64,2048]{1,0:T(8,128)(2,1)S(1)}, bf16[64,2048]{1,0:T(8,128)(2,1)}, u32[]{:S(2)}) copy-start(bf16[64,2048]{1,0:T(8,128)(2,1)} %param.13) | copy-start | bytes 786436
  84.3 3.2 %copy-start.5 = (f32[2048]{0:T(1024)S(1)}, f32[2048]{0:T(1024)}, u32[]{:S(2)}) copy-start(f32[2048]{0:T(1024)} %param.19) | copy-start | bytes 24580
  87.7 13.7 %copy-start.1 = (bf16[1,1024,1408]{2,1,0:T(8,128)(2,1)S(1)}, bf16[1,1024,1408]{2,1,0:T(8,128)(2,1)}, u32[]{:S(2)}) copy-start(bf16[1,1024,1408]{2,1,0:T(8,128)(2,1)} %param.22) | copy-start | bytes 8650756
  89.8 54.6 %all-to-all-start.2 = ((bf16[16,32,2048]{2,1,0:T(8,128)(2,1)}), bf16[16,32,2048]{2,1,0:T(8,128)(2,1)}, u32[]{:S(2)}, u32[]{:S(2)}) async-start(bf16[16,32,2048]{2,1,0:T(8,128)(2,1)} %bitcast.19), calls=%async_computation.2 | async-start | bytes 4194304 | tf_op jit(solution)/shard_map/all_to_all | solution.py:158
  101.4 7.5 %copy-start.2 = (bf16[1,704,1024]{2,1,0:T(8,128)(2,1)S(1)}, bf16[1,704,1024]{2,1,0:T(8,128)(2,1)}, u32[]{:S(2)}) copy-start(bf16[1,704,1024]{2,1,0:T(8,128)(2,1)} %param.23) | copy-start | bytes 4325380
  154.0 5.0 %copy-start.6 = (f32[64,6]{0,1:T(8,128)S(1)}, f32[64,6]{0,1:T(8,128)}, u32[]{:S(2)}) copy-start(f32[64,6]{0,1:T(8,128)} %param.21) | copy-start | bytes 4612
  154.0 52.4 %all-to-all-start.3 = ((bf16[16,32,2048]{2,1,0:T(8,128)(2,1)}), bf16[16,32,2048]{2,1,0:T(8,128)(2,1)S(1)}, u32[]{:S(2)}, u32[]{:S(2)}) async-start(bf16[16,32,2048]{2,1,0:T(8,128)(2,1)} %bitcast.71), calls=%async_computation.3 | async-start | bytes 4194304 | tf_op jit(solution)/shard_map/all_to_all | solution.py:181

commit v17 on v16

--- a/solution.py
+++ b/solution.py
@@ -77,8 +77,7 @@
     kv_send = jnp.concatenate([q_out, kv_out], axis=1)
     if n_mp == 1 << bits:
         block = wo_rows[None]
-        if bits > 1:
-            b = bits - 1
+        for b in reversed(range(max(1, bits - 2), bits)):
             pair = lax.ppermute(block, "mp", [(m, m ^ (1 << b)) for m in range(n_mp)])
             low = (column >> b) % 2 == 0
             block = jnp.concatenate(
@@ -108,7 +107,7 @@
 
     bits = n_mp.bit_length() - 1
     if n_mp == 1 << bits:
-        for b in reversed(range(1, bits - 1)):
+        for b in reversed(range(1, max(1, bits - 2))):
             pair = lax.ppermute(block, "mp", [(m, m ^ (1 << b)) for m in range(n_mp)])
             low = (column >> b) % 2 == 0
             block = jnp.concatenate(

time: 209 us -> 209 us (level)
    ppermute x3, waiting for transfers between devices: 35.8 us -> 38.1 us  [on_device(): pair = lax.ppermute(block, 'mp', [(m, m ^ 1 << b) for m in range(n_mp)])]
  transfers between devices with their start and end apart: 11 -> 11, of which waited for: 8 -> 8; matrix products, arithmetic and copies ran while one was open for 14% -> 13% of each run, Pallas kernels for 0% -> 0%
where the time goes in v17:
time: 209 us
  waiting for transfers between devices  131 us (63%)
  starting transfers between devices  37.5 us (18%)
  matrix products  18.3 us (9%)
  other arithmetic  16 us (8%)
  local copies, waits for them, and re-layouts  5.42 us (3%)
    all_to_all x1, waiting for transfers between devices, on_device(): lax.all_to_all(outcome.reshape(n_mp, capacity, d_model), 'mp', split_axis...  47.2 us
    ppermute x3, waiting for transfers between devices, on_device(): pair = lax.ppermute(block, 'mp', [(m, m ^ 1 << b) for m in range(n_mp)])  38.1 us
    all_to_all x1, waiting for transfers between devices, on_device(): lax.all_to_all(sending.reshape(n_mp, capacity, d_model), 'mp', split_axis...  33.2 us
    all_to_all x1, starting transfers between devices, on_device(): lax.all_to_all(kv_send, 'mp', split_axis=0, concat_axis=0, tiled=True)  8.21 us
    ppermute x3, waiting for transfers between devices, swap_dp(): return lax.ppermute(x, 'dp', [(0, 1), (1, 0)])  7.54 us
    select_n x1, other arithmetic, on_device(): jnp.where(first, jnp.concatenate([experts_in[0], in_other[0]], axis=0), j...  7.48 us
    all_to_all x1, starting transfers between devices, on_device(): lax.all_to_all(blended.reshape(n_mp, sub, HD), 'mp', split_axis=0, concat...  7.09 us
    all_to_all x1, starting transfers between devices, on_device(): lax.all_to_all(sending.reshape(n_mp, capacity, d_model), 'mp', split_axis...  7.07 us
  transfers between devices with their start and end apart: 11, of which 8 were waited for; matrix products, arithmetic and copies ran while one was open for 13% of the time, Pallas kernels for 0%

profile of v17, /device:TPU:11, one launch (start us, length us, event | category | flops | bytes accessed | tf_op | source)
XLA Modules:
  0.0 208.8 jit_solution(1804830227500591185)
XLA Ops:
  0.0 1.3 collective-permute-start
  1.3 3.3 %collective-permute-done = bf16[512,128]{1,0:T(8,128)(2,1)S(1)} collective-permute-done((bf16[512,128]{1,0:T(8,128)(2,1)}, bf16[512,128]{1,0:T(8,128)(2,1)S(1)}, u32[]{:S(2)}, u32[]{:S(2)}) %collective-permute-start) | collective-permute-done | bytes 131104 | tf_op jit(solution)/shard_map/ppermute | solution.py:29
  4.7 1.1 maximum_select_fusion.3
  5.7 2.4 %collective-permute-start.1 = (bf16[1,1024,128]{2,1,0:T(8,128)(2,1)S(1)}, bf16[1,1024,128]{2,1,0:T(8,128)(2,1)S(1)}, u32[]{:S(2)}, u32[]{:S(2)}) collective-permute-start(bf16[1,1024,128]{2,1,0:T(8,128)(2,1)S(1)} %maximum_select_fusion.3), channel_id=1, source_target_pairs={{0,8},{1,9},{2,10},{3,11},{4,12},{5,13},{6,14},{7,15},{8,0},{9,1},... | collective-permute-start | bytes 786440 | tf_op jit(solution)/shard_map/ppermute | solution.py:81
  8.1 1.2 collective-permute-start.5
  9.3 0.2 collective-permute-start.6
  9.6 0.8 copy.72
  10.5 0.9 reduce-window.6
  11.4 8.3 %collective-permute-done.1 = bf16[1,1024,128]{2,1,0:T(8,128)(2,1)S(1)} collective-permute-done((bf16[1,1024,128]{2,1,0:T(8,128)(2,1)S(1)}, bf16[1,1024,128]{2,1,0:T(8,128)(2,1)S(1)}, u32[]{:S(2)}, u32[]{:S(2)}) %collective-permute-start.1) | collective-permute-done | bytes 262176 | tf_op jit(solution)/shard_map/ppermute | solution.py:81
  19.8 0.2 slice_reduce_fusion
  20.2 0.3 reshape.227
  20.4 0.3 copy.66
  21.0 0.6 tile.8
  21.6 1.0 pad_maximum_fusion.2
  22.6 10.3 %collective-permute-done.2 = bf16[2,1024,128]{2,1,0:T(8,128)(2,1)S(1)} collective-permute-done((bf16[2,1024,128]{2,1,0:T(8,128)(2,1)S(1)}, bf16[2,1024,128]{2,1,0:T(8,128)(2,1)S(1)}, u32[]{:S(2)}, u32[]{:S(2)}) %collective-permute-start.2) | collective-permute-done | bytes 524320 | tf_op jit(solution)/shard_map/ppermute | solution.py:81
  33.1 0.3 collective-permute-start.3
  33.4 0.2 select_reduce_fusion.1
  33.6 0.6 dynamic_slice.7
  34.2 8.2 %all-to-all-start = ((bf16[16,224,128]{2,1,0:T(8,128)(2,1)}), bf16[16,224,128]{2,1,0:T(8,128)(2,1)S(1)}, u32[]{:S(2)}, u32[]{:S(2)}) async-start(bf16[16,224,128]{2,1,0:T(8,128)(2,1)} %pad_maximum_fusion.2), calls=%async_computation | async-start | bytes 1835008 | tf_op jit(solution)/shard_map/all_to_all | solution.py:87
  42.4 0.7 fusion.19
  43.2 19.6 %collective-permute-done.3 = bf16[4,1024,128]{2,1,0:T(8,128)(2,1)S(1)} collective-permute-done((bf16[4,1024,128]{2,1,0:T(8,128)(2,1)S(1)}, bf16[4,1024,128]{2,1,0:T(8,128)(2,1)S(1)}, u32[]{:S(2)}, u32[]{:S(2)}) %collective-permute-start.3) | collective-permute-done | bytes 1048608 | tf_op jit(solution)/shard_map/ppermute | solution.py:111
  62.9 0.2 pad_maximum_fusion
  63.1 4.6 %collective-permute-start.4 = (bf16[8,1024,128]{2,1,0:T(8,128)(2,1)S(1)}, bf16[8,1024,128]{2,1,0:T(8,128)(2,1)}, u32[]{:S(2)}, u32[]{:S(2)}) collective-permute-start(bf16[8,1024,128]{2,1,0:T(8,128)(2,1)S(1)} %pad_maximum_fusion), channel_id=1, source_target_pairs={{0,1},{1,0},{2,3},{3,2},{4,5},{5,4},{6,7},{7,6},{8,9},{9,8},{10,11... | collective-permute-start | bytes 6291464 | tf_op jit(solution)/shard_map/ppermute | solution.py:116
  68.2 0.5 copy.67
  68.7 0.2 fusion.22
  69.1 0.7 fusion.23
  69.9 0.6 fusion.1
  70.4 1.4 fusion.5
  71.8 7.1 %all-to-all-start.1 = ((bf16[16,32,128]{2,1,0:T(8,128)(2,1)}), bf16[16,32,128]{2,1,0:T(8,128)(2,1)S(1)}, u32[]{:S(2)}, u32[]{:S(2)}) async-start(bf16[16,32,128]{2,1,0:T(8,128)(2,1)} %bitcast.13), calls=%async_computation.1 | async-start | bytes 262144 | tf_op jit(solution)/shard_map/all_to_all | solution.py:105
  78.9 0.2 fusion.8
  79.1 5.0 %all-to-all-done.1 = bf16[16,32,128]{2,1,0:T(8,128)(2,1)S(1)} async-done(((bf16[16,32,128]{2,1,0:T(8,128)(2,1)}), bf16[16,32,128]{2,1,0:T(8,128)(2,1)S(1)}, u32[]{:S(2)}, u32[]{:S(2)}) %all-to-all-start.1) | async-done | bytes 131104 | tf_op jit(solution)/shard_map/all_to_all | solution.py:105
  84.2 0.5 fusion.24
  84.7 2.1 %fusion.25 = f32[64,8,128]{2,0,1:T(8,128)S(1)} fusion(bf16[64,1024,1]{1,0,2:T(8,128)(2,1)S(1)} %reshape.239, bf16[8,1024,128]{2,1,0:T(8,128)(2,1)} %collective-permute-done.4), kind=kOutput, calls=%fused_computation.73 | convolution fusion | flops 134217728 | bytes 2490368 | tf_op jit(solution)/shard_map/tk,jkc->tjc/dot_general | solution.py:118
  86.9 0.4 copy.71
  87.3 0.4 reshape.233
  87.7 0.2 fusion.9
  88.1 2.1 convolution_convert_fusion.1
  90.2 7.1 %all-to-all-start.2 = ((bf16[16,32,2048]{2,1,0:T(8,128)(2,1)}), bf16[16,32,2048]{2,1,0:T(8,128)(2,1)}, u32[]{:S(2)}, u32[]{:S(2)}) async-start(bf16[16,32,2048]{2,1,0:T(8,128)(2,1)} %bitcast.19), calls=%async_computation.2 | async-start | bytes 4194304 | tf_op jit(solution)/shard_map/all_to_all | solution.py:157
  97.2 4.2 %collective-permute-done.6 = bf16[1,1024,1408]{2,1,0:T(8,128)(2,1)} collective-permute-done((bf16[1,1024,1408]{2,1,0:T(8,128)(2,1)}, bf16[1,1024,1408]{2,1,0:T(8,128)(2,1)}, u32[]{:S(2)}, u32[]{:S(2)}) %collective-permute-start.6) | collective-permute-done | bytes 2883616 | tf_op jit(solution)/shard_map/ppermute | solution.py:29
  101.5 7.5 %maximum_select_fusion = bf16[2048,1408]{1,0:T(8,128)(2,1)} fusion(bf16[1024,1408]{1,0:T(8,128)(2,1)} %bitcast.24, bf16[1024,1408]{1,0:T(8,128)(2,1)S(1)} %bitcast.70, pred[]{:T(512)S(6)} %eq.85), kind=kLoop, calls=%fused_computation | loop fusion | flops 25952256 | bytes 11534337 | tf_op jit(solution)/shard_map/jit(_where)/select_n | solution.py:163
  108.9 2.6 %maximum_select_fusion.1 = bf16[704,2048]{1,0:T(8,128)(2,1)S(1)} fusion(bf16[704,1024]{1,0:T(8,128)(2,1)} %bitcast.22, bf16[704,1024]{1,0:T(8,128)(2,1)S(1)} %bitcast.74, pred[]{:T(512)S(6)} %eq.85), kind=kLoop, calls=%fused_computation.7 | loop fusion | flops 12976128 | bytes 5767169 | tf_op jit(solution)/shard_map/jit(_where)/select_n | solution.py:168
  111.6 33.2 %all-to-all-done.2 = bf16[16,32,2048]{2,1,0:T(8,128)(2,1)} async-done(((bf16[16,32,2048]{2,1,0:T(8,128)(2,1)}), bf16[16,32,2048]{2,1,0:T(8,128)(2,1)}, u32[]{:S(2)}, u32[]{:S(2)}) %all-to-all-start.2) | async-done | bytes 2097184 | tf_op jit(solution)/shard_map/all_to_all | solution.py:157
  144.8 6.4 %fusion.26 = f32[512,1408]{1,0:T(8,128)S(1)} fusion(bf16[512,2048]{1,0:T(8,128)(2,1)} %bitcast.20, bf16[2048,1408]{1,0:T(8,128)(2,1)} %maximum_select_fusion), kind=kOutput, calls=%fused_computation.74 | convolution fusion | flops 2952790016 | bytes 10747904 | tf_op jit(solution)/shard_map/dot_general | solution.py:177
  151.2 3.3 %convolution_convert_fusion = bf16[512,2048]{1,0:T(8,128)(2,1)} fusion(bf16[704,2048]{1,0:T(8,128)(2,1)S(1)} %maximum_select_fusion.1, f32[512,1408]{1,0:T(8,128)S(1)} %fusion.26), kind=kOutput, calls=%fused_computation.5 | convolution fusion | flops 1479606272 | bytes 8126464 | tf_op jit(solution)/shard_map/dot_general | solution.py:179
  154.4 5.0 %all-to-all-start.3 = ((bf16[16,32,2048]{2,1,0:T(8,128)(2,1)}), bf16[16,32,2048]{2,1,0:T(8,128)(2,1)S(1)}, u32[]{:S(2)}, u32[]{:S(2)}) async-start(bf16[16,32,2048]{2,1,0:T(8,128)(2,1)} %bitcast.71), calls=%async_computation.3 | async-start | bytes 4194304 | tf_op jit(solution)/shard_map/all_to_all | solution.py:180
  159.5 0.2 select_reduce_fusion
  159.6 47.2 %all-to-all-done.3 = bf16[16,32,2048]{2,1,0:T(8,128)(2,1)S(1)} async-done(((bf16[16,32,2048]{2,1,0:T(8,128)(2,1)}), bf16[16,32,2048]{2,1,0:T(8,128)(2,1)S(1)}, u32[]{:S(2)}, u32[]{:S(2)}) %all-to-all-start.3) | async-done | bytes 2097184 | tf_op jit(solution)/shard_map/all_to_all | solution.py:180
  206.9 1.9 fusion.2
  (59 shorter events, 2.1 us)
Async XLA Ops:
  0.0 20.9 %copy-start = (s32[2,96]{1,0:T(2,128)S(1)}, s32[2,96]{1,0:T(2,128)}, u32[]{:S(2)}) copy-start(s32[2,96]{1,0:T(2,128)} %param.15) | copy-start | bytes 2308
  0.0 20.2 %copy-start.3 = (bf16[6,16,2,1024]{3,2,1,0:T(2,128)(2,1)S(1)}, bf16[6,16,2,1024]{3,2,1,0:T(2,128)(2,1)}, u32[]{:S(2)}) copy-start(bf16[6,16,2,1024]{3,2,1,0:T(2,128)(2,1)} %param.14) | copy-start | bytes 1179652
  0.0 20.7 %copy-start.5 = (bf16[64,1024]{1,0:T(8,128)(2,1)S(1)}, bf16[64,1024]{1,0:T(8,128)(2,1)}, u32[]{:S(2)}) copy-start(bf16[64,1024]{1,0:T(8,128)(2,1)} %param.12) | copy-start | bytes 393220
  0.0 4.6 %collective-permute-start = (bf16[512,128]{1,0:T(8,128)(2,1)}, bf16[512,128]{1,0:T(8,128)(2,1)S(1)}, u32[]{:S(2)}, u32[]{:S(2)}) collective-permute-start(bf16[512,128]{1,0:T(8,128)(2,1)} %param.18), channel_id=1, source_target_pairs={{0,16},{16,0},{1,17},{17,1},{2,18},{18,2},{3,19},{19,3},{4,20},{20... | collective-permute-start | bytes 393224 | tf_op jit(solution)/shard_map/ppermute | solution.py:29
  5.7 13.9 %collective-permute-start.1 = (bf16[1,1024,128]{2,1,0:T(8,128)(2,1)S(1)}, bf16[1,1024,128]{2,1,0:T(8,128)(2,1)S(1)}, u32[]{:S(2)}, u32[]{:S(2)}) collective-permute-start(bf16[1,1024,128]{2,1,0:T(8,128)(2,1)S(1)} %maximum_select_fusion.3), channel_id=1, source_target_pairs={{0,8},{1,9},{2,10},{3,11},{4,12},{5,13},{6,14},{7,15},{8,0},{9,1},... | collective-permute-start | bytes 786440 | tf_op jit(solution)/shard_map/ppermute | solution.py:81
  8.1 80.0 %collective-permute-start.5 = (bf16[1,704,1024]{2,1,0:T(8,128)(2,1)}, bf16[1,704,1024]{2,1,0:T(8,128)(2,1)}, u32[]{:S(2)}, u32[]{:S(2)}) collective-permute-start(bf16[1,704,1024]{2,1,0:T(8,128)(2,1)} %param.23), channel_id=1, source_target_pairs={{0,16},{16,0},{1,17},{17,1},{2,18},{18,2},{3,19},{19,3},{4,20},{20... | collective-permute-start | bytes 4325384 | tf_op jit(solution)/shard_map/ppermute | solution.py:29
  9.3 92.1 %collective-permute-start.6 = (bf16[1,1024,1408]{2,1,0:T(8,128)(2,1)}, bf16[1,1024,1408]{2,1,0:T(8,128)(2,1)}, u32[]{:S(2)}, u32[]{:S(2)}) collective-permute-start(bf16[1,1024,1408]{2,1,0:T(8,128)(2,1)} %param.22), channel_id=1, source_target_pairs={{0,16},{16,0},{1,17},{17,1},{2,18},{18,2},{3,19},{19,3},{4,20},{20... | collective-permute-start | bytes 8650760 | tf_op jit(solution)/shard_map/ppermute | solution.py:29
  19.7 13.2 %collective-permute-start.2 = (bf16[2,1024,128]{2,1,0:T(8,128)(2,1)S(1)}, bf16[2,1024,128]{2,1,0:T(8,128)(2,1)S(1)}, u32[]{:S(2)}, u32[]{:S(2)}) collective-permute-start(bf16[2,1024,128]{2,1,0:T(8,128)(2,1)S(1)} %pad_maximum_fusion.3), channel_id=1, source_target_pairs={{0,4},{1,5},{2,6},{3,7},{4,0},{5,1},{6,2},{7,3},{8,12},{9,13},{10,... | collective-permute-start | bytes 1572872 | tf_op jit(solution)/shard_map/ppermute | solution.py:81
  21.6 12.0 %copy-start.9 = (s32[2]{0:T(128)S(1)}, s32[2]{0:T(128)}, u32[]{:S(2)}) copy-start(s32[2]{0:T(128)} %param.16) | copy-start | bytes 28
  22.6 19.8 %copy-start.10 = (s32[1,16]{1,0:T(1,128)S(1)}, s32[1,16]{1,0:T(1,128)}, u32[]{:S(2)}) copy-start(s32[1,16]{1,0:T(1,128)} %param.17) | copy-start | bytes 196
  33.1 29.7 %collective-permute-start.3 = (bf16[4,1024,128]{2,1,0:T(8,128)(2,1)S(1)}, bf16[4,1024,128]{2,1,0:T(8,128)(2,1)S(1)}, u32[]{:S(2)}, u32[]{:S(2)}) collective-permute-start(bf16[4,1024,128]{2,1,0:T(8,128)(2,1)S(1)} %pad_maximum_fusion.1), channel_id=1, source_target_pairs={{0,2},{1,3},{2,0},{3,1},{4,6},{5,7},{6,4},{7,5},{8,10},{9,11},{10,... | collective-permute-start | bytes 3145736 | tf_op jit(solution)/shard_map/ppermute | solution.py:111
  34.2 33.9 %all-to-all-start = ((bf16[16,224,128]{2,1,0:T(8,128)(2,1)}), bf16[16,224,128]{2,1,0:T(8,128)(2,1)S(1)}, u32[]{:S(2)}, u32[]{:S(2)}) async-start(bf16[16,224,128]{2,1,0:T(8,128)(2,1)} %pad_maximum_fusion.2), calls=%async_computation | async-start | bytes 1835008 | tf_op jit(solution)/shard_map/all_to_all | solution.py:87
  63.1 21.6 %collective-permute-start.4 = (bf16[8,1024,128]{2,1,0:T(8,128)(2,1)S(1)}, bf16[8,1024,128]{2,1,0:T(8,128)(2,1)}, u32[]{:S(2)}, u32[]{:S(2)}) collective-permute-start(bf16[8,1024,128]{2,1,0:T(8,128)(2,1)S(1)} %pad_maximum_fusion), channel_id=1, source_target_pairs={{0,1},{1,0},{2,3},{3,2},{4,5},{5,4},{6,7},{7,6},{8,9},{9,8},{10,11... | collective-permute-start | bytes 6291464 | tf_op jit(solution)/shard_map/ppermute | solution.py:116
  70.4 8.5 %copy-start.6 = (s32[64,6]{0,1:T(8,128)S(1)}, s32[64,6]{0,1:T(8,128)}, u32[]{:S(2)}) copy-start(s32[64,6]{0,1:T(8,128)} %param.20) | copy-start | bytes 4612
  71.8 12.3 %all-to-all-start.1 = ((bf16[16,32,128]{2,1,0:T(8,128)(2,1)}), bf16[16,32,128]{2,1,0:T(8,128)(2,1)S(1)}, u32[]{:S(2)}, u32[]{:S(2)}) async-start(bf16[16,32,128]{2,1,0:T(8,128)(2,1)} %bitcast.13), calls=%async_computation.1 | async-start | bytes 262144 | tf_op jit(solution)/shard_map/all_to_all | solution.py:105
  84.7 3.0 %copy-start.4 = (bf16[64,2048]{1,0:T(8,128)(2,1)S(1)}, bf16[64,2048]{1,0:T(8,128)(2,1)}, u32[]{:S(2)}) copy-start(bf16[64,2048]{1,0:T(8,128)(2,1)} %param.13) | copy-start | bytes 786436
  84.7 3.2 %copy-start.7 = (f32[2048]{0:T(1024)S(1)}, f32[2048]{0:T(1024)}, u32[]{:S(2)}) copy-start(f32[2048]{0:T(1024)} %param.19) | copy-start | bytes 24580
  88.1 13.4 %copy-start.1 = (bf16[1,1024,1408]{2,1,0:T(8,128)(2,1)S(1)}, bf16[1,1024,1408]{2,1,0:T(8,128)(2,1)}, u32[]{:S(2)}) copy-start(bf16[1,1024,1408]{2,1,0:T(8,128)(2,1)} %param.22) | copy-start | bytes 8650756
  90.2 54.6 %all-to-all-start.2 = ((bf16[16,32,2048]{2,1,0:T(8,128)(2,1)}), bf16[16,32,2048]{2,1,0:T(8,128)(2,1)}, u32[]{:S(2)}, u32[]{:S(2)}) async-start(bf16[16,32,2048]{2,1,0:T(8,128)(2,1)} %bitcast.19), calls=%async_computation.2 | async-start | bytes 4194304 | tf_op jit(solution)/shard_map/all_to_all | solution.py:157
  101.5 7.5 %copy-start.2 = (bf16[1,704,1024]{2,1,0:T(8,128)(2,1)S(1)}, bf16[1,704,1024]{2,1,0:T(8,128)(2,1)}, u32[]{:S(2)}) copy-start(bf16[1,704,1024]{2,1,0:T(8,128)(2,1)} %param.23) | copy-start | bytes 4325380
  154.4 5.0 %copy-start.8 = (f32[64,6]{0,1:T(8,128)S(1)}, f32[64,6]{0,1:T(8,128)}, u32[]{:S(2)}) copy-start(f32[64,6]{0,1:T(8,128)} %param.21) | copy-start | bytes 4612
  154.4 52.4 %all-to-all-start.3 = ((bf16[16,32,2048]{2,1,0:T(8,128)(2,1)}), bf16[16,32,2048]{2,1,0:T(8,128)(2,1)S(1)}, u32[]{:S(2)}, u32[]{:S(2)}) async-start(bf16[16,32,2048]{2,1,0:T(8,128)(2,1)} %bitcast.71), calls=%async_computation.3 | async-start | bytes 4194304 | tf_op jit(solution)/shard_map/all_to_all | solution.py:180

commit v18 on v16

--- a/solution.py
+++ b/solution.py
@@ -181,11 +181,11 @@
     results = lax.all_to_all(
         outcome.reshape(n_mp, capacity, d_model), "mp", split_axis=0, concat_axis=0, tiled=True
     )
-    expert_sum = jnp.dot(
-        combine,
-        results.reshape(-1, d_model).astype(jnp.float32),
-        precision=lax.Precision.HIGHEST,
-        preferred_element_type=jnp.float32,
+    comb_hi = combine.astype(jnp.bfloat16)
+    comb_lo = (combine - comb_hi.astype(jnp.float32)).astype(jnp.bfloat16)
+    flat_results = results.reshape(-1, d_model)
+    expert_sum = jnp.dot(comb_hi, flat_results, preferred_element_type=jnp.float32) + jnp.dot(
+        comb_lo, flat_results, preferred_element_type=jnp.float32
     )
     return (resid_f + expert_sum).astype(jnp.bfloat16)
 

time: 209 us -> 209 us (level)
  no operation moved by 1% of the time
where the time goes in v18:
time: 209 us; the launch traced here: 208 us
  waiting for transfers between devices  129 us (62%)
  starting transfers between devices  36.5 us (17%)
  matrix products  18.1 us (9%)
  other arithmetic  17 us (8%)
  local copies, waits for them, and re-layouts  7.32 us (4%)
    all_to_all x1, waiting for transfers between devices, on_device(): lax.all_to_all(outcome.reshape(n_mp, capacity, d_model), 'mp', split_axis...  47.2 us
    ppermute x3, waiting for transfers between devices, on_device(): pair = lax.ppermute(block, 'mp', [(m, m ^ 1 << b) for m in range(n_mp)])  35.8 us
    all_to_all x1, waiting for transfers between devices, on_device(): lax.all_to_all(sending.reshape(n_mp, capacity, d_model), 'mp', split_axis...  32.9 us
    all_to_all x1, starting transfers between devices, on_device(): lax.all_to_all(blended.reshape(n_mp, sub, HD), 'mp', split_axis=0, concat...  8.27 us
    ppermute x3, waiting for transfers between devices, swap_dp(): return lax.ppermute(x, 'dp', [(0, 1), (1, 0)])  7.89 us
    all_to_all x1, starting transfers between devices, on_device(): lax.all_to_all(kv_send, 'mp', split_axis=0, concat_axis=0, tiled=True)  7.82 us
    select_n x1, other arithmetic, on_device(): jnp.where(first, jnp.concatenate([experts_in[0], in_other[0]], axis=0), j...  7.49 us
    all_to_all x1, starting transfers between devices, on_device(): lax.all_to_all(sending.reshape(n_mp, capacity, d_model), 'mp', split_axis...  7.06 us
  transfers between devices with their start and end apart: 11, of which 8 were waited for; matrix products, arithmetic and copies ran while one was open for 14% of the time, Pallas kernels for 0%

profile of v18, /device:TPU:11, one launch (start us, length us, event | category | flops | bytes accessed | tf_op | source)
XLA Modules:
  0.0 208.1 jit_solution(7964058473098763135)
XLA Ops:
  0.0 1.2 collective-permute-start
  1.2 3.3 %collective-permute-done = bf16[512,128]{1,0:T(8,128)(2,1)S(1)} collective-permute-done((bf16[512,128]{1,0:T(8,128)(2,1)}, bf16[512,128]{1,0:T(8,128)(2,1)S(1)}, u32[]{:S(2)}, u32[]{:S(2)}) %collective-permute-start) | collective-permute-done | bytes 131104 | tf_op jit(solution)/shard_map/ppermute | solution.py:29
  4.6 1.1 maximum_select_fusion.3
  5.6 2.4 %collective-permute-start.1 = (bf16[1,1024,128]{2,1,0:T(8,128)(2,1)S(1)}, bf16[1,1024,128]{2,1,0:T(8,128)(2,1)S(1)}, u32[]{:S(2)}, u32[]{:S(2)}) collective-permute-start(bf16[1,1024,128]{2,1,0:T(8,128)(2,1)S(1)} %maximum_select_fusion.3), channel_id=1, source_target_pairs={{0,8},{1,9},{2,10},{3,11},{4,12},{5,13},{6,14},{7,15},{8,0},{9,1},... | collective-permute-start | bytes 786440 | tf_op jit(solution)/shard_map/ppermute | solution.py:82
  8.0 1.2 collective-permute-start.5
  9.3 0.2 collective-permute-start.6
  9.5 1.2 reshape.227
  10.7 0.3 copy.66
  11.0 0.9 copy.77
  12.0 0.8 copy.72
  12.9 0.6 tile.8
  13.5 1.0 pad_maximum_fusion.2
  14.5 5.0 %collective-permute-done.1 = bf16[1,1024,128]{2,1,0:T(8,128)(2,1)S(1)} collective-permute-done((bf16[1,1024,128]{2,1,0:T(8,128)(2,1)S(1)}, bf16[1,1024,128]{2,1,0:T(8,128)(2,1)S(1)}, u32[]{:S(2)}, u32[]{:S(2)}) %collective-permute-start.1) | collective-permute-done | bytes 262176 | tf_op jit(solution)/shard_map/ppermute | solution.py:82
  19.8 0.9 reduce-window.6
  20.7 0.2 slice_reduce_fusion
  21.1 7.8 %all-to-all-start = ((bf16[16,224,128]{2,1,0:T(8,128)(2,1)}), bf16[16,224,128]{2,1,0:T(8,128)(2,1)S(1)}, u32[]{:S(2)}, u32[]{:S(2)}) async-start(bf16[16,224,128]{2,1,0:T(8,128)(2,1)} %pad_maximum_fusion.2), calls=%async_computation | async-start | bytes 1835008 | tf_op jit(solution)/shard_map/all_to_all | solution.py:88
  28.9 3.9 %collective-permute-done.2 = bf16[2,1024,128]{2,1,0:T(8,128)(2,1)S(1)} collective-permute-done((bf16[2,1024,128]{2,1,0:T(8,128)(2,1)S(1)}, bf16[2,1024,128]{2,1,0:T(8,128)(2,1)S(1)}, u32[]{:S(2)}, u32[]{:S(2)}) %collective-permute-start.2) | collective-permute-done | bytes 524320 | tf_op jit(solution)/shard_map/ppermute | solution.py:112
  32.9 1.2 pad_maximum_fusion.1
  34.0 0.3 collective-permute-start.3
  34.5 0.6 dynamic_slice.7
  35.2 0.7 fusion.23
  36.0 26.8 %collective-permute-done.3 = bf16[4,1024,128]{2,1,0:T(8,128)(2,1)S(1)} collective-permute-done((bf16[4,1024,128]{2,1,0:T(8,128)(2,1)}, bf16[4,1024,128]{2,1,0:T(8,128)(2,1)S(1)}, u32[]{:S(2)}, u32[]{:S(2)}) %collective-permute-start.3) | collective-permute-done | bytes 1048608 | tf_op jit(solution)/shard_map/ppermute | solution.py:112
  63.0 0.2 pad_maximum_fusion
  63.2 2.9 %collective-permute-start.4 = (bf16[8,1024,128]{2,1,0:T(8,128)(2,1)S(1)}, bf16[8,1024,128]{2,1,0:T(8,128)(2,1)}, u32[]{:S(2)}, u32[]{:S(2)}) collective-permute-start(bf16[8,1024,128]{2,1,0:T(8,128)(2,1)S(1)} %pad_maximum_fusion), channel_id=1, source_target_pairs={{0,1},{1,0},{2,3},{3,2},{4,5},{5,4},{6,7},{7,6},{8,9},{9,8},{10,11... | collective-permute-start | bytes 6291464 | tf_op jit(solution)/shard_map/ppermute | solution.py:117
  66.6 0.5 copy.67
  67.1 0.2 fusion.26
  67.5 0.7 fusion.27
  68.3 0.6 fusion.1
  68.8 1.4 fusion.6
  70.2 8.3 %all-to-all-start.1 = ((bf16[16,32,128]{2,1,0:T(8,128)(2,1)}), bf16[16,32,128]{2,1,0:T(8,128)(2,1)S(1)}, u32[]{:S(2)}, u32[]{:S(2)}) async-start(bf16[16,32,128]{2,1,0:T(8,128)(2,1)} %bitcast.13), calls=%async_computation.1 | async-start | bytes 262144 | tf_op jit(solution)/shard_map/all_to_all | solution.py:106
  78.7 5.0 %all-to-all-done.1 = bf16[16,32,128]{2,1,0:T(8,128)(2,1)S(1)} async-done(((bf16[16,32,128]{2,1,0:T(8,128)(2,1)}), bf16[16,32,128]{2,1,0:T(8,128)(2,1)S(1)}, u32[]{:S(2)}, u32[]{:S(2)}) %all-to-all-start.1) | async-done | bytes 131104 | tf_op jit(solution)/shard_map/all_to_all | solution.py:106
  83.8 0.5 fusion.28
  84.3 2.1 %fusion.29 = f32[64,8,128]{2,0,1:T(8,128)S(1)} fusion(bf16[64,1024,1]{1,0,2:T(8,128)(2,1)S(1)} %reshape.239, bf16[8,1024,128]{2,1,0:T(8,128)(2,1)} %collective-permute-done.4), kind=kOutput, calls=%fused_computation.78 | convolution fusion | flops 134217728 | bytes 2490368 | tf_op jit(solution)/shard_map/tk,jkc->tjc/dot_general | solution.py:119
  86.5 0.4 copy.71
  86.9 0.4 reshape.233
  87.3 0.2 fusion.10
  87.7 2.1 %convolution_convert_fusion.1 = bf16[512,2048]{1,0:T(8,128)(2,1)} fusion(pred[64,512]{1,0:T(8,128)(4,1)S(1)} %fusion.9, bf16[64,2048]{1,0:T(8,128)(2,1)S(1)} %fusion.12), kind=kOutput, calls=%fused_computation.6 | convolution fusion | flops 135266304 | bytes 2392064 | tf_op jit(solution)/shard_map/dot_general | solution.py:155
  89.8 7.1 %all-to-all-start.2 = ((bf16[16,32,2048]{2,1,0:T(8,128)(2,1)}), bf16[16,32,2048]{2,1,0:T(8,128)(2,1)}, u32[]{:S(2)}, u32[]{:S(2)}) async-start(bf16[16,32,2048]{2,1,0:T(8,128)(2,1)} %bitcast.19), calls=%async_computation.2 | async-start | bytes 4194304 | tf_op jit(solution)/shard_map/all_to_all | solution.py:158
  96.8 4.5 %collective-permute-done.6 = bf16[1,1024,1408]{2,1,0:T(8,128)(2,1)} collective-permute-done((bf16[1,1024,1408]{2,1,0:T(8,128)(2,1)}, bf16[1,1024,1408]{2,1,0:T(8,128)(2,1)}, u32[]{:S(2)}, u32[]{:S(2)}) %collective-permute-start.6) | collective-permute-done | bytes 2883616 | tf_op jit(solution)/shard_map/ppermute | solution.py:29
  101.4 7.5 %maximum_select_fusion = bf16[2048,1408]{1,0:T(8,128)(2,1)} fusion(bf16[1024,1408]{1,0:T(8,128)(2,1)} %bitcast.24, bf16[1024,1408]{1,0:T(8,128)(2,1)S(1)} %bitcast.71, pred[]{:T(512)S(6)} %eq.84), kind=kLoop, calls=%fused_computation | loop fusion | flops 25952256 | bytes 11534337 | tf_op jit(solution)/shard_map/jit(_where)/select_n | solution.py:164
  108.9 2.6 %maximum_select_fusion.1 = bf16[704,2048]{1,0:T(8,128)(2,1)S(1)} fusion(bf16[704,1024]{1,0:T(8,128)(2,1)} %bitcast.22, bf16[704,1024]{1,0:T(8,128)(2,1)S(1)} %bitcast.75, pred[]{:T(512)S(6)} %eq.84), kind=kLoop, calls=%fused_computation.7 | loop fusion | flops 12976128 | bytes 5767169 | tf_op jit(solution)/shard_map/jit(_where)/select_n | solution.py:169
  111.5 32.9 %all-to-all-done.2 = bf16[16,32,2048]{2,1,0:T(8,128)(2,1)} async-done(((bf16[16,32,2048]{2,1,0:T(8,128)(2,1)}), bf16[16,32,2048]{2,1,0:T(8,128)(2,1)}, u32[]{:S(2)}, u32[]{:S(2)}) %all-to-all-start.2) | async-done | bytes 2097184 | tf_op jit(solution)/shard_map/all_to_all | solution.py:158
  144.4 6.4 %fusion.30 = f32[512,1408]{1,0:T(8,128)S(1)} fusion(bf16[512,2048]{1,0:T(8,128)(2,1)} %bitcast.20, bf16[2048,1408]{1,0:T(8,128)(2,1)} %maximum_select_fusion), kind=kOutput, calls=%fused_computation.79 | convolution fusion | flops 2952790016 | bytes 10747904 | tf_op jit(solution)/shard_map/dot_general | solution.py:178
  150.8 3.3 %convolution_convert_fusion = bf16[512,2048]{1,0:T(8,128)(2,1)} fusion(bf16[704,2048]{1,0:T(8,128)(2,1)S(1)} %maximum_select_fusion.1, f32[512,1408]{1,0:T(8,128)S(1)} %fusion.30), kind=kOutput, calls=%fused_computation.5 | convolution fusion | flops 1479606272 | bytes 8126464 | tf_op jit(solution)/shard_map/dot_general | solution.py:180
  154.0 5.0 %all-to-all-start.3 = ((bf16[16,32,2048]{2,1,0:T(8,128)(2,1)}), bf16[16,32,2048]{2,1,0:T(8,128)(2,1)S(1)}, u32[]{:S(2)}, u32[]{:S(2)}) async-start(bf16[16,32,2048]{2,1,0:T(8,128)(2,1)} %bitcast.72), calls=%async_computation.3 | async-start | bytes 4194304 | tf_op jit(solution)/shard_map/all_to_all | solution.py:181
  159.2 47.2 %all-to-all-done.3 = bf16[16,32,2048]{2,1,0:T(8,128)(2,1)S(1)} async-done(((bf16[16,32,2048]{2,1,0:T(8,128)(2,1)}), bf16[16,32,2048]{2,1,0:T(8,128)(2,1)S(1)}, u32[]{:S(2)}, u32[]{:S(2)}) %all-to-all-start.3) | async-done | bytes 2097184 | tf_op jit(solution)/shard_map/all_to_all | solution.py:181
  206.5 0.5 fusion.14
  206.9 1.2 fusion.3
  (56 shorter events, 2.5 us)
Async XLA Ops:
  0.0 20.6 %copy-start = (s32[2,96]{1,0:T(2,128)S(1)}, s32[2,96]{1,0:T(2,128)}, u32[]{:S(2)}) copy-start(s32[2,96]{1,0:T(2,128)} %param.15) | copy-start | bytes 2308
  0.0 4.6 %collective-permute-start = (bf16[512,128]{1,0:T(8,128)(2,1)}, bf16[512,128]{1,0:T(8,128)(2,1)S(1)}, u32[]{:S(2)}, u32[]{:S(2)}) collective-permute-start(bf16[512,128]{1,0:T(8,128)(2,1)} %param.18), channel_id=1, source_target_pairs={{0,16},{16,0},{1,17},{17,1},{2,18},{18,2},{3,19},{19,3},{4,20},{20... | collective-permute-start | bytes 393224 | tf_op jit(solution)/shard_map/ppermute | solution.py:29
  5.6 13.9 %collective-permute-start.1 = (bf16[1,1024,128]{2,1,0:T(8,128)(2,1)S(1)}, bf16[1,1024,128]{2,1,0:T(8,128)(2,1)S(1)}, u32[]{:S(2)}, u32[]{:S(2)}) collective-permute-start(bf16[1,1024,128]{2,1,0:T(8,128)(2,1)S(1)} %maximum_select_fusion.3), channel_id=1, source_target_pairs={{0,8},{1,9},{2,10},{3,11},{4,12},{5,13},{6,14},{7,15},{8,0},{9,1},... | collective-permute-start | bytes 786440 | tf_op jit(solution)/shard_map/ppermute | solution.py:82
  8.0 79.7 %collective-permute-start.5 = (bf16[1,704,1024]{2,1,0:T(8,128)(2,1)}, bf16[1,704,1024]{2,1,0:T(8,128)(2,1)}, u32[]{:S(2)}, u32[]{:S(2)}) collective-permute-start(bf16[1,704,1024]{2,1,0:T(8,128)(2,1)} %param.23), channel_id=1, source_target_pairs={{0,16},{16,0},{1,17},{17,1},{2,18},{18,2},{3,19},{19,3},{4,20},{20... | collective-permute-start | bytes 4325384 | tf_op jit(solution)/shard_map/ppermute | solution.py:29
  9.3 92.1 %collective-permute-start.6 = (bf16[1,1024,1408]{2,1,0:T(8,128)(2,1)}, bf16[1,1024,1408]{2,1,0:T(8,128)(2,1)}, u32[]{:S(2)}, u32[]{:S(2)}) collective-permute-start(bf16[1,1024,1408]{2,1,0:T(8,128)(2,1)} %param.22), channel_id=1, source_target_pairs={{0,16},{16,0},{1,17},{17,1},{2,18},{18,2},{3,19},{19,3},{4,20},{20... | collective-permute-start | bytes 8650760 | tf_op jit(solution)/shard_map/ppermute | solution.py:29
  19.6 13.2 %collective-permute-start.2 = (bf16[2,1024,128]{2,1,0:T(8,128)(2,1)S(1)}, bf16[2,1024,128]{2,1,0:T(8,128)(2,1)S(1)}, u32[]{:S(2)}, u32[]{:S(2)}) collective-permute-start(bf16[2,1024,128]{2,1,0:T(8,128)(2,1)S(1)} %pad_maximum_fusion.3), channel_id=1, source_target_pairs={{0,4},{1,5},{2,6},{3,7},{4,0},{5,1},{6,2},{7,3},{8,12},{9,13},{10,... | collective-permute-start | bytes 1572872 | tf_op jit(solution)/shard_map/ppermute | solution.py:112
  21.1 13.4 %copy-start.7 = (s32[2]{0:T(128)S(1)}, s32[2]{0:T(128)}, u32[]{:S(2)}) copy-start(s32[2]{0:T(128)} %param.16) | copy-start | bytes 28
  21.1 14.1 %copy-start.8 = (s32[1,16]{1,0:T(1,128)S(1)}, s32[1,16]{1,0:T(1,128)}, u32[]{:S(2)}) copy-start(s32[1,16]{1,0:T(1,128)} %param.17) | copy-start | bytes 196
  21.1 45.4 %all-to-all-start = ((bf16[16,224,128]{2,1,0:T(8,128)(2,1)}), bf16[16,224,128]{2,1,0:T(8,128)(2,1)S(1)}, u32[]{:S(2)}, u32[]{:S(2)}) async-start(bf16[16,224,128]{2,1,0:T(8,128)(2,1)} %pad_maximum_fusion.2), calls=%async_computation | async-start | bytes 1835008 | tf_op jit(solution)/shard_map/all_to_all | solution.py:88
  34.0 28.8 %collective-permute-start.3 = (bf16[4,1024,128]{2,1,0:T(8,128)(2,1)}, bf16[4,1024,128]{2,1,0:T(8,128)(2,1)S(1)}, u32[]{:S(2)}, u32[]{:S(2)}) collective-permute-start(bf16[4,1024,128]{2,1,0:T(8,128)(2,1)} %pad_maximum_fusion.1), channel_id=1, source_target_pairs={{0,2},{1,3},{2,0},{3,1},{4,6},{5,7},{6,4},{7,5},{8,10},{9,11},{10,... | collective-permute-start | bytes 3145736 | tf_op jit(solution)/shard_map/ppermute | solution.py:112
  63.2 21.1 %collective-permute-start.4 = (bf16[8,1024,128]{2,1,0:T(8,128)(2,1)S(1)}, bf16[8,1024,128]{2,1,0:T(8,128)(2,1)}, u32[]{:S(2)}, u32[]{:S(2)}) collective-permute-start(bf16[8,1024,128]{2,1,0:T(8,128)(2,1)S(1)} %pad_maximum_fusion), channel_id=1, source_target_pairs={{0,1},{1,0},{2,3},{3,2},{4,5},{5,4},{6,7},{7,6},{8,9},{9,8},{10,11... | collective-permute-start | bytes 6291464 | tf_op jit(solution)/shard_map/ppermute | solution.py:117
  68.8 9.7 %copy-start.4 = (s32[64,6]{0,1:T(8,128)S(1)}, s32[64,6]{0,1:T(8,128)}, u32[]{:S(2)}) copy-start(s32[64,6]{0,1:T(8,128)} %param.20) | copy-start | bytes 4612
  70.2 13.4 %all-to-all-start.1 = ((bf16[16,32,128]{2,1,0:T(8,128)(2,1)}), bf16[16,32,128]{2,1,0:T(8,128)(2,1)S(1)}, u32[]{:S(2)}, u32[]{:S(2)}) async-start(bf16[16,32,128]{2,1,0:T(8,128)(2,1)} %bitcast.13), calls=%async_computation.1 | async-start | bytes 262144 | tf_op jit(solution)/shard_map/all_to_all | solution.py:106
  84.3 3.0 %copy-start.3 = (bf16[64,2048]{1,0:T(8,128)(2,1)S(1)}, bf16[64,2048]{1,0:T(8,128)(2,1)}, u32[]{:S(2)}) copy-start(bf16[64,2048]{1,0:T(8,128)(2,1)} %param.13) | copy-start | bytes 786436
  84.3 3.2 %copy-start.5 = (f32[2048]{0:T(1024)S(1)}, f32[2048]{0:T(1024)}, u32[]{:S(2)}) copy-start(f32[2048]{0:T(1024)} %param.19) | copy-start | bytes 24580
  87.7 13.7 %copy-start.1 = (bf16[1,1024,1408]{2,1,0:T(8,128)(2,1)S(1)}, bf16[1,1024,1408]{2,1,0:T(8,128)(2,1)}, u32[]{:S(2)}) copy-start(bf16[1,1024,1408]{2,1,0:T(8,128)(2,1)} %param.22) | copy-start | bytes 8650756
  89.8 54.6 %all-to-all-start.2 = ((bf16[16,32,2048]{2,1,0:T(8,128)(2,1)}), bf16[16,32,2048]{2,1,0:T(8,128)(2,1)}, u32[]{:S(2)}, u32[]{:S(2)}) async-start(bf16[16,32,2048]{2,1,0:T(8,128)(2,1)} %bitcast.19), calls=%async_computation.2 | async-start | bytes 4194304 | tf_op jit(solution)/shard_map/all_to_all | solution.py:158
  101.4 7.5 %copy-start.2 = (bf16[1,704,1024]{2,1,0:T(8,128)(2,1)S(1)}, bf16[1,704,1024]{2,1,0:T(8,128)(2,1)}, u32[]{:S(2)}) copy-start(bf16[1,704,1024]{2,1,0:T(8,128)(2,1)} %param.23) | copy-start | bytes 4325380
  154.0 5.0 %copy-start.6 = (f32[64,6]{0,1:T(8,128)S(1)}, f32[64,6]{0,1:T(8,128)}, u32[]{:S(2)}) copy-start(f32[64,6]{0,1:T(8,128)} %param.21) | copy-start | bytes 4612
  154.0 52.4 %all-to-all-start.3 = ((bf16[16,32,2048]{2,1,0:T(8,128)(2,1)}), bf16[16,32,2048]{2,1,0:T(8,128)(2,1)S(1)}, u32[]{:S(2)}, u32[]{:S(2)}) async-start(bf16[16,32,2048]{2,1,0:T(8,128)(2,1)} %bitcast.72), calls=%async_computation.3 | async-start | bytes 4194304 | tf_op jit(solution)/shard_map/all_to_all | solution.py:181

commit v19 on v16

--- a/solution.py
+++ b/solution.py
@@ -77,7 +77,22 @@
     kv_send = jnp.concatenate([q_out, kv_out], axis=1)
     if n_mp == 1 << bits:
         block = wo_rows[None]
-        if bits > 1:
+        if bits > 1 and n_dp == 2:
+            far = 1 << (bits - 1)
+            mid = lax.ppermute(out_weight, "mp", [(m, m ^ far) for m in range(n_mp)])
+            diag = lax.ppermute(
+                out_weight,
+                ("dp", "mp"),
+                [(d * n_mp + m, (1 - d) * n_mp + (m ^ far)) for d in range(2) for m in range(n_mp)],
+            )
+            far_rows = jnp.where(
+                row_index == 0,
+                jnp.concatenate([mid, diag], axis=0),
+                jnp.concatenate([diag, mid], axis=0),
+            )
+            low = (column >> (bits - 1)) % 2 == 0
+            block = jnp.stack([jnp.where(low, wo_rows, far_rows), jnp.where(low, far_rows, wo_rows)])
+        elif bits > 1:
             b = bits - 1
             pair = lax.ppermute(block, "mp", [(m, m ^ (1 << b)) for m in range(n_mp)])
             low = (column >> b) % 2 == 0

time: 209 us -> 205 us (0.981)
  waiting for transfers between devices: 129 us -> 126 us
    ppermute x0 -> x2, waiting for transfers between devices: none -> 5.33 us  [the longest x1 2.81 us: on_device(): lax.ppermute(out_weight, ('dp', 'mp'), [(d * n_mp + m, (1 - d) * n_mp + (...]
    ppermute x3 -> x2, waiting for transfers between devices: 35.8 us -> 30.9 us  [on_device(): pair = lax.ppermute(block, 'mp', [(m, m ^ 1 << b) for m in range(n_mp)])]
    all_to_all x1, waiting for transfers between devices: 32.9 us -> 29.9 us  [on_device(): lax.all_to_all(sending.reshape(n_mp, capacity, d_model), 'mp', split_axis...]
    ppermute x3 -> x2, starting transfers between devices: 2.7 us -> 0.33 us  [on_device(): pair = lax.ppermute(block, 'mp', [(m, m ^ 1 << b) for m in range(n_mp)])]
    ppermute x0 -> x2, starting transfers between devices: none -> 2.31 us  [the longest x1 2.31 us: on_device(): mid = lax.ppermute(out_weight, 'mp', [(m, m ^ far) for m in range(n_mp)])]
  transfers between devices with their start and end apart: 11 -> 12, of which waited for: 8 -> 8; matrix products, arithmetic and copies ran while one was open for 14% -> 15% of each run, Pallas kernels for 0% -> 0%
where the time goes in v19:
time: 205 us; the launch traced here: 204 us
  waiting for transfers between devices  126 us (61%)
  starting transfers between devices  36 us (18%)
  matrix products  18.3 us (9%)
  other arithmetic  16.1 us (8%)
  local copies, waits for them, and re-layouts  7.33 us (4%)
    all_to_all x1, waiting for transfers between devices, on_device(): lax.all_to_all(outcome.reshape(n_mp, capacity, d_model), 'mp', split_axis...  47.2 us
    ppermute x2, waiting for transfers between devices, on_device(): pair = lax.ppermute(block, 'mp', [(m, m ^ 1 << b) for m in range(n_mp)])  30.9 us
    all_to_all x1, waiting for transfers between devices, on_device(): lax.all_to_all(sending.reshape(n_mp, capacity, d_model), 'mp', split_axis...  29.9 us
    all_to_all x1, starting transfers between devices, on_device(): lax.all_to_all(blended.reshape(n_mp, sub, HD), 'mp', split_axis=0, concat...  7.99 us
    all_to_all x1, starting transfers between devices, on_device(): lax.all_to_all(kv_send, 'mp', split_axis=0, concat_axis=0, tiled=True)  7.76 us
    ppermute x3, waiting for transfers between devices, swap_dp(): return lax.ppermute(x, 'dp', [(0, 1), (1, 0)])  7.54 us
    select_n x1, other arithmetic, on_device(): jnp.where(first, jnp.concatenate([experts_in[0], in_other[0]], axis=0), j...  7.48 us
    all_to_all x1, starting transfers between devices, on_device(): lax.all_to_all(sending.reshape(n_mp, capacity, d_model), 'mp', split_axis...  7.07 us
  transfers between devices with their start and end apart: 12, of which 8 were waited for; matrix products, arithmetic and copies ran while one was open for 15% of the time, Pallas kernels for 0%

profile of v19, /device:TPU:11, one launch (start us, length us, event | category | flops | bytes accessed | tf_op | source)
XLA Modules:
  0.0 204.1 jit_solution(702342146396421508)
XLA Ops:
  0.0 1.2 collective-permute-start
  1.2 2.3 %collective-permute-start.1 = (bf16[512,128]{1,0:T(8,128)(2,1)}, bf16[512,128]{1,0:T(8,128)(2,1)S(1)}, u32[]{:S(2)}, u32[]{:S(2)}) collective-permute-start(bf16[512,128]{1,0:T(8,128)(2,1)} %param.18), channel_id=1, source_target_pairs={{0,8},{1,9},{2,10},{3,11},{4,12},{5,13},{6,14},{7,15},{8,0},{9,1},... | collective-permute-start | bytes 393224 | tf_op jit(solution)/shard_map/ppermute | solution.py:82
  3.6 1.2 collective-permute-start.6
  4.8 0.2 collective-permute-start.7
  5.0 1.2 reshape.320
  6.3 0.3 copy.66
  6.6 0.9 copy.77
  7.6 0.8 copy.72
  8.5 0.6 tile.8
  9.1 1.0 pad_maximum_fusion.2
  10.1 2.5 %collective-permute-done.1 = bf16[512,128]{1,0:T(8,128)(2,1)S(1)} collective-permute-done((bf16[512,128]{1,0:T(8,128)(2,1)}, bf16[512,128]{1,0:T(8,128)(2,1)S(1)}, u32[]{:S(2)}, u32[]{:S(2)}) %collective-permute-start.1) | collective-permute-done | bytes 131104 | tf_op jit(solution)/shard_map/ppermute | solution.py:82
  12.6 2.8 %collective-permute-done.2 = bf16[512,128]{1,0:T(8,128)(2,1)S(1)} collective-permute-done((bf16[512,128]{1,0:T(8,128)(2,1)}, bf16[512,128]{1,0:T(8,128)(2,1)S(1)}, u32[]{:S(2)}, u32[]{:S(2)}) %collective-permute-start.2) | collective-permute-done | bytes 131104 | tf_op jit(solution)/shard_map/ppermute | solution.py:83
  15.4 0.2 broadcast_select_fusion.5
  15.7 0.9 reduce-window.6
  16.7 0.2 slice_reduce_fusion
  16.9 0.2 select_reduce_fusion.1
  17.1 7.8 %all-to-all-start = ((bf16[16,224,128]{2,1,0:T(8,128)(2,1)}), bf16[16,224,128]{2,1,0:T(8,128)(2,1)S(1)}, u32[]{:S(2)}, u32[]{:S(2)}) async-start(bf16[16,224,128]{2,1,0:T(8,128)(2,1)} %pad_maximum_fusion.2), calls=%async_computation | async-start | bytes 1835008 | tf_op jit(solution)/shard_map/all_to_all | solution.py:103
  24.8 4.0 %collective-permute-done.3 = bf16[2,1024,128]{2,1,0:T(8,128)(2,1)S(1)} collective-permute-done((bf16[2,1024,128]{2,1,0:T(8,128)(2,1)S(1)}, bf16[2,1024,128]{2,1,0:T(8,128)(2,1)S(1)}, u32[]{:S(2)}, u32[]{:S(2)}) %collective-permute-start.3) | collective-permute-done | bytes 524320 | tf_op jit(solution)/shard_map/ppermute | solution.py:127
  28.9 1.1 pad_maximum_fusion.1
  30.0 0.3 collective-permute-start.4
  30.5 0.6 dynamic_slice.7
  31.2 0.7 fusion.19
  32.0 27.0 %collective-permute-done.4 = bf16[4,1024,128]{2,1,0:T(8,128)(2,1)S(1)} collective-permute-done((bf16[4,1024,128]{2,1,0:T(8,128)(2,1)}, bf16[4,1024,128]{2,1,0:T(8,128)(2,1)S(1)}, u32[]{:S(2)}, u32[]{:S(2)}) %collective-permute-start.4) | collective-permute-done | bytes 1048608 | tf_op jit(solution)/shard_map/ppermute | solution.py:127
  59.1 0.2 pad_maximum_fusion
  59.3 2.9 %collective-permute-start.5 = (bf16[8,1024,128]{2,1,0:T(8,128)(2,1)S(1)}, bf16[8,1024,128]{2,1,0:T(8,128)(2,1)}, u32[]{:S(2)}, u32[]{:S(2)}) collective-permute-start(bf16[8,1024,128]{2,1,0:T(8,128)(2,1)S(1)} %pad_maximum_fusion), channel_id=1, source_target_pairs={{0,1},{1,0},{2,3},{3,2},{4,5},{5,4},{6,7},{7,6},{8,9},{9,8},{10,11... | collective-permute-start | bytes 6291464 | tf_op jit(solution)/shard_map/ppermute | solution.py:132
  62.6 0.5 copy.67
  63.2 0.2 fusion.22
  63.6 0.7 fusion.23
  64.3 0.6 fusion.1
  64.9 1.4 fusion.5
  66.3 8.0 %all-to-all-start.1 = ((bf16[16,32,128]{2,1,0:T(8,128)(2,1)}), bf16[16,32,128]{2,1,0:T(8,128)(2,1)S(1)}, u32[]{:S(2)}, u32[]{:S(2)}) async-start(bf16[16,32,128]{2,1,0:T(8,128)(2,1)} %bitcast.15), calls=%async_computation.1 | async-start | bytes 262144 | tf_op jit(solution)/shard_map/all_to_all | solution.py:121
  74.4 5.0 %all-to-all-done.1 = bf16[16,32,128]{2,1,0:T(8,128)(2,1)S(1)} async-done(((bf16[16,32,128]{2,1,0:T(8,128)(2,1)}), bf16[16,32,128]{2,1,0:T(8,128)(2,1)S(1)}, u32[]{:S(2)}, u32[]{:S(2)}) %all-to-all-start.1) | async-done | bytes 131104 | tf_op jit(solution)/shard_map/all_to_all | solution.py:121
  79.5 0.5 fusion.24
  80.1 2.1 %fusion.25 = f32[64,8,128]{2,0,1:T(8,128)S(1)} fusion(bf16[64,1024,1]{1,0,2:T(8,128)(2,1)S(1)} %reshape.332, bf16[8,1024,128]{2,1,0:T(8,128)(2,1)} %collective-permute-done.5), kind=kOutput, calls=%fused_computation.74 | convolution fusion | flops 134217728 | bytes 2490368 | tf_op jit(solution)/shard_map/tk,jkc->tjc/dot_general | solution.py:134
  82.2 0.4 copy.71
  82.6 0.4 reshape.326
  83.1 0.2 fusion.9
  83.4 2.1 %convolution_convert_fusion.1 = bf16[512,2048]{1,0:T(8,128)(2,1)} fusion(pred[64,512]{1,0:T(8,128)(4,1)S(1)} %fusion.8, bf16[64,2048]{1,0:T(8,128)(2,1)S(1)} %fusion.11), kind=kOutput, calls=%fused_computation.6 | convolution fusion | flops 135266304 | bytes 2392064 | tf_op jit(solution)/shard_map/dot_general | solution.py:170
  85.5 7.1 %all-to-all-start.2 = ((bf16[16,32,2048]{2,1,0:T(8,128)(2,1)}), bf16[16,32,2048]{2,1,0:T(8,128)(2,1)}, u32[]{:S(2)}, u32[]{:S(2)}) async-start(bf16[16,32,2048]{2,1,0:T(8,128)(2,1)} %bitcast.21), calls=%async_computation.2 | async-start | bytes 4194304 | tf_op jit(solution)/shard_map/all_to_all | solution.py:173
  92.6 7.5 %collective-permute-done.7 = bf16[1,1024,1408]{2,1,0:T(8,128)(2,1)} collective-permute-done((bf16[1,1024,1408]{2,1,0:T(8,128)(2,1)}, bf16[1,1024,1408]{2,1,0:T(8,128)(2,1)}, u32[]{:S(2)}, u32[]{:S(2)}) %collective-permute-start.7) | collective-permute-done | bytes 2883616 | tf_op jit(solution)/shard_map/ppermute | solution.py:29
  100.1 7.5 %maximum_select_fusion = bf16[2048,1408]{1,0:T(8,128)(2,1)} fusion(bf16[1024,1408]{1,0:T(8,128)(2,1)} %bitcast.26, bf16[1024,1408]{1,0:T(8,128)(2,1)S(1)} %bitcast.72, pred[]{:T(512)S(6)} %eq.85), kind=kLoop, calls=%fused_computation | loop fusion | flops 25952256 | bytes 11534337 | tf_op jit(solution)/shard_map/jit(_where)/select_n | solution.py:179
  107.6 2.6 %maximum_select_fusion.1 = bf16[704,2048]{1,0:T(8,128)(2,1)S(1)} fusion(bf16[704,1024]{1,0:T(8,128)(2,1)} %bitcast.24, bf16[704,1024]{1,0:T(8,128)(2,1)S(1)} %bitcast.76, pred[]{:T(512)S(6)} %eq.85), kind=kLoop, calls=%fused_computation.7 | loop fusion | flops 12976128 | bytes 5767169 | tf_op jit(solution)/shard_map/jit(_where)/select_n | solution.py:184
  110.2 29.9 %all-to-all-done.2 = bf16[16,32,2048]{2,1,0:T(8,128)(2,1)} async-done(((bf16[16,32,2048]{2,1,0:T(8,128)(2,1)}), bf16[16,32,2048]{2,1,0:T(8,128)(2,1)}, u32[]{:S(2)}, u32[]{:S(2)}) %all-to-all-start.2) | async-done | bytes 2097184 | tf_op jit(solution)/shard_map/all_to_all | solution.py:173
  140.1 6.4 %fusion.26 = f32[512,1408]{1,0:T(8,128)S(1)} fusion(bf16[512,2048]{1,0:T(8,128)(2,1)} %bitcast.22, bf16[2048,1408]{1,0:T(8,128)(2,1)} %maximum_select_fusion), kind=kOutput, calls=%fused_computation.75 | convolution fusion | flops 2952790016 | bytes 10747904 | tf_op jit(solution)/shard_map/dot_general | solution.py:193
  146.5 3.3 %convolution_convert_fusion = bf16[512,2048]{1,0:T(8,128)(2,1)} fusion(bf16[704,2048]{1,0:T(8,128)(2,1)S(1)} %maximum_select_fusion.1, f32[512,1408]{1,0:T(8,128)S(1)} %fusion.26), kind=kOutput, calls=%fused_computation.5 | convolution fusion | flops 1479606272 | bytes 8126464 | tf_op jit(solution)/shard_map/dot_general | solution.py:195
  149.8 5.0 %all-to-all-start.3 = ((bf16[16,32,2048]{2,1,0:T(8,128)(2,1)}), bf16[16,32,2048]{2,1,0:T(8,128)(2,1)S(1)}, u32[]{:S(2)}, u32[]{:S(2)}) async-start(bf16[16,32,2048]{2,1,0:T(8,128)(2,1)} %bitcast.73), calls=%async_computation.3 | async-start | bytes 4194304 | tf_op jit(solution)/shard_map/all_to_all | solution.py:196
  155.0 47.2 %all-to-all-done.3 = bf16[16,32,2048]{2,1,0:T(8,128)(2,1)S(1)} async-done(((bf16[16,32,2048]{2,1,0:T(8,128)(2,1)}), bf16[16,32,2048]{2,1,0:T(8,128)(2,1)S(1)}, u32[]{:S(2)}, u32[]{:S(2)}) %all-to-all-start.3) | async-done | bytes 2097184 | tf_op jit(solution)/shard_map/all_to_all | solution.py:196
  202.2 1.9 fusion.2
  (58 shorter events, 2.3 us)
Async XLA Ops:
  0.0 16.6 %copy-start = (s32[2,96]{1,0:T(2,128)S(1)}, s32[2,96]{1,0:T(2,128)}, u32[]{:S(2)}) copy-start(s32[2,96]{1,0:T(2,128)} %param.15) | copy-start | bytes 2308
  0.0 15.4 %copy-start.4 = (bf16[512,128]{1,0:T(8,128)(2,1)S(1)}, bf16[512,128]{1,0:T(8,128)(2,1)}, u32[]{:S(2)}) copy-start(bf16[512,128]{1,0:T(8,128)(2,1)} %param.18) | copy-start | bytes 393220
  0.0 10.1 %collective-permute-start = (bf16[512,128]{1,0:T(8,128)(2,1)}, bf16[512,128]{1,0:T(8,128)(2,1)S(1)}, u32[]{:S(2)}, u32[]{:S(2)}) collective-permute-start(bf16[512,128]{1,0:T(8,128)(2,1)} %param.18), channel_id=1, source_target_pairs={{0,16},{16,0},{1,17},{17,1},{2,18},{18,2},{3,19},{19,3},{4,20},{20... | collective-permute-start | bytes 393224 | tf_op jit(solution)/shard_map/ppermute | solution.py:29
  1.2 11.3 %collective-permute-start.1 = (bf16[512,128]{1,0:T(8,128)(2,1)}, bf16[512,128]{1,0:T(8,128)(2,1)S(1)}, u32[]{:S(2)}, u32[]{:S(2)}) collective-permute-start(bf16[512,128]{1,0:T(8,128)(2,1)} %param.18), channel_id=1, source_target_pairs={{0,8},{1,9},{2,10},{3,11},{4,12},{5,13},{6,14},{7,15},{8,0},{9,1},... | collective-permute-start | bytes 393224 | tf_op jit(solution)/shard_map/ppermute | solution.py:82
  3.6 11.8 %collective-permute-start.2 = (bf16[512,128]{1,0:T(8,128)(2,1)}, bf16[512,128]{1,0:T(8,128)(2,1)S(1)}, u32[]{:S(2)}, u32[]{:S(2)}) collective-permute-start(bf16[512,128]{1,0:T(8,128)(2,1)} %param.18), channel_id=1, source_target_pairs={{0,24},{1,25},{2,26},{3,27},{4,28},{5,29},{6,30},{7,31},{8,16},{9,... | collective-permute-start | bytes 393224 | tf_op jit(solution)/shard_map/ppermute | solution.py:83
  3.6 79.9 %collective-permute-start.6 = (bf16[1,704,1024]{2,1,0:T(8,128)(2,1)}, bf16[1,704,1024]{2,1,0:T(8,128)(2,1)}, u32[]{:S(2)}, u32[]{:S(2)}) collective-permute-start(bf16[1,704,1024]{2,1,0:T(8,128)(2,1)} %param.23), channel_id=1, source_target_pairs={{0,16},{16,0},{1,17},{17,1},{2,18},{18,2},{3,19},{19,3},{4,20},{20... | collective-permute-start | bytes 4325384 | tf_op jit(solution)/shard_map/ppermute | solution.py:29
  4.8 95.3 %collective-permute-start.7 = (bf16[1,1024,1408]{2,1,0:T(8,128)(2,1)}, bf16[1,1024,1408]{2,1,0:T(8,128)(2,1)}, u32[]{:S(2)}, u32[]{:S(2)}) collective-permute-start(bf16[1,1024,1408]{2,1,0:T(8,128)(2,1)} %param.22), channel_id=1, source_target_pairs={{0,16},{16,0},{1,17},{17,1},{2,18},{18,2},{3,19},{19,3},{4,20},{20... | collective-permute-start | bytes 8650760 | tf_op jit(solution)/shard_map/ppermute | solution.py:29
  15.6 13.2 %collective-permute-start.3 = (bf16[2,1024,128]{2,1,0:T(8,128)(2,1)S(1)}, bf16[2,1024,128]{2,1,0:T(8,128)(2,1)S(1)}, u32[]{:S(2)}, u32[]{:S(2)}) collective-permute-start(bf16[2,1024,128]{2,1,0:T(8,128)(2,1)S(1)} %pad_maximum_fusion.3), channel_id=1, source_target_pairs={{0,4},{1,5},{2,6},{3,7},{4,0},{5,1},{6,2},{7,3},{8,12},{9,13},{10,... | collective-permute-start | bytes 1572872 | tf_op jit(solution)/shard_map/ppermute | solution.py:127
  17.1 13.4 %copy-start.8 = (s32[2]{0:T(128)S(1)}, s32[2]{0:T(128)}, u32[]{:S(2)}) copy-start(s32[2]{0:T(128)} %param.16) | copy-start | bytes 28
  17.1 14.1 %copy-start.9 = (s32[1,16]{1,0:T(1,128)S(1)}, s32[1,16]{1,0:T(1,128)}, u32[]{:S(2)}) copy-start(s32[1,16]{1,0:T(1,128)} %param.17) | copy-start | bytes 196
  17.1 45.5 %all-to-all-start = ((bf16[16,224,128]{2,1,0:T(8,128)(2,1)}), bf16[16,224,128]{2,1,0:T(8,128)(2,1)S(1)}, u32[]{:S(2)}, u32[]{:S(2)}) async-start(bf16[16,224,128]{2,1,0:T(8,128)(2,1)} %pad_maximum_fusion.2), calls=%async_computation | async-start | bytes 1835008 | tf_op jit(solution)/shard_map/all_to_all | solution.py:103
  30.0 28.9 %collective-permute-start.4 = (bf16[4,1024,128]{2,1,0:T(8,128)(2,1)}, bf16[4,1024,128]{2,1,0:T(8,128)(2,1)S(1)}, u32[]{:S(2)}, u32[]{:S(2)}) collective-permute-start(bf16[4,1024,128]{2,1,0:T(8,128)(2,1)} %pad_maximum_fusion.1), channel_id=1, source_target_pairs={{0,2},{1,3},{2,0},{3,1},{4,6},{5,7},{6,4},{7,5},{8,10},{9,11},{10,... | collective-permute-start | bytes 3145736 | tf_op jit(solution)/shard_map/ppermute | solution.py:127
  59.3 20.8 %collective-permute-start.5 = (bf16[8,1024,128]{2,1,0:T(8,128)(2,1)S(1)}, bf16[8,1024,128]{2,1,0:T(8,128)(2,1)}, u32[]{:S(2)}, u32[]{:S(2)}) collective-permute-start(bf16[8,1024,128]{2,1,0:T(8,128)(2,1)S(1)} %pad_maximum_fusion), channel_id=1, source_target_pairs={{0,1},{1,0},{2,3},{3,2},{4,5},{5,4},{6,7},{7,6},{8,9},{9,8},{10,11... | collective-permute-start | bytes 6291464 | tf_op jit(solution)/shard_map/ppermute | solution.py:132
  64.9 9.4 %copy-start.5 = (s32[64,6]{0,1:T(8,128)S(1)}, s32[64,6]{0,1:T(8,128)}, u32[]{:S(2)}) copy-start(s32[64,6]{0,1:T(8,128)} %param.20) | copy-start | bytes 4612
  66.3 13.2 %all-to-all-start.1 = ((bf16[16,32,128]{2,1,0:T(8,128)(2,1)}), bf16[16,32,128]{2,1,0:T(8,128)(2,1)S(1)}, u32[]{:S(2)}, u32[]{:S(2)}) async-start(bf16[16,32,128]{2,1,0:T(8,128)(2,1)} %bitcast.15), calls=%async_computation.1 | async-start | bytes 262144 | tf_op jit(solution)/shard_map/all_to_all | solution.py:121
  80.0 3.0 %copy-start.3 = (bf16[64,2048]{1,0:T(8,128)(2,1)S(1)}, bf16[64,2048]{1,0:T(8,128)(2,1)}, u32[]{:S(2)}) copy-start(bf16[64,2048]{1,0:T(8,128)(2,1)} %param.13) | copy-start | bytes 786436
  80.0 3.2 %copy-start.6 = (f32[2048]{0:T(1024)S(1)}, f32[2048]{0:T(1024)}, u32[]{:S(2)}) copy-start(f32[2048]{0:T(1024)} %param.19) | copy-start | bytes 24580
  83.4 16.7 %copy-start.1 = (bf16[1,1024,1408]{2,1,0:T(8,128)(2,1)S(1)}, bf16[1,1024,1408]{2,1,0:T(8,128)(2,1)}, u32[]{:S(2)}) copy-start(bf16[1,1024,1408]{2,1,0:T(8,128)(2,1)} %param.22) | copy-start | bytes 8650756
  85.5 54.6 %all-to-all-start.2 = ((bf16[16,32,2048]{2,1,0:T(8,128)(2,1)}), bf16[16,32,2048]{2,1,0:T(8,128)(2,1)}, u32[]{:S(2)}, u32[]{:S(2)}) async-start(bf16[16,32,2048]{2,1,0:T(8,128)(2,1)} %bitcast.21), calls=%async_computation.2 | async-start | bytes 4194304 | tf_op jit(solution)/shard_map/all_to_all | solution.py:173
  100.1 7.5 %copy-start.2 = (bf16[1,704,1024]{2,1,0:T(8,128)(2,1)S(1)}, bf16[1,704,1024]{2,1,0:T(8,128)(2,1)}, u32[]{:S(2)}) copy-start(bf16[1,704,1024]{2,1,0:T(8,128)(2,1)} %param.23) | copy-start | bytes 4325380
  149.8 5.0 %copy-start.7 = (f32[64,6]{0,1:T(8,128)S(1)}, f32[64,6]{0,1:T(8,128)}, u32[]{:S(2)}) copy-start(f32[64,6]{0,1:T(8,128)} %param.21) | copy-start | bytes 4612
  149.8 52.4 %all-to-all-start.3 = ((bf16[16,32,2048]{2,1,0:T(8,128)(2,1)}), bf16[16,32,2048]{2,1,0:T(8,128)(2,1)S(1)}, u32[]{:S(2)}, u32[]{:S(2)}) async-start(bf16[16,32,2048]{2,1,0:T(8,128)(2,1)} %bitcast.73), calls=%async_computation.3 | async-start | bytes 4194304 | tf_op jit(solution)/shard_map/all_to_all | solution.py:196

commit v20 on v16

--- a/solution.py
+++ b/solution.py
@@ -77,7 +77,41 @@
     kv_send = jnp.concatenate([q_out, kv_out], axis=1)
     if n_mp == 1 << bits:
         block = wo_rows[None]
-        if bits > 1:
+        if bits > 2 and n_dp == 2:
+            t1, t2 = bits - 1, bits - 2
+            fetched = {}
+            for a in range(2):
+                for c in range(2):
+                    off = (a << t1) | (c << t2)
+                    near = out_weight if off == 0 else lax.ppermute(
+                        out_weight, "mp", [(m, m ^ off) for m in range(n_mp)]
+                    )
+                    other = lax.ppermute(
+                        out_weight,
+                        ("dp", "mp"),
+                        [(d * n_mp + m, (1 - d) * n_mp + (m ^ off)) for d in range(2) for m in range(n_mp)],
+                    )
+                    fetched[a, c] = jnp.where(
+                        row_index == 0,
+                        jnp.concatenate([near, other], axis=0),
+                        jnp.concatenate([other, near], axis=0),
+                    )
+            b1 = (column >> t1) % 2
+            b2 = (column >> t2) % 2
+            shards = []
+            for x2 in range(2):
+                for x3 in range(2):
+                    a0 = (b1 ^ x3) == 0
+                    c0 = (b2 ^ x2) == 0
+                    shards.append(
+                        jnp.where(
+                            a0,
+                            jnp.where(c0, fetched[0, 0], fetched[0, 1]),
+                            jnp.where(c0, fetched[1, 0], fetched[1, 1]),
+                        )
+                    )
+            block = jnp.stack(shards)
+        elif bits > 1:
             b = bits - 1
             pair = lax.ppermute(block, "mp", [(m, m ^ (1 << b)) for m in range(n_mp)])
             low = (column >> b) % 2 == 0
@@ -108,7 +142,7 @@
 
     bits = n_mp.bit_length() - 1
     if n_mp == 1 << bits:
-        for b in reversed(range(1, bits - 1)):
+        for b in reversed(range(1, bits - 2 if n_dp == 2 and bits > 2 else bits - 1)):
             pair = lax.ppermute(block, "mp", [(m, m ^ (1 << b)) for m in range(n_mp)])
             low = (column >> b) % 2 == 0
             block = jnp.concatenate(

time: 209 us -> 203 us (0.971)
  waiting for transfers between devices: 129 us -> 122 us
    all_to_all x1, waiting for transfers between devices: 32.9 us -> 15.9 us  [on_device(): lax.all_to_all(sending.reshape(n_mp, capacity, d_model), 'mp', split_axis...]
    ppermute x3 -> x1, waiting for transfers between devices: 35.8 us -> 23.9 us  [on_device(): pair = lax.ppermute(block, 'mp', [(m, m ^ 1 << b) for m in range(n_mp)])]
    ppermute x3 -> x2, waiting for transfers between devices: 7.89 us -> 19.4 us  [swap_dp(): return lax.ppermute(x, 'dp', [(0, 1), (1, 0)])]
    ppermute x0 -> x7, waiting for transfers between devices: none -> 11 us  [the longest x4 7.35 us: on_device(): lax.ppermute(out_weight, ('dp', 'mp'), [(d * n_mp + m, (1 - d) * n_mp + (...]
    ppermute x0 -> x7, starting transfers between devices: none -> 8.43 us  [the longest x4 5.64 us: on_device(): lax.ppermute(out_weight, ('dp', 'mp'), [(d * n_mp + m, (1 - d) * n_mp + (...]
    all_to_all x1, starting transfers between devices: 8.27 us -> 5.74 us  [on_device(): lax.all_to_all(blended.reshape(n_mp, sub, HD), 'mp', split_axis=0, concat...]
    ppermute x3 -> x1, starting transfers between devices: 2.7 us -> 0.32 us  [on_device(): pair = lax.ppermute(block, 'mp', [(m, m ^ 1 << b) for m in range(n_mp)])]
  transfers between devices with their start and end apart: 11 -> 15, of which waited for: 8 -> 7; matrix products, arithmetic and copies ran while one was open for 14% -> 16% of each run, Pallas kernels for 0% -> 0%
where the time goes in v20:
time: 203 us
  waiting for transfers between devices  122 us (60%)
  starting transfers between devices  36.1 us (18%)
  matrix products  18.3 us (9%)
  other arithmetic  18 us (9%)
  local copies, waits for them, and re-layouts  7.32 us (4%)
    all_to_all x1, waiting for transfers between devices, on_device(): lax.all_to_all(outcome.reshape(n_mp, capacity, d_model), 'mp', split_axis...  47.2 us
    ppermute x1, waiting for transfers between devices, on_device(): pair = lax.ppermute(block, 'mp', [(m, m ^ 1 << b) for m in range(n_mp)])  23.9 us
    ppermute x2, waiting for transfers between devices, swap_dp(): return lax.ppermute(x, 'dp', [(0, 1), (1, 0)])  19.4 us
    all_to_all x1, waiting for transfers between devices, on_device(): lax.all_to_all(sending.reshape(n_mp, capacity, d_model), 'mp', split_axis...  15.9 us
    select_n x1, other arithmetic, on_device(): jnp.where(first, jnp.concatenate([experts_in[0], in_other[0]], axis=0), j...  8.66 us
    ppermute x4, waiting for transfers between devices, on_device(): lax.ppermute(out_weight, ('dp', 'mp'), [(d * n_mp + m, (1 - d) * n_mp + (...  7.35 us
    all_to_all x1, starting transfers between devices, on_device(): lax.all_to_all(sending.reshape(n_mp, capacity, d_model), 'mp', split_axis...  7.07 us
    dot_general x1, matrix products, on_device(): gate_vals = jnp.dot(flat_rows, gate_up, preferred_element_type=jnp.float32)  6.38 us
  transfers between devices with their start and end apart: 15, of which 7 were waited for; matrix products, arithmetic and copies ran while one was open for 16% of the time, Pallas kernels for 0%

profile of v20, /device:TPU:11, one launch (start us, length us, event | category | flops | bytes accessed | tf_op | source)
XLA Modules:
  0.0 202.7 jit_solution(180145341147619317)
XLA Ops:
  0.0 2.3 %collective-permute-start.6 = (bf16[512,128]{1,0:T(8,128)(2,1)}, bf16[512,128]{1,0:T(8,128)(2,1)S(1)}, u32[]{:S(2)}, u32[]{:S(2)}) collective-permute-start(bf16[512,128]{1,0:T(8,128)(2,1)} %param.18), channel_id=1, source_target_pairs={{0,28},{1,29},{2,30},{3,31},{4,24},{5,25},{6,26},{7,27},{8,20},{9,... | collective-permute-start | bytes 393224 | tf_op jit(solution)/shard_map/ppermute | solution.py:89
  2.3 0.2 collective-permute-start
  2.5 2.2 %collective-permute-start.1 = (bf16[512,128]{1,0:T(8,128)(2,1)}, bf16[512,128]{1,0:T(8,128)(2,1)S(1)}, u32[]{:S(2)}, u32[]{:S(2)}) collective-permute-start(bf16[512,128]{1,0:T(8,128)(2,1)} %param.18), channel_id=1, source_target_pairs={{0,4},{1,5},{2,6},{3,7},{4,0},{5,1},{6,2},{7,3},{8,12},{9,13},{10,... | collective-permute-start | bytes 393224 | tf_op jit(solution)/shard_map/ppermute | solution.py:86
  4.7 1.0 collective-permute-start.2
  5.9 0.8 copy.72
  6.8 0.9 reduce-window.6
  8.1 1.2 reshape.608
  9.4 0.3 copy.66
  9.7 0.9 copy.77
  10.8 2.2 %collective-permute-start.4 = (bf16[512,128]{1,0:T(8,128)(2,1)}, bf16[512,128]{1,0:T(8,128)(2,1)S(1)}, u32[]{:S(2)}, u32[]{:S(2)}) collective-permute-start(bf16[512,128]{1,0:T(8,128)(2,1)} %param.18), channel_id=1, source_target_pairs={{0,24},{1,25},{2,26},{3,27},{4,28},{5,29},{6,30},{7,31},{8,16},{9,... | collective-permute-start | bytes 393224 | tf_op jit(solution)/shard_map/ppermute | solution.py:89
  13.0 0.4 collective-permute-start.5
  13.4 0.6 tile.8
  14.0 1.0 pad_maximum_fusion.2
  15.0 1.1 collective-permute-start.9
  16.1 0.4 collective-permute-start.10
  16.4 7.3 %collective-permute-done.4 = bf16[512,128]{1,0:T(8,128)(2,1)S(1)} collective-permute-done((bf16[512,128]{1,0:T(8,128)(2,1)}, bf16[512,128]{1,0:T(8,128)(2,1)S(1)}, u32[]{:S(2)}, u32[]{:S(2)}) %collective-permute-start.4) | collective-permute-done | bytes 131104 | tf_op jit(solution)/shard_map/ppermute | solution.py:89
  23.8 3.7 %collective-permute-done.5 = bf16[512,128]{1,0:T(8,128)(2,1)S(1)} collective-permute-done((bf16[512,128]{1,0:T(8,128)(2,1)}, bf16[512,128]{1,0:T(8,128)(2,1)S(1)}, u32[]{:S(2)}, u32[]{:S(2)}) %collective-permute-start.5) | collective-permute-done | bytes 131104 | tf_op jit(solution)/shard_map/ppermute | solution.py:86
  27.5 0.3 broadcast_select_fusion.4
  27.7 0.3 broadcast_select_fusion.5
  28.0 0.3 broadcast_select_fusion.8
  28.3 0.3 broadcast_select_fusion.9
  28.8 0.3 collective-permute-start.7
  29.3 0.6 dynamic_slice.7
  29.9 6.0 %all-to-all-start = ((bf16[16,224,128]{2,1,0:T(8,128)(2,1)}), bf16[16,224,128]{2,1,0:T(8,128)(2,1)S(1)}, u32[]{:S(2)}, u32[]{:S(2)}) async-start(bf16[16,224,128]{2,1,0:T(8,128)(2,1)} %pad_maximum_fusion.2), calls=%async_computation | async-start | bytes 1835008 | tf_op jit(solution)/shard_map/all_to_all | solution.py:122
  35.9 0.7 fusion.19
  36.7 23.9 %collective-permute-done.7 = bf16[4,1024,128]{2,1,0:T(8,128)(2,1)S(1)} collective-permute-done((bf16[4,1024,128]{2,1,0:T(8,128)(2,1)S(1)}, bf16[4,1024,128]{2,1,0:T(8,128)(2,1)S(1)}, u32[]{:S(2)}, u32[]{:S(2)}) %collective-permute-start.7) | collective-permute-done | bytes 1048608 | tf_op jit(solution)/shard_map/ppermute | solution.py:146
  61.0 2.0 collective-permute-start.8
  63.5 0.5 copy.67
  64.4 0.7 fusion.23
  65.1 0.6 fusion.1
  65.7 1.4 fusion.5
  67.1 5.7 %all-to-all-start.1 = ((bf16[16,32,128]{2,1,0:T(8,128)(2,1)}), bf16[16,32,128]{2,1,0:T(8,128)(2,1)S(1)}, u32[]{:S(2)}, u32[]{:S(2)}) async-start(bf16[16,32,128]{2,1,0:T(8,128)(2,1)} %bitcast.19), calls=%async_computation.1 | async-start | bytes 262144 | tf_op jit(solution)/shard_map/all_to_all | solution.py:140
  73.0 5.0 %all-to-all-done.1 = bf16[16,32,128]{2,1,0:T(8,128)(2,1)S(1)} async-done(((bf16[16,32,128]{2,1,0:T(8,128)(2,1)}), bf16[16,32,128]{2,1,0:T(8,128)(2,1)S(1)}, u32[]{:S(2)}, u32[]{:S(2)}) %all-to-all-start.1) | async-done | bytes 131104 | tf_op jit(solution)/shard_map/all_to_all | solution.py:140
  78.1 0.5 fusion.24
  78.6 2.1 %fusion.25 = f32[64,8,128]{2,0,1:T(8,128)S(1)} fusion(bf16[64,1024,1]{1,0,2:T(8,128)(2,1)S(1)} %reshape.620, bf16[8,1024,128]{2,1,0:T(8,128)(2,1)} %collective-permute-done.8), kind=kOutput, calls=%fused_computation.79 | convolution fusion | flops 134217728 | bytes 2490368 | tf_op jit(solution)/shard_map/tk,jkc->tjc/dot_general | solution.py:153
  80.8 0.4 copy.71
  81.2 0.4 reshape.614
  82.0 2.1 %convolution_convert_fusion.1 = bf16[512,2048]{1,0:T(8,128)(2,1)} fusion(pred[64,512]{1,0:T(8,128)(4,1)S(1)} %fusion.8, bf16[64,2048]{1,0:T(8,128)(2,1)S(1)} %fusion.11), kind=kOutput, calls=%fused_computation.6 | convolution fusion | flops 135266304 | bytes 2392064 | tf_op jit(solution)/shard_map/dot_general | solution.py:189
  84.1 7.1 %all-to-all-start.2 = ((bf16[16,32,2048]{2,1,0:T(8,128)(2,1)}), bf16[16,32,2048]{2,1,0:T(8,128)(2,1)}, u32[]{:S(2)}, u32[]{:S(2)}) async-start(bf16[16,32,2048]{2,1,0:T(8,128)(2,1)} %bitcast.25), calls=%async_computation.2 | async-start | bytes 4194304 | tf_op jit(solution)/shard_map/all_to_all | solution.py:192
  91.2 19.4 %collective-permute-done.10 = bf16[1,1024,1408]{2,1,0:T(8,128)(2,1)} collective-permute-done((bf16[1,1024,1408]{2,1,0:T(8,128)(2,1)}, bf16[1,1024,1408]{2,1,0:T(8,128)(2,1)}, u32[]{:S(2)}, u32[]{:S(2)}) %collective-permute-start.10) | collective-permute-done | bytes 2883616 | tf_op jit(solution)/shard_map/ppermute | solution.py:29
  110.6 8.7 %maximum_select_fusion = bf16[2048,1408]{1,0:T(8,128)(2,1)} fusion(bf16[1024,1408]{1,0:T(8,128)(2,1)} %bitcast.30, bf16[1024,1408]{1,0:T(8,128)(2,1)} %bitcast.29, pred[]{:T(512)S(6)} %eq.98), kind=kLoop, calls=%fused_computation | loop fusion | flops 25952256 | bytes 11534337 | tf_op jit(solution)/shard_map/jit(_where)/select_n | solution.py:198
  119.2 3.5 %maximum_select_fusion.1 = bf16[704,2048]{1,0:T(8,128)(2,1)S(1)} fusion(bf16[704,1024]{1,0:T(8,128)(2,1)} %bitcast.28, bf16[704,1024]{1,0:T(8,128)(2,1)} %bitcast.27, pred[]{:T(512)S(6)} %eq.98), kind=kLoop, calls=%fused_computation.7 | loop fusion | flops 12976128 | bytes 5767169 | tf_op jit(solution)/shard_map/jit(_where)/select_n | solution.py:203
  122.8 15.9 %all-to-all-done.2 = bf16[16,32,2048]{2,1,0:T(8,128)(2,1)} async-done(((bf16[16,32,2048]{2,1,0:T(8,128)(2,1)}), bf16[16,32,2048]{2,1,0:T(8,128)(2,1)}, u32[]{:S(2)}, u32[]{:S(2)}) %all-to-all-start.2) | async-done | bytes 2097184 | tf_op jit(solution)/shard_map/all_to_all | solution.py:192
  138.7 6.4 %fusion.26 = f32[512,1408]{1,0:T(8,128)S(1)} fusion(bf16[512,2048]{1,0:T(8,128)(2,1)} %bitcast.26, bf16[2048,1408]{1,0:T(8,128)(2,1)} %maximum_select_fusion), kind=kOutput, calls=%fused_computation.80 | convolution fusion | flops 2952790016 | bytes 10747904 | tf_op jit(solution)/shard_map/dot_general | solution.py:212
  145.1 3.3 %convolution_convert_fusion = bf16[512,2048]{1,0:T(8,128)(2,1)} fusion(bf16[704,2048]{1,0:T(8,128)(2,1)S(1)} %maximum_select_fusion.1, f32[512,1408]{1,0:T(8,128)S(1)} %fusion.26), kind=kOutput, calls=%fused_computation.5 | convolution fusion | flops 1479606272 | bytes 8126464 | tf_op jit(solution)/shard_map/dot_general | solution.py:214
  148.3 5.0 %all-to-all-start.3 = ((bf16[16,32,2048]{2,1,0:T(8,128)(2,1)}), bf16[16,32,2048]{2,1,0:T(8,128)(2,1)S(1)}, u32[]{:S(2)}, u32[]{:S(2)}) async-start(bf16[16,32,2048]{2,1,0:T(8,128)(2,1)} %bitcast.76), calls=%async_computation.3 | async-start | bytes 4194304 | tf_op jit(solution)/shard_map/all_to_all | solution.py:215
  153.5 47.2 %all-to-all-done.3 = bf16[16,32,2048]{2,1,0:T(8,128)(2,1)S(1)} async-done(((bf16[16,32,2048]{2,1,0:T(8,128)(2,1)}), bf16[16,32,2048]{2,1,0:T(8,128)(2,1)S(1)}, u32[]{:S(2)}, u32[]{:S(2)}) %all-to-all-start.3) | async-done | bytes 2097184 | tf_op jit(solution)/shard_map/all_to_all | solution.py:215
  200.8 1.9 fusion.2
  (61 shorter events, 3.4 us)
Async XLA Ops:
  0.0 7.9 %copy-start = (s32[2,96]{1,0:T(2,128)S(1)}, s32[2,96]{1,0:T(2,128)}, u32[]{:S(2)}) copy-start(s32[2,96]{1,0:T(2,128)} %param.15) | copy-start | bytes 2308
  0.0 27.4 %copy-start.1 = (bf16[512,128]{1,0:T(8,128)(2,1)S(1)}, bf16[512,128]{1,0:T(8,128)(2,1)}, u32[]{:S(2)}) copy-start(bf16[512,128]{1,0:T(8,128)(2,1)} %param.18) | copy-start | bytes 393220
  0.0 10.8 %collective-permute-start.6 = (bf16[512,128]{1,0:T(8,128)(2,1)}, bf16[512,128]{1,0:T(8,128)(2,1)S(1)}, u32[]{:S(2)}, u32[]{:S(2)}) collective-permute-start(bf16[512,128]{1,0:T(8,128)(2,1)} %param.18), channel_id=1, source_target_pairs={{0,28},{1,29},{2,30},{3,31},{4,24},{5,25},{6,26},{7,27},{8,20},{9,... | collective-permute-start | bytes 393224 | tf_op jit(solution)/shard_map/ppermute | solution.py:89
  2.3 10.7 %collective-permute-start = (bf16[512,128]{1,0:T(8,128)(2,1)}, bf16[512,128]{1,0:T(8,128)(2,1)S(1)}, u32[]{:S(2)}, u32[]{:S(2)}) collective-permute-start(bf16[512,128]{1,0:T(8,128)(2,1)} %param.18), channel_id=1, source_target_pairs={{0,16},{1,17},{2,18},{3,19},{4,20},{5,21},{6,22},{7,23},{8,24},{9,... | collective-permute-start | bytes 393224 | tf_op jit(solution)/shard_map/ppermute | solution.py:89
  2.5 12.5 %collective-permute-start.1 = (bf16[512,128]{1,0:T(8,128)(2,1)}, bf16[512,128]{1,0:T(8,128)(2,1)S(1)}, u32[]{:S(2)}, u32[]{:S(2)}) collective-permute-start(bf16[512,128]{1,0:T(8,128)(2,1)} %param.18), channel_id=1, source_target_pairs={{0,4},{1,5},{2,6},{3,7},{4,0},{5,1},{6,2},{7,3},{8,12},{9,13},{10,... | collective-permute-start | bytes 393224 | tf_op jit(solution)/shard_map/ppermute | solution.py:86
  4.7 11.4 %collective-permute-start.2 = (bf16[512,128]{1,0:T(8,128)(2,1)}, bf16[512,128]{1,0:T(8,128)(2,1)S(1)}, u32[]{:S(2)}, u32[]{:S(2)}) collective-permute-start(bf16[512,128]{1,0:T(8,128)(2,1)} %param.18), channel_id=1, source_target_pairs={{0,20},{1,21},{2,22},{3,23},{4,16},{5,17},{6,18},{7,19},{8,28},{9,... | collective-permute-start | bytes 393224 | tf_op jit(solution)/shard_map/ppermute | solution.py:89
  5.6 10.8 %collective-permute-start.3 = (bf16[512,128]{1,0:T(8,128)(2,1)}, bf16[512,128]{1,0:T(8,128)(2,1)S(1)}, u32[]{:S(2)}, u32[]{:S(2)}) collective-permute-start(bf16[512,128]{1,0:T(8,128)(2,1)} %param.18), channel_id=1, source_target_pairs={{0,8},{1,9},{2,10},{3,11},{4,12},{5,13},{6,14},{7,15},{8,0},{9,1},... | collective-permute-start | bytes 393224 | tf_op jit(solution)/shard_map/ppermute | solution.py:86
  10.8 13.0 %collective-permute-start.4 = (bf16[512,128]{1,0:T(8,128)(2,1)}, bf16[512,128]{1,0:T(8,128)(2,1)S(1)}, u32[]{:S(2)}, u32[]{:S(2)}) collective-permute-start(bf16[512,128]{1,0:T(8,128)(2,1)} %param.18), channel_id=1, source_target_pairs={{0,24},{1,25},{2,26},{3,27},{4,28},{5,29},{6,30},{7,31},{8,16},{9,... | collective-permute-start | bytes 393224 | tf_op jit(solution)/shard_map/ppermute | solution.py:89
  13.0 14.5 %collective-permute-start.5 = (bf16[512,128]{1,0:T(8,128)(2,1)}, bf16[512,128]{1,0:T(8,128)(2,1)S(1)}, u32[]{:S(2)}, u32[]{:S(2)}) collective-permute-start(bf16[512,128]{1,0:T(8,128)(2,1)} %param.18), channel_id=1, source_target_pairs={{0,12},{1,13},{2,14},{3,15},{4,8},{5,9},{6,10},{7,11},{8,4},{9,5},... | collective-permute-start | bytes 393224 | tf_op jit(solution)/shard_map/ppermute | solution.py:86
  15.0 67.0 %collective-permute-start.9 = (bf16[1,704,1024]{2,1,0:T(8,128)(2,1)}, bf16[1,704,1024]{2,1,0:T(8,128)(2,1)}, u32[]{:S(2)}, u32[]{:S(2)}) collective-permute-start(bf16[1,704,1024]{2,1,0:T(8,128)(2,1)} %param.23), channel_id=1, source_target_pairs={{0,16},{16,0},{1,17},{17,1},{2,18},{18,2},{3,19},{19,3},{4,20},{20... | collective-permute-start | bytes 4325384 | tf_op jit(solution)/shard_map/ppermute | solution.py:29
  16.1 94.5 %collective-permute-start.10 = (bf16[1,1024,1408]{2,1,0:T(8,128)(2,1)}, bf16[1,1024,1408]{2,1,0:T(8,128)(2,1)}, u32[]{:S(2)}, u32[]{:S(2)}) collective-permute-start(bf16[1,1024,1408]{2,1,0:T(8,128)(2,1)} %param.22), channel_id=1, source_target_pairs={{0,16},{16,0},{1,17},{17,1},{2,18},{18,2},{3,19},{19,3},{4,20},{20... | collective-permute-start | bytes 8650760 | tf_op jit(solution)/shard_map/ppermute | solution.py:29
  27.7 1.5 copy-start.6
  28.3 7.6 %copy-start.7 = (s32[1,16]{1,0:T(1,128)S(1)}, s32[1,16]{1,0:T(1,128)}, u32[]{:S(2)}) copy-start(s32[1,16]{1,0:T(1,128)} %param.17) | copy-start | bytes 196
  28.8 31.9 %collective-permute-start.7 = (bf16[4,1024,128]{2,1,0:T(8,128)(2,1)S(1)}, bf16[4,1024,128]{2,1,0:T(8,128)(2,1)S(1)}, u32[]{:S(2)}, u32[]{:S(2)}) collective-permute-start(bf16[4,1024,128]{2,1,0:T(8,128)(2,1)S(1)} %pad_maximum_fusion.1), channel_id=1, source_target_pairs={{0,2},{1,3},{2,0},{3,1},{4,6},{5,7},{6,4},{7,5},{8,10},{9,11},{10,... | collective-permute-start | bytes 3145736 | tf_op jit(solution)/shard_map/ppermute | solution.py:146
  29.9 33.5 %all-to-all-start = ((bf16[16,224,128]{2,1,0:T(8,128)(2,1)}), bf16[16,224,128]{2,1,0:T(8,128)(2,1)S(1)}, u32[]{:S(2)}, u32[]{:S(2)}) async-start(bf16[16,224,128]{2,1,0:T(8,128)(2,1)} %pad_maximum_fusion.2), calls=%async_computation | async-start | bytes 1835008 | tf_op jit(solution)/shard_map/all_to_all | solution.py:122
  61.0 17.6 %collective-permute-start.8 = (bf16[8,1024,128]{2,1,0:T(8,128)(2,1)S(1)}, bf16[8,1024,128]{2,1,0:T(8,128)(2,1)}, u32[]{:S(2)}, u32[]{:S(2)}) collective-permute-start(bf16[8,1024,128]{2,1,0:T(8,128)(2,1)S(1)} %pad_maximum_fusion), channel_id=1, source_target_pairs={{0,1},{1,0},{2,3},{3,2},{4,5},{5,4},{6,7},{7,6},{8,9},{9,8},{10,11... | collective-permute-start | bytes 6291464 | tf_op jit(solution)/shard_map/ppermute | solution.py:151
  65.7 7.1 %copy-start.3 = (s32[64,6]{0,1:T(8,128)S(1)}, s32[64,6]{0,1:T(8,128)}, u32[]{:S(2)}) copy-start(s32[64,6]{0,1:T(8,128)} %param.20) | copy-start | bytes 4612
  67.1 10.9 %all-to-all-start.1 = ((bf16[16,32,128]{2,1,0:T(8,128)(2,1)}), bf16[16,32,128]{2,1,0:T(8,128)(2,1)S(1)}, u32[]{:S(2)}, u32[]{:S(2)}) async-start(bf16[16,32,128]{2,1,0:T(8,128)(2,1)} %bitcast.19), calls=%async_computation.1 | async-start | bytes 262144 | tf_op jit(solution)/shard_map/all_to_all | solution.py:140
  78.6 3.0 %copy-start.2 = (bf16[64,2048]{1,0:T(8,128)(2,1)S(1)}, bf16[64,2048]{1,0:T(8,128)(2,1)}, u32[]{:S(2)}) copy-start(bf16[64,2048]{1,0:T(8,128)(2,1)} %param.13) | copy-start | bytes 786436
  78.6 3.2 %copy-start.4 = (f32[2048]{0:T(1024)S(1)}, f32[2048]{0:T(1024)}, u32[]{:S(2)}) copy-start(f32[2048]{0:T(1024)} %param.19) | copy-start | bytes 24580
  84.1 54.6 %all-to-all-start.2 = ((bf16[16,32,2048]{2,1,0:T(8,128)(2,1)}), bf16[16,32,2048]{2,1,0:T(8,128)(2,1)}, u32[]{:S(2)}, u32[]{:S(2)}) async-start(bf16[16,32,2048]{2,1,0:T(8,128)(2,1)} %bitcast.25), calls=%async_computation.2 | async-start | bytes 4194304 | tf_op jit(solution)/shard_map/all_to_all | solution.py:192
  148.3 5.0 %copy-start.5 = (f32[64,6]{0,1:T(8,128)S(1)}, f32[64,6]{0,1:T(8,128)}, u32[]{:S(2)}) copy-start(f32[64,6]{0,1:T(8,128)} %param.21) | copy-start | bytes 4612
  148.3 52.4 %all-to-all-start.3 = ((bf16[16,32,2048]{2,1,0:T(8,128)(2,1)}), bf16[16,32,2048]{2,1,0:T(8,128)(2,1)S(1)}, u32[]{:S(2)}, u32[]{:S(2)}) async-start(bf16[16,32,2048]{2,1,0:T(8,128)(2,1)} %bitcast.76), calls=%async_computation.3 | async-start | bytes 4194304 | tf_op jit(solution)/shard_map/all_to_all | solution.py:215

commit v21 on v16

--- a/solution.py
+++ b/solution.py
@@ -77,7 +77,36 @@
     kv_send = jnp.concatenate([q_out, kv_out], axis=1)
     if n_mp == 1 << bits:
         block = wo_rows[None]
-        if bits > 1:
+        steps = min(3, bits - 1)
+        if steps > 1 and n_dp == 2:
+            tops = [bits - 1 - i for i in range(steps)]
+            fetched = []
+            for code in range(1 << steps):
+                off = sum(((code >> i) & 1) << t for i, t in enumerate(tops))
+                near = out_weight if off == 0 else lax.ppermute(
+                    out_weight, "mp", [(m, m ^ off) for m in range(n_mp)]
+                )
+                other = lax.ppermute(
+                    out_weight,
+                    ("dp", "mp"),
+                    [(d * n_mp + m, (1 - d) * n_mp + (m ^ off)) for d in range(2) for m in range(n_mp)],
+                )
+                fetched.append(
+                    jnp.where(
+                        row_index == 0,
+                        jnp.concatenate([near, other], axis=0),
+                        jnp.concatenate([other, near], axis=0),
+                    )
+                )
+            fetched = jnp.stack(fetched)
+            mine = [(column >> t) % 2 for t in tops]
+            shards = []
+            for j in range(1 << steps):
+                want = [(j >> i) & 1 for i in range(steps)]
+                code = sum((mine[i] ^ want[i]) << i for i in range(steps))
+                shards.append(lax.dynamic_index_in_dim(fetched, code, 0, keepdims=False))
+            block = jnp.stack(shards)
+        elif bits > 1:
             b = bits - 1
             pair = lax.ppermute(block, "mp", [(m, m ^ (1 << b)) for m in range(n_mp)])
             low = (column >> b) % 2 == 0
@@ -108,7 +137,7 @@
 
     bits = n_mp.bit_length() - 1
     if n_mp == 1 << bits:
-        for b in reversed(range(1, bits - 1)):
+        for b in reversed(range(1, bits - steps if n_dp == 2 and steps > 1 else bits - 1)):
             pair = lax.ppermute(block, "mp", [(m, m ^ (1 << b)) for m in range(n_mp)])
             low = (column >> b) % 2 == 0
             block = jnp.concatenate(

time: 209 us -> 245 us (1.17)
  waiting for transfers between devices: 129 us -> 158 us
  starting transfers between devices: 36.5 us -> 44.1 us
    ppermute x3 -> x2, waiting for transfers between devices: 7.89 us -> 59 us  [swap_dp(): return lax.ppermute(x, 'dp', [(0, 1), (1, 0)])]
    all_to_all x1, waiting for transfers between devices: 32.9 us -> 0.01 us  [on_device(): lax.all_to_all(sending.reshape(n_mp, capacity, d_model), 'mp', split_axis...]
    all_to_all x1, waiting for transfers between devices: 0.01 us -> 19.1 us  [on_device(): lax.all_to_all(kv_send, 'mp', split_axis=0, concat_axis=0, tiled=True)]
    ppermute x3 -> x15, starting transfers between devices: 2.7 us -> 16.7 us  [the longest x7 9.78 us: on_device(): lax.ppermute(out_weight, 'mp', [(m, m ^ off) for m in range(n_mp)])]
    ppermute x3 -> x15, waiting for transfers between devices: 35.8 us -> 28.1 us  [the longest x8 21 us: on_device(): lax.ppermute(out_weight, ('dp', 'mp'), [(d * n_mp + m, (1 - d) * n_mp + (...]
    all_to_all x1, starting transfers between devices: 8.27 us -> 4.95 us  [on_device(): lax.all_to_all(blended.reshape(n_mp, sub, HD), 'mp', split_axis=0, concat...]
    all_to_all x1, starting transfers between devices: 7.82 us -> 4.67 us  [on_device(): lax.all_to_all(kv_send, 'mp', split_axis=0, concat_axis=0, tiled=True)]
    ppermute x1, starting transfers between devices: 2.93 us -> 0.43 us  [on_device(): pair = lax.ppermute(block, 'mp', [(m, m ^ 1) for m in range(n_mp)])]
  transfers between devices with their start and end apart: 11 -> 22, of which waited for: 8 -> 12; matrix products, arithmetic and copies ran while one was open for 14% -> 11% of each run, Pallas kernels for 0% -> 0%
where the time goes in v21:
time: 245 us
  waiting for transfers between devices  158 us (64%)
  starting transfers between devices  44.1 us (18%)
  matrix products  18.4 us (8%)
  other arithmetic  16.2 us (7%)
  local copies, waits for them, and re-layouts  7.01 us (3%)
    ppermute x2, waiting for transfers between devices, swap_dp(): return lax.ppermute(x, 'dp', [(0, 1), (1, 0)])  59 us
    all_to_all x1, waiting for transfers between devices, on_device(): lax.all_to_all(outcome.reshape(n_mp, capacity, d_model), 'mp', split_axis...  47.2 us
    ppermute x8, waiting for transfers between devices, on_device(): lax.ppermute(out_weight, ('dp', 'mp'), [(d * n_mp + m, (1 - d) * n_mp + (...  21 us
    all_to_all x1, waiting for transfers between devices, on_device(): lax.all_to_all(kv_send, 'mp', split_axis=0, concat_axis=0, tiled=True)  19.1 us
    ppermute x7, starting transfers between devices, on_device(): lax.ppermute(out_weight, 'mp', [(m, m ^ off) for m in range(n_mp)])  9.78 us
    select_n x1, other arithmetic, on_device(): jnp.where(first, jnp.concatenate([experts_in[0], in_other[0]], axis=0), j...  7.43 us
    all_to_all x1, starting transfers between devices, on_device(): lax.all_to_all(sending.reshape(n_mp, capacity, d_model), 'mp', split_axis...  7.07 us
    ppermute x7, waiting for transfers between devices, on_device(): lax.ppermute(out_weight, 'mp', [(m, m ^ off) for m in range(n_mp)])  7.03 us
  transfers between devices with their start and end apart: 22, of which 12 were waited for; matrix products, arithmetic and copies ran while one was open for 11% of the time, Pallas kernels for 0%

profile of v21, /device:TPU:11, one launch (start us, length us, event | category | flops | bytes accessed | tf_op | source)
XLA Modules:
  0.0 244.7 jit_solution(2987444626017422499)
XLA Ops:
  0.0 1.2 collective-permute-start
  1.2 2.3 collective-permute-start.1
  3.7 2.2 collective-permute-start.4
  6.0 1.2 reshape.612
  7.2 0.3 copy.66
  7.5 1.0 copy.77
  8.8 0.6 tile.8
  9.4 1.0 pad_maximum_fusion
  10.4 0.8 reduce-window.6
  11.3 1.3 collective-permute-start.6
  12.9 2.5 %collective-permute-done.2 = bf16[512,128]{1,0:T(8,128)(2,1)S(1)} collective-permute-done((bf16[512,128]{1,0:T(8,128)(2,1)}, bf16[512,128]{1,0:T(8,128)(2,1)S(1)}, u32[]{:S(2)}, u32[]{:S(2)}) %collective-permute-start.2) | collective-permute-done | bytes 131104 | tf_op jit(solution)/shard_map/ppermute | solution.py:89
  15.8 1.2 collective-permute-start.8
  17.0 4.2 %collective-permute-start.9 = (bf16[512,128]{1,0:T(8,128)(2,1)S(1)}, bf16[512,128]{1,0:T(8,128)(2,1)S(1)}, u32[]{:S(2)}, u32[]{:S(2)}) collective-permute-start(bf16[512,128]{1,0:T(8,128)(2,1)S(1)} %copy-done.2), channel_id=1, source_target_pairs={{0,10},{1,11},{2,8},{3,9},{4,14},{5,15},{6,12},{7,13},{8,2},{9,3},... | collective-permute-start | bytes 393224 | tf_op jit(solution)/shard_map/ppermute | solution.py:86
  21.3 4.8 %collective-permute-done.6 = bf16[512,128]{1,0:T(8,128)(2,1)S(1)} collective-permute-done((bf16[512,128]{1,0:T(8,128)(2,1)S(1)}, bf16[512,128]{1,0:T(8,128)(2,1)S(1)}, u32[]{:S(2)}, u32[]{:S(2)}) %collective-permute-start.6) | collective-permute-done | bytes 131104 | tf_op jit(solution)/shard_map/ppermute | solution.py:89
  26.1 4.3 %collective-permute-done.5 = bf16[512,128]{1,0:T(8,128)(2,1)S(1)} collective-permute-done((bf16[512,128]{1,0:T(8,128)(2,1)S(1)}, bf16[512,128]{1,0:T(8,128)(2,1)S(1)}, u32[]{:S(2)}, u32[]{:S(2)}) %collective-permute-start.5) | collective-permute-done | bytes 131104 | tf_op jit(solution)/shard_map/ppermute | solution.py:86
  30.4 2.4 collective-permute-start.11
  33.4 2.2 collective-permute-done.9
  35.6 0.8 collective-permute-start.14
  36.4 2.5 %collective-permute-done.10 = bf16[512,128]{1,0:T(8,128)(2,1)S(1)} collective-permute-done((bf16[512,128]{1,0:T(8,128)(2,1)S(1)}, bf16[512,128]{1,0:T(8,128)(2,1)S(1)}, u32[]{:S(2)}, u32[]{:S(2)}) %collective-permute-start.10) | collective-permute-done | bytes 131104 | tf_op jit(solution)/shard_map/ppermute | solution.py:89
  39.0 0.5 collective-permute-done.11
  39.5 8.4 %collective-permute-done.12 = bf16[512,128]{1,0:T(8,128)(2,1)S(1)} collective-permute-done((bf16[512,128]{1,0:T(8,128)(2,1)S(1)}, bf16[512,128]{1,0:T(8,128)(2,1)S(1)}, u32[]{:S(2)}, u32[]{:S(2)}) %collective-permute-start.12) | collective-permute-done | bytes 131104 | tf_op jit(solution)/shard_map/ppermute | solution.py:89
  48.1 2.8 %collective-permute-done.14 = bf16[512,128]{1,0:T(8,128)(2,1)S(1)} collective-permute-done((bf16[512,128]{1,0:T(8,128)(2,1)S(1)}, bf16[512,128]{1,0:T(8,128)(2,1)S(1)}, u32[]{:S(2)}, u32[]{:S(2)}) %collective-permute-start.14) | collective-permute-done | bytes 131104 | tf_op jit(solution)/shard_map/ppermute | solution.py:89
  51.4 4.7 %all-to-all-start = ((bf16[16,224,128]{2,1,0:T(8,128)(2,1)}), bf16[16,224,128]{2,1,0:T(8,128)(2,1)S(1)}, u32[]{:S(2)}, u32[]{:S(2)}) async-start(bf16[16,224,128]{2,1,0:T(8,128)(2,1)} %pad_maximum_fusion), calls=%async_computation | async-start | bytes 1835008 | tf_op jit(solution)/shard_map/all_to_all | solution.py:117
  56.5 0.6 dynamic_slice.32
  57.4 0.7 fusion.27
  58.2 0.4 collective-permute-start.15
  59.0 19.1 %all-to-all-done = bf16[16,224,128]{2,1,0:T(8,128)(2,1)S(1)} async-done(((bf16[16,224,128]{2,1,0:T(8,128)(2,1)}), bf16[16,224,128]{2,1,0:T(8,128)(2,1)S(1)}, u32[]{:S(2)}, u32[]{:S(2)}) %all-to-all-start) | async-done | bytes 917536 | tf_op jit(solution)/shard_map/all_to_all | solution.py:117
  78.2 0.5 copy.67
  79.2 0.7 fusion.32
  79.9 0.6 fusion.1
  80.5 1.4 fusion.5
  81.8 4.9 %all-to-all-start.1 = ((bf16[16,32,128]{2,1,0:T(8,128)(2,1)}), bf16[16,32,128]{2,1,0:T(8,128)(2,1)S(1)}, u32[]{:S(2)}, u32[]{:S(2)}) async-start(bf16[16,32,128]{2,1,0:T(8,128)(2,1)} %bitcast.27), calls=%async_computation.1 | async-start | bytes 262144 | tf_op jit(solution)/shard_map/all_to_all | solution.py:135
  87.0 5.0 %all-to-all-done.1 = bf16[16,32,128]{2,1,0:T(8,128)(2,1)S(1)} async-done(((bf16[16,32,128]{2,1,0:T(8,128)(2,1)}), bf16[16,32,128]{2,1,0:T(8,128)(2,1)S(1)}, u32[]{:S(2)}, u32[]{:S(2)}) %all-to-all-start.1) | async-done | bytes 131104 | tf_op jit(solution)/shard_map/all_to_all | solution.py:135
  92.1 0.5 fusion.33
  92.6 2.1 fusion.34
  94.7 0.4 copy.71
  95.1 0.4 reshape.618
  96.0 2.1 convolution_convert_fusion.1
  98.1 7.1 %all-to-all-start.2 = ((bf16[16,32,2048]{2,1,0:T(8,128)(2,1)}), bf16[16,32,2048]{2,1,0:T(8,128)(2,1)}, u32[]{:S(2)}, u32[]{:S(2)}) async-start(bf16[16,32,2048]{2,1,0:T(8,128)(2,1)} %bitcast.33), calls=%async_computation.2 | async-start | bytes 4194304 | tf_op jit(solution)/shard_map/all_to_all | solution.py:187
  105.2 3.6 %collective-permute-start.17 = (bf16[1,1024,1408]{2,1,0:T(8,128)(2,1)}, bf16[1,1024,1408]{2,1,0:T(8,128)(2,1)S(1)}, u32[]{:S(2)}, u32[]{:S(2)}) collective-permute-start(bf16[1,1024,1408]{2,1,0:T(8,128)(2,1)} %param.22), channel_id=1, source_target_pairs={{0,16},{16,0},{1,17},{17,1},{2,18},{18,2},{3,19},{19,3},{4,20},{20... | collective-permute-start | bytes 8650760 | tf_op jit(solution)/shard_map/ppermute | solution.py:29
  108.7 3.7 %maximum_select_fusion.1 = bf16[704,2048]{1,0:T(8,128)(2,1)S(1)} fusion(bf16[704,1024]{1,0:T(8,128)(2,1)} %bitcast.36, bf16[704,1024]{1,0:T(8,128)(2,1)} %bitcast.35, pred[]{:T(512)S(6)} %eq.81), kind=kLoop, calls=%fused_computation.7 | loop fusion | flops 12976128 | bytes 5767169 | tf_op jit(solution)/shard_map/jit(_where)/select_n | solution.py:198
  112.5 59.0 %collective-permute-done.17 = bf16[1,1024,1408]{2,1,0:T(8,128)(2,1)S(1)} collective-permute-done((bf16[1,1024,1408]{2,1,0:T(8,128)(2,1)}, bf16[1,1024,1408]{2,1,0:T(8,128)(2,1)S(1)}, u32[]{:S(2)}, u32[]{:S(2)}) %collective-permute-start.17) | collective-permute-done | bytes 2883616 | tf_op jit(solution)/shard_map/ppermute | solution.py:29
  171.5 7.4 %maximum_select_fusion = bf16[2048,1408]{1,0:T(8,128)(2,1)} fusion(bf16[1024,1408]{1,0:T(8,128)(2,1)S(1)} %bitcast.84, bf16[1024,1408]{1,0:T(8,128)(2,1)} %bitcast.37, pred[]{:T(512)S(6)} %eq.81), kind=kLoop, calls=%fused_computation | loop fusion | flops 25952256 | bytes 11534337 | tf_op jit(solution)/shard_map/jit(_where)/select_n | solution.py:193
  179.0 6.4 %fusion.35 = f32[512,1408]{1,0:T(8,128)S(1)} fusion(bf16[512,2048]{1,0:T(8,128)(2,1)} %bitcast.34, bf16[2048,1408]{1,0:T(8,128)(2,1)} %maximum_select_fusion), kind=kOutput, calls=%fused_computation.89 | convolution fusion | flops 2952790016 | bytes 10747904 | tf_op jit(solution)/shard_map/dot_general | solution.py:207
  185.4 3.3 %convolution_convert_fusion = bf16[512,2048]{1,0:T(8,128)(2,1)} fusion(bf16[704,2048]{1,0:T(8,128)(2,1)S(1)} %maximum_select_fusion.1, f32[512,1408]{1,0:T(8,128)S(1)} %fusion.35), kind=kOutput, calls=%fused_computation.5 | convolution fusion | flops 1479606272 | bytes 8126464 | tf_op jit(solution)/shard_map/dot_general | solution.py:209
  188.6 6.7 %all-to-all-start.3 = ((bf16[16,32,2048]{2,1,0:T(8,128)(2,1)}), bf16[16,32,2048]{2,1,0:T(8,128)(2,1)S(1)}, u32[]{:S(2)}, u32[]{:S(2)}) async-start(bf16[16,32,2048]{2,1,0:T(8,128)(2,1)} %bitcast.85), calls=%async_computation.3 | async-start | bytes 4194304 | tf_op jit(solution)/shard_map/all_to_all | solution.py:210
  195.5 47.2 %all-to-all-done.3 = bf16[16,32,2048]{2,1,0:T(8,128)(2,1)S(1)} async-done(((bf16[16,32,2048]{2,1,0:T(8,128)(2,1)}), bf16[16,32,2048]{2,1,0:T(8,128)(2,1)S(1)}, u32[]{:S(2)}, u32[]{:S(2)}) %all-to-all-start.3) | async-done | bytes 2097184 | tf_op jit(solution)/shard_map/all_to_all | solution.py:210
  242.8 1.9 fusion.2
  (84 shorter events, 5.0 us)
Async XLA Ops:
  0.0 57.1 %copy-start = (s32[2,96]{1,0:T(2,128)S(1)}, s32[2,96]{1,0:T(2,128)}, u32[]{:S(2)}) copy-start(s32[2,96]{1,0:T(2,128)} %param.15) | copy-start | bytes 2308
  0.0 8.6 %copy-start.3 = (s32[64,6]{0,1:T(8,128)S(1)}, s32[64,6]{0,1:T(8,128)}, u32[]{:S(2)}) copy-start(s32[64,6]{0,1:T(8,128)} %param.20) | copy-start | bytes 4612
  0.0 11.3 %collective-permute-start = (bf16[512,128]{1,0:T(8,128)(2,1)}, bf16[512,128]{1,0:T(8,128)(2,1)S(1)}, u32[]{:S(2)}, u32[]{:S(2)}) collective-permute-start(bf16[512,128]{1,0:T(8,128)(2,1)} %param.18), channel_id=1, source_target_pairs={{0,16},{1,17},{2,18},{3,19},{4,20},{5,21},{6,22},{7,23},{8,24},{9,... | collective-permute-start | bytes 393224 | tf_op jit(solution)/shard_map/ppermute | solution.py:89
  1.2 11.4 %collective-permute-start.1 = (bf16[512,128]{1,0:T(8,128)(2,1)}, bf16[512,128]{1,0:T(8,128)(2,1)S(1)}, u32[]{:S(2)}, u32[]{:S(2)}) collective-permute-start(bf16[512,128]{1,0:T(8,128)(2,1)} %param.18), channel_id=1, source_target_pairs={{0,8},{1,9},{2,10},{3,11},{4,12},{5,13},{6,14},{7,15},{8,0},{9,1},... | collective-permute-start | bytes 393224 | tf_op jit(solution)/shard_map/ppermute | solution.py:86
  3.6 11.9 %collective-permute-start.2 = (bf16[512,128]{1,0:T(8,128)(2,1)}, bf16[512,128]{1,0:T(8,128)(2,1)S(1)}, u32[]{:S(2)}, u32[]{:S(2)}) collective-permute-start(bf16[512,128]{1,0:T(8,128)(2,1)} %param.18), channel_id=1, source_target_pairs={{0,24},{1,25},{2,26},{3,27},{4,28},{5,29},{6,30},{7,31},{8,16},{9,... | collective-permute-start | bytes 393224 | tf_op jit(solution)/shard_map/ppermute | solution.py:89
  3.6 12.2 %collective-permute-start.3 = (bf16[512,128]{1,0:T(8,128)(2,1)}, bf16[512,128]{1,0:T(8,128)(2,1)S(1)}, u32[]{:S(2)}, u32[]{:S(2)}) collective-permute-start(bf16[512,128]{1,0:T(8,128)(2,1)} %param.18), channel_id=1, source_target_pairs={{0,4},{1,5},{2,6},{3,7},{4,0},{5,1},{6,2},{7,3},{8,12},{9,13},{10,... | collective-permute-start | bytes 393224 | tf_op jit(solution)/shard_map/ppermute | solution.py:86
  3.7 13.3 %collective-permute-start.4 = (bf16[512,128]{1,0:T(8,128)(2,1)}, bf16[512,128]{1,0:T(8,128)(2,1)S(1)}, u32[]{:S(2)}, u32[]{:S(2)}) collective-permute-start(bf16[512,128]{1,0:T(8,128)(2,1)} %param.18), channel_id=1, source_target_pairs={{0,20},{1,21},{2,22},{3,23},{4,16},{5,17},{6,18},{7,19},{8,28},{9,... | collective-permute-start | bytes 393224 | tf_op jit(solution)/shard_map/ppermute | solution.py:89
  7.5 3.8 %copy-start.2 = (bf16[512,128]{1,0:T(8,128)(2,1)S(1)}, bf16[512,128]{1,0:T(8,128)(2,1)}, u32[]{:S(2)}) copy-start(bf16[512,128]{1,0:T(8,128)(2,1)} %param.18) | copy-start | bytes 393220
  11.3 14.8 %collective-permute-start.6 = (bf16[512,128]{1,0:T(8,128)(2,1)S(1)}, bf16[512,128]{1,0:T(8,128)(2,1)S(1)}, u32[]{:S(2)}, u32[]{:S(2)}) collective-permute-start(bf16[512,128]{1,0:T(8,128)(2,1)S(1)} %copy-done.2), channel_id=1, source_target_pairs={{0,28},{1,29},{2,30},{3,31},{4,24},{5,25},{6,26},{7,27},{8,20},{9,... | collective-permute-start | bytes 393224 | tf_op jit(solution)/shard_map/ppermute | solution.py:89
  12.7 17.7 %collective-permute-start.5 = (bf16[512,128]{1,0:T(8,128)(2,1)S(1)}, bf16[512,128]{1,0:T(8,128)(2,1)S(1)}, u32[]{:S(2)}, u32[]{:S(2)}) collective-permute-start(bf16[512,128]{1,0:T(8,128)(2,1)S(1)} %copy-done.2), channel_id=1, source_target_pairs={{0,12},{1,13},{2,14},{3,15},{4,8},{5,9},{6,10},{7,11},{8,4},{9,5},... | collective-permute-start | bytes 393224 | tf_op jit(solution)/shard_map/ppermute | solution.py:86
  15.4 17.5 %collective-permute-start.7 = (bf16[512,128]{1,0:T(8,128)(2,1)S(1)}, bf16[512,128]{1,0:T(8,128)(2,1)S(1)}, u32[]{:S(2)}, u32[]{:S(2)}) collective-permute-start(bf16[512,128]{1,0:T(8,128)(2,1)S(1)} %copy-done.2), channel_id=1, source_target_pairs={{0,2},{1,3},{2,0},{3,1},{4,6},{5,7},{6,4},{7,5},{8,10},{9,11},{10,... | collective-permute-start | bytes 393224 | tf_op jit(solution)/shard_map/ppermute | solution.py:86
  15.8 17.2 %collective-permute-start.8 = (bf16[512,128]{1,0:T(8,128)(2,1)S(1)}, bf16[512,128]{1,0:T(8,128)(2,1)S(1)}, u32[]{:S(2)}, u32[]{:S(2)}) collective-permute-start(bf16[512,128]{1,0:T(8,128)(2,1)S(1)} %copy-done.2), channel_id=1, source_target_pairs={{0,18},{1,19},{2,16},{3,17},{4,22},{5,23},{6,20},{7,21},{8,26},{9,... | collective-permute-start | bytes 393224 | tf_op jit(solution)/shard_map/ppermute | solution.py:89
  17.0 18.6 %collective-permute-start.9 = (bf16[512,128]{1,0:T(8,128)(2,1)S(1)}, bf16[512,128]{1,0:T(8,128)(2,1)S(1)}, u32[]{:S(2)}, u32[]{:S(2)}) collective-permute-start(bf16[512,128]{1,0:T(8,128)(2,1)S(1)} %copy-done.2), channel_id=1, source_target_pairs={{0,10},{1,11},{2,8},{3,9},{4,14},{5,15},{6,12},{7,13},{8,2},{9,3},... | collective-permute-start | bytes 393224 | tf_op jit(solution)/shard_map/ppermute | solution.py:86
  26.1 12.8 %collective-permute-start.10 = (bf16[512,128]{1,0:T(8,128)(2,1)S(1)}, bf16[512,128]{1,0:T(8,128)(2,1)S(1)}, u32[]{:S(2)}, u32[]{:S(2)}) collective-permute-start(bf16[512,128]{1,0:T(8,128)(2,1)S(1)} %copy-done.2), channel_id=1, source_target_pairs={{0,26},{1,27},{2,24},{3,25},{4,30},{5,31},{6,28},{7,29},{8,18},{9,... | collective-permute-start | bytes 393224 | tf_op jit(solution)/shard_map/ppermute | solution.py:89
  30.4 9.1 %collective-permute-start.11 = (bf16[512,128]{1,0:T(8,128)(2,1)S(1)}, bf16[512,128]{1,0:T(8,128)(2,1)S(1)}, u32[]{:S(2)}, u32[]{:S(2)}) collective-permute-start(bf16[512,128]{1,0:T(8,128)(2,1)S(1)} %copy-done.2), channel_id=1, source_target_pairs={{0,6},{1,7},{2,4},{3,5},{4,2},{5,3},{6,0},{7,1},{8,14},{9,15},{10,... | collective-permute-start | bytes 393224 | tf_op jit(solution)/shard_map/ppermute | solution.py:86
  32.9 15.0 %collective-permute-start.12 = (bf16[512,128]{1,0:T(8,128)(2,1)S(1)}, bf16[512,128]{1,0:T(8,128)(2,1)S(1)}, u32[]{:S(2)}, u32[]{:S(2)}) collective-permute-start(bf16[512,128]{1,0:T(8,128)(2,1)S(1)} %copy-done.2), channel_id=1, source_target_pairs={{0,22},{1,23},{2,20},{3,21},{4,18},{5,19},{6,16},{7,17},{8,30},{9,... | collective-permute-start | bytes 393224 | tf_op jit(solution)/shard_map/ppermute | solution.py:89
  33.0 15.0 %collective-permute-start.13 = (bf16[512,128]{1,0:T(8,128)(2,1)S(1)}, bf16[512,128]{1,0:T(8,128)(2,1)S(1)}, u32[]{:S(2)}, u32[]{:S(2)}) collective-permute-start(bf16[512,128]{1,0:T(8,128)(2,1)S(1)} %copy-done.2), channel_id=1, source_target_pairs={{0,14},{1,15},{2,12},{3,13},{4,10},{5,11},{6,8},{7,9},{8,6},{9,7},... | collective-permute-start | bytes 393224 | tf_op jit(solution)/shard_map/ppermute | solution.py:86
  35.6 15.3 %collective-permute-start.14 = (bf16[512,128]{1,0:T(8,128)(2,1)S(1)}, bf16[512,128]{1,0:T(8,128)(2,1)S(1)}, u32[]{:S(2)}, u32[]{:S(2)}) collective-permute-start(bf16[512,128]{1,0:T(8,128)(2,1)S(1)} %copy-done.2), channel_id=1, source_target_pairs={{0,30},{1,31},{2,28},{3,29},{4,26},{5,27},{6,24},{7,25},{8,22},{9,... | collective-permute-start | bytes 393224 | tf_op jit(solution)/shard_map/ppermute | solution.py:89
  38.9 57.0 %collective-permute-start.16 = (bf16[1,704,1024]{2,1,0:T(8,128)(2,1)}, bf16[1,704,1024]{2,1,0:T(8,128)(2,1)}, u32[]{:S(2)}, u32[]{:S(2)}) collective-permute-start(bf16[1,704,1024]{2,1,0:T(8,128)(2,1)} %param.23), channel_id=1, source_target_pairs={{0,16},{16,0},{1,17},{17,1},{2,18},{18,2},{3,19},{19,3},{4,20},{20... | collective-permute-start | bytes 4325384 | tf_op jit(solution)/shard_map/ppermute | solution.py:29
  51.2 5.3 %copy-start.6 = (s32[2]{0:T(128)S(1)}, s32[2]{0:T(128)}, u32[]{:S(2)}) copy-start(s32[2]{0:T(128)} %param.16) | copy-start | bytes 28
  51.2 6.2 %copy-start.7 = (s32[1,16]{1,0:T(1,128)S(1)}, s32[1,16]{1,0:T(1,128)}, u32[]{:S(2)}) copy-start(s32[1,16]{1,0:T(1,128)} %param.17) | copy-start | bytes 196
  51.4 26.7 %all-to-all-start = ((bf16[16,224,128]{2,1,0:T(8,128)(2,1)}), bf16[16,224,128]{2,1,0:T(8,128)(2,1)S(1)}, u32[]{:S(2)}, u32[]{:S(2)}) async-start(bf16[16,224,128]{2,1,0:T(8,128)(2,1)} %pad_maximum_fusion), calls=%async_computation | async-start | bytes 1835008 | tf_op jit(solution)/shard_map/all_to_all | solution.py:117
  58.2 34.3 %collective-permute-start.15 = (bf16[8,1024,128]{2,1,0:T(8,128)(2,1)S(1)}, bf16[8,1024,128]{2,1,0:T(8,128)(2,1)}, u32[]{:S(2)}, u32[]{:S(2)}) collective-permute-start(bf16[8,1024,128]{2,1,0:T(8,128)(2,1)S(1)} %dynamic-slice_dynamic-update-slice_fusion), channel_id=1, source_target_pairs={{0,1},{1,0},{2,3},{3,2},{4,5},{5,4},{6,7},{7,6},{8,9},{9,8},{10,11... | collective-permute-start | bytes 6291464 | tf_op jit(solution)/shard_map/ppermute | solution.py:146
  81.8 10.1 %all-to-all-start.1 = ((bf16[16,32,128]{2,1,0:T(8,128)(2,1)}), bf16[16,32,128]{2,1,0:T(8,128)(2,1)S(1)}, u32[]{:S(2)}, u32[]{:S(2)}) async-start(bf16[16,32,128]{2,1,0:T(8,128)(2,1)} %bitcast.27), calls=%async_computation.1 | async-start | bytes 262144 | tf_op jit(solution)/shard_map/all_to_all | solution.py:135
  94.7 1.0 copy-start.1
  94.7 1.1 copy-start.4
  98.1 80.9 %all-to-all-start.2 = ((bf16[16,32,2048]{2,1,0:T(8,128)(2,1)}), bf16[16,32,2048]{2,1,0:T(8,128)(2,1)}, u32[]{:S(2)}, u32[]{:S(2)}) async-start(bf16[16,32,2048]{2,1,0:T(8,128)(2,1)} %bitcast.33), calls=%async_computation.2 | async-start | bytes 4194304 | tf_op jit(solution)/shard_map/all_to_all | solution.py:187
  105.2 66.4 %collective-permute-start.17 = (bf16[1,1024,1408]{2,1,0:T(8,128)(2,1)}, bf16[1,1024,1408]{2,1,0:T(8,128)(2,1)S(1)}, u32[]{:S(2)}, u32[]{:S(2)}) collective-permute-start(bf16[1,1024,1408]{2,1,0:T(8,128)(2,1)} %param.22), channel_id=1, source_target_pairs={{0,16},{16,0},{1,17},{17,1},{2,18},{18,2},{3,19},{19,3},{4,20},{20... | collective-permute-start | bytes 8650760 | tf_op jit(solution)/shard_map/ppermute | solution.py:29
  188.6 6.7 %copy-start.5 = (f32[64,6]{0,1:T(8,128)S(1)}, f32[64,6]{0,1:T(8,128)}, u32[]{:S(2)}) copy-start(f32[64,6]{0,1:T(8,128)} %param.21) | copy-start | bytes 4612
  188.6 54.1 %all-to-all-start.3 = ((bf16[16,32,2048]{2,1,0:T(8,128)(2,1)}), bf16[16,32,2048]{2,1,0:T(8,128)(2,1)S(1)}, u32[]{:S(2)}, u32[]{:S(2)}) async-start(bf16[16,32,2048]{2,1,0:T(8,128)(2,1)} %bitcast.85), calls=%async_computation.3 | async-start | bytes 4194304 | tf_op jit(solution)/shard_map/all_to_all | solution.py:210
